TPU v7x, 32 devices: a whole 2x2x4 slice. The times are simulated.
32 devices in a mesh: groups: 2 (over y), expert: 16 (over z, x, core).
Axes of the slice: x: 2, y: 2, z: 4, core: 2. Of those that a mesh axis runs over, the one named last changes fastest.
Arguments:
- tokens: bfloat16 [2048, 2048], P(('groups', 'expert')), parts along dimension 0, may hold values from -6 to 6
- expert_ids: int32 [2048, 8], P(('groups', 'expert')), parts along dimension 0, may hold values from 0 to 15, all different within a row; in each aligned block of 64 rows (0 to 63, 64 to 127, ...) at most 48 rows name the same one
- gate_scores: float32 [2048, 8], P(('groups', 'expert')), parts along dimension 0, may hold values from 0.05 to 1
- host_expert: int32 [16], replicated, may hold values from 0 to 15, each once
- w_in: bfloat16 [16, 2048, 1536], P('expert'), may hold values from -0.125 to 0.125
- w_down: bfloat16 [16, 768, 2048], P('expert'), may hold values from -0.625 to 0.625
Outputs:
- mixed: bfloat16 [2048, 2048], P(('groups', 'expert')), parts along dimension 0
There are 2 independent parts, one for each index of `groups`. A program takes and returns all parts, laid end to end along the dimension named above; an argument that names none is the same for every part. Nothing has to cross between parts.
Inputs may be any that keep to these rules, and one draw needn't show every extreme that they name: `expert_ids`: each token names 8 different experts; the tokens of one device name no expert more than 48 times, a bound that some block reaches. `host_expert`: each expert stands in exactly one slot.
All inputs are finite; a program needn't handle non-finite values.
Results may differ from a plain program's by a relative error of at most 0.0057.
Values may be sent and summed in bfloat16 or wider, within the bound.
No kernel may reach another device: no remote copies, remote signals or barrier semaphores. Data moves between devices by JAX's collectives and lax.ppermute only.
A program may use at most 64 MiB of HBM per device.

v0:
```python
import jax
import jax.numpy as jnp
from jax import lax
from jax.sharding import PartitionSpec as P


def expert_block(rows_in, gate_up, down_proj, hidden_width):
    pair = jnp.dot(rows_in, gate_up, preferred_element_type=jnp.float32)
    active = (jax.nn.silu(pair[:, :hidden_width]) * pair[:, hidden_width:]).astype(jnp.bfloat16)
    return jnp.dot(active, down_proj, preferred_element_type=jnp.float32).astype(jnp.bfloat16)


def shards(tokens, expert_ids, gate_scores, host_expert, w_in, w_down):
    tok_rows, width_model = tokens.shape
    top_count = expert_ids.shape[1]
    hosts = lax.axis_size("expert")
    experts = host_expert.shape[0]
    capacity = 3 * tok_rows * top_count // (2 * experts)
    hidden_width = w_down.shape[1]
    routed = tok_rows * top_count
    slots = hosts * capacity
    gate_up = w_in[0]
    down_proj = w_down[0]
    expert_range = jnp.arange(experts, dtype=jnp.int32)
    host_range = jnp.arange(hosts, dtype=jnp.int32)
    placed = (host_expert[:, None] == expert_range[None, :]).astype(jnp.int32)
    host_of = jnp.sum(placed * host_range[:, None], axis=0)
    flat_ids = expert_ids.reshape(-1)
    id_match = flat_ids[:, None] == expert_range[None, :]
    dest_host = jnp.sum(jnp.where(id_match, host_of[None, :], 0), axis=1)
    row_token = jnp.arange(routed, dtype=jnp.int32) // top_count
    padded_tokens = jnp.concatenate([tokens, jnp.zeros((1, width_model), tokens.dtype)], axis=0)
    earlier = (
        lax.broadcasted_iota(jnp.int32, (routed, routed), 0)
        > lax.broadcasted_iota(jnp.int32, (routed, routed), 1)
    ).astype(jnp.bfloat16)
    dest_match = dest_host[:, None] == host_range[None, :]
    before = jnp.dot(earlier, dest_match.astype(jnp.bfloat16), preferred_element_type=jnp.float32)
    position = jnp.sum(jnp.where(dest_match, before, 0.0), axis=1).astype(jnp.int32)
    slot_of_row = dest_host * capacity + position
    source_row = jnp.full((slots + 1,), tok_rows, jnp.int32).at[slot_of_row].set(row_token)[:slots]
    outgoing = padded_tokens[source_row].reshape(hosts, capacity, width_model)
    received = lax.all_to_all(outgoing, "expert", split_axis=0, concat_axis=0, tiled=True)
    flat_in = received.reshape(-1, width_model)
    served = expert_block(flat_in, gate_up, down_proj, hidden_width).reshape(received.shape)
    returned = lax.all_to_all(served, "expert", split_axis=0, concat_axis=0, tiled=True)
    expert_rows = returned.reshape(slots, width_model)[slot_of_row]
    weights = gate_scores / jnp.sum(gate_scores, axis=1, keepdims=True)
    mixed = jnp.sum(
        weights[:, :, None]
        * expert_rows.reshape(tok_rows, top_count, width_model).astype(jnp.float32),
        axis=1,
    )
    return mixed.astype(jnp.bfloat16)


def solution(mesh):
    placed = (
        P(("groups", "expert"), None),
        P(("groups", "expert"), None),
        P(("groups", "expert"), None),
        P(),
        P("expert", None, None),
        P("expert", None, None),
    )
    return jax.shard_map(
        shards, mesh=mesh, in_specs=placed, out_specs=P(("groups", "expert"), None), check_vma=False
    )
```

profile of v0, /device:TPU:15, one launch (start us, length us, event | category | flops | bytes accessed | tf_op | source)
XLA Modules:
  0.0 184.3 jit_solution(10069609783765678601)
XLA Ops:
  0.0 0.0 copy-start
  0.0 0.9 copy.11
  0.9 0.1 eq.20
  1.0 0.7 select_reduce_fusion.1
  1.8 0.1 select_reduce_fusion
  1.9 0.3 fusion.7
  2.2 2.4 %scatter_custom_fusion = s32[769]{0:T(1024)S(1)} fusion(s32[512]{0:T(512)S(1)} %bitcast.22, s32[512]{0:T(512)S(1)} %add_select_fusion, s32[]{:T(128)} %constant.28.clone.1), kind=kCustom, calls=%fused_computation.33 | custom fusion | bytes 3080 | tf_op jit(solution)/shard_map/scatter | solution.py:41
  4.6 1.0 concatenate.3
  5.6 4.3 %gather_fusion = bf16[768,2048]{1,0:T(8,128)(2,1)} fusion(bf16[65,2048]{1,0:T(8,128)(2,1)S(1)} %concatenate.3, s32[1024]{0:T(1024)S(1)} %pad_clamp_fusion.1), kind=kCustom, calls=%fused_computation | custom fusion | bytes 6294528 | tf_op jit(solution)/shard_map/gather | solution.py:42
  9.9 76.3 %all_to_all.10 = bf16[16,48,2048]{2,1,0:T(8,128)(2,1)S(1)} all-to-all(bf16[16,48,2048]{2,1,0:T(8,128)(2,1)} %bitcast.17), channel_id=1, replica_groups=mesh['groups'=2,'expert'=16] {'expert'}, dimensions={0} | all-to-all | bytes 6291456 | tf_op jit(solution)/shard_map/all_to_all | solution.py:43
  86.1 7.1 %fusion = f32[768,1536]{1,0:T(8,128)S(1)} fusion(bf16[768,2048]{1,0:T(8,128)(2,1)S(1)} %bitcast.19, bf16[1,2048,1536]{2,1,0:T(8,128)(2,1)} %param.10), kind=kOutput, calls=%fused_computation.3 | convolution fusion | flops 4831838208 | bytes 14155776 | tf_op jit(solution)/shard_map/dot_general | solution.py:8
  93.3 0.0 copy-done
  93.3 4.1 %convolution_convert_fusion = bf16[768,2048]{1,0:T(8,128)(2,1)} fusion(bf16[1,768,2048]{2,1,0:T(8,128)(2,1)S(1)} %copy-done, f32[768,1536]{1,0:T(8,128)S(1)} %fusion), kind=kOutput, calls=%fused_computation.7 | convolution fusion | flops 2421030912 | bytes 11010048 | tf_op jit(solution)/shard_map/dot_general | solution.py:10
  97.4 0.0 copy-start.1
  97.4 5.2 %all-to-all-start.1 = ((bf16[16,48,2048]{2,1,0:T(8,128)(2,1)}), bf16[16,48,2048]{2,1,0:T(8,128)(2,1)}, u32[]{:S(2)}, u32[]{:S(2)}) async-start(bf16[16,48,2048]{2,1,0:T(8,128)(2,1)} %bitcast.18), calls=%async_computation.1 | async-start | bytes 6291456 | tf_op jit(solution)/shard_map/all_to_all | solution.py:46
  102.7 0.0 copy-done.1
  102.7 0.1 copy.10
  102.8 69.9 %all-to-all-done.1 = bf16[16,48,2048]{2,1,0:T(8,128)(2,1)} async-done(((bf16[16,48,2048]{2,1,0:T(8,128)(2,1)}), bf16[16,48,2048]{2,1,0:T(8,128)(2,1)}, u32[]{:S(2)}, u32[]{:S(2)}) %all-to-all-start.1) | async-done | bytes 3145760 | tf_op jit(solution)/shard_map/all_to_all | solution.py:46
  172.7 7.5 %gather_fusion.1 = bf16[512,2048]{1,0:T(8,128)(2,1)} fusion(bf16[768,2048]{1,0:T(8,128)(2,1)} %bitcast.7, s32[1024]{0:T(1024)S(1)} %pad_clamp_fusion), kind=kCustom, calls=%fused_computation.1 | custom fusion | bytes 4196352 | tf_op jit(solution)/shard_map/gather | solution.py:47
  180.2 4.1 %fusion.2 = bf16[64,2048]{1,0:T(8,128)(2,1)} fusion(bf16[512,2048]{1,0:T(8,128)(2,1)} %gather_fusion.1, f32[64,8]{1,0:T(8,128)S(1)} %copy.10), kind=kLoop, calls=%fused_computation.6 | loop fusion | flops 3014656 | bytes 2361344 | tf_op jit(solution)/shard_map/reduce_sum | solution.py:49
  (8 shorter events, 0.1 us)
Async XLA Ops:
  0.0 93.3 %copy-start = (bf16[1,768,2048]{2,1,0:T(8,128)(2,1)S(1)}, bf16[1,768,2048]{2,1,0:T(8,128)(2,1)}, u32[]{:S(2)}) copy-start(bf16[1,768,2048]{2,1,0:T(8,128)(2,1)} %param.11) | copy-start | bytes 9437188
  97.4 5.2 %copy-start.1 = (f32[64,8]{0,1:T(8,128)S(1)}, f32[64,8]{0,1:T(8,128)}, u32[]{:S(2)}) copy-start(f32[64,8]{0,1:T(8,128)} %param.8) | copy-start | bytes 6148
  97.4 75.2 %all-to-all-start.1 = ((bf16[16,48,2048]{2,1,0:T(8,128)(2,1)}), bf16[16,48,2048]{2,1,0:T(8,128)(2,1)}, u32[]{:S(2)}, u32[]{:S(2)}) async-start(bf16[16,48,2048]{2,1,0:T(8,128)(2,1)} %bitcast.18), calls=%async_computation.1 | async-start | bytes 6291456 | tf_op jit(solution)/shard_map/all_to_all | solution.py:46
where the time goes:
time: 185 us; the launch traced here: 184 us
  blocking collectives  76.3 us (41%)
  waiting for transfers between devices  69.9 us (38%)
  local copies, waits for them, and re-layouts  16.3 us (9%)
  matrix products  11.5 us (6%)
  starting transfers between devices  5.24 us (3%)
  other arithmetic  5.03 us (3%)
    all_to_all x1, blocking collectives, shards(): lax.all_to_all(outgoing, 'expert', split_axis=0, concat_axis=0, tiled=True)  76.3 us
    all_to_all x1, waiting for transfers between devices, shards(): lax.all_to_all(served, 'expert', split_axis=0, concat_axis=0, tiled=True)  69.9 us
    gather x1, local copies, waits for them, and re-layouts, shards(): expert_rows = returned.reshape(slots, width_model)[slot_of_row]  7.52 us
    dot_general x1, matrix products, expert_block(): pair = jnp.dot(rows_in, gate_up, preferred_element_type=jnp.float32)  7.14 us
    all_to_all x1, starting transfers between devices, shards(): lax.all_to_all(served, 'expert', split_axis=0, concat_axis=0, tiled=True)  5.24 us
    gather x1, local copies, waits for them, and re-layouts, shards(): outgoing = padded_tokens[source_row].reshape(hosts, capacity, width_model)  4.27 us
    reduce_sum x1, other arithmetic, shards(): jnp.sum(weights[:, :, None] * expert_rows.reshape(tok_rows, top_count, wi...  4.14 us
    dot_general x1, matrix products, expert_block(): jnp.dot(active, down_proj, preferred_element_type=jnp.float32)  4.13 us
  transfers between devices with their start and end apart: 1, of which 1 were waited for; matrix products, arithmetic and copies ran while one was open for 0% of the time, Pallas kernels for 0%

commit v1 on v0

--- a/solution.py
+++ b/solution.py
@@ -1,7 +1,8 @@
 import jax
 import jax.numpy as jnp
+import numpy as np
 from jax import lax
-from jax.sharding import PartitionSpec as P
+from jax.sharding import Mesh, PartitionSpec as P
 
 
 def expert_block(rows_in, gate_up, down_proj, hidden_width):
@@ -54,6 +55,44 @@
     return mixed.astype(jnp.bfloat16)
 
 
+AXES = ("ez", "ex", "ec")
+
+
+def dense_shards(tokens, expert_ids, gate_scores, host_expert, w_in, w_down):
+    tok_rows, width_model = tokens.shape
+    hidden_width = w_down.shape[1]
+    experts = host_expert.shape[0]
+    me = (lax.axis_index("ez") * lax.axis_size("ex") + lax.axis_index("ex")) * lax.axis_size("ec") + lax.axis_index("ec")
+    my_expert = jnp.sum(jnp.where(jnp.arange(experts, dtype=jnp.int32) == me, host_expert, 0))
+    weights = gate_scores / jnp.sum(gate_scores, axis=1, keepdims=True)
+    rows = tokens
+    gate = expert_ids
+    score = weights
+    for axis in AXES:
+        rows = lax.all_gather(rows, axis, tiled=True)
+        gate = lax.all_gather(gate, axis, tiled=True)
+        score = lax.all_gather(score, axis, tiled=True)
+    mine_all = jnp.sum(jnp.where(gate == my_expert, score, 0.0), axis=1)
+    out = expert_block(rows, w_in[0], w_down[0], hidden_width)
+    part = (out.astype(jnp.float32) * mine_all[:, None]).astype(jnp.bfloat16)
+    for axis in AXES[::-1]:
+        part = lax.psum_scatter(part, axis, scatter_dimension=0, tiled=True)
+    return part
+
+
+def factor_expert(mesh):
+    row = mesh.devices[0]
+    try:
+        cores = len({d.core_on_chip for d in row})
+        xs = len({d.coords[0] for d in row})
+        zs = len({d.coords[2] for d in row})
+    except AttributeError:
+        return None
+    if cores * xs * zs != row.shape[0]:
+        return None
+    return zs, xs, cores
+
+
 def solution(mesh):
     placed = (
         P(("groups", "expert"), None),
@@ -63,6 +102,12 @@
         P("expert", None, None),
         P("expert", None, None),
     )
-    return jax.shard_map(
-        shards, mesh=mesh, in_specs=placed, out_specs=P(("groups", "expert"), None), check_vma=False
-    )
+    factors = factor_expert(mesh)
+    if factors is None or mesh.shape["expert"] > 16:
+        return jax.shard_map(
+            shards, mesh=mesh, in_specs=placed, out_specs=P(("groups", "expert"), None), check_vma=False
+        )
+    sub = Mesh(mesh.devices.reshape((mesh.shape["groups"],) + factors), ("groups",) + AXES)
+    rows = P(("groups",) + AXES, None)
+    placed = (rows, rows, rows, P(), P(AXES, None, None), P(AXES, None, None))
+    return jax.shard_map(dense_shards, mesh=sub, in_specs=placed, out_specs=rows, check_vma=False)

time: 185 us -> 215 us (1.16)
  the two profiles are of different devices: /device:TPU:15 before, /device:TPU:0 now
where the time goes in v1:
time: 215 us
  waiting for transfers between devices  144 us (67%)
  blocking collectives  38.9 us (18%)
  matrix products  15.1 us (7%)
  between operations  13.5 us (6%)
  other arithmetic  3.35 us (2%)
    reduce_scatter x3, waiting for transfers between devices, dense_shards(): part = lax.psum_scatter(part, axis, scatter_dimension=0, tiled=True)  76.8 us
    all_gather x3, waiting for transfers between devices, dense_shards(): rows = lax.all_gather(rows, axis, tiled=True)  66.3 us
    all_gather x3, blocking collectives, dense_shards(): gate = lax.all_gather(gate, axis, tiled=True)  19.5 us
    all_gather x3, blocking collectives, dense_shards(): score = lax.all_gather(score, axis, tiled=True)  19.4 us
    dot_general x1, matrix products, expert_block(): pair = jnp.dot(rows_in, gate_up, preferred_element_type=jnp.float32)  10 us
    dot_general x1, matrix products, expert_block(): jnp.dot(active, down_proj, preferred_element_type=jnp.float32)  5.05 us
  transfers between devices with their start and end apart: 6, of which 5 were waited for; matrix products, arithmetic and copies ran while one was open for 2% of the time, Pallas kernels for 0%

profile of v1, /device:TPU:0, one launch (start us, length us, event | category | flops | bytes accessed | tf_op | source)
XLA Modules:
  0.0 215.2 jit_solution(9596105018070481493)
XLA Ops:
  6.5 0.0 copy-start
  6.5 0.0 all-gather.6.cloned.1.call-start
  6.5 0.7 all-gather.6.cloned.1.call-update
  7.3 0.0 all-gather.8.cloned.1.call-start
  7.3 32.3 %all-gather.6.cloned.1.call-done = bf16[256,2048]{1,0:T(8,128)(2,1)} async-done(((bf16[64,2048]{1,0:T(8,128)(2,1)}), bf16[256,2048]{1,0:T(8,128)(2,1)}) %all-gather.6.cloned.1.call-update) | async-done | bytes 1048592 | tf_op jit(solution)/shard_map/all_gather | solution.py:72
  39.6 0.0 all-gather.8.cloned.1.call-update
  39.7 0.0 all-gather.10.cloned.1.call-start
  39.7 34.0 %all-gather.8.cloned.1.call-done = bf16[512,2048]{1,0:T(8,128)(2,1)} async-done(((bf16[256,2048]{1,0:T(8,128)(2,1)}), bf16[512,2048]{1,0:T(8,128)(2,1)}) %all-gather.8.cloned.1.call-update) | async-done | bytes 2097168 | tf_op jit(solution)/shard_map/all_gather | solution.py:72
  73.7 0.0 all-gather.10.cloned.1.call-update
  73.7 0.0 reduce-scatter.4.cloned.1.call-start
  73.8 0.7 reduce_sum.28
  74.5 0.7 divide_bitcast_fusion
  75.2 13.2 %all-gather.1 = f32[4,64,8]{1,2,0:T(8,128)S(1)} all-gather(f32[1,64,8]{1,2,0:T(8,128)S(1)} %divide_bitcast_fusion), channel_id=1, replica_groups=mesh['groups'=2,'ez'=4,'ex'=2,'ec'=2] {'ez'}, dimensions={0}, use_global_device_ids=true | all-gather | bytes 10240 | tf_op jit(solution)/shard_map/all_gather | solution.py:74
  88.4 0.1 reshape.5
  88.5 13.3 %all-gather = s32[4,64,8]{1,2,0:T(8,128)S(1)} all-gather(s32[1,64,8]{1,2,0:T(8,128)} %bitcast.14), channel_id=1, replica_groups=mesh['groups'=2,'ez'=4,'ex'=2,'ec'=2] {'ez'}, dimensions={0}, use_global_device_ids=true | all-gather | bytes 10240 | tf_op jit(solution)/shard_map/all_gather | solution.py:73
  101.8 0.1 reshape.3
  101.9 4.4 %all_gather.34 = f32[512,8]{0,1:T(8,128)S(1)} all-gather(f32[256,8]{0,1:T(8,128)S(1)} %reshape.5), channel_id=1, replica_groups=mesh['groups'=2,'ez'=4,'ex'=2,'ec'=2] {'ex'}, dimensions={0}, use_global_device_ids=true | all-gather | bytes 24576 | tf_op jit(solution)/shard_map/all_gather | solution.py:74
  106.3 4.3 %all_gather.31 = s32[512,8]{0,1:T(8,128)S(1)} all-gather(s32[256,8]{0,1:T(8,128)S(1)} %reshape.3), channel_id=1, replica_groups=mesh['groups'=2,'ez'=4,'ex'=2,'ec'=2] {'ex'}, dimensions={0}, use_global_device_ids=true | all-gather | bytes 24576 | tf_op jit(solution)/shard_map/all_gather | solution.py:73
  110.6 1.8 all_gather.35
  112.4 1.8 all_gather.32
  114.3 1.3 fusion.6
  115.6 0.7 select_reduce_fusion
  116.2 0.0 all-gather.10.cloned.1.call-done
  116.3 10.0 %fusion = f32[1024,1536]{1,0:T(8,128)S(1)} fusion(bf16[1024,2048]{1,0:T(8,128)(2,1)} %all-gather.10.cloned.1.call-done, bf16[1,2048,1536]{2,1,0:T(8,128)(2,1)} %param.10), kind=kOutput, calls=%fused_computation.1 | convolution fusion | flops 6442450944 | bytes 16777216 | tf_op jit(solution)/shard_map/dot_general | solution.py:9
  126.3 0.0 copy-done
  126.3 5.1 %multiply_convert_fusion = bf16[1024,2048]{1,0:T(8,128)(2,1)} fusion(f32[1024]{0:T(1024)S(1)} %select_reduce_fusion, bf16[1,768,2048]{2,1,0:T(8,128)(2,1)S(1)} %copy-done, f32[1024,1536]{1,0:T(8,128)S(1)} %fusion), kind=kOutput, calls=%fused_computation | convolution fusion | flops 3234332672 | bytes 13635584 | tf_op jit(solution)/shard_map/dot_general | solution.py:11
  131.3 0.0 reduce-scatter.4.cloned.1.call-update
  131.4 0.0 reduce-scatter.6.cloned.1.call-start
  131.4 12.1 %reduce-scatter.4.cloned.1.call-done = bf16[512,2048]{1,0:T(8,128)(2,1)} async-done(((bf16[1024,2048]{1,0:T(8,128)(2,1)}), bf16[512,2048]{1,0:T(8,128)(2,1)}) %reduce-scatter.4.cloned.1.call-update) | async-done | bytes 2097168 | tf_op jit(solution)/shard_map/reduce_scatter | solution.py:79
  143.5 0.0 reduce-scatter.6.cloned.1.call-update
  143.6 0.0 reduce-scatter.8.cloned.1.call-start
  143.6 35.2 %reduce-scatter.6.cloned.1.call-done = bf16[256,2048]{1,0:T(8,128)(2,1)} async-done(((bf16[512,2048]{1,0:T(8,128)(2,1)}), bf16[256,2048]{1,0:T(8,128)(2,1)}) %reduce-scatter.6.cloned.1.call-update) | async-done | bytes 1048592 | tf_op jit(solution)/shard_map/reduce_scatter | solution.py:79
  178.9 0.0 reduce-scatter.8.cloned.1.call-update
  178.9 29.4 %reduce-scatter.8.cloned.1.call-done = bf16[64,2048]{1,0:T(8,128)(2,1)} async-done(((bf16[256,2048]{1,0:T(8,128)(2,1)}), bf16[64,2048]{1,0:T(8,128)(2,1)}) %reduce-scatter.8.cloned.1.call-update) | async-done | bytes 262160 | tf_op jit(solution)/shard_map/reduce_scatter | solution.py:79
  (2 shorter events, 0.0 us)
Async XLA Ops:
  6.5 119.7 %copy-start = (bf16[1,768,2048]{2,1,0:T(8,128)(2,1)S(1)}, bf16[1,768,2048]{2,1,0:T(8,128)(2,1)}, u32[]{:S(2)}) copy-start(bf16[1,768,2048]{2,1,0:T(8,128)(2,1)} %param.11) | copy-start | bytes 9437188
  6.5 33.1 %all-gather.6.cloned.1.call-start = ((), (), s32[]{:S(2)}) async-start(), calls=%async_computation.3 | async-start | bytes 1310720 | tf_op jit(solution)/shard_map/all_gather | solution.py:72
  7.3 66.4 %all-gather.8.cloned.1.call-start = ((), (), s32[]{:S(2)}) async-start(), calls=%async_computation.4 | async-start | bytes 3145728 | tf_op jit(solution)/shard_map/all_gather | solution.py:72
  39.7 76.6 %all-gather.10.cloned.1.call-start = ((), (), s32[]{:S(2)}) async-start(), calls=%async_computation.5 | async-start | bytes 6291456 | tf_op jit(solution)/shard_map/all_gather | solution.py:72
  73.7 69.8 %reduce-scatter.4.cloned.1.call-start = ((), (), s32[]{:S(2)}) async-start(), calls=%async_computation.6 | async-start | bytes 6291456 | tf_op jit(solution)/shard_map/reduce_scatter | solution.py:79
  131.4 47.5 %reduce-scatter.6.cloned.1.call-start = ((), (), s32[]{:S(2)}) async-start(), calls=%async_computation.7 | async-start | bytes 3145728 | tf_op jit(solution)/shard_map/reduce_scatter | solution.py:79
  143.6 64.8 %reduce-scatter.8.cloned.1.call-start = ((), (), s32[]{:S(2)}) async-start(), calls=%async_computation.8 | async-start | bytes 1310720 | tf_op jit(solution)/shard_map/reduce_scatter | solution.py:79
Sparse Core Ops, SparseCore 0:
  8.9 30.6 all-gather.5
  41.2 32.4 all-gather.7
  75.2 13.6 all-gather.9
  131.5 12.0 reduce-scatter.3
  145.6 33.1 reduce-scatter.5
  181.0 27.2 reduce-scatter.7

commit v2 on v1

--- a/solution.py
+++ b/solution.py
@@ -58,26 +58,40 @@
 AXES = ("ez", "ex", "ec")
 
 
+def gather_stage(blocks, axis, size):
+    got = [blocks]
+    for shift in range(1, size):
+        pairs = [(i, (i + shift) % size) for i in range(size)]
+        got.append(jax.tree.map(lambda b: lax.ppermute(b, axis, pairs), blocks))
+    return jax.tree.map(lambda *parts: jnp.concatenate(parts, axis=0), *got)
+
+
+def scatter_stage(part, axis, size):
+    pieces = jnp.split(part, size, axis=0)
+    total = pieces[0].astype(jnp.float32)
+    for shift in range(1, size):
+        pairs = [(i, (i - shift) % size) for i in range(size)]
+        total = total + lax.ppermute(pieces[shift].astype(jnp.bfloat16), axis, pairs).astype(jnp.float32)
+    return total
+
+
 def dense_shards(tokens, expert_ids, gate_scores, host_expert, w_in, w_down):
-    tok_rows, width_model = tokens.shape
     hidden_width = w_down.shape[1]
     experts = host_expert.shape[0]
-    me = (lax.axis_index("ez") * lax.axis_size("ex") + lax.axis_index("ex")) * lax.axis_size("ec") + lax.axis_index("ec")
+    sizes = [lax.axis_size(a) for a in AXES]
+    me = (lax.axis_index("ez") * sizes[1] + lax.axis_index("ex")) * sizes[2] + lax.axis_index("ec")
     my_expert = jnp.sum(jnp.where(jnp.arange(experts, dtype=jnp.int32) == me, host_expert, 0))
     weights = gate_scores / jnp.sum(gate_scores, axis=1, keepdims=True)
-    rows = tokens
-    gate = expert_ids
-    score = weights
-    for axis in AXES:
-        rows = lax.all_gather(rows, axis, tiled=True)
-        gate = lax.all_gather(gate, axis, tiled=True)
-        score = lax.all_gather(score, axis, tiled=True)
-    mine_all = jnp.sum(jnp.where(gate == my_expert, score, 0.0), axis=1)
+    blocks = (tokens, expert_ids, weights)
+    for axis, size in zip(AXES, sizes):
+        blocks = gather_stage(blocks, axis, size)
+    rows, gate, score = blocks
+    mine = jnp.sum(jnp.where(gate == my_expert, score, 0.0), axis=1)
     out = expert_block(rows, w_in[0], w_down[0], hidden_width)
-    part = (out.astype(jnp.float32) * mine_all[:, None]).astype(jnp.bfloat16)
-    for axis in AXES[::-1]:
-        part = lax.psum_scatter(part, axis, scatter_dimension=0, tiled=True)
-    return part
+    part = out.astype(jnp.float32) * mine[:, None]
+    for axis, size in list(zip(AXES, sizes))[::-1]:
+        part = scatter_stage(part, axis, size)
+    return part.astype(jnp.bfloat16)
 
 
 def factor_expert(mesh):

time: 215 us -> 147 us (0.68)
  waiting for transfers between devices: 144 us -> 94.3 us
  blocking collectives: 38.9 us -> 0 us
  starting transfers between devices: 0.2 us -> 23.3 us
  between operations: 13.5 us -> 0.17 us
  local copies, waits for them, and re-layouts: 0.18 us -> 11 us
    ppermute x0 -> x20, waiting for transfers between devices: none -> 94.3 us  [the longest x5 48.3 us: scatter_stage(): lax.ppermute(pieces[shift].astype(jnp.bfloat16), axis, pairs)]
    reduce_scatter x3 -> x0, waiting for transfers between devices: 76.8 us -> none  [dense_shards(): part = lax.psum_scatter(part, axis, scatter_dimension=0, tiled=True)]
    all_gather x3 -> x0, waiting for transfers between devices: 66.3 us -> none  [dense_shards(): rows = lax.all_gather(rows, axis, tiled=True)]
    all_gather x6 -> x0, blocking collectives: 38.9 us -> none  [the longest x3 19.5 us: dense_shards(): gate = lax.all_gather(gate, axis, tiled=True)]
    ppermute x0 -> x20, starting transfers between devices: none -> 23.3 us  [the longest x15 18.3 us: gather_stage(): got.append(jax.tree.map(lambda b: lax.ppermute(b, axis, pairs), blocks))]
    unnamed x4 -> x14, local copies, waits for them, and re-layouts: 0.17 us -> 5.87 us
    concatenate x0 -> x6, local copies, waits for them, and re-layouts: none -> 4.68 us  [gather_stage(): return jax.tree.map(lambda *parts: jnp.concatenate(parts, axis=0), *got)]
  transfers between devices with their start and end apart: 6 -> 20, of which waited for: 5 -> 13; matrix products, arithmetic and copies ran while one was open for 2% -> 4% of each run, Pallas kernels for 0% -> 0%
where the time goes in v2:
time: 147 us
  waiting for transfers between devices  94.3 us (64%)
  starting transfers between devices  23.3 us (16%)
  matrix products  13.5 us (9%)
  local copies, waits for them, and re-layouts  11 us (7%)
  other arithmetic  4.61 us (3%)
    ppermute x5, waiting for transfers between devices, scatter_stage(): lax.ppermute(pieces[shift].astype(jnp.bfloat16), axis, pairs)  48.3 us
    ppermute x15, waiting for transfers between devices, gather_stage(): got.append(jax.tree.map(lambda b: lax.ppermute(b, axis, pairs), blocks))  45.9 us
    ppermute x15, starting transfers between devices, gather_stage(): got.append(jax.tree.map(lambda b: lax.ppermute(b, axis, pairs), blocks))  18.3 us
    dot_general x1, matrix products, expert_block(): pair = jnp.dot(rows_in, gate_up, preferred_element_type=jnp.float32)  10 us
    unnamed x14, local copies, waits for them, and re-layouts  5.87 us
    ppermute x5, starting transfers between devices, scatter_stage(): lax.ppermute(pieces[shift].astype(jnp.bfloat16), axis, pairs)  4.92 us
    concatenate x6, local copies, waits for them, and re-layouts, gather_stage(): return jax.tree.map(lambda *parts: jnp.concatenate(parts, axis=0), *got)  4.68 us
    dot_general x1, matrix products, expert_block(): jnp.dot(active, down_proj, preferred_element_type=jnp.float32)  3.5 us
  transfers between devices with their start and end apart: 20, of which 13 were waited for; matrix products, arithmetic and copies ran while one was open for 4% of the time, Pallas kernels for 0%

profile of v2, /device:TPU:0, one launch (start us, length us, event | category | flops | bytes accessed | tf_op | source)
XLA Modules:
  0.0 146.9 jit_solution(14449919291564263134)
XLA Ops:
  0.0 5.1 %collective-permute-start.2 = (bf16[64,2048]{1,0:T(8,128)(2,1)}, bf16[64,2048]{1,0:T(8,128)(2,1)S(1)}, u32[]{:S(2)}, u32[]{:S(2)}) collective-permute-start(bf16[64,2048]{1,0:T(8,128)(2,1)} %param.6), channel_id=1, source_target_pairs={{0,12},{4,0},{8,4},{12,8},{1,13},{5,1},{9,5},{13,9},{2,14},{6,2},{... | collective-permute-start | bytes 786440 | tf_op jit(solution)/shard_map/ppermute | solution.py:65
  5.1 1.0 collective-permute-start
  6.1 6.0 %collective-permute-done.2 = bf16[64,2048]{1,0:T(8,128)(2,1)S(1)} collective-permute-done((bf16[64,2048]{1,0:T(8,128)(2,1)}, bf16[64,2048]{1,0:T(8,128)(2,1)S(1)}, u32[]{:S(2)}, u32[]{:S(2)}) %collective-permute-start.2) | collective-permute-done | bytes 262176 | tf_op jit(solution)/shard_map/ppermute | solution.py:65
  12.1 15.5 %collective-permute-done.1 = bf16[64,2048]{1,0:T(8,128)(2,1)S(1)} collective-permute-done((bf16[64,2048]{1,0:T(8,128)(2,1)}, bf16[64,2048]{1,0:T(8,128)(2,1)S(1)}, u32[]{:S(2)}, u32[]{:S(2)}) %collective-permute-start.1) | collective-permute-done | bytes 262176 | tf_op jit(solution)/shard_map/ppermute | solution.py:65
  27.6 1.1 pad_maximum_fusion
  28.7 1.6 %collective-permute-start.3 = (bf16[256,2048]{1,0:T(8,128)(2,1)S(1)}, bf16[256,2048]{1,0:T(8,128)(2,1)S(1)}, u32[]{:S(2)}, u32[]{:S(2)}) collective-permute-start(bf16[256,2048]{1,0:T(8,128)(2,1)S(1)} %pad_maximum_fusion), channel_id=1, source_target_pairs={{0,2},{2,0},{1,3},{3,1},{4,6},{6,4},{5,7},{7,5},{8,10},{10,8},{9,1... | collective-permute-start | bytes 3145736 | tf_op jit(solution)/shard_map/ppermute | solution.py:65
  30.3 1.7 %constant_dynamic-update-slice_fusion.4 = (bf16[512,2048]{1,0:T(8,128)(2,1)}, bf16[1024,2048]{1,0:T(8,128)(2,1)S(1)}) fusion(bf16[64,2048]{1,0:T(8,128)(2,1)} %param.6), kind=kLoop, calls=%fused_computation.21 | loop fusion | bytes 786432
  32.0 0.7 constant_dynamic-update-slice_fusion.3
  32.7 0.7 constant_dynamic-update-slice_fusion.2
  33.5 0.7 constant_dynamic-update-slice_fusion.1
  34.2 18.6 %collective-permute-done.3 = bf16[256,2048]{1,0:T(8,128)(2,1)S(1)} collective-permute-done((bf16[256,2048]{1,0:T(8,128)(2,1)S(1)}, bf16[256,2048]{1,0:T(8,128)(2,1)S(1)}, u32[]{:S(2)}, u32[]{:S(2)}) %collective-permute-start.3) | collective-permute-done | bytes 1048608 | tf_op jit(solution)/shard_map/ppermute | solution.py:65
  52.8 1.2 constant_dynamic-update-slice_fusion
  54.1 1.9 %copy-done.2 = bf16[1024,2048]{1,0:T(8,128)(2,1)} copy-done((bf16[1024,2048]{1,0:T(8,128)(2,1)}, bf16[1024,2048]{1,0:T(8,128)(2,1)S(1)}, u32[]{:S(2)}) %copy-start.2) | copy-done | bytes 4194328
  56.1 3.2 %collective-permute-start.11 = (f32[64,8]{0,1:T(8,128)S(1)}, f32[64,8]{0,1:T(8,128)S(1)}, u32[]{:S(2)}, u32[]{:S(2)}) collective-permute-start(f32[64,8]{0,1:T(8,128)S(1)} %broadcast_divide_fusion), channel_id=1, source_target_pairs={{0,8},{4,12},{8,0},{12,4},{1,9},{5,13},{9,1},{13,5},{2,10},{6,14},... | collective-permute-start | bytes 6152 | tf_op jit(solution)/shard_map/ppermute | solution.py:65
  59.3 1.9 %collective-permute-start.10 = (f32[64,8]{0,1:T(8,128)S(1)}, f32[64,8]{0,1:T(8,128)S(1)}, u32[]{:S(2)}, u32[]{:S(2)}) collective-permute-start(f32[64,8]{0,1:T(8,128)S(1)} %broadcast_divide_fusion), channel_id=1, source_target_pairs={{0,4},{4,8},{8,12},{12,0},{1,5},{5,9},{9,13},{13,1},{2,6},{6,10},{... | collective-permute-start | bytes 6152 | tf_op jit(solution)/shard_map/ppermute | solution.py:65
  61.2 1.9 %collective-permute-start.7 = (s32[64,8]{0,1:T(8,128)S(1)}, s32[64,8]{0,1:T(8,128)S(1)}, u32[]{:S(2)}, u32[]{:S(2)}) collective-permute-start(s32[64,8]{0,1:T(8,128)S(1)} %copy-done.1), channel_id=1, source_target_pairs={{0,12},{4,0},{8,4},{12,8},{1,13},{5,1},{9,5},{13,9},{2,14},{6,2},{... | collective-permute-start | bytes 6152 | tf_op jit(solution)/shard_map/ppermute | solution.py:65
  63.1 0.6 collective-permute-start.5
  63.7 0.9 collective-permute-done.10
  64.7 1.5 %collective-permute-start.13 = (f32[256,8]{0,1:T(8,128)S(1)}, f32[256,8]{0,1:T(8,128)S(1)}, u32[]{:S(2)}, u32[]{:S(2)}) collective-permute-start(f32[256,8]{0,1:T(8,128)S(1)} %pad_maximum_fusion.1), channel_id=1, source_target_pairs={{0,2},{2,0},{1,3},{3,1},{4,6},{6,4},{5,7},{7,5},{8,10},{10,8},{9,1... | collective-permute-start | bytes 24584 | tf_op jit(solution)/shard_map/ppermute | solution.py:65
  66.2 1.4 collective-permute-done.6
  67.6 1.0 collective-permute-done.5
  68.6 1.5 %collective-permute-start.8 = (s32[256,8]{0,1:T(8,128)S(1)}, s32[256,8]{0,1:T(8,128)S(1)}, u32[]{:S(2)}, u32[]{:S(2)}) collective-permute-start(s32[256,8]{0,1:T(8,128)S(1)} %pad_add_fusion), channel_id=1, source_target_pairs={{0,2},{2,0},{1,3},{3,1},{4,6},{6,4},{5,7},{7,5},{8,10},{10,8},{9,1... | collective-permute-start | bytes 24584 | tf_op jit(solution)/shard_map/ppermute | solution.py:65
  70.1 0.1 concatenate.40
  70.2 2.1 %collective-permute-done.8 = s32[256,8]{0,1:T(8,128)S(1)} collective-permute-done((s32[256,8]{0,1:T(8,128)S(1)}, s32[256,8]{0,1:T(8,128)S(1)}, u32[]{:S(2)}, u32[]{:S(2)}) %collective-permute-start.8) | collective-permute-done | bytes 8224 | tf_op jit(solution)/shard_map/ppermute | solution.py:65
  72.3 0.1 concatenate.37
  72.4 0.6 fusion.9
  73.0 0.1 concatenate.41
  73.1 0.4 collective-permute-done.9
  73.5 0.1 concatenate.38
  73.6 0.7 select_reduce_fusion
  74.3 3.1 %constant_dynamic-update-slice_fusion.5 = bf16[1024,2048]{1,0:T(8,128)(2,1)} fusion(bf16[1024,2048]{1,0:T(8,128)(2,1)} %copy-done.2, bf16[512,2048]{1,0:T(8,128)(2,1)} %collective-permute-done.4), kind=kLoop, calls=%fused_computation.22 | loop fusion | bytes 4194304 | tf_op jit(solution)/shard_map/concatenate | solution.py:66
  77.4 10.0 %fusion = f32[1024,1536]{1,0:T(8,128)S(1)} fusion(bf16[1024,2048]{1,0:T(8,128)(2,1)} %constant_dynamic-update-slice_fusion.5, bf16[1,2048,1536]{2,1,0:T(8,128)(2,1)} %param.10), kind=kOutput, calls=%fused_computation.1 | convolution fusion | flops 6442450944 | bytes 16777216 | tf_op jit(solution)/shard_map/dot_general | solution.py:9
  87.5 3.5 %convert_multiply_fusion = f32[1024,2048]{1,0:T(8,128)S(1)} fusion(f32[1024]{0:T(1024)S(1)} %select_reduce_fusion, bf16[1,768,2048]{2,1,0:T(8,128)(2,1)S(1)} %copy-done, f32[1024,1536]{1,0:T(8,128)S(1)} %fusion), kind=kOutput, calls=%fused_computation | convolution fusion | flops 3232235520 | bytes 17829888 | tf_op jit(solution)/shard_map/dot_general | solution.py:11
  91.0 0.3 split.56
  91.3 0.2 collective-permute-start.15
  91.5 4.0 %collective-permute-done.15 = bf16[512,2048]{1,0:T(8,128)(2,1)S(1)} collective-permute-done((bf16[512,2048]{1,0:T(8,128)(2,1)S(1)}, bf16[512,2048]{1,0:T(8,128)(2,1)S(1)}, u32[]{:S(2)}, u32[]{:S(2)}) %collective-permute-start.15) | collective-permute-done | bytes 2097184 | tf_op jit(solution)/shard_map/ppermute | solution.py:74
  95.5 0.9 slice_add_fusion
  96.4 0.1 split.57
  96.5 1.6 %collective-permute-start.16 = (bf16[256,2048]{1,0:T(8,128)(2,1)S(1)}, bf16[256,2048]{1,0:T(8,128)(2,1)S(1)}, u32[]{:S(2)}, u32[]{:S(2)}) collective-permute-start(bf16[256,2048]{1,0:T(8,128)(2,1)S(1)} %split.57), channel_id=1, source_target_pairs={{0,2},{2,0},{1,3},{3,1},{4,6},{6,4},{5,7},{7,5},{8,10},{10,8},{9,1... | collective-permute-start | bytes 3145736 | tf_op jit(solution)/shard_map/ppermute | solution.py:74
  98.1 23.7 %collective-permute-done.16 = bf16[256,2048]{1,0:T(8,128)(2,1)S(1)} collective-permute-done((bf16[256,2048]{1,0:T(8,128)(2,1)S(1)}, bf16[256,2048]{1,0:T(8,128)(2,1)S(1)}, u32[]{:S(2)}, u32[]{:S(2)}) %collective-permute-start.16) | collective-permute-done | bytes 1048608 | tf_op jit(solution)/shard_map/ppermute | solution.py:74
  121.8 0.4 fusion.11
  122.3 0.7 collective-permute-start.17
  123.0 1.4 collective-permute-start.19
  124.3 1.1 collective-permute-start.18
  125.4 10.4 %collective-permute-done.17 = bf16[64,2048]{1,0:T(8,128)(2,1)S(1)} collective-permute-done((bf16[64,2048]{1,0:T(8,128)(2,1)S(1)}, bf16[64,2048]{1,0:T(8,128)(2,1)S(1)}, u32[]{:S(2)}, u32[]{:S(2)}) %collective-permute-start.17) | collective-permute-done | bytes 262176 | tf_op jit(solution)/shard_map/ppermute | solution.py:74
  135.8 1.9 %collective-permute-done.19 = bf16[64,2048]{1,0:T(8,128)(2,1)S(1)} collective-permute-done((bf16[64,2048]{1,0:T(8,128)(2,1)S(1)}, bf16[64,2048]{1,0:T(8,128)(2,1)S(1)}, u32[]{:S(2)}, u32[]{:S(2)}) %collective-permute-start.19) | collective-permute-done | bytes 262176 | tf_op jit(solution)/shard_map/ppermute | solution.py:74
  137.7 8.3 %collective-permute-done.18 = bf16[64,2048]{1,0:T(8,128)(2,1)S(1)} collective-permute-done((bf16[64,2048]{1,0:T(8,128)(2,1)S(1)}, bf16[64,2048]{1,0:T(8,128)(2,1)S(1)}, u32[]{:S(2)}, u32[]{:S(2)}) %collective-permute-start.18) | collective-permute-done | bytes 262176 | tf_op jit(solution)/shard_map/ppermute | solution.py:74
  146.0 0.8 fusion.8
  (27 shorter events, 0.3 us)
Async XLA Ops:
  0.0 87.4 %copy-start = (bf16[1,768,2048]{2,1,0:T(8,128)(2,1)S(1)}, bf16[1,768,2048]{2,1,0:T(8,128)(2,1)}, u32[]{:S(2)}) copy-start(bf16[1,768,2048]{2,1,0:T(8,128)(2,1)} %param.11) | copy-start | bytes 9437188
  0.0 12.1 %collective-permute-start.2 = (bf16[64,2048]{1,0:T(8,128)(2,1)}, bf16[64,2048]{1,0:T(8,128)(2,1)S(1)}, u32[]{:S(2)}, u32[]{:S(2)}) collective-permute-start(bf16[64,2048]{1,0:T(8,128)(2,1)} %param.6), channel_id=1, source_target_pairs={{0,12},{4,0},{8,4},{12,8},{1,13},{5,1},{9,5},{13,9},{2,14},{6,2},{... | collective-permute-start | bytes 786440 | tf_op jit(solution)/shard_map/ppermute | solution.py:65
  5.1 22.5 %collective-permute-start.1 = (bf16[64,2048]{1,0:T(8,128)(2,1)}, bf16[64,2048]{1,0:T(8,128)(2,1)S(1)}, u32[]{:S(2)}, u32[]{:S(2)}) collective-permute-start(bf16[64,2048]{1,0:T(8,128)(2,1)} %param.6), channel_id=1, source_target_pairs={{0,8},{4,12},{8,0},{12,4},{1,9},{5,13},{9,1},{13,5},{2,10},{6,14},... | collective-permute-start | bytes 786440 | tf_op jit(solution)/shard_map/ppermute | solution.py:65
  5.1 22.5 %collective-permute-start = (bf16[64,2048]{1,0:T(8,128)(2,1)}, bf16[64,2048]{1,0:T(8,128)(2,1)S(1)}, u32[]{:S(2)}, u32[]{:S(2)}) collective-permute-start(bf16[64,2048]{1,0:T(8,128)(2,1)} %param.6), channel_id=1, source_target_pairs={{0,4},{4,8},{8,12},{12,0},{1,5},{5,9},{9,13},{13,1},{2,6},{6,10},{... | collective-permute-start | bytes 786440 | tf_op jit(solution)/shard_map/ppermute | solution.py:65
  28.7 27.3 %copy-start.3 = (f32[64,8]{0,1:T(8,128)S(1)}, f32[64,8]{0,1:T(8,128)}, u32[]{:S(2)}) copy-start(f32[64,8]{0,1:T(8,128)} %param.8) | copy-start | bytes 6148
  28.7 32.5 %copy-start.1 = (s32[64,8]{0,1:T(8,128)S(1)}, s32[64,8]{0,1:T(8,128)}, u32[]{:S(2)}) copy-start(s32[64,8]{0,1:T(8,128)} %param.7) | copy-start | bytes 6148
  28.7 43.7 %copy-start.4 = (s32[16]{0:T(128)S(1)}, s32[16]{0:T(128)}, u32[]{:S(2)}) copy-start(s32[16]{0:T(128)} %param.9) | copy-start | bytes 196
  28.7 24.1 %collective-permute-start.3 = (bf16[256,2048]{1,0:T(8,128)(2,1)S(1)}, bf16[256,2048]{1,0:T(8,128)(2,1)S(1)}, u32[]{:S(2)}, u32[]{:S(2)}) collective-permute-start(bf16[256,2048]{1,0:T(8,128)(2,1)S(1)} %pad_maximum_fusion), channel_id=1, source_target_pairs={{0,2},{2,0},{1,3},{3,1},{4,6},{6,4},{5,7},{7,5},{8,10},{10,8},{9,1... | collective-permute-start | bytes 3145736 | tf_op jit(solution)/shard_map/ppermute | solution.py:65
  54.0 1.9 %copy-start.2 = (bf16[1024,2048]{1,0:T(8,128)(2,1)}, bf16[1024,2048]{1,0:T(8,128)(2,1)S(1)}, u32[]{:S(2)}) copy-start(bf16[1024,2048]{1,0:T(8,128)(2,1)S(1)} %get-tuple-element.11) | copy-start | bytes 12582916
  56.0 18.3 %collective-permute-start.4 = (bf16[512,2048]{1,0:T(8,128)(2,1)}, bf16[512,2048]{1,0:T(8,128)(2,1)}, u32[]{:S(2)}, u32[]{:S(2)}) collective-permute-start(bf16[512,2048]{1,0:T(8,128)(2,1)} %get-tuple-element.10), channel_id=1, source_target_pairs={{0,1},{1,0},{2,3},{3,2},{4,5},{5,4},{6,7},{7,6},{8,9},{9,8},{10,11... | collective-permute-start | bytes 6291464 | tf_op jit(solution)/shard_map/ppermute | solution.py:65
  56.0 7.1 %collective-permute-start.12 = (f32[64,8]{0,1:T(8,128)S(1)}, f32[64,8]{0,1:T(8,128)S(1)}, u32[]{:S(2)}, u32[]{:S(2)}) collective-permute-start(f32[64,8]{0,1:T(8,128)S(1)} %broadcast_divide_fusion), channel_id=1, source_target_pairs={{0,12},{4,0},{8,4},{12,8},{1,13},{5,1},{9,5},{13,9},{2,14},{6,2},{... | collective-permute-start | bytes 6152 | tf_op jit(solution)/shard_map/ppermute | solution.py:65
  56.1 7.0 %collective-permute-start.11 = (f32[64,8]{0,1:T(8,128)S(1)}, f32[64,8]{0,1:T(8,128)S(1)}, u32[]{:S(2)}, u32[]{:S(2)}) collective-permute-start(f32[64,8]{0,1:T(8,128)S(1)} %broadcast_divide_fusion), channel_id=1, source_target_pairs={{0,8},{4,12},{8,0},{12,4},{1,9},{5,13},{9,1},{13,5},{2,10},{6,14},... | collective-permute-start | bytes 6152 | tf_op jit(solution)/shard_map/ppermute | solution.py:65
  59.3 5.4 %collective-permute-start.10 = (f32[64,8]{0,1:T(8,128)S(1)}, f32[64,8]{0,1:T(8,128)S(1)}, u32[]{:S(2)}, u32[]{:S(2)}) collective-permute-start(f32[64,8]{0,1:T(8,128)S(1)} %broadcast_divide_fusion), channel_id=1, source_target_pairs={{0,4},{4,8},{8,12},{12,0},{1,5},{5,9},{9,13},{13,1},{2,6},{6,10},{... | collective-permute-start | bytes 6152 | tf_op jit(solution)/shard_map/ppermute | solution.py:65
  61.2 5.0 %collective-permute-start.7 = (s32[64,8]{0,1:T(8,128)S(1)}, s32[64,8]{0,1:T(8,128)S(1)}, u32[]{:S(2)}, u32[]{:S(2)}) collective-permute-start(s32[64,8]{0,1:T(8,128)S(1)} %copy-done.1), channel_id=1, source_target_pairs={{0,12},{4,0},{8,4},{12,8},{1,13},{5,1},{9,5},{13,9},{2,14},{6,2},{... | collective-permute-start | bytes 6152 | tf_op jit(solution)/shard_map/ppermute | solution.py:65
  63.1 4.5 %collective-permute-start.6 = (s32[64,8]{0,1:T(8,128)S(1)}, s32[64,8]{0,1:T(8,128)S(1)}, u32[]{:S(2)}, u32[]{:S(2)}) collective-permute-start(s32[64,8]{0,1:T(8,128)S(1)} %copy-done.1), channel_id=1, source_target_pairs={{0,8},{4,12},{8,0},{12,4},{1,9},{5,13},{9,1},{13,5},{2,10},{6,14},... | collective-permute-start | bytes 6152 | tf_op jit(solution)/shard_map/ppermute | solution.py:65
  63.1 5.5 %collective-permute-start.5 = (s32[64,8]{0,1:T(8,128)S(1)}, s32[64,8]{0,1:T(8,128)S(1)}, u32[]{:S(2)}, u32[]{:S(2)}) collective-permute-start(s32[64,8]{0,1:T(8,128)S(1)} %copy-done.1), channel_id=1, source_target_pairs={{0,4},{4,8},{8,12},{12,0},{1,5},{5,9},{9,13},{13,1},{2,6},{6,10},{... | collective-permute-start | bytes 6152 | tf_op jit(solution)/shard_map/ppermute | solution.py:65
  64.7 5.4 %collective-permute-start.13 = (f32[256,8]{0,1:T(8,128)S(1)}, f32[256,8]{0,1:T(8,128)S(1)}, u32[]{:S(2)}, u32[]{:S(2)}) collective-permute-start(f32[256,8]{0,1:T(8,128)S(1)} %pad_maximum_fusion.1), channel_id=1, source_target_pairs={{0,2},{2,0},{1,3},{3,1},{4,6},{6,4},{5,7},{7,5},{8,10},{10,8},{9,1... | collective-permute-start | bytes 24584 | tf_op jit(solution)/shard_map/ppermute | solution.py:65
  68.6 3.7 %collective-permute-start.8 = (s32[256,8]{0,1:T(8,128)S(1)}, s32[256,8]{0,1:T(8,128)S(1)}, u32[]{:S(2)}, u32[]{:S(2)}) collective-permute-start(s32[256,8]{0,1:T(8,128)S(1)} %pad_add_fusion), channel_id=1, source_target_pairs={{0,2},{2,0},{1,3},{3,1},{4,6},{6,4},{5,7},{7,5},{8,10},{10,8},{9,1... | collective-permute-start | bytes 24584 | tf_op jit(solution)/shard_map/ppermute | solution.py:65
  70.2 2.8 %collective-permute-start.14 = (f32[512,8]{0,1:T(8,128)S(1)}, f32[512,8]{0,1:T(8,128)S(1)}, u32[]{:S(2)}, u32[]{:S(2)}) collective-permute-start(f32[512,8]{0,1:T(8,128)S(1)} %concatenate.40), channel_id=1, source_target_pairs={{0,1},{1,0},{2,3},{3,2},{4,5},{5,4},{6,7},{7,6},{8,9},{9,8},{10,11... | collective-permute-start | bytes 49160 | tf_op jit(solution)/shard_map/ppermute | solution.py:65
  72.4 1.2 collective-permute-start.9
  91.3 4.2 %collective-permute-start.15 = (bf16[512,2048]{1,0:T(8,128)(2,1)S(1)}, bf16[512,2048]{1,0:T(8,128)(2,1)S(1)}, u32[]{:S(2)}, u32[]{:S(2)}) collective-permute-start(bf16[512,2048]{1,0:T(8,128)(2,1)S(1)} %split.56), channel_id=1, source_target_pairs={{0,1},{1,0},{2,3},{3,2},{4,5},{5,4},{6,7},{7,6},{8,9},{9,8},{10,11... | collective-permute-start | bytes 6291464 | tf_op jit(solution)/shard_map/ppermute | solution.py:74
  96.5 25.3 %collective-permute-start.16 = (bf16[256,2048]{1,0:T(8,128)(2,1)S(1)}, bf16[256,2048]{1,0:T(8,128)(2,1)S(1)}, u32[]{:S(2)}, u32[]{:S(2)}) collective-permute-start(bf16[256,2048]{1,0:T(8,128)(2,1)S(1)} %split.57), channel_id=1, source_target_pairs={{0,2},{2,0},{1,3},{3,1},{4,6},{6,4},{5,7},{7,5},{8,10},{10,8},{9,1... | collective-permute-start | bytes 3145736 | tf_op jit(solution)/shard_map/ppermute | solution.py:74
  122.3 13.6 %collective-permute-start.17 = (bf16[64,2048]{1,0:T(8,128)(2,1)S(1)}, bf16[64,2048]{1,0:T(8,128)(2,1)S(1)}, u32[]{:S(2)}, u32[]{:S(2)}) collective-permute-start(bf16[64,2048]{1,0:T(8,128)(2,1)S(1)} %get-tuple-element.7), channel_id=1, source_target_pairs={{0,12},{4,0},{8,4},{12,8},{1,13},{5,1},{9,5},{13,9},{2,14},{6,2},{... | collective-permute-start | bytes 786440 | tf_op jit(solution)/shard_map/ppermute | solution.py:74
  123.0 14.8 %collective-permute-start.19 = (bf16[64,2048]{1,0:T(8,128)(2,1)S(1)}, bf16[64,2048]{1,0:T(8,128)(2,1)S(1)}, u32[]{:S(2)}, u32[]{:S(2)}) collective-permute-start(bf16[64,2048]{1,0:T(8,128)(2,1)S(1)} %get-tuple-element.8), channel_id=1, source_target_pairs={{0,4},{4,8},{8,12},{12,0},{1,5},{5,9},{9,13},{13,1},{2,6},{6,10},{... | collective-permute-start | bytes 786440 | tf_op jit(solution)/shard_map/ppermute | solution.py:74
  124.3 21.7 %collective-permute-start.18 = (bf16[64,2048]{1,0:T(8,128)(2,1)S(1)}, bf16[64,2048]{1,0:T(8,128)(2,1)S(1)}, u32[]{:S(2)}, u32[]{:S(2)}) collective-permute-start(bf16[64,2048]{1,0:T(8,128)(2,1)S(1)} %get-tuple-element.9), channel_id=1, source_target_pairs={{0,8},{4,12},{8,0},{12,4},{1,9},{5,13},{9,1},{13,5},{2,10},{6,14},... | collective-permute-start | bytes 786440 | tf_op jit(solution)/shard_map/ppermute | solution.py:74

commit v3 on v2

--- a/solution.py
+++ b/solution.py
@@ -82,16 +82,30 @@
     me = (lax.axis_index("ez") * sizes[1] + lax.axis_index("ex")) * sizes[2] + lax.axis_index("ec")
     my_expert = jnp.sum(jnp.where(jnp.arange(experts, dtype=jnp.int32) == me, host_expert, 0))
     weights = gate_scores / jnp.sum(gate_scores, axis=1, keepdims=True)
-    blocks = (tokens, expert_ids, weights)
-    for axis, size in zip(AXES, sizes):
-        blocks = gather_stage(blocks, axis, size)
-    rows, gate, score = blocks
-    mine = jnp.sum(jnp.where(gate == my_expert, score, 0.0), axis=1)
-    out = expert_block(rows, w_in[0], w_down[0], hidden_width)
-    part = out.astype(jnp.float32) * mine[:, None]
-    for axis, size in list(zip(AXES, sizes))[::-1]:
-        part = scatter_stage(part, axis, size)
-    return part.astype(jnp.bfloat16)
+    streams = [
+        jax.tree.map(lambda a: jnp.split(a, STREAMS, axis=0)[k], (tokens, expert_ids, weights))
+        for k in range(STREAMS)
+    ]
+    results = []
+    held = None
+    for blocks in streams:
+        if held is not None:
+            held, blocks = lax.optimization_barrier((held, blocks))
+        blocks = gather_stage(blocks, AXES[0], sizes[0])
+        held = blocks[0]
+        for axis, size in zip(AXES[1:], sizes[1:]):
+            blocks = gather_stage(blocks, axis, size)
+        rows, gate, score = blocks
+        mine = jnp.sum(jnp.where(gate == my_expert, score, 0.0), axis=1)
+        out = expert_block(rows, w_in[0], w_down[0], hidden_width)
+        part = out.astype(jnp.float32) * mine[:, None]
+        for axis, size in list(zip(AXES, sizes))[::-1]:
+            part = scatter_stage(part, axis, size)
+        results.append(part)
+    return jnp.concatenate(results, axis=0).astype(jnp.bfloat16)
+
+
+STREAMS = 2
 
 
 def factor_expert(mesh):

time: 147 us -> 139 us (0.946)
  waiting for transfers between devices: 94.3 us -> 41 us
  starting transfers between devices: 23.3 us -> 45.8 us
  local copies, waits for them, and re-layouts: 11 us -> 24 us
  other arithmetic: 4.61 us -> 13.9 us
    ppermute x15 -> x30, waiting for transfers between devices: 45.9 us -> 11.7 us  [gather_stage(): got.append(jax.tree.map(lambda b: lax.ppermute(b, axis, pairs), blocks))]
    ppermute x5 -> x10, waiting for transfers between devices: 48.3 us -> 29.3 us  [scatter_stage(): lax.ppermute(pieces[shift].astype(jnp.bfloat16), axis, pairs)]
    ppermute x15 -> x30, starting transfers between devices: 18.3 us -> 35.8 us  [gather_stage(): got.append(jax.tree.map(lambda b: lax.ppermute(b, axis, pairs), blocks))]
    concatenate x6 -> x12, local copies, waits for them, and re-layouts: 4.68 us -> 11.2 us  [gather_stage(): return jax.tree.map(lambda *parts: jnp.concatenate(parts, axis=0), *got)]
    concatenate x3 -> x6, other arithmetic: 1.21 us -> 6.41 us  [gather_stage(): return jax.tree.map(lambda *parts: jnp.concatenate(parts, axis=0), *got)]
    ppermute x5 -> x10, starting transfers between devices: 4.92 us -> 10 us  [scatter_stage(): lax.ppermute(pieces[shift].astype(jnp.bfloat16), axis, pairs)]
    unnamed x14 -> x50, local copies, waits for them, and re-layouts: 5.87 us -> 10.2 us
    split x0 -> x2, local copies, waits for them, and re-layouts: none -> 2.09 us  [dense_shards(): jnp.split(a, STREAMS, axis=0)[k]]
  transfers between devices with their start and end apart: 20 -> 40, of which waited for: 13 -> 10; matrix products, arithmetic and copies ran while one was open for 4% -> 32% of each run, Pallas kernels for 0% -> 0%
where the time goes in v3:
time: 139 us; the launch traced here: 138 us
  starting transfers between devices  45.8 us (33%)
  waiting for transfers between devices  41 us (29%)
  local copies, waits for them, and re-layouts  24 us (17%)
  other arithmetic  13.9 us (10%)
  matrix products  12.8 us (9%)
    ppermute x30, starting transfers between devices, gather_stage(): got.append(jax.tree.map(lambda b: lax.ppermute(b, axis, pairs), blocks))  35.8 us
    ppermute x10, waiting for transfers between devices, scatter_stage(): lax.ppermute(pieces[shift].astype(jnp.bfloat16), axis, pairs)  29.3 us
    ppermute x30, waiting for transfers between devices, gather_stage(): got.append(jax.tree.map(lambda b: lax.ppermute(b, axis, pairs), blocks))  11.7 us
    concatenate x12, local copies, waits for them, and re-layouts, gather_stage(): return jax.tree.map(lambda *parts: jnp.concatenate(parts, axis=0), *got)  11.2 us
    unnamed x50, local copies, waits for them, and re-layouts  10.2 us
    ppermute x10, starting transfers between devices, scatter_stage(): lax.ppermute(pieces[shift].astype(jnp.bfloat16), axis, pairs)  10 us
    dot_general x2, matrix products, expert_block(): pair = jnp.dot(rows_in, gate_up, preferred_element_type=jnp.float32)  9.12 us
    concatenate x6, other arithmetic, gather_stage(): return jax.tree.map(lambda *parts: jnp.concatenate(parts, axis=0), *got)  6.41 us
  transfers between devices with their start and end apart: 40, of which 10 were waited for; matrix products, arithmetic and copies ran while one was open for 32% of the time, Pallas kernels for 0%

profile of v3, /device:TPU:0, one launch (start us, length us, event | category | flops | bytes accessed | tf_op | source)
XLA Modules:
  0.0 137.9 jit_solution(16209069881305543815)
XLA Ops:
  2.3 3.1 %collective-permute-start.10 = (f32[32,8]{0,1:T(8,128)S(1)}, f32[32,8]{0,1:T(8,128)S(1)}, u32[]{:S(2)}, u32[]{:S(2)}) collective-permute-start(f32[32,8]{0,1:T(8,128)S(1)} %get-tuple-element.45), channel_id=1, source_target_pairs={{0,4},{4,8},{8,12},{12,0},{1,5},{5,9},{9,13},{13,1},{2,6},{6,10},{... | collective-permute-start | bytes 3080 | tf_op jit(solution)/shard_map/ppermute | solution.py:65
  5.4 2.6 %collective-permute-start.11 = (f32[32,8]{0,1:T(8,128)S(1)}, f32[32,8]{0,1:T(8,128)S(1)}, u32[]{:S(2)}, u32[]{:S(2)}) collective-permute-start(f32[32,8]{0,1:T(8,128)S(1)} %get-tuple-element.45), channel_id=1, source_target_pairs={{0,8},{4,12},{8,0},{12,4},{1,9},{5,13},{9,1},{13,5},{2,10},{6,14},... | collective-permute-start | bytes 3080 | tf_op jit(solution)/shard_map/ppermute | solution.py:65
  8.0 1.3 collective-permute-start.12
  9.3 1.4 %fusion.41 = (s32[32,8]{0,1:T(8,128)S(1)}, s32[32,8]{0,1:T(8,128)}) fusion(s32[64,8]{0,1:T(8,128)} %param.7), kind=kLoop, calls=%fused_computation.74 | loop fusion | bytes 4096 | tf_op jit(solution)/shard_map/split | solution.py:86
  11.8 2.9 %collective-permute-start.7 = (s32[32,8]{0,1:T(8,128)S(1)}, s32[32,8]{0,1:T(8,128)S(1)}, u32[]{:S(2)}, u32[]{:S(2)}) collective-permute-start(s32[32,8]{0,1:T(8,128)S(1)} %get-tuple-element.43), channel_id=1, source_target_pairs={{0,12},{4,0},{8,4},{12,8},{1,13},{5,1},{9,5},{13,9},{2,14},{6,2},{... | collective-permute-start | bytes 3080 | tf_op jit(solution)/shard_map/ppermute | solution.py:65
  15.3 1.5 %collective-permute-start.13 = (f32[128,8]{0,1:T(8,128)}, f32[128,8]{0,1:T(8,128)}, u32[]{:S(2)}, u32[]{:S(2)}) collective-permute-start(f32[128,8]{0,1:T(8,128)} %pad_maximum_fusion.3), channel_id=1, source_target_pairs={{0,2},{2,0},{1,3},{3,1},{4,6},{6,4},{5,7},{7,5},{8,10},{10,8},{9,1... | collective-permute-start | bytes 12296 | tf_op jit(solution)/shard_map/ppermute | solution.py:65
  17.5 1.4 %collective-permute-start.8 = (s32[128,8]{0,1:T(8,128)}, s32[128,8]{0,1:T(8,128)}, u32[]{:S(2)}, u32[]{:S(2)}) collective-permute-start(s32[128,8]{0,1:T(8,128)} %pad_add_fusion), channel_id=1, source_target_pairs={{0,2},{2,0},{1,3},{3,1},{4,6},{6,4},{5,7},{7,5},{8,10},{10,8},{9,1... | collective-permute-start | bytes 12296 | tf_op jit(solution)/shard_map/ppermute | solution.py:65
  19.0 1.7 %constant_dynamic-update-slice_fusion.4 = (bf16[256,2048]{1,0:T(8,128)(2,1)}, bf16[512,2048]{1,0:T(8,128)(2,1)}, bf16[32,2048]{1,0:T(8,128)(2,1)S(1)}, bf16[32,2048]{1,0:T(8,128)(2,1)}) fusion(bf16[64,2048]{1,0:T(8,128)(2,1)} %param.6), kind=kLoop, calls=%fused_computation.41 | loop fusion | bytes 786432
  20.7 2.0 %collective-permute-start = (bf16[32,2048]{1,0:T(8,128)(2,1)}, bf16[32,2048]{1,0:T(8,128)(2,1)}, u32[]{:S(2)}, u32[]{:S(2)}) collective-permute-start(bf16[32,2048]{1,0:T(8,128)(2,1)} %get-tuple-element.28), channel_id=1, source_target_pairs={{0,4},{4,8},{8,12},{12,0},{1,5},{5,9},{9,13},{13,1},{2,6},{6,10},{... | collective-permute-start | bytes 393224 | tf_op jit(solution)/shard_map/ppermute | solution.py:65
  22.7 1.9 %collective-permute-start.1 = (bf16[32,2048]{1,0:T(8,128)(2,1)}, bf16[32,2048]{1,0:T(8,128)(2,1)S(1)}, u32[]{:S(2)}, u32[]{:S(2)}) collective-permute-start(bf16[32,2048]{1,0:T(8,128)(2,1)} %get-tuple-element.28), channel_id=1, source_target_pairs={{0,8},{4,12},{8,0},{12,4},{1,9},{5,13},{9,1},{13,5},{2,10},{6,14},... | collective-permute-start | bytes 393224 | tf_op jit(solution)/shard_map/ppermute | solution.py:65
  25.1 1.4 concatenate.77
  26.4 1.4 concatenate.74
  28.3 1.3 fusion.34
  30.5 1.4 %concatenate.75 = s32[512,8]{0,1:T(8,128)} concatenate(s32[32,8]{0,1:T(8,128)} %copy-done.4, s32[32,8]{0,1:T(8,128)} %copy-done.7, s32[32,8]{0,1:T(8,128)} %copy-done.9, s32[32,8]{0,1:T(8,128)} %copy-done.10, s32[128,8]{0,1:T(8,128)} %collective-permute-done.8, s32[256,8]{0,1:T(8,128)} %collective-permute-done.9), dimensions={0} | concatenate | bytes 32768 | tf_op jit(solution)/shard_map/concatenate | solution.py:66
  31.8 1.9 %select_reduce_fusion.1 = f32[512]{0:T(512)} fusion(f32[512,8]{0,1:T(8,128)S(1)} %concatenate.78, s32[512,8]{0,1:T(8,128)} %concatenate.75, s32[]{:T(128)} %fusion.34), kind=kLoop, calls=%fused_computation.60 | loop fusion | flops 11776 | bytes 34820 | tf_op jit(solution)/shard_map/reduce_sum | solution.py:99
  33.8 1.8 %pad_maximum_fusion = bf16[128,2048]{1,0:T(8,128)(2,1)} fusion(bf16[32,2048]{1,0:T(8,128)(2,1)S(1)} %collective-permute-done.2, bf16[32,2048]{1,0:T(8,128)(2,1)S(1)} %collective-permute-done.1, bf16[32,2048]{1,0:T(8,128)(2,1)} %collective-permute-done, bf16[32,2048]{1,0:T(8,128)(2,1)} %get-tuple-element.28), kind=kLoop, calls=%fused_computation.26 | loop fusion | flops 2097152 | bytes 1048576 | tf_op jit(solution)/shard_map/concatenate | solution.py:66
  35.7 1.2 collective-permute-start.3
  37.5 0.9 collective-permute-start.20
  39.0 2.9 %collective-permute-start.26 = (s32[32,8]{0,1:T(8,128)}, s32[32,8]{0,1:T(8,128)S(1)}, u32[]{:S(2)}, u32[]{:S(2)}) collective-permute-start(s32[32,8]{0,1:T(8,128)} %get-tuple-element.9), channel_id=1, source_target_pairs={{0,8},{4,12},{8,0},{12,4},{1,9},{5,13},{9,1},{13,5},{2,10},{6,14},... | collective-permute-start | bytes 3080 | tf_op jit(solution)/shard_map/ppermute | solution.py:65
  42.4 1.6 %constant_dynamic-update-slice_fusion.3 = (bf16[256,2048]{1,0:T(8,128)(2,1)}, bf16[512,2048]{1,0:T(8,128)(2,1)}) fusion(bf16[256,2048]{1,0:T(8,128)(2,1)} %get-tuple-element.25, bf16[32,2048]{1,0:T(8,128)(2,1)} %collective-permute-done, bf16[512,2048]{1,0:T(8,128)(2,1)} %get-tuple-element.26), kind=kLoop, calls=%fused_computation.40 | loop fusion | bytes 393216
  45.6 1.1 collective-permute-start.31
  46.6 2.2 %collective-permute-start.32 = (f32[32,8]{0,1:T(8,128)}, f32[32,8]{0,1:T(8,128)S(1)}, u32[]{:S(2)}, u32[]{:S(2)}) collective-permute-start(f32[32,8]{0,1:T(8,128)} %get-tuple-element.10), channel_id=1, source_target_pairs={{0,12},{4,0},{8,4},{12,8},{1,13},{5,1},{9,5},{13,9},{2,14},{6,2},{... | collective-permute-start | bytes 3080 | tf_op jit(solution)/shard_map/ppermute | solution.py:65
  50.4 1.0 collective-permute-start.21
  51.4 0.9 collective-permute-start.28
  52.3 1.4 pad_maximum_fusion.4
  53.7 1.2 collective-permute-start.33
  56.4 1.2 collective-permute-done.33
  59.1 2.2 %collective-permute-start.22 = (bf16[32,2048]{1,0:T(8,128)(2,1)S(1)}, bf16[32,2048]{1,0:T(8,128)(2,1)S(1)}, u32[]{:S(2)}, u32[]{:S(2)}) collective-permute-start(bf16[32,2048]{1,0:T(8,128)(2,1)S(1)} %get-tuple-element.8), channel_id=1, source_target_pairs={{0,12},{4,0},{8,4},{12,8},{1,13},{5,1},{9,5},{13,9},{2,14},{6,2},{... | collective-permute-start | bytes 393224 | tf_op jit(solution)/shard_map/ppermute | solution.py:65
  63.6 2.2 %constant_dynamic-update-slice_fusion = (bf16[256,2048]{1,0:T(8,128)(2,1)}, bf16[512,2048]{1,0:T(8,128)(2,1)}) fusion(bf16[256,2048]{1,0:T(8,128)(2,1)} %get-tuple-element.29, bf16[128,2048]{1,0:T(8,128)(2,1)} %collective-permute-done.3, bf16[512,2048]{1,0:T(8,128)(2,1)} %get-tuple-element.30), kind=kLoop, calls=%fused_computation.37 | loop fusion | bytes 1572864 | tf_op jit(solution)/shard_map/concatenate | solution.py:66
  66.0 1.1 pad_maximum_fusion.1
  67.1 1.6 %collective-permute-start.23 = (bf16[128,2048]{1,0:T(8,128)(2,1)S(1)}, bf16[128,2048]{1,0:T(8,128)(2,1)S(1)}, u32[]{:S(2)}, u32[]{:S(2)}) collective-permute-start(bf16[128,2048]{1,0:T(8,128)(2,1)S(1)} %pad_maximum_fusion.1), channel_id=1, source_target_pairs={{0,2},{2,0},{1,3},{3,1},{4,6},{6,4},{5,7},{7,5},{8,10},{10,8},{9,1... | collective-permute-start | bytes 1572872 | tf_op jit(solution)/shard_map/ppermute | solution.py:65
  68.7 1.6 %constant_dynamic-update-slice_fusion.14 = (bf16[256,2048]{1,0:T(8,128)(2,1)S(1)}, bf16[512,2048]{1,0:T(8,128)(2,1)}) fusion(bf16[256,2048]{1,0:T(8,128)(2,1)S(1)} %copy-done.15, bf16[32,2048]{1,0:T(8,128)(2,1)} %collective-permute-done.20, bf16[512,2048]{1,0:T(8,128)(2,1)} %get-tuple-element.42), kind=kLoop, calls=%fused_computation.51 | loop fusion | bytes 393216
  70.2 1.6 %constant_dynamic-update-slice_fusion.13 = (bf16[256,2048]{1,0:T(8,128)(2,1)S(1)}, bf16[512,2048]{1,0:T(8,128)(2,1)}) fusion(bf16[256,2048]{1,0:T(8,128)(2,1)S(1)} %get-tuple-element.39, bf16[32,2048]{1,0:T(8,128)(2,1)} %collective-permute-done.21, bf16[512,2048]{1,0:T(8,128)(2,1)} %get-tuple-element.40), kind=kLoop, calls=%fused_computation.50 | loop fusion | bytes 393216
  72.5 8.8 %collective-permute-done.23 = bf16[128,2048]{1,0:T(8,128)(2,1)S(1)} collective-permute-done((bf16[128,2048]{1,0:T(8,128)(2,1)S(1)}, bf16[128,2048]{1,0:T(8,128)(2,1)S(1)}, u32[]{:S(2)}, u32[]{:S(2)}) %collective-permute-start.23) | collective-permute-done | bytes 524320 | tf_op jit(solution)/shard_map/ppermute | solution.py:65
  81.3 0.9 constant_dynamic-update-slice_fusion.11
  82.4 5.7 %fusion.2 = f32[512,1536]{1,0:T(8,128)S(1)} fusion(bf16[512,2048]{1,0:T(8,128)(2,1)S(1)} %constant_dynamic-update-slice_fusion.5, bf16[1,2048,1536]{2,1,0:T(8,128)(2,1)} %param.10), kind=kOutput, calls=%fused_computation.2 | convolution fusion | flops 3221225472 | bytes 11534336 | tf_op jit(solution)/shard_map/dot_general | solution.py:9
  88.1 1.8 %convert_multiply_fusion.1 = f32[512,2048]{1,0:T(8,128)S(1)} fusion(f32[512]{0:T(512)S(1)} %copy-done.18, bf16[1,768,2048]{2,1,0:T(8,128)(2,1)S(1)} %copy-done, f32[512,1536]{1,0:T(8,128)S(1)} %fusion.2), kind=kOutput, calls=%fused_computation.5 | convolution fusion | flops 1616117760 | bytes 10487808 | tf_op jit(solution)/shard_map/dot_general | solution.py:11
  90.6 0.9 copy-done.16
  91.7 3.4 %fusion = f32[512,1536]{1,0:T(8,128)S(1)} fusion(bf16[512,2048]{1,0:T(8,128)(2,1)S(1)} %constant_dynamic-update-slice_fusion.16, bf16[1,2048,1536]{2,1,0:T(8,128)(2,1)S(1)} %bitcast.21), kind=kOutput, calls=%fused_computation | convolution fusion | flops 3221225472 | bytes 11534336 | tf_op jit(solution)/shard_map/dot_general | solution.py:9
  95.1 1.8 %convert_multiply_fusion = f32[512,2048]{1,0:T(8,128)S(1)} fusion(f32[512]{0:T(512)S(1)} %select_reduce_fusion, bf16[1,768,2048]{2,1,0:T(8,128)(2,1)S(1)} %copy-done, f32[512,1536]{1,0:T(8,128)S(1)} %fusion), kind=kOutput, calls=%fused_computation.4 | convolution fusion | flops 1616117760 | bytes 10487808 | tf_op jit(solution)/shard_map/dot_general | solution.py:11
  98.1 1.6 %collective-permute-start.16 = (bf16[128,2048]{1,0:T(8,128)(2,1)S(1)}, bf16[128,2048]{1,0:T(8,128)(2,1)S(1)}, u32[]{:S(2)}, u32[]{:S(2)}) collective-permute-start(bf16[128,2048]{1,0:T(8,128)(2,1)S(1)} %split.141), channel_id=1, source_target_pairs={{0,2},{2,0},{1,3},{3,1},{4,6},{6,4},{5,7},{7,5},{8,10},{10,8},{9,1... | collective-permute-start | bytes 1572872 | tf_op jit(solution)/shard_map/ppermute | solution.py:74
  100.3 1.6 %collective-permute-start.36 = (bf16[128,2048]{1,0:T(8,128)(2,1)S(1)}, bf16[128,2048]{1,0:T(8,128)(2,1)S(1)}, u32[]{:S(2)}, u32[]{:S(2)}) collective-permute-start(bf16[128,2048]{1,0:T(8,128)(2,1)S(1)} %split.140), channel_id=1, source_target_pairs={{0,2},{2,0},{1,3},{3,1},{4,6},{6,4},{5,7},{7,5},{8,10},{10,8},{9,1... | collective-permute-start | bytes 1572872 | tf_op jit(solution)/shard_map/ppermute | solution.py:74
  101.9 11.1 %collective-permute-done.16 = bf16[128,2048]{1,0:T(8,128)(2,1)S(1)} collective-permute-done((bf16[128,2048]{1,0:T(8,128)(2,1)S(1)}, bf16[128,2048]{1,0:T(8,128)(2,1)S(1)}, u32[]{:S(2)}, u32[]{:S(2)}) %collective-permute-start.16) | collective-permute-done | bytes 524320 | tf_op jit(solution)/shard_map/ppermute | solution.py:74
  113.1 2.3 %collective-permute-start.17 = (bf16[32,2048]{1,0:T(8,128)(2,1)S(1)}, bf16[32,2048]{1,0:T(8,128)(2,1)S(1)}, u32[]{:S(2)}, u32[]{:S(2)}) collective-permute-start(bf16[32,2048]{1,0:T(8,128)(2,1)S(1)} %get-tuple-element.15), channel_id=1, source_target_pairs={{0,12},{4,0},{8,4},{12,8},{1,13},{5,1},{9,5},{13,9},{2,14},{6,2},{... | collective-permute-start | bytes 393224 | tf_op jit(solution)/shard_map/ppermute | solution.py:74
  116.0 7.2 %collective-permute-done.36 = bf16[128,2048]{1,0:T(8,128)(2,1)S(1)} collective-permute-done((bf16[128,2048]{1,0:T(8,128)(2,1)S(1)}, bf16[128,2048]{1,0:T(8,128)(2,1)S(1)}, u32[]{:S(2)}, u32[]{:S(2)}) %collective-permute-start.36) | collective-permute-done | bytes 524320 | tf_op jit(solution)/shard_map/ppermute | solution.py:74
  123.4 2.3 %collective-permute-start.37 = (bf16[32,2048]{1,0:T(8,128)(2,1)S(1)}, bf16[32,2048]{1,0:T(8,128)(2,1)S(1)}, u32[]{:S(2)}, u32[]{:S(2)}) collective-permute-start(bf16[32,2048]{1,0:T(8,128)(2,1)S(1)} %get-tuple-element.20), channel_id=1, source_target_pairs={{0,12},{4,0},{8,4},{12,8},{1,13},{5,1},{9,5},{13,9},{2,14},{6,2},{... | collective-permute-start | bytes 393224 | tf_op jit(solution)/shard_map/ppermute | solution.py:74
  127.2 2.4 %collective-permute-done.37 = bf16[32,2048]{1,0:T(8,128)(2,1)S(1)} collective-permute-done((bf16[32,2048]{1,0:T(8,128)(2,1)S(1)}, bf16[32,2048]{1,0:T(8,128)(2,1)S(1)}, u32[]{:S(2)}, u32[]{:S(2)}) %collective-permute-start.37) | collective-permute-done | bytes 131104 | tf_op jit(solution)/shard_map/ppermute | solution.py:74
  129.6 7.5 %collective-permute-done.38 = bf16[32,2048]{1,0:T(8,128)(2,1)S(1)} collective-permute-done((bf16[32,2048]{1,0:T(8,128)(2,1)S(1)}, bf16[32,2048]{1,0:T(8,128)(2,1)S(1)}, u32[]{:S(2)}, u32[]{:S(2)}) %collective-permute-start.38) | collective-permute-done | bytes 131104 | tf_op jit(solution)/shard_map/ppermute | solution.py:74
  (125 shorter events, 23.7 us)
Async XLA Ops:
  0.0 88.1 %copy-start = (bf16[1,768,2048]{2,1,0:T(8,128)(2,1)S(1)}, bf16[1,768,2048]{2,1,0:T(8,128)(2,1)}, u32[]{:S(2)}) copy-start(bf16[1,768,2048]{2,1,0:T(8,128)(2,1)} %param.11) | copy-start | bytes 9437188
  2.3 27.3 %copy-start.3 = (f32[32,8]{0,1:T(8,128)}, f32[32,8]{0,1:T(8,128)S(1)}, u32[]{:S(2)}) copy-start(f32[32,8]{0,1:T(8,128)S(1)} %get-tuple-element.45) | copy-start | bytes 3076
  2.3 9.4 %collective-permute-start.10 = (f32[32,8]{0,1:T(8,128)S(1)}, f32[32,8]{0,1:T(8,128)S(1)}, u32[]{:S(2)}, u32[]{:S(2)}) collective-permute-start(f32[32,8]{0,1:T(8,128)S(1)} %get-tuple-element.45), channel_id=1, source_target_pairs={{0,4},{4,8},{8,12},{12,0},{1,5},{5,9},{9,13},{13,1},{2,6},{6,10},{... | collective-permute-start | bytes 3080 | tf_op jit(solution)/shard_map/ppermute | solution.py:65
  5.4 9.2 %collective-permute-start.11 = (f32[32,8]{0,1:T(8,128)S(1)}, f32[32,8]{0,1:T(8,128)S(1)}, u32[]{:S(2)}, u32[]{:S(2)}) collective-permute-start(f32[32,8]{0,1:T(8,128)S(1)} %get-tuple-element.45), channel_id=1, source_target_pairs={{0,8},{4,12},{8,0},{12,4},{1,9},{5,13},{9,1},{13,5},{2,10},{6,14},... | collective-permute-start | bytes 3080 | tf_op jit(solution)/shard_map/ppermute | solution.py:65
  8.0 6.7 %collective-permute-start.12 = (f32[32,8]{0,1:T(8,128)S(1)}, f32[32,8]{0,1:T(8,128)S(1)}, u32[]{:S(2)}, u32[]{:S(2)}) collective-permute-start(f32[32,8]{0,1:T(8,128)S(1)} %get-tuple-element.45), channel_id=1, source_target_pairs={{0,12},{4,0},{8,4},{12,8},{1,13},{5,1},{9,5},{13,9},{2,14},{6,2},{... | collective-permute-start | bytes 3080 | tf_op jit(solution)/shard_map/ppermute | solution.py:65
  10.7 18.9 %copy-start.4 = (s32[32,8]{0,1:T(8,128)}, s32[32,8]{0,1:T(8,128)S(1)}, u32[]{:S(2)}) copy-start(s32[32,8]{0,1:T(8,128)S(1)} %get-tuple-element.43) | copy-start | bytes 3076
  10.7 6.1 %collective-permute-start.5 = (s32[32,8]{0,1:T(8,128)S(1)}, s32[32,8]{0,1:T(8,128)S(1)}, u32[]{:S(2)}, u32[]{:S(2)}) collective-permute-start(s32[32,8]{0,1:T(8,128)S(1)} %get-tuple-element.43), channel_id=1, source_target_pairs={{0,4},{4,8},{8,12},{12,0},{1,5},{5,9},{9,13},{13,1},{2,6},{6,10},{... | collective-permute-start | bytes 3080 | tf_op jit(solution)/shard_map/ppermute | solution.py:65
  11.4 5.4 %collective-permute-start.6 = (s32[32,8]{0,1:T(8,128)S(1)}, s32[32,8]{0,1:T(8,128)S(1)}, u32[]{:S(2)}, u32[]{:S(2)}) collective-permute-start(s32[32,8]{0,1:T(8,128)S(1)} %get-tuple-element.43), channel_id=1, source_target_pairs={{0,8},{4,12},{8,0},{12,4},{1,9},{5,13},{9,1},{13,5},{2,10},{6,14},... | collective-permute-start | bytes 3080 | tf_op jit(solution)/shard_map/ppermute | solution.py:65
  11.8 17.9 %copy-start.5 = (f32[32,8]{0,1:T(8,128)}, f32[32,8]{0,1:T(8,128)S(1)}, u32[]{:S(2)}) copy-start(f32[32,8]{0,1:T(8,128)S(1)} %collective-permute-done.10) | copy-start | bytes 3076
  11.8 5.1 %collective-permute-start.7 = (s32[32,8]{0,1:T(8,128)S(1)}, s32[32,8]{0,1:T(8,128)S(1)}, u32[]{:S(2)}, u32[]{:S(2)}) collective-permute-start(s32[32,8]{0,1:T(8,128)S(1)} %get-tuple-element.43), channel_id=1, source_target_pairs={{0,12},{4,0},{8,4},{12,8},{1,13},{5,1},{9,5},{13,9},{2,14},{6,2},{... | collective-permute-start | bytes 3080 | tf_op jit(solution)/shard_map/ppermute | solution.py:65
  14.6 15.0 %copy-start.6 = (f32[32,8]{0,1:T(8,128)}, f32[32,8]{0,1:T(8,128)S(1)}, u32[]{:S(2)}) copy-start(f32[32,8]{0,1:T(8,128)S(1)} %collective-permute-done.11) | copy-start | bytes 3076
  15.3 9.8 %collective-permute-start.13 = (f32[128,8]{0,1:T(8,128)}, f32[128,8]{0,1:T(8,128)}, u32[]{:S(2)}, u32[]{:S(2)}) collective-permute-start(f32[128,8]{0,1:T(8,128)} %pad_maximum_fusion.3), channel_id=1, source_target_pairs={{0,2},{2,0},{1,3},{3,1},{4,6},{6,4},{5,7},{7,5},{8,10},{10,8},{9,1... | collective-permute-start | bytes 12296 | tf_op jit(solution)/shard_map/ppermute | solution.py:65
  17.5 8.9 %collective-permute-start.8 = (s32[128,8]{0,1:T(8,128)}, s32[128,8]{0,1:T(8,128)}, u32[]{:S(2)}, u32[]{:S(2)}) collective-permute-start(s32[128,8]{0,1:T(8,128)} %pad_add_fusion), channel_id=1, source_target_pairs={{0,2},{2,0},{1,3},{3,1},{4,6},{6,4},{5,7},{7,5},{8,10},{10,8},{9,1... | collective-permute-start | bytes 12296 | tf_op jit(solution)/shard_map/ppermute | solution.py:65
  20.7 13.1 %collective-permute-start = (bf16[32,2048]{1,0:T(8,128)(2,1)}, bf16[32,2048]{1,0:T(8,128)(2,1)}, u32[]{:S(2)}, u32[]{:S(2)}) collective-permute-start(bf16[32,2048]{1,0:T(8,128)(2,1)} %get-tuple-element.28), channel_id=1, source_target_pairs={{0,4},{4,8},{8,12},{12,0},{1,5},{5,9},{9,13},{13,1},{2,6},{6,10},{... | collective-permute-start | bytes 393224 | tf_op jit(solution)/shard_map/ppermute | solution.py:65
  22.7 11.1 %collective-permute-start.1 = (bf16[32,2048]{1,0:T(8,128)(2,1)}, bf16[32,2048]{1,0:T(8,128)(2,1)S(1)}, u32[]{:S(2)}, u32[]{:S(2)}) collective-permute-start(bf16[32,2048]{1,0:T(8,128)(2,1)} %get-tuple-element.28), channel_id=1, source_target_pairs={{0,8},{4,12},{8,0},{12,4},{1,9},{5,13},{9,1},{13,5},{2,10},{6,14},... | collective-permute-start | bytes 393224 | tf_op jit(solution)/shard_map/ppermute | solution.py:65
  24.6 9.2 %collective-permute-start.2 = (bf16[32,2048]{1,0:T(8,128)(2,1)}, bf16[32,2048]{1,0:T(8,128)(2,1)S(1)}, u32[]{:S(2)}, u32[]{:S(2)}) collective-permute-start(bf16[32,2048]{1,0:T(8,128)(2,1)} %get-tuple-element.28), channel_id=1, source_target_pairs={{0,12},{4,0},{8,4},{12,8},{1,13},{5,1},{9,5},{13,9},{2,14},{6,2},{... | collective-permute-start | bytes 393224 | tf_op jit(solution)/shard_map/ppermute | solution.py:65
  26.4 3.2 %collective-permute-start.14 = (f32[256,8]{0,1:T(8,128)}, f32[256,8]{0,1:T(8,128)}, u32[]{:S(2)}, u32[]{:S(2)}) collective-permute-start(f32[256,8]{0,1:T(8,128)} %concatenate.77), channel_id=1, source_target_pairs={{0,1},{1,0},{2,3},{3,2},{4,5},{5,4},{6,7},{7,6},{8,9},{9,8},{10,11... | collective-permute-start | bytes 24584 | tf_op jit(solution)/shard_map/ppermute | solution.py:65
  27.8 2.7 %collective-permute-start.9 = (s32[256,8]{0,1:T(8,128)}, s32[256,8]{0,1:T(8,128)}, u32[]{:S(2)}, u32[]{:S(2)}) collective-permute-start(s32[256,8]{0,1:T(8,128)} %concatenate.74), channel_id=1, source_target_pairs={{0,1},{1,0},{2,3},{3,2},{4,5},{5,4},{6,7},{7,6},{8,9},{9,8},{10,11... | collective-permute-start | bytes 24584 | tf_op jit(solution)/shard_map/ppermute | solution.py:65
  33.8 21.8 %copy-start.2 = (s32[32,8]{0,1:T(8,128)S(1)}, s32[32,8]{0,1:T(8,128)}, u32[]{:S(2)}) copy-start(s32[32,8]{0,1:T(8,128)} %get-tuple-element.9) | copy-start | bytes 3076
  33.8 23.8 %copy-start.1 = (f32[32,8]{0,1:T(8,128)S(1)}, f32[32,8]{0,1:T(8,128)}, u32[]{:S(2)}) copy-start(f32[32,8]{0,1:T(8,128)} %get-tuple-element.10) | copy-start | bytes 3076
  35.7 27.9 %collective-permute-start.3 = (bf16[128,2048]{1,0:T(8,128)(2,1)}, bf16[128,2048]{1,0:T(8,128)(2,1)}, u32[]{:S(2)}, u32[]{:S(2)}) collective-permute-start(bf16[128,2048]{1,0:T(8,128)(2,1)} %pad_maximum_fusion), channel_id=1, source_target_pairs={{0,2},{2,0},{1,3},{3,1},{4,6},{6,4},{5,7},{7,5},{8,10},{10,8},{9,1... | collective-permute-start | bytes 1572872 | tf_op jit(solution)/shard_map/ppermute | solution.py:65
  37.5 28.4 %collective-permute-start.20 = (bf16[32,2048]{1,0:T(8,128)(2,1)S(1)}, bf16[32,2048]{1,0:T(8,128)(2,1)}, u32[]{:S(2)}, u32[]{:S(2)}) collective-permute-start(bf16[32,2048]{1,0:T(8,128)(2,1)S(1)} %get-tuple-element.8), channel_id=1, source_target_pairs={{0,4},{4,8},{8,12},{12,0},{1,5},{5,9},{9,13},{13,1},{2,6},{6,10},{... | collective-permute-start | bytes 393224 | tf_op jit(solution)/shard_map/ppermute | solution.py:65
  38.4 6.4 %collective-permute-start.25 = (s32[32,8]{0,1:T(8,128)}, s32[32,8]{0,1:T(8,128)S(1)}, u32[]{:S(2)}, u32[]{:S(2)}) collective-permute-start(s32[32,8]{0,1:T(8,128)} %get-tuple-element.9), channel_id=1, source_target_pairs={{0,4},{4,8},{8,12},{12,0},{1,5},{5,9},{9,13},{13,1},{2,6},{6,10},{... | collective-permute-start | bytes 3080 | tf_op jit(solution)/shard_map/ppermute | solution.py:65
  39.0 6.5 %collective-permute-start.26 = (s32[32,8]{0,1:T(8,128)}, s32[32,8]{0,1:T(8,128)S(1)}, u32[]{:S(2)}, u32[]{:S(2)}) collective-permute-start(s32[32,8]{0,1:T(8,128)} %get-tuple-element.9), channel_id=1, source_target_pairs={{0,8},{4,12},{8,0},{12,4},{1,9},{5,13},{9,1},{13,5},{2,10},{6,14},... | collective-permute-start | bytes 3080 | tf_op jit(solution)/shard_map/ppermute | solution.py:65
  41.9 4.7 %collective-permute-start.27 = (s32[32,8]{0,1:T(8,128)}, s32[32,8]{0,1:T(8,128)S(1)}, u32[]{:S(2)}, u32[]{:S(2)}) collective-permute-start(s32[32,8]{0,1:T(8,128)} %get-tuple-element.9), channel_id=1, source_target_pairs={{0,12},{4,0},{8,4},{12,8},{1,13},{5,1},{9,5},{13,9},{2,14},{6,2},{... | collective-permute-start | bytes 3080 | tf_op jit(solution)/shard_map/ppermute | solution.py:65
  44.8 5.6 %collective-permute-start.30 = (f32[32,8]{0,1:T(8,128)}, f32[32,8]{0,1:T(8,128)S(1)}, u32[]{:S(2)}, u32[]{:S(2)}) collective-permute-start(f32[32,8]{0,1:T(8,128)} %get-tuple-element.10), channel_id=1, source_target_pairs={{0,4},{4,8},{8,12},{12,0},{1,5},{5,9},{9,13},{13,1},{2,6},{6,10},{... | collective-permute-start | bytes 3080 | tf_op jit(solution)/shard_map/ppermute | solution.py:65
  45.6 5.9 %collective-permute-start.31 = (f32[32,8]{0,1:T(8,128)}, f32[32,8]{0,1:T(8,128)S(1)}, u32[]{:S(2)}, u32[]{:S(2)}) collective-permute-start(f32[32,8]{0,1:T(8,128)} %get-tuple-element.10), channel_id=1, source_target_pairs={{0,8},{4,12},{8,0},{12,4},{1,9},{5,13},{9,1},{13,5},{2,10},{6,14},... | collective-permute-start | bytes 3080 | tf_op jit(solution)/shard_map/ppermute | solution.py:65
  46.6 5.7 %collective-permute-start.32 = (f32[32,8]{0,1:T(8,128)}, f32[32,8]{0,1:T(8,128)S(1)}, u32[]{:S(2)}, u32[]{:S(2)}) collective-permute-start(f32[32,8]{0,1:T(8,128)} %get-tuple-element.10), channel_id=1, source_target_pairs={{0,12},{4,0},{8,4},{12,8},{1,13},{5,1},{9,5},{13,9},{2,14},{6,2},{... | collective-permute-start | bytes 3080 | tf_op jit(solution)/shard_map/ppermute | solution.py:65
  50.4 15.6 %collective-permute-start.21 = (bf16[32,2048]{1,0:T(8,128)(2,1)S(1)}, bf16[32,2048]{1,0:T(8,128)(2,1)}, u32[]{:S(2)}, u32[]{:S(2)}) collective-permute-start(bf16[32,2048]{1,0:T(8,128)(2,1)S(1)} %get-tuple-element.8), channel_id=1, source_target_pairs={{0,8},{4,12},{8,0},{12,4},{1,9},{5,13},{9,1},{13,5},{2,10},{6,14},... | collective-permute-start | bytes 393224 | tf_op jit(solution)/shard_map/ppermute | solution.py:65
  51.4 4.1 %collective-permute-start.28 = (s32[128,8]{0,1:T(8,128)S(1)}, s32[128,8]{0,1:T(8,128)}, u32[]{:S(2)}, u32[]{:S(2)}) collective-permute-start(s32[128,8]{0,1:T(8,128)S(1)} %pad_add_fusion.1), channel_id=1, source_target_pairs={{0,2},{2,0},{1,3},{3,1},{4,6},{6,4},{5,7},{7,5},{8,10},{10,8},{9,1... | collective-permute-start | bytes 12296 | tf_op jit(solution)/shard_map/ppermute | solution.py:65
  53.7 3.9 %collective-permute-start.33 = (f32[128,8]{0,1:T(8,128)}, f32[128,8]{0,1:T(8,128)}, u32[]{:S(2)}, u32[]{:S(2)}) collective-permute-start(f32[128,8]{0,1:T(8,128)} %pad_maximum_fusion.4), channel_id=1, source_target_pairs={{0,2},{2,0},{1,3},{3,1},{4,6},{6,4},{5,7},{7,5},{8,10},{10,8},{9,1... | collective-permute-start | bytes 12296 | tf_op jit(solution)/shard_map/ppermute | solution.py:65
  56.4 2.7 %collective-permute-start.29 = (s32[256,8]{0,1:T(8,128)S(1)}, s32[256,8]{0,1:T(8,128)S(1)}, u32[]{:S(2)}, u32[]{:S(2)}) collective-permute-start(s32[256,8]{0,1:T(8,128)S(1)} %concatenate.83), channel_id=1, source_target_pairs={{0,1},{1,0},{2,3},{3,2},{4,5},{5,4},{6,7},{7,6},{8,9},{9,8},{10,11... | collective-permute-start | bytes 24584 | tf_op jit(solution)/shard_map/ppermute | solution.py:65
  58.4 3.7 %collective-permute-start.34 = (f32[256,8]{0,1:T(8,128)S(1)}, f32[256,8]{0,1:T(8,128)S(1)}, u32[]{:S(2)}, u32[]{:S(2)}) collective-permute-start(f32[256,8]{0,1:T(8,128)S(1)} %concatenate.86), channel_id=1, source_target_pairs={{0,1},{1,0},{2,3},{3,2},{4,5},{5,4},{6,7},{7,6},{8,9},{9,8},{10,11... | collective-permute-start | bytes 24584 | tf_op jit(solution)/shard_map/ppermute | solution.py:65
  59.1 6.9 %collective-permute-start.22 = (bf16[32,2048]{1,0:T(8,128)(2,1)S(1)}, bf16[32,2048]{1,0:T(8,128)(2,1)S(1)}, u32[]{:S(2)}, u32[]{:S(2)}) collective-permute-start(bf16[32,2048]{1,0:T(8,128)(2,1)S(1)} %get-tuple-element.8), channel_id=1, source_target_pairs={{0,12},{4,0},{8,4},{12,8},{1,13},{5,1},{9,5},{13,9},{2,14},{6,2},{... | collective-permute-start | bytes 393224 | tf_op jit(solution)/shard_map/ppermute | solution.py:65
  65.7 16.5 %copy-start.17 = (bf16[512,2048]{1,0:T(8,128)(2,1)S(1)}, bf16[512,2048]{1,0:T(8,128)(2,1)}, u32[]{:S(2)}) copy-start(bf16[512,2048]{1,0:T(8,128)(2,1)} %get-tuple-element.19) | copy-start | bytes 6291460
  65.7 16.5 %collective-permute-start.4 = (bf16[256,2048]{1,0:T(8,128)(2,1)}, bf16[256,2048]{1,0:T(8,128)(2,1)S(1)}, u32[]{:S(2)}, u32[]{:S(2)}) collective-permute-start(bf16[256,2048]{1,0:T(8,128)(2,1)} %get-tuple-element.18), channel_id=1, source_target_pairs={{0,1},{1,0},{2,3},{3,2},{4,5},{5,4},{6,7},{7,6},{8,9},{9,8},{10,11... | collective-permute-start | bytes 3145736 | tf_op jit(solution)/shard_map/ppermute | solution.py:65
  67.1 14.2 %collective-permute-start.23 = (bf16[128,2048]{1,0:T(8,128)(2,1)S(1)}, bf16[128,2048]{1,0:T(8,128)(2,1)S(1)}, u32[]{:S(2)}, u32[]{:S(2)}) collective-permute-start(bf16[128,2048]{1,0:T(8,128)(2,1)S(1)} %pad_maximum_fusion.1), channel_id=1, source_target_pairs={{0,2},{2,0},{1,3},{3,1},{4,6},{6,4},{5,7},{7,5},{8,10},{10,8},{9,1... | collective-permute-start | bytes 1572872 | tf_op jit(solution)/shard_map/ppermute | solution.py:65
  82.2 8.5 %collective-permute-start.24 = (bf16[256,2048]{1,0:T(8,128)(2,1)S(1)}, bf16[256,2048]{1,0:T(8,128)(2,1)S(1)}, u32[]{:S(2)}, u32[]{:S(2)}) collective-permute-start(bf16[256,2048]{1,0:T(8,128)(2,1)S(1)} %get-tuple-element.23), channel_id=1, source_target_pairs={{0,1},{1,0},{2,3},{3,2},{4,5},{5,4},{6,7},{7,6},{8,9},{9,8},{10,11... | collective-permute-start | bytes 3145736 | tf_op jit(solution)/shard_map/ppermute | solution.py:65
  90.1 7.6 %collective-permute-start.15 = (bf16[256,2048]{1,0:T(8,128)(2,1)S(1)}, bf16[256,2048]{1,0:T(8,128)(2,1)S(1)}, u32[]{:S(2)}, u32[]{:S(2)}) collective-permute-start(bf16[256,2048]{1,0:T(8,128)(2,1)S(1)} %split.139), channel_id=1, source_target_pairs={{0,1},{1,0},{2,3},{3,2},{4,5},{5,4},{6,7},{7,6},{8,9},{9,8},{10,11... | collective-permute-start | bytes 3145736 | tf_op jit(solution)/shard_map/ppermute | solution.py:74
  97.1 2.8 %collective-permute-start.35 = (bf16[256,2048]{1,0:T(8,128)(2,1)S(1)}, bf16[256,2048]{1,0:T(8,128)(2,1)S(1)}, u32[]{:S(2)}, u32[]{:S(2)}) collective-permute-start(bf16[256,2048]{1,0:T(8,128)(2,1)S(1)} %split.138), channel_id=1, source_target_pairs={{0,1},{1,0},{2,3},{3,2},{4,5},{5,4},{6,7},{7,6},{8,9},{9,8},{10,11... | collective-permute-start | bytes 3145736 | tf_op jit(solution)/shard_map/ppermute | solution.py:74
  98.1 14.9 %collective-permute-start.16 = (bf16[128,2048]{1,0:T(8,128)(2,1)S(1)}, bf16[128,2048]{1,0:T(8,128)(2,1)S(1)}, u32[]{:S(2)}, u32[]{:S(2)}) collective-permute-start(bf16[128,2048]{1,0:T(8,128)(2,1)S(1)} %split.141), channel_id=1, source_target_pairs={{0,2},{2,0},{1,3},{3,1},{4,6},{6,4},{5,7},{7,5},{8,10},{10,8},{9,1... | collective-permute-start | bytes 1572872 | tf_op jit(solution)/shard_map/ppermute | solution.py:74
  100.3 22.9 %collective-permute-start.36 = (bf16[128,2048]{1,0:T(8,128)(2,1)S(1)}, bf16[128,2048]{1,0:T(8,128)(2,1)S(1)}, u32[]{:S(2)}, u32[]{:S(2)}) collective-permute-start(bf16[128,2048]{1,0:T(8,128)(2,1)S(1)} %split.140), channel_id=1, source_target_pairs={{0,2},{2,0},{1,3},{3,1},{4,6},{6,4},{5,7},{7,5},{8,10},{10,8},{9,1... | collective-permute-start | bytes 1572872 | tf_op jit(solution)/shard_map/ppermute | solution.py:74
  113.1 12.6 %collective-permute-start.17 = (bf16[32,2048]{1,0:T(8,128)(2,1)S(1)}, bf16[32,2048]{1,0:T(8,128)(2,1)S(1)}, u32[]{:S(2)}, u32[]{:S(2)}) collective-permute-start(bf16[32,2048]{1,0:T(8,128)(2,1)S(1)} %get-tuple-element.15), channel_id=1, source_target_pairs={{0,12},{4,0},{8,4},{12,8},{1,13},{5,1},{9,5},{13,9},{2,14},{6,2},{... | collective-permute-start | bytes 393224 | tf_op jit(solution)/shard_map/ppermute | solution.py:74
  115.4 11.7 %collective-permute-start.18 = (bf16[32,2048]{1,0:T(8,128)(2,1)S(1)}, bf16[32,2048]{1,0:T(8,128)(2,1)S(1)}, u32[]{:S(2)}, u32[]{:S(2)}) collective-permute-start(bf16[32,2048]{1,0:T(8,128)(2,1)S(1)} %get-tuple-element.17), channel_id=1, source_target_pairs={{0,8},{4,12},{8,0},{12,4},{1,9},{5,13},{9,1},{13,5},{2,10},{6,14},... | collective-permute-start | bytes 393224 | tf_op jit(solution)/shard_map/ppermute | solution.py:74
  115.4 11.7 %collective-permute-start.19 = (bf16[32,2048]{1,0:T(8,128)(2,1)S(1)}, bf16[32,2048]{1,0:T(8,128)(2,1)S(1)}, u32[]{:S(2)}, u32[]{:S(2)}) collective-permute-start(bf16[32,2048]{1,0:T(8,128)(2,1)S(1)} %get-tuple-element.16), channel_id=1, source_target_pairs={{0,4},{4,8},{8,12},{12,0},{1,5},{5,9},{9,13},{13,1},{2,6},{6,10},{... | collective-permute-start | bytes 393224 | tf_op jit(solution)/shard_map/ppermute | solution.py:74
  123.4 6.1 %collective-permute-start.37 = (bf16[32,2048]{1,0:T(8,128)(2,1)S(1)}, bf16[32,2048]{1,0:T(8,128)(2,1)S(1)}, u32[]{:S(2)}, u32[]{:S(2)}) collective-permute-start(bf16[32,2048]{1,0:T(8,128)(2,1)S(1)} %get-tuple-element.20), channel_id=1, source_target_pairs={{0,12},{4,0},{8,4},{12,8},{1,13},{5,1},{9,5},{13,9},{2,14},{6,2},{... | collective-permute-start | bytes 393224 | tf_op jit(solution)/shard_map/ppermute | solution.py:74
  125.7 11.4 %collective-permute-start.38 = (bf16[32,2048]{1,0:T(8,128)(2,1)S(1)}, bf16[32,2048]{1,0:T(8,128)(2,1)S(1)}, u32[]{:S(2)}, u32[]{:S(2)}) collective-permute-start(bf16[32,2048]{1,0:T(8,128)(2,1)S(1)} %get-tuple-element.22), channel_id=1, source_target_pairs={{0,8},{4,12},{8,0},{12,4},{1,9},{5,13},{9,1},{13,5},{2,10},{6,14},... | collective-permute-start | bytes 393224 | tf_op jit(solution)/shard_map/ppermute | solution.py:74
  125.7 11.4 %collective-permute-start.39 = (bf16[32,2048]{1,0:T(8,128)(2,1)S(1)}, bf16[32,2048]{1,0:T(8,128)(2,1)S(1)}, u32[]{:S(2)}, u32[]{:S(2)}) collective-permute-start(bf16[32,2048]{1,0:T(8,128)(2,1)S(1)} %get-tuple-element.21), channel_id=1, source_target_pairs={{0,4},{4,8},{8,12},{12,0},{1,5},{5,9},{9,13},{13,1},{2,6},{6,10},{... | collective-permute-start | bytes 393224 | tf_op jit(solution)/shard_map/ppermute | solution.py:74
  (13 other events, 58.4 us)

commit v4 on v3

--- a/solution.py
+++ b/solution.py
@@ -58,12 +58,12 @@
 AXES = ("ez", "ex", "ec")
 
 
-def gather_stage(blocks, axis, size):
-    got = [blocks]
+def gather_stage(block, axis, size):
+    got = [block]
     for shift in range(1, size):
         pairs = [(i, (i + shift) % size) for i in range(size)]
-        got.append(jax.tree.map(lambda b: lax.ppermute(b, axis, pairs), blocks))
-    return jax.tree.map(lambda *parts: jnp.concatenate(parts, axis=0), *got)
+        got.append(lax.ppermute(block, axis, pairs))
+    return jnp.concatenate(got, axis=0)
 
 
 def scatter_stage(part, axis, size):
@@ -76,28 +76,36 @@
 
 
 def dense_shards(tokens, expert_ids, gate_scores, host_expert, w_in, w_down):
+    tok_rows, width_model = tokens.shape
     hidden_width = w_down.shape[1]
     experts = host_expert.shape[0]
     sizes = [lax.axis_size(a) for a in AXES]
+    hosts = sizes[0] * sizes[1] * sizes[2]
     me = (lax.axis_index("ez") * sizes[1] + lax.axis_index("ex")) * sizes[2] + lax.axis_index("ec")
-    my_expert = jnp.sum(jnp.where(jnp.arange(experts, dtype=jnp.int32) == me, host_expert, 0))
     weights = gate_scores / jnp.sum(gate_scores, axis=1, keepdims=True)
-    streams = [
-        jax.tree.map(lambda a: jnp.split(a, STREAMS, axis=0)[k], (tokens, expert_ids, weights))
-        for k in range(STREAMS)
-    ]
+    chosen = expert_ids[:, :, None] == host_expert[None, None, :]
+    per_host = jnp.sum(jnp.where(chosen, weights[:, :, None], 0.0), axis=1)
+    hi = per_host.astype(jnp.bfloat16)
+    rest = per_host - hi.astype(jnp.float32)
+    lo = rest.astype(jnp.bfloat16)
+    lo2 = (rest - lo.astype(jnp.float32)).astype(jnp.bfloat16)
+    extra = -(-3 * hosts // 128) * 128
+    meta = jnp.concatenate([hi, lo, lo2, jnp.zeros((tok_rows, extra - 3 * hosts), jnp.bfloat16)], axis=1)
+    carried = jnp.concatenate([tokens, meta], axis=1)
+    pick = (jnp.arange(hosts, dtype=jnp.int32) == me).astype(jnp.float32)
     results = []
     held = None
-    for blocks in streams:
+    for rows in jnp.split(carried, STREAMS, axis=0):
         if held is not None:
-            held, blocks = lax.optimization_barrier((held, blocks))
-        blocks = gather_stage(blocks, AXES[0], sizes[0])
-        held = blocks[0]
+            held, rows = lax.optimization_barrier((held, rows))
+        rows = gather_stage(rows, AXES[0], sizes[0])
+        held = rows
         for axis, size in zip(AXES[1:], sizes[1:]):
-            blocks = gather_stage(blocks, axis, size)
-        rows, gate, score = blocks
-        mine = jnp.sum(jnp.where(gate == my_expert, score, 0.0), axis=1)
-        out = expert_block(rows, w_in[0], w_down[0], hidden_width)
+            rows = gather_stage(rows, axis, size)
+        tail = rows[:, width_model:width_model + 3 * hosts].astype(jnp.float32)
+        gate = tail[:, :hosts] + tail[:, hosts:2 * hosts] + tail[:, 2 * hosts:]
+        mine = jnp.sum(gate * pick[None, :], axis=1)
+        out = expert_block(rows[:, :width_model], w_in[0], w_down[0], hidden_width)
         part = out.astype(jnp.float32) * mine[:, None]
         for axis, size in list(zip(AXES, sizes))[::-1]:
             part = scatter_stage(part, axis, size)

time: 139 us -> 106 us (0.76)
  starting transfers between devices: 45.8 us -> 29.1 us
  local copies, waits for them, and re-layouts: 24 us -> 10.8 us
  other arithmetic: 13.9 us -> 6.12 us
  waiting for transfers between devices: 41 us -> 48.5 us
  matrix products: 12.8 us -> 10.6 us
    ppermute x30 -> x10, starting transfers between devices: 35.8 us -> 15.2 us  [gather_stage(): got.append(lax.ppermute(block, axis, pairs))]
    ppermute x30 -> x10, waiting for transfers between devices: 11.7 us -> 23.5 us  [gather_stage(): got.append(lax.ppermute(block, axis, pairs))]
    concatenate x12 -> x5, local copies, waits for them, and re-layouts: 11.2 us -> 3.25 us  [the longest x1 1.74 us: dense_shards(): carried = jnp.concatenate([tokens, meta], axis=1)]
    unnamed x50 -> x13, local copies, waits for them, and re-layouts: 10.2 us -> 5 us
    concatenate x6 -> x2, other arithmetic: 6.41 us -> 1.27 us  [gather_stage(): return jnp.concatenate(got, axis=0)]
    ppermute x10, waiting for transfers between devices: 29.3 us -> 25 us  [scatter_stage(): lax.ppermute(pieces[shift].astype(jnp.bfloat16), axis, pairs)]
    ppermute x10, starting transfers between devices: 10 us -> 13.9 us  [scatter_stage(): lax.ppermute(pieces[shift].astype(jnp.bfloat16), axis, pairs)]
    reduce_sum x3 -> x2, other arithmetic: 4.01 us -> 1.31 us  [the longest x1 0.77 us: dense_shards(): per_host = jnp.sum(jnp.where(chosen, weights[:, :, None], 0.0), axis=1)]
  transfers between devices with their start and end apart: 40 -> 20, of which waited for: 10 -> 10; matrix products, arithmetic and copies ran while one was open for 32% -> 12% of each run, Pallas kernels for 0% -> 0%
where the time goes in v4:
time: 106 us; the launch traced here: 105 us
  waiting for transfers between devices  48.5 us (46%)
  starting transfers between devices  29.1 us (27%)
  local copies, waits for them, and re-layouts  10.8 us (10%)
  matrix products  10.6 us (10%)
  other arithmetic  6.12 us (6%)
    ppermute x10, waiting for transfers between devices, scatter_stage(): lax.ppermute(pieces[shift].astype(jnp.bfloat16), axis, pairs)  25 us
    ppermute x10, waiting for transfers between devices, gather_stage(): got.append(lax.ppermute(block, axis, pairs))  23.5 us
    ppermute x10, starting transfers between devices, gather_stage(): got.append(lax.ppermute(block, axis, pairs))  15.2 us
    ppermute x10, starting transfers between devices, scatter_stage(): lax.ppermute(pieces[shift].astype(jnp.bfloat16), axis, pairs)  13.9 us
    dot_general x2, matrix products, expert_block(): pair = jnp.dot(rows_in, gate_up, preferred_element_type=jnp.float32)  6.9 us
    unnamed x13, local copies, waits for them, and re-layouts  5 us
    dot_general x2, matrix products, expert_block(): jnp.dot(active, down_proj, preferred_element_type=jnp.float32)  3.69 us
  transfers between devices with their start and end apart: 20, of which 10 were waited for; matrix products, arithmetic and copies ran while one was open for 12% of the time, Pallas kernels for 0%

profile of v4, /device:TPU:0, one launch (start us, length us, event | category | flops | bytes accessed | tf_op | source)
XLA Modules:
  0.0 105.3 jit_solution(16085936494176398874)
XLA Ops:
  0.0 0.9 reduce_sum.36
  0.9 0.8 broadcast_divide_fusion
  1.7 0.8 select_reduce_fusion
  2.8 1.7 %concatenate.29 = bf16[64,2176]{1,0:T(8,128)(2,1)} concatenate(bf16[64,2048]{1,0:T(8,128)(2,1)} %param.6, bf16[64,16]{1,0:T(8,128)(2,1)S(1)} %copy.9, bf16[64,16]{1,0:T(8,128)(2,1)S(1)} %copy.10, bf16[64,16]{1,0:T(8,128)(2,1)S(1)} %copy.11, bf16[64,80]{1,0:T(8,128)(2,1)S(1)} %broadcast_in_dim.16), dimensions={1} | concatenate | bytes 557056 | tf_op jit(solution)/shard_map/concatenate | solution.py:94
  4.5 1.7 %fusion.43 = (bf16[32,2176]{1,0:T(8,128)(2,1)S(1)}, bf16[256,2176]{1,0:T(8,128)(2,1)}, bf16[512,2176]{1,0:T(8,128)(2,1)}, bf16[32,2176]{1,0:T(8,128)(2,1)S(1)}) fusion(bf16[64,2176]{1,0:T(8,128)(2,1)} %concatenate.29), kind=kLoop, calls=%fused_computation.83 | loop fusion | bytes 835584 | tf_op jit(solution)/shard_map/split | solution.py:98
  6.2 3.1 %collective-permute-start = (bf16[32,2176]{1,0:T(8,128)(2,1)S(1)}, bf16[32,2176]{1,0:T(8,128)(2,1)}, u32[]{:S(2)}, u32[]{:S(2)}) collective-permute-start(bf16[32,2176]{1,0:T(8,128)(2,1)S(1)} %get-tuple-element.26), channel_id=1, source_target_pairs={{0,4},{4,8},{8,12},{12,0},{1,5},{5,9},{9,13},{13,1},{2,6},{6,10},{... | collective-permute-start | bytes 417800 | tf_op jit(solution)/shard_map/ppermute | solution.py:65
  9.3 2.6 %collective-permute-start.1 = (bf16[32,2176]{1,0:T(8,128)(2,1)S(1)}, bf16[32,2176]{1,0:T(8,128)(2,1)}, u32[]{:S(2)}, u32[]{:S(2)}) collective-permute-start(bf16[32,2176]{1,0:T(8,128)(2,1)S(1)} %get-tuple-element.26), channel_id=1, source_target_pairs={{0,8},{4,12},{8,0},{12,4},{1,9},{5,13},{9,1},{13,5},{2,10},{6,14},... | collective-permute-start | bytes 417800 | tf_op jit(solution)/shard_map/ppermute | solution.py:65
  11.9 1.3 %collective-permute-start.2 = (bf16[32,2176]{1,0:T(8,128)(2,1)S(1)}, bf16[32,2176]{1,0:T(8,128)(2,1)}, u32[]{:S(2)}, u32[]{:S(2)}) collective-permute-start(bf16[32,2176]{1,0:T(8,128)(2,1)S(1)} %get-tuple-element.26), channel_id=1, source_target_pairs={{0,12},{4,0},{8,4},{12,8},{1,13},{5,1},{9,5},{13,9},{2,14},{6,2},{... | collective-permute-start | bytes 417800 | tf_op jit(solution)/shard_map/ppermute | solution.py:65
  13.2 2.8 %collective-permute-done = bf16[32,2176]{1,0:T(8,128)(2,1)} collective-permute-done((bf16[32,2176]{1,0:T(8,128)(2,1)S(1)}, bf16[32,2176]{1,0:T(8,128)(2,1)}, u32[]{:S(2)}, u32[]{:S(2)}) %collective-permute-start) | collective-permute-done | bytes 139296 | tf_op jit(solution)/shard_map/ppermute | solution.py:65
  16.0 5.1 %collective-permute-done.1 = bf16[32,2176]{1,0:T(8,128)(2,1)} collective-permute-done((bf16[32,2176]{1,0:T(8,128)(2,1)S(1)}, bf16[32,2176]{1,0:T(8,128)(2,1)}, u32[]{:S(2)}, u32[]{:S(2)}) %collective-permute-start.1) | collective-permute-done | bytes 139296 | tf_op jit(solution)/shard_map/ppermute | solution.py:65
  21.2 1.2 %pad_maximum_fusion = bf16[128,2176]{1,0:T(8,128)(2,1)S(1)} fusion(bf16[32,2176]{1,0:T(8,128)(2,1)} %collective-permute-done.2, bf16[32,2176]{1,0:T(8,128)(2,1)} %collective-permute-done.1, bf16[32,2176]{1,0:T(8,128)(2,1)} %collective-permute-done, bf16[32,2176]{1,0:T(8,128)(2,1)S(1)} %get-tuple-element.26), kind=kLoop, calls=%fused_computation.28 | loop fusion | flops 2228224 | bytes 1114112 | tf_op jit(solution)/shard_map/concatenate | solution.py:66
  22.4 1.6 %collective-permute-start.3 = (bf16[128,2176]{1,0:T(8,128)(2,1)S(1)}, bf16[128,2176]{1,0:T(8,128)(2,1)S(1)}, u32[]{:S(2)}, u32[]{:S(2)}) collective-permute-start(bf16[128,2176]{1,0:T(8,128)(2,1)S(1)} %pad_maximum_fusion), channel_id=1, source_target_pairs={{0,2},{2,0},{1,3},{3,1},{4,6},{6,4},{5,7},{7,5},{8,10},{10,8},{9,1... | collective-permute-start | bytes 1671176 | tf_op jit(solution)/shard_map/ppermute | solution.py:65
  24.0 3.5 %collective-permute-start.10 = (bf16[32,2176]{1,0:T(8,128)(2,1)S(1)}, bf16[32,2176]{1,0:T(8,128)(2,1)S(1)}, u32[]{:S(2)}, u32[]{:S(2)}) collective-permute-start(bf16[32,2176]{1,0:T(8,128)(2,1)S(1)} %get-tuple-element.6), channel_id=1, source_target_pairs={{0,4},{4,8},{8,12},{12,0},{1,5},{5,9},{9,13},{13,1},{2,6},{6,10},{... | collective-permute-start | bytes 417800 | tf_op jit(solution)/shard_map/ppermute | solution.py:65
  27.5 1.6 %collective-permute-start.11 = (bf16[32,2176]{1,0:T(8,128)(2,1)S(1)}, bf16[32,2176]{1,0:T(8,128)(2,1)S(1)}, u32[]{:S(2)}, u32[]{:S(2)}) collective-permute-start(bf16[32,2176]{1,0:T(8,128)(2,1)S(1)} %get-tuple-element.6), channel_id=1, source_target_pairs={{0,8},{4,12},{8,0},{12,4},{1,9},{5,13},{9,1},{13,5},{2,10},{6,14},... | collective-permute-start | bytes 417800 | tf_op jit(solution)/shard_map/ppermute | solution.py:65
  29.1 0.8 collective-permute-start.12
  29.9 1.6 %constant_dynamic-update-slice_fusion.3 = (bf16[256,2176]{1,0:T(8,128)(2,1)}, bf16[512,2176]{1,0:T(8,128)(2,1)}) fusion(bf16[256,2176]{1,0:T(8,128)(2,1)} %get-tuple-element.24, bf16[32,2176]{1,0:T(8,128)(2,1)} %collective-permute-done, bf16[512,2176]{1,0:T(8,128)(2,1)} %get-tuple-element.25), kind=kLoop, calls=%fused_computation.53 | loop fusion | bytes 417792
  31.5 1.6 %constant_dynamic-update-slice_fusion.2 = (bf16[256,2176]{1,0:T(8,128)(2,1)}, bf16[512,2176]{1,0:T(8,128)(2,1)}) fusion(bf16[256,2176]{1,0:T(8,128)(2,1)} %get-tuple-element.39, bf16[32,2176]{1,0:T(8,128)(2,1)} %collective-permute-done.1, bf16[512,2176]{1,0:T(8,128)(2,1)} %get-tuple-element.40), kind=kLoop, calls=%fused_computation.52 | loop fusion | bytes 417792
  33.2 1.6 %constant_dynamic-update-slice_fusion.1 = (bf16[256,2176]{1,0:T(8,128)(2,1)}, bf16[512,2176]{1,0:T(8,128)(2,1)}) fusion(bf16[256,2176]{1,0:T(8,128)(2,1)} %get-tuple-element.37, bf16[32,2176]{1,0:T(8,128)(2,1)} %collective-permute-done.2, bf16[512,2176]{1,0:T(8,128)(2,1)} %get-tuple-element.38), kind=kLoop, calls=%fused_computation.51 | loop fusion | bytes 417792
  34.8 2.8 %collective-permute-done.11 = bf16[32,2176]{1,0:T(8,128)(2,1)S(1)} collective-permute-done((bf16[32,2176]{1,0:T(8,128)(2,1)S(1)}, bf16[32,2176]{1,0:T(8,128)(2,1)S(1)}, u32[]{:S(2)}, u32[]{:S(2)}) %collective-permute-start.11) | collective-permute-done | bytes 139296 | tf_op jit(solution)/shard_map/ppermute | solution.py:65
  37.7 0.6 collective-permute-start.13
  38.3 1.1 %constant_dynamic-update-slice_fusion = (bf16[256,2176]{1,0:T(8,128)(2,1)}, bf16[512,2176]{1,0:T(8,128)(2,1)}) fusion(bf16[256,2176]{1,0:T(8,128)(2,1)} %get-tuple-element.35, bf16[128,2176]{1,0:T(8,128)(2,1)S(1)} %collective-permute-done.3, bf16[512,2176]{1,0:T(8,128)(2,1)} %get-tuple-element.36), kind=kLoop, calls=%fused_computation.50 | loop fusion | bytes 1671168 | tf_op jit(solution)/shard_map/concatenate | solution.py:66
  39.5 12.7 %collective-permute-done.13 = bf16[128,2176]{1,0:T(8,128)(2,1)S(1)} collective-permute-done((bf16[128,2176]{1,0:T(8,128)(2,1)S(1)}, bf16[128,2176]{1,0:T(8,128)(2,1)S(1)}, u32[]{:S(2)}, u32[]{:S(2)}) %collective-permute-start.13) | collective-permute-done | bytes 557088 | tf_op jit(solution)/shard_map/ppermute | solution.py:65
  52.6 3.4 %fusion.2 = f32[512,1536]{1,0:T(8,128)S(1)} fusion(bf16[1,2048,1536]{2,1,0:T(8,128)(2,1)S(1)} %copy-done.2, bf16[512,2176]{1,0:T(8,128)(2,1)S(1)} %constant_dynamic-update-slice_fusion.5), kind=kOutput, calls=%fused_computation.2 | convolution fusion | flops 3221225472 | bytes 11534336 | tf_op jit(solution)/shard_map/dot_general | solution.py:9
  56.1 0.1 constant_dynamic-update-slice_fusion.16
  56.3 3.4 %fusion = f32[512,1536]{1,0:T(8,128)S(1)} fusion(bf16[1,2048,1536]{2,1,0:T(8,128)(2,1)S(1)} %copy-done.2, bf16[512,2176]{1,0:T(8,128)(2,1)S(1)} %constant_dynamic-update-slice_fusion.16), kind=kOutput, calls=%fused_computation | convolution fusion | flops 3221225472 | bytes 11534336 | tf_op jit(solution)/shard_map/dot_general | solution.py:9
  59.7 0.5 fusion.35
  60.3 1.8 %convert_multiply_fusion = f32[512,2048]{1,0:T(8,128)S(1)} fusion(bf16[1,768,2048]{2,1,0:T(8,128)(2,1)S(1)} %copy-done, f32[512]{0:T(512)S(1)} %get-tuple-element.8, f32[512,1536]{1,0:T(8,128)S(1)} %fusion), kind=kOutput, calls=%fused_computation.4 | convolution fusion | flops 1616117760 | bytes 10487808 | tf_op jit(solution)/shard_map/dot_general | solution.py:11
  62.3 0.5 collective-permute-start.15
  62.8 1.8 %convert_multiply_fusion.1 = f32[512,2048]{1,0:T(8,128)S(1)} fusion(bf16[1,768,2048]{2,1,0:T(8,128)(2,1)S(1)} %copy-done, f32[512]{0:T(512)S(1)} %get-tuple-element.7, f32[512,1536]{1,0:T(8,128)S(1)} %fusion.2), kind=kOutput, calls=%fused_computation.5 | convolution fusion | flops 1616117760 | bytes 10487808 | tf_op jit(solution)/shard_map/dot_general | solution.py:11
  64.9 0.2 collective-permute-done.15
  65.1 0.3 slice_add_fusion
  65.5 0.6 collective-permute-start.16
  66.1 1.4 %collective-permute-done.5 = bf16[256,2048]{1,0:T(8,128)(2,1)S(1)} collective-permute-done((bf16[256,2048]{1,0:T(8,128)(2,1)S(1)}, bf16[256,2048]{1,0:T(8,128)(2,1)S(1)}, u32[]{:S(2)}, u32[]{:S(2)}) %collective-permute-start.5) | collective-permute-done | bytes 1048608 | tf_op jit(solution)/shard_map/ppermute | solution.py:74
  67.5 0.3 slice_add_fusion.1
  68.0 0.6 collective-permute-start.6
  68.6 11.8 %collective-permute-done.16 = bf16[128,2048]{1,0:T(8,128)(2,1)S(1)} collective-permute-done((bf16[128,2048]{1,0:T(8,128)(2,1)S(1)}, bf16[128,2048]{1,0:T(8,128)(2,1)S(1)}, u32[]{:S(2)}, u32[]{:S(2)}) %collective-permute-start.16) | collective-permute-done | bytes 524320 | tf_op jit(solution)/shard_map/ppermute | solution.py:74
  80.4 0.1 fusion.40
  80.6 3.6 %collective-permute-start.19 = (bf16[32,2048]{1,0:T(8,128)(2,1)S(1)}, bf16[32,2048]{1,0:T(8,128)(2,1)S(1)}, u32[]{:S(2)}, u32[]{:S(2)}) collective-permute-start(bf16[32,2048]{1,0:T(8,128)(2,1)S(1)} %get-tuple-element.21), channel_id=1, source_target_pairs={{0,4},{4,8},{8,12},{12,0},{1,5},{5,9},{9,13},{13,1},{2,6},{6,10},{... | collective-permute-start | bytes 393224 | tf_op jit(solution)/shard_map/ppermute | solution.py:74
  84.2 1.0 collective-permute-start.18
  85.2 1.5 %collective-permute-start.17 = (bf16[32,2048]{1,0:T(8,128)(2,1)S(1)}, bf16[32,2048]{1,0:T(8,128)(2,1)S(1)}, u32[]{:S(2)}, u32[]{:S(2)}) collective-permute-start(bf16[32,2048]{1,0:T(8,128)(2,1)S(1)} %get-tuple-element.20), channel_id=1, source_target_pairs={{0,12},{4,0},{8,4},{12,8},{1,13},{5,1},{9,5},{13,9},{2,14},{6,2},{... | collective-permute-start | bytes 393224 | tf_op jit(solution)/shard_map/ppermute | solution.py:74
  86.6 4.4 %collective-permute-done.6 = bf16[128,2048]{1,0:T(8,128)(2,1)S(1)} collective-permute-done((bf16[128,2048]{1,0:T(8,128)(2,1)S(1)}, bf16[128,2048]{1,0:T(8,128)(2,1)S(1)}, u32[]{:S(2)}, u32[]{:S(2)}) %collective-permute-start.6) | collective-permute-done | bytes 524320 | tf_op jit(solution)/shard_map/ppermute | solution.py:74
  91.0 0.2 fusion.39
  91.2 3.6 %collective-permute-start.9 = (bf16[32,2048]{1,0:T(8,128)(2,1)S(1)}, bf16[32,2048]{1,0:T(8,128)(2,1)S(1)}, u32[]{:S(2)}, u32[]{:S(2)}) collective-permute-start(bf16[32,2048]{1,0:T(8,128)(2,1)S(1)} %get-tuple-element.18), channel_id=1, source_target_pairs={{0,4},{4,8},{8,12},{12,0},{1,5},{5,9},{9,13},{13,1},{2,6},{6,10},{... | collective-permute-start | bytes 393224 | tf_op jit(solution)/shard_map/ppermute | solution.py:74
  94.8 1.0 collective-permute-start.8
  95.8 1.5 %collective-permute-start.7 = (bf16[32,2048]{1,0:T(8,128)(2,1)S(1)}, bf16[32,2048]{1,0:T(8,128)(2,1)S(1)}, u32[]{:S(2)}, u32[]{:S(2)}) collective-permute-start(bf16[32,2048]{1,0:T(8,128)(2,1)S(1)} %get-tuple-element.17), channel_id=1, source_target_pairs={{0,12},{4,0},{8,4},{12,8},{1,13},{5,1},{9,5},{13,9},{2,14},{6,2},{... | collective-permute-start | bytes 393224 | tf_op jit(solution)/shard_map/ppermute | solution.py:74
  97.4 2.3 %collective-permute-done.9 = bf16[32,2048]{1,0:T(8,128)(2,1)S(1)} collective-permute-done((bf16[32,2048]{1,0:T(8,128)(2,1)S(1)}, bf16[32,2048]{1,0:T(8,128)(2,1)S(1)}, u32[]{:S(2)}, u32[]{:S(2)}) %collective-permute-start.9) | collective-permute-done | bytes 131104 | tf_op jit(solution)/shard_map/ppermute | solution.py:74
  99.6 4.8 %collective-permute-done.8 = bf16[32,2048]{1,0:T(8,128)(2,1)S(1)} collective-permute-done((bf16[32,2048]{1,0:T(8,128)(2,1)S(1)}, bf16[32,2048]{1,0:T(8,128)(2,1)S(1)}, u32[]{:S(2)}, u32[]{:S(2)}) %collective-permute-start.8) | collective-permute-done | bytes 131104 | tf_op jit(solution)/shard_map/ppermute | solution.py:74
  104.5 0.7 pad_maximum_fusion.2
  (42 shorter events, 1.6 us)
Async XLA Ops:
  0.0 60.3 %copy-start = (bf16[1,768,2048]{2,1,0:T(8,128)(2,1)S(1)}, bf16[1,768,2048]{2,1,0:T(8,128)(2,1)}, u32[]{:S(2)}) copy-start(bf16[1,768,2048]{2,1,0:T(8,128)(2,1)} %param.11) | copy-start | bytes 9437188
  6.2 9.8 %collective-permute-start = (bf16[32,2176]{1,0:T(8,128)(2,1)S(1)}, bf16[32,2176]{1,0:T(8,128)(2,1)}, u32[]{:S(2)}, u32[]{:S(2)}) collective-permute-start(bf16[32,2176]{1,0:T(8,128)(2,1)S(1)} %get-tuple-element.26), channel_id=1, source_target_pairs={{0,4},{4,8},{8,12},{12,0},{1,5},{5,9},{9,13},{13,1},{2,6},{6,10},{... | collective-permute-start | bytes 417800 | tf_op jit(solution)/shard_map/ppermute | solution.py:65
  9.3 11.9 %collective-permute-start.1 = (bf16[32,2176]{1,0:T(8,128)(2,1)S(1)}, bf16[32,2176]{1,0:T(8,128)(2,1)}, u32[]{:S(2)}, u32[]{:S(2)}) collective-permute-start(bf16[32,2176]{1,0:T(8,128)(2,1)S(1)} %get-tuple-element.26), channel_id=1, source_target_pairs={{0,8},{4,12},{8,0},{12,4},{1,9},{5,13},{9,1},{13,5},{2,10},{6,14},... | collective-permute-start | bytes 417800 | tf_op jit(solution)/shard_map/ppermute | solution.py:65
  11.9 9.3 %collective-permute-start.2 = (bf16[32,2176]{1,0:T(8,128)(2,1)S(1)}, bf16[32,2176]{1,0:T(8,128)(2,1)}, u32[]{:S(2)}, u32[]{:S(2)}) collective-permute-start(bf16[32,2176]{1,0:T(8,128)(2,1)S(1)} %get-tuple-element.26), channel_id=1, source_target_pairs={{0,12},{4,0},{8,4},{12,8},{1,13},{5,1},{9,5},{13,9},{2,14},{6,2},{... | collective-permute-start | bytes 417800 | tf_op jit(solution)/shard_map/ppermute | solution.py:65
  21.2 31.5 %copy-start.2 = (bf16[1,2048,1536]{2,1,0:T(8,128)(2,1)S(1)}, bf16[1,2048,1536]{2,1,0:T(8,128)(2,1)}, u32[]{:S(2)}) copy-start(bf16[1,2048,1536]{2,1,0:T(8,128)(2,1)} %param.10) | copy-start | bytes 18874372
  22.4 15.9 %collective-permute-start.3 = (bf16[128,2176]{1,0:T(8,128)(2,1)S(1)}, bf16[128,2176]{1,0:T(8,128)(2,1)S(1)}, u32[]{:S(2)}, u32[]{:S(2)}) collective-permute-start(bf16[128,2176]{1,0:T(8,128)(2,1)S(1)} %pad_maximum_fusion), channel_id=1, source_target_pairs={{0,2},{2,0},{1,3},{3,1},{4,6},{6,4},{5,7},{7,5},{8,10},{10,8},{9,1... | collective-permute-start | bytes 1671176 | tf_op jit(solution)/shard_map/ppermute | solution.py:65
  24.0 10.8 %collective-permute-start.10 = (bf16[32,2176]{1,0:T(8,128)(2,1)S(1)}, bf16[32,2176]{1,0:T(8,128)(2,1)S(1)}, u32[]{:S(2)}, u32[]{:S(2)}) collective-permute-start(bf16[32,2176]{1,0:T(8,128)(2,1)S(1)} %get-tuple-element.6), channel_id=1, source_target_pairs={{0,4},{4,8},{8,12},{12,0},{1,5},{5,9},{9,13},{13,1},{2,6},{6,10},{... | collective-permute-start | bytes 417800 | tf_op jit(solution)/shard_map/ppermute | solution.py:65
  27.5 10.2 %collective-permute-start.11 = (bf16[32,2176]{1,0:T(8,128)(2,1)S(1)}, bf16[32,2176]{1,0:T(8,128)(2,1)S(1)}, u32[]{:S(2)}, u32[]{:S(2)}) collective-permute-start(bf16[32,2176]{1,0:T(8,128)(2,1)S(1)} %get-tuple-element.6), channel_id=1, source_target_pairs={{0,8},{4,12},{8,0},{12,4},{1,9},{5,13},{9,1},{13,5},{2,10},{6,14},... | collective-permute-start | bytes 417800 | tf_op jit(solution)/shard_map/ppermute | solution.py:65
  29.1 8.5 %collective-permute-start.12 = (bf16[32,2176]{1,0:T(8,128)(2,1)S(1)}, bf16[32,2176]{1,0:T(8,128)(2,1)S(1)}, u32[]{:S(2)}, u32[]{:S(2)}) collective-permute-start(bf16[32,2176]{1,0:T(8,128)(2,1)S(1)} %get-tuple-element.6), channel_id=1, source_target_pairs={{0,12},{4,0},{8,4},{12,8},{1,13},{5,1},{9,5},{13,9},{2,14},{6,2},{... | collective-permute-start | bytes 417800 | tf_op jit(solution)/shard_map/ppermute | solution.py:65
  37.7 14.5 %collective-permute-start.13 = (bf16[128,2176]{1,0:T(8,128)(2,1)S(1)}, bf16[128,2176]{1,0:T(8,128)(2,1)S(1)}, u32[]{:S(2)}, u32[]{:S(2)}) collective-permute-start(bf16[128,2176]{1,0:T(8,128)(2,1)S(1)} %pad_maximum_fusion.1), channel_id=1, source_target_pairs={{0,2},{2,0},{1,3},{3,1},{4,6},{6,4},{5,7},{7,5},{8,10},{10,8},{9,1... | collective-permute-start | bytes 1671176 | tf_op jit(solution)/shard_map/ppermute | solution.py:65
  39.4 13.1 %copy-start.1 = (bf16[512,2176]{1,0:T(8,128)(2,1)S(1)}, bf16[512,2176]{1,0:T(8,128)(2,1)}, u32[]{:S(2)}) copy-start(bf16[512,2176]{1,0:T(8,128)(2,1)} %get-tuple-element.16) | copy-start | bytes 6684676
  39.4 13.1 %collective-permute-start.4 = (bf16[256,2176]{1,0:T(8,128)(2,1)}, bf16[256,2176]{1,0:T(8,128)(2,1)S(1)}, u32[]{:S(2)}, u32[]{:S(2)}) collective-permute-start(bf16[256,2176]{1,0:T(8,128)(2,1)} %get-tuple-element.15), channel_id=1, source_target_pairs={{0,1},{1,0},{2,3},{3,2},{4,5},{5,4},{6,7},{7,6},{8,9},{9,8},{10,11... | collective-permute-start | bytes 3342344 | tf_op jit(solution)/shard_map/ppermute | solution.py:65
  52.3 3.7 %collective-permute-start.14 = (bf16[256,2176]{1,0:T(8,128)(2,1)S(1)}, bf16[256,2176]{1,0:T(8,128)(2,1)S(1)}, u32[]{:S(2)}, u32[]{:S(2)}) collective-permute-start(bf16[256,2176]{1,0:T(8,128)(2,1)S(1)} %get-tuple-element.13), channel_id=1, source_target_pairs={{0,1},{1,0},{2,3},{3,2},{4,5},{5,4},{6,7},{7,6},{8,9},{9,8},{10,11... | collective-permute-start | bytes 3342344 | tf_op jit(solution)/shard_map/ppermute | solution.py:65
  62.3 2.8 %collective-permute-start.15 = (bf16[256,2048]{1,0:T(8,128)(2,1)S(1)}, bf16[256,2048]{1,0:T(8,128)(2,1)S(1)}, u32[]{:S(2)}, u32[]{:S(2)}) collective-permute-start(bf16[256,2048]{1,0:T(8,128)(2,1)S(1)} %split.124), channel_id=1, source_target_pairs={{0,1},{1,0},{2,3},{3,2},{4,5},{5,4},{6,7},{7,6},{8,9},{9,8},{10,11... | collective-permute-start | bytes 3145736 | tf_op jit(solution)/shard_map/ppermute | solution.py:74
  64.8 2.7 %collective-permute-start.5 = (bf16[256,2048]{1,0:T(8,128)(2,1)S(1)}, bf16[256,2048]{1,0:T(8,128)(2,1)S(1)}, u32[]{:S(2)}, u32[]{:S(2)}) collective-permute-start(bf16[256,2048]{1,0:T(8,128)(2,1)S(1)} %split.125), channel_id=1, source_target_pairs={{0,1},{1,0},{2,3},{3,2},{4,5},{5,4},{6,7},{7,6},{8,9},{9,8},{10,11... | collective-permute-start | bytes 3145736 | tf_op jit(solution)/shard_map/ppermute | solution.py:74
  65.5 14.9 %collective-permute-start.16 = (bf16[128,2048]{1,0:T(8,128)(2,1)S(1)}, bf16[128,2048]{1,0:T(8,128)(2,1)S(1)}, u32[]{:S(2)}, u32[]{:S(2)}) collective-permute-start(bf16[128,2048]{1,0:T(8,128)(2,1)S(1)} %split.126), channel_id=1, source_target_pairs={{0,2},{2,0},{1,3},{3,1},{4,6},{6,4},{5,7},{7,5},{8,10},{10,8},{9,1... | collective-permute-start | bytes 1572872 | tf_op jit(solution)/shard_map/ppermute | solution.py:74
  68.0 23.1 %collective-permute-start.6 = (bf16[128,2048]{1,0:T(8,128)(2,1)S(1)}, bf16[128,2048]{1,0:T(8,128)(2,1)S(1)}, u32[]{:S(2)}, u32[]{:S(2)}) collective-permute-start(bf16[128,2048]{1,0:T(8,128)(2,1)S(1)} %split.127), channel_id=1, source_target_pairs={{0,2},{2,0},{1,3},{3,1},{4,6},{6,4},{5,7},{7,5},{8,10},{10,8},{9,1... | collective-permute-start | bytes 1572872 | tf_op jit(solution)/shard_map/ppermute | solution.py:74
  80.6 15.2 %collective-permute-start.19 = (bf16[32,2048]{1,0:T(8,128)(2,1)S(1)}, bf16[32,2048]{1,0:T(8,128)(2,1)S(1)}, u32[]{:S(2)}, u32[]{:S(2)}) collective-permute-start(bf16[32,2048]{1,0:T(8,128)(2,1)S(1)} %get-tuple-element.21), channel_id=1, source_target_pairs={{0,4},{4,8},{8,12},{12,0},{1,5},{5,9},{9,13},{13,1},{2,6},{6,10},{... | collective-permute-start | bytes 393224 | tf_op jit(solution)/shard_map/ppermute | solution.py:74
  84.2 13.1 %collective-permute-start.18 = (bf16[32,2048]{1,0:T(8,128)(2,1)S(1)}, bf16[32,2048]{1,0:T(8,128)(2,1)S(1)}, u32[]{:S(2)}, u32[]{:S(2)}) collective-permute-start(bf16[32,2048]{1,0:T(8,128)(2,1)S(1)} %get-tuple-element.22), channel_id=1, source_target_pairs={{0,8},{4,12},{8,0},{12,4},{1,9},{5,13},{9,1},{13,5},{2,10},{6,14},... | collective-permute-start | bytes 393224 | tf_op jit(solution)/shard_map/ppermute | solution.py:74
  85.2 12.1 %collective-permute-start.17 = (bf16[32,2048]{1,0:T(8,128)(2,1)S(1)}, bf16[32,2048]{1,0:T(8,128)(2,1)S(1)}, u32[]{:S(2)}, u32[]{:S(2)}) collective-permute-start(bf16[32,2048]{1,0:T(8,128)(2,1)S(1)} %get-tuple-element.20), channel_id=1, source_target_pairs={{0,12},{4,0},{8,4},{12,8},{1,13},{5,1},{9,5},{13,9},{2,14},{6,2},{... | collective-permute-start | bytes 393224 | tf_op jit(solution)/shard_map/ppermute | solution.py:74
  91.2 8.4 %collective-permute-start.9 = (bf16[32,2048]{1,0:T(8,128)(2,1)S(1)}, bf16[32,2048]{1,0:T(8,128)(2,1)S(1)}, u32[]{:S(2)}, u32[]{:S(2)}) collective-permute-start(bf16[32,2048]{1,0:T(8,128)(2,1)S(1)} %get-tuple-element.18), channel_id=1, source_target_pairs={{0,4},{4,8},{8,12},{12,0},{1,5},{5,9},{9,13},{13,1},{2,6},{6,10},{... | collective-permute-start | bytes 393224 | tf_op jit(solution)/shard_map/ppermute | solution.py:74
  94.8 9.6 %collective-permute-start.8 = (bf16[32,2048]{1,0:T(8,128)(2,1)S(1)}, bf16[32,2048]{1,0:T(8,128)(2,1)S(1)}, u32[]{:S(2)}, u32[]{:S(2)}) collective-permute-start(bf16[32,2048]{1,0:T(8,128)(2,1)S(1)} %get-tuple-element.19), channel_id=1, source_target_pairs={{0,8},{4,12},{8,0},{12,4},{1,9},{5,13},{9,1},{13,5},{2,10},{6,14},... | collective-permute-start | bytes 393224 | tf_op jit(solution)/shard_map/ppermute | solution.py:74
  95.8 8.7 %collective-permute-start.7 = (bf16[32,2048]{1,0:T(8,128)(2,1)S(1)}, bf16[32,2048]{1,0:T(8,128)(2,1)S(1)}, u32[]{:S(2)}, u32[]{:S(2)}) collective-permute-start(bf16[32,2048]{1,0:T(8,128)(2,1)S(1)} %get-tuple-element.17), channel_id=1, source_target_pairs={{0,12},{4,0},{8,4},{12,8},{1,13},{5,1},{9,5},{13,9},{2,14},{6,2},{... | collective-permute-start | bytes 393224 | tf_op jit(solution)/shard_map/ppermute | solution.py:74

commit v5 on v4

--- a/solution.py
+++ b/solution.py
@@ -85,12 +85,13 @@
     weights = gate_scores / jnp.sum(gate_scores, axis=1, keepdims=True)
     chosen = expert_ids[:, :, None] == host_expert[None, None, :]
     per_host = jnp.sum(jnp.where(chosen, weights[:, :, None], 0.0), axis=1)
-    hi = per_host.astype(jnp.bfloat16)
-    rest = per_host - hi.astype(jnp.float32)
-    lo = rest.astype(jnp.bfloat16)
-    lo2 = (rest - lo.astype(jnp.float32)).astype(jnp.bfloat16)
+    hi = lax.reduce_precision(per_host, exponent_bits=8, mantissa_bits=7)
+    rest = per_host - hi
+    lo = lax.reduce_precision(rest, exponent_bits=8, mantissa_bits=7)
+    lo2 = rest - lo
     extra = -(-3 * hosts // 128) * 128
-    meta = jnp.concatenate([hi, lo, lo2, jnp.zeros((tok_rows, extra - 3 * hosts), jnp.bfloat16)], axis=1)
+    meta = jnp.concatenate([hi, lo, lo2, jnp.zeros((tok_rows, extra - 3 * hosts), jnp.float32)], axis=1)
+    meta = meta.astype(jnp.bfloat16)
     carried = jnp.concatenate([tokens, meta], axis=1)
     pick = (jnp.arange(hosts, dtype=jnp.int32) == me).astype(jnp.float32)
     results = []

time: 106 us -> 106 us (level)
  no operation moved by 1% of the time
where the time goes in v5:
time: 106 us; the launch traced here: 105 us
  waiting for transfers between devices  48.5 us (46%)
  starting transfers between devices  29.1 us (27%)
  local copies, waits for them, and re-layouts  10.8 us (10%)
  matrix products  10.6 us (10%)
  other arithmetic  6.12 us (6%)
    ppermute x10, waiting for transfers between devices, scatter_stage(): lax.ppermute(pieces[shift].astype(jnp.bfloat16), axis, pairs)  25 us
    ppermute x10, waiting for transfers between devices, gather_stage(): got.append(lax.ppermute(block, axis, pairs))  23.5 us
    ppermute x10, starting transfers between devices, gather_stage(): got.append(lax.ppermute(block, axis, pairs))  15.2 us
    ppermute x10, starting transfers between devices, scatter_stage(): lax.ppermute(pieces[shift].astype(jnp.bfloat16), axis, pairs)  13.9 us
    dot_general x2, matrix products, expert_block(): pair = jnp.dot(rows_in, gate_up, preferred_element_type=jnp.float32)  6.9 us
    unnamed x13, local copies, waits for them, and re-layouts  5 us
    dot_general x2, matrix products, expert_block(): jnp.dot(active, down_proj, preferred_element_type=jnp.float32)  3.69 us
  transfers between devices with their start and end apart: 20, of which 10 were waited for; matrix products, arithmetic and copies ran while one was open for 12% of the time, Pallas kernels for 0%

profile of v5, /device:TPU:0, one launch (start us, length us, event | category | flops | bytes accessed | tf_op | source)
XLA Modules:
  0.0 105.3 jit_solution(15176952585232790392)
XLA Ops:
  0.0 0.9 reduce_sum.36
  0.9 0.8 broadcast_divide_fusion
  1.7 0.8 select_reduce_fusion
  2.8 1.7 %concatenate.32 = bf16[64,2176]{1,0:T(8,128)(2,1)} concatenate(bf16[64,2048]{1,0:T(8,128)(2,1)} %param.6, bf16[64,16]{1,0:T(8,128)(2,1)S(1)} %copy.9, bf16[64,16]{1,0:T(8,128)(2,1)S(1)} %copy.10, bf16[64,16]{1,0:T(8,128)(2,1)S(1)} %copy.11, bf16[64,80]{1,0:T(8,128)(2,1)S(1)} %broadcast_in_dim.16), dimensions={1} | concatenate | bytes 557056 | tf_op jit(solution)/shard_map/concatenate | solution.py:95
  4.5 1.7 %fusion.43 = (bf16[32,2176]{1,0:T(8,128)(2,1)S(1)}, bf16[256,2176]{1,0:T(8,128)(2,1)}, bf16[512,2176]{1,0:T(8,128)(2,1)}, bf16[32,2176]{1,0:T(8,128)(2,1)S(1)}) fusion(bf16[64,2176]{1,0:T(8,128)(2,1)} %concatenate.32), kind=kLoop, calls=%fused_computation.85 | loop fusion | bytes 835584 | tf_op jit(solution)/shard_map/split | solution.py:99
  6.2 3.1 %collective-permute-start = (bf16[32,2176]{1,0:T(8,128)(2,1)S(1)}, bf16[32,2176]{1,0:T(8,128)(2,1)}, u32[]{:S(2)}, u32[]{:S(2)}) collective-permute-start(bf16[32,2176]{1,0:T(8,128)(2,1)S(1)} %get-tuple-element.26), channel_id=1, source_target_pairs={{0,4},{4,8},{8,12},{12,0},{1,5},{5,9},{9,13},{13,1},{2,6},{6,10},{... | collective-permute-start | bytes 417800 | tf_op jit(solution)/shard_map/ppermute | solution.py:65
  9.3 2.6 %collective-permute-start.1 = (bf16[32,2176]{1,0:T(8,128)(2,1)S(1)}, bf16[32,2176]{1,0:T(8,128)(2,1)}, u32[]{:S(2)}, u32[]{:S(2)}) collective-permute-start(bf16[32,2176]{1,0:T(8,128)(2,1)S(1)} %get-tuple-element.26), channel_id=1, source_target_pairs={{0,8},{4,12},{8,0},{12,4},{1,9},{5,13},{9,1},{13,5},{2,10},{6,14},... | collective-permute-start | bytes 417800 | tf_op jit(solution)/shard_map/ppermute | solution.py:65
  11.9 1.3 %collective-permute-start.2 = (bf16[32,2176]{1,0:T(8,128)(2,1)S(1)}, bf16[32,2176]{1,0:T(8,128)(2,1)}, u32[]{:S(2)}, u32[]{:S(2)}) collective-permute-start(bf16[32,2176]{1,0:T(8,128)(2,1)S(1)} %get-tuple-element.26), channel_id=1, source_target_pairs={{0,12},{4,0},{8,4},{12,8},{1,13},{5,1},{9,5},{13,9},{2,14},{6,2},{... | collective-permute-start | bytes 417800 | tf_op jit(solution)/shard_map/ppermute | solution.py:65
  13.2 2.8 %collective-permute-done = bf16[32,2176]{1,0:T(8,128)(2,1)} collective-permute-done((bf16[32,2176]{1,0:T(8,128)(2,1)S(1)}, bf16[32,2176]{1,0:T(8,128)(2,1)}, u32[]{:S(2)}, u32[]{:S(2)}) %collective-permute-start) | collective-permute-done | bytes 139296 | tf_op jit(solution)/shard_map/ppermute | solution.py:65
  16.0 5.1 %collective-permute-done.1 = bf16[32,2176]{1,0:T(8,128)(2,1)} collective-permute-done((bf16[32,2176]{1,0:T(8,128)(2,1)S(1)}, bf16[32,2176]{1,0:T(8,128)(2,1)}, u32[]{:S(2)}, u32[]{:S(2)}) %collective-permute-start.1) | collective-permute-done | bytes 139296 | tf_op jit(solution)/shard_map/ppermute | solution.py:65
  21.2 1.2 %pad_maximum_fusion = bf16[128,2176]{1,0:T(8,128)(2,1)S(1)} fusion(bf16[32,2176]{1,0:T(8,128)(2,1)} %collective-permute-done.2, bf16[32,2176]{1,0:T(8,128)(2,1)} %collective-permute-done.1, bf16[32,2176]{1,0:T(8,128)(2,1)} %collective-permute-done, bf16[32,2176]{1,0:T(8,128)(2,1)S(1)} %get-tuple-element.26), kind=kLoop, calls=%fused_computation.28 | loop fusion | flops 2228224 | bytes 1114112 | tf_op jit(solution)/shard_map/concatenate | solution.py:66
  22.4 1.6 %collective-permute-start.3 = (bf16[128,2176]{1,0:T(8,128)(2,1)S(1)}, bf16[128,2176]{1,0:T(8,128)(2,1)S(1)}, u32[]{:S(2)}, u32[]{:S(2)}) collective-permute-start(bf16[128,2176]{1,0:T(8,128)(2,1)S(1)} %pad_maximum_fusion), channel_id=1, source_target_pairs={{0,2},{2,0},{1,3},{3,1},{4,6},{6,4},{5,7},{7,5},{8,10},{10,8},{9,1... | collective-permute-start | bytes 1671176 | tf_op jit(solution)/shard_map/ppermute | solution.py:65
  24.0 3.5 %collective-permute-start.10 = (bf16[32,2176]{1,0:T(8,128)(2,1)S(1)}, bf16[32,2176]{1,0:T(8,128)(2,1)S(1)}, u32[]{:S(2)}, u32[]{:S(2)}) collective-permute-start(bf16[32,2176]{1,0:T(8,128)(2,1)S(1)} %get-tuple-element.6), channel_id=1, source_target_pairs={{0,4},{4,8},{8,12},{12,0},{1,5},{5,9},{9,13},{13,1},{2,6},{6,10},{... | collective-permute-start | bytes 417800 | tf_op jit(solution)/shard_map/ppermute | solution.py:65
  27.5 1.6 %collective-permute-start.11 = (bf16[32,2176]{1,0:T(8,128)(2,1)S(1)}, bf16[32,2176]{1,0:T(8,128)(2,1)S(1)}, u32[]{:S(2)}, u32[]{:S(2)}) collective-permute-start(bf16[32,2176]{1,0:T(8,128)(2,1)S(1)} %get-tuple-element.6), channel_id=1, source_target_pairs={{0,8},{4,12},{8,0},{12,4},{1,9},{5,13},{9,1},{13,5},{2,10},{6,14},... | collective-permute-start | bytes 417800 | tf_op jit(solution)/shard_map/ppermute | solution.py:65
  29.1 0.8 collective-permute-start.12
  29.9 1.6 %constant_dynamic-update-slice_fusion.3 = (bf16[256,2176]{1,0:T(8,128)(2,1)}, bf16[512,2176]{1,0:T(8,128)(2,1)}) fusion(bf16[256,2176]{1,0:T(8,128)(2,1)} %get-tuple-element.24, bf16[32,2176]{1,0:T(8,128)(2,1)} %collective-permute-done, bf16[512,2176]{1,0:T(8,128)(2,1)} %get-tuple-element.25), kind=kLoop, calls=%fused_computation.53 | loop fusion | bytes 417792
  31.5 1.6 %constant_dynamic-update-slice_fusion.2 = (bf16[256,2176]{1,0:T(8,128)(2,1)}, bf16[512,2176]{1,0:T(8,128)(2,1)}) fusion(bf16[256,2176]{1,0:T(8,128)(2,1)} %get-tuple-element.39, bf16[32,2176]{1,0:T(8,128)(2,1)} %collective-permute-done.1, bf16[512,2176]{1,0:T(8,128)(2,1)} %get-tuple-element.40), kind=kLoop, calls=%fused_computation.52 | loop fusion | bytes 417792
  33.2 1.6 %constant_dynamic-update-slice_fusion.1 = (bf16[256,2176]{1,0:T(8,128)(2,1)}, bf16[512,2176]{1,0:T(8,128)(2,1)}) fusion(bf16[256,2176]{1,0:T(8,128)(2,1)} %get-tuple-element.37, bf16[32,2176]{1,0:T(8,128)(2,1)} %collective-permute-done.2, bf16[512,2176]{1,0:T(8,128)(2,1)} %get-tuple-element.38), kind=kLoop, calls=%fused_computation.51 | loop fusion | bytes 417792
  34.8 2.8 %collective-permute-done.11 = bf16[32,2176]{1,0:T(8,128)(2,1)S(1)} collective-permute-done((bf16[32,2176]{1,0:T(8,128)(2,1)S(1)}, bf16[32,2176]{1,0:T(8,128)(2,1)S(1)}, u32[]{:S(2)}, u32[]{:S(2)}) %collective-permute-start.11) | collective-permute-done | bytes 139296 | tf_op jit(solution)/shard_map/ppermute | solution.py:65
  37.7 0.6 collective-permute-start.13
  38.3 1.1 %constant_dynamic-update-slice_fusion = (bf16[256,2176]{1,0:T(8,128)(2,1)}, bf16[512,2176]{1,0:T(8,128)(2,1)}) fusion(bf16[256,2176]{1,0:T(8,128)(2,1)} %get-tuple-element.35, bf16[128,2176]{1,0:T(8,128)(2,1)S(1)} %collective-permute-done.3, bf16[512,2176]{1,0:T(8,128)(2,1)} %get-tuple-element.36), kind=kLoop, calls=%fused_computation.50 | loop fusion | bytes 1671168 | tf_op jit(solution)/shard_map/concatenate | solution.py:66
  39.5 12.7 %collective-permute-done.13 = bf16[128,2176]{1,0:T(8,128)(2,1)S(1)} collective-permute-done((bf16[128,2176]{1,0:T(8,128)(2,1)S(1)}, bf16[128,2176]{1,0:T(8,128)(2,1)S(1)}, u32[]{:S(2)}, u32[]{:S(2)}) %collective-permute-start.13) | collective-permute-done | bytes 557088 | tf_op jit(solution)/shard_map/ppermute | solution.py:65
  52.6 3.4 %fusion.2 = f32[512,1536]{1,0:T(8,128)S(1)} fusion(bf16[1,2048,1536]{2,1,0:T(8,128)(2,1)S(1)} %copy-done.2, bf16[512,2176]{1,0:T(8,128)(2,1)S(1)} %constant_dynamic-update-slice_fusion.5), kind=kOutput, calls=%fused_computation.2 | convolution fusion | flops 3221225472 | bytes 11534336 | tf_op jit(solution)/shard_map/dot_general | solution.py:9
  56.1 0.1 constant_dynamic-update-slice_fusion.16
  56.3 3.4 %fusion = f32[512,1536]{1,0:T(8,128)S(1)} fusion(bf16[1,2048,1536]{2,1,0:T(8,128)(2,1)S(1)} %copy-done.2, bf16[512,2176]{1,0:T(8,128)(2,1)S(1)} %constant_dynamic-update-slice_fusion.16), kind=kOutput, calls=%fused_computation | convolution fusion | flops 3221225472 | bytes 11534336 | tf_op jit(solution)/shard_map/dot_general | solution.py:9
  59.7 0.5 fusion.35
  60.3 1.8 %convert_multiply_fusion = f32[512,2048]{1,0:T(8,128)S(1)} fusion(bf16[1,768,2048]{2,1,0:T(8,128)(2,1)S(1)} %copy-done, f32[512]{0:T(512)S(1)} %get-tuple-element.8, f32[512,1536]{1,0:T(8,128)S(1)} %fusion), kind=kOutput, calls=%fused_computation.4 | convolution fusion | flops 1616117760 | bytes 10487808 | tf_op jit(solution)/shard_map/dot_general | solution.py:11
  62.3 0.5 collective-permute-start.15
  62.8 1.8 %convert_multiply_fusion.1 = f32[512,2048]{1,0:T(8,128)S(1)} fusion(bf16[1,768,2048]{2,1,0:T(8,128)(2,1)S(1)} %copy-done, f32[512]{0:T(512)S(1)} %get-tuple-element.7, f32[512,1536]{1,0:T(8,128)S(1)} %fusion.2), kind=kOutput, calls=%fused_computation.5 | convolution fusion | flops 1616117760 | bytes 10487808 | tf_op jit(solution)/shard_map/dot_general | solution.py:11
  64.9 0.2 collective-permute-done.15
  65.1 0.3 slice_add_fusion
  65.5 0.6 collective-permute-start.16
  66.1 1.4 %collective-permute-done.5 = bf16[256,2048]{1,0:T(8,128)(2,1)S(1)} collective-permute-done((bf16[256,2048]{1,0:T(8,128)(2,1)S(1)}, bf16[256,2048]{1,0:T(8,128)(2,1)S(1)}, u32[]{:S(2)}, u32[]{:S(2)}) %collective-permute-start.5) | collective-permute-done | bytes 1048608 | tf_op jit(solution)/shard_map/ppermute | solution.py:74
  67.5 0.3 slice_add_fusion.1
  68.0 0.6 collective-permute-start.6
  68.6 11.8 %collective-permute-done.16 = bf16[128,2048]{1,0:T(8,128)(2,1)S(1)} collective-permute-done((bf16[128,2048]{1,0:T(8,128)(2,1)S(1)}, bf16[128,2048]{1,0:T(8,128)(2,1)S(1)}, u32[]{:S(2)}, u32[]{:S(2)}) %collective-permute-start.16) | collective-permute-done | bytes 524320 | tf_op jit(solution)/shard_map/ppermute | solution.py:74
  80.4 0.1 fusion.40
  80.6 3.6 %collective-permute-start.19 = (bf16[32,2048]{1,0:T(8,128)(2,1)S(1)}, bf16[32,2048]{1,0:T(8,128)(2,1)S(1)}, u32[]{:S(2)}, u32[]{:S(2)}) collective-permute-start(bf16[32,2048]{1,0:T(8,128)(2,1)S(1)} %get-tuple-element.21), channel_id=1, source_target_pairs={{0,4},{4,8},{8,12},{12,0},{1,5},{5,9},{9,13},{13,1},{2,6},{6,10},{... | collective-permute-start | bytes 393224 | tf_op jit(solution)/shard_map/ppermute | solution.py:74
  84.2 1.0 collective-permute-start.18
  85.2 1.5 %collective-permute-start.17 = (bf16[32,2048]{1,0:T(8,128)(2,1)S(1)}, bf16[32,2048]{1,0:T(8,128)(2,1)S(1)}, u32[]{:S(2)}, u32[]{:S(2)}) collective-permute-start(bf16[32,2048]{1,0:T(8,128)(2,1)S(1)} %get-tuple-element.20), channel_id=1, source_target_pairs={{0,12},{4,0},{8,4},{12,8},{1,13},{5,1},{9,5},{13,9},{2,14},{6,2},{... | collective-permute-start | bytes 393224 | tf_op jit(solution)/shard_map/ppermute | solution.py:74
  86.6 4.4 %collective-permute-done.6 = bf16[128,2048]{1,0:T(8,128)(2,1)S(1)} collective-permute-done((bf16[128,2048]{1,0:T(8,128)(2,1)S(1)}, bf16[128,2048]{1,0:T(8,128)(2,1)S(1)}, u32[]{:S(2)}, u32[]{:S(2)}) %collective-permute-start.6) | collective-permute-done | bytes 524320 | tf_op jit(solution)/shard_map/ppermute | solution.py:74
  91.0 0.2 fusion.39
  91.2 3.6 %collective-permute-start.9 = (bf16[32,2048]{1,0:T(8,128)(2,1)S(1)}, bf16[32,2048]{1,0:T(8,128)(2,1)S(1)}, u32[]{:S(2)}, u32[]{:S(2)}) collective-permute-start(bf16[32,2048]{1,0:T(8,128)(2,1)S(1)} %get-tuple-element.18), channel_id=1, source_target_pairs={{0,4},{4,8},{8,12},{12,0},{1,5},{5,9},{9,13},{13,1},{2,6},{6,10},{... | collective-permute-start | bytes 393224 | tf_op jit(solution)/shard_map/ppermute | solution.py:74
  94.8 1.0 collective-permute-start.8
  95.8 1.5 %collective-permute-start.7 = (bf16[32,2048]{1,0:T(8,128)(2,1)S(1)}, bf16[32,2048]{1,0:T(8,128)(2,1)S(1)}, u32[]{:S(2)}, u32[]{:S(2)}) collective-permute-start(bf16[32,2048]{1,0:T(8,128)(2,1)S(1)} %get-tuple-element.17), channel_id=1, source_target_pairs={{0,12},{4,0},{8,4},{12,8},{1,13},{5,1},{9,5},{13,9},{2,14},{6,2},{... | collective-permute-start | bytes 393224 | tf_op jit(solution)/shard_map/ppermute | solution.py:74
  97.4 2.3 %collective-permute-done.9 = bf16[32,2048]{1,0:T(8,128)(2,1)S(1)} collective-permute-done((bf16[32,2048]{1,0:T(8,128)(2,1)S(1)}, bf16[32,2048]{1,0:T(8,128)(2,1)S(1)}, u32[]{:S(2)}, u32[]{:S(2)}) %collective-permute-start.9) | collective-permute-done | bytes 131104 | tf_op jit(solution)/shard_map/ppermute | solution.py:74
  99.6 4.8 %collective-permute-done.8 = bf16[32,2048]{1,0:T(8,128)(2,1)S(1)} collective-permute-done((bf16[32,2048]{1,0:T(8,128)(2,1)S(1)}, bf16[32,2048]{1,0:T(8,128)(2,1)S(1)}, u32[]{:S(2)}, u32[]{:S(2)}) %collective-permute-start.8) | collective-permute-done | bytes 131104 | tf_op jit(solution)/shard_map/ppermute | solution.py:74
  104.5 0.7 pad_maximum_fusion.2
  (42 shorter events, 1.6 us)
Async XLA Ops:
  0.0 60.3 %copy-start = (bf16[1,768,2048]{2,1,0:T(8,128)(2,1)S(1)}, bf16[1,768,2048]{2,1,0:T(8,128)(2,1)}, u32[]{:S(2)}) copy-start(bf16[1,768,2048]{2,1,0:T(8,128)(2,1)} %param.11) | copy-start | bytes 9437188
  6.2 9.8 %collective-permute-start = (bf16[32,2176]{1,0:T(8,128)(2,1)S(1)}, bf16[32,2176]{1,0:T(8,128)(2,1)}, u32[]{:S(2)}, u32[]{:S(2)}) collective-permute-start(bf16[32,2176]{1,0:T(8,128)(2,1)S(1)} %get-tuple-element.26), channel_id=1, source_target_pairs={{0,4},{4,8},{8,12},{12,0},{1,5},{5,9},{9,13},{13,1},{2,6},{6,10},{... | collective-permute-start | bytes 417800 | tf_op jit(solution)/shard_map/ppermute | solution.py:65
  9.3 11.9 %collective-permute-start.1 = (bf16[32,2176]{1,0:T(8,128)(2,1)S(1)}, bf16[32,2176]{1,0:T(8,128)(2,1)}, u32[]{:S(2)}, u32[]{:S(2)}) collective-permute-start(bf16[32,2176]{1,0:T(8,128)(2,1)S(1)} %get-tuple-element.26), channel_id=1, source_target_pairs={{0,8},{4,12},{8,0},{12,4},{1,9},{5,13},{9,1},{13,5},{2,10},{6,14},... | collective-permute-start | bytes 417800 | tf_op jit(solution)/shard_map/ppermute | solution.py:65
  11.9 9.3 %collective-permute-start.2 = (bf16[32,2176]{1,0:T(8,128)(2,1)S(1)}, bf16[32,2176]{1,0:T(8,128)(2,1)}, u32[]{:S(2)}, u32[]{:S(2)}) collective-permute-start(bf16[32,2176]{1,0:T(8,128)(2,1)S(1)} %get-tuple-element.26), channel_id=1, source_target_pairs={{0,12},{4,0},{8,4},{12,8},{1,13},{5,1},{9,5},{13,9},{2,14},{6,2},{... | collective-permute-start | bytes 417800 | tf_op jit(solution)/shard_map/ppermute | solution.py:65
  21.2 31.5 %copy-start.2 = (bf16[1,2048,1536]{2,1,0:T(8,128)(2,1)S(1)}, bf16[1,2048,1536]{2,1,0:T(8,128)(2,1)}, u32[]{:S(2)}) copy-start(bf16[1,2048,1536]{2,1,0:T(8,128)(2,1)} %param.10) | copy-start | bytes 18874372
  22.4 15.9 %collective-permute-start.3 = (bf16[128,2176]{1,0:T(8,128)(2,1)S(1)}, bf16[128,2176]{1,0:T(8,128)(2,1)S(1)}, u32[]{:S(2)}, u32[]{:S(2)}) collective-permute-start(bf16[128,2176]{1,0:T(8,128)(2,1)S(1)} %pad_maximum_fusion), channel_id=1, source_target_pairs={{0,2},{2,0},{1,3},{3,1},{4,6},{6,4},{5,7},{7,5},{8,10},{10,8},{9,1... | collective-permute-start | bytes 1671176 | tf_op jit(solution)/shard_map/ppermute | solution.py:65
  24.0 10.8 %collective-permute-start.10 = (bf16[32,2176]{1,0:T(8,128)(2,1)S(1)}, bf16[32,2176]{1,0:T(8,128)(2,1)S(1)}, u32[]{:S(2)}, u32[]{:S(2)}) collective-permute-start(bf16[32,2176]{1,0:T(8,128)(2,1)S(1)} %get-tuple-element.6), channel_id=1, source_target_pairs={{0,4},{4,8},{8,12},{12,0},{1,5},{5,9},{9,13},{13,1},{2,6},{6,10},{... | collective-permute-start | bytes 417800 | tf_op jit(solution)/shard_map/ppermute | solution.py:65
  27.5 10.2 %collective-permute-start.11 = (bf16[32,2176]{1,0:T(8,128)(2,1)S(1)}, bf16[32,2176]{1,0:T(8,128)(2,1)S(1)}, u32[]{:S(2)}, u32[]{:S(2)}) collective-permute-start(bf16[32,2176]{1,0:T(8,128)(2,1)S(1)} %get-tuple-element.6), channel_id=1, source_target_pairs={{0,8},{4,12},{8,0},{12,4},{1,9},{5,13},{9,1},{13,5},{2,10},{6,14},... | collective-permute-start | bytes 417800 | tf_op jit(solution)/shard_map/ppermute | solution.py:65
  29.1 8.5 %collective-permute-start.12 = (bf16[32,2176]{1,0:T(8,128)(2,1)S(1)}, bf16[32,2176]{1,0:T(8,128)(2,1)S(1)}, u32[]{:S(2)}, u32[]{:S(2)}) collective-permute-start(bf16[32,2176]{1,0:T(8,128)(2,1)S(1)} %get-tuple-element.6), channel_id=1, source_target_pairs={{0,12},{4,0},{8,4},{12,8},{1,13},{5,1},{9,5},{13,9},{2,14},{6,2},{... | collective-permute-start | bytes 417800 | tf_op jit(solution)/shard_map/ppermute | solution.py:65
  37.7 14.5 %collective-permute-start.13 = (bf16[128,2176]{1,0:T(8,128)(2,1)S(1)}, bf16[128,2176]{1,0:T(8,128)(2,1)S(1)}, u32[]{:S(2)}, u32[]{:S(2)}) collective-permute-start(bf16[128,2176]{1,0:T(8,128)(2,1)S(1)} %pad_maximum_fusion.1), channel_id=1, source_target_pairs={{0,2},{2,0},{1,3},{3,1},{4,6},{6,4},{5,7},{7,5},{8,10},{10,8},{9,1... | collective-permute-start | bytes 1671176 | tf_op jit(solution)/shard_map/ppermute | solution.py:65
  39.4 13.1 %copy-start.1 = (bf16[512,2176]{1,0:T(8,128)(2,1)S(1)}, bf16[512,2176]{1,0:T(8,128)(2,1)}, u32[]{:S(2)}) copy-start(bf16[512,2176]{1,0:T(8,128)(2,1)} %get-tuple-element.16) | copy-start | bytes 6684676
  39.4 13.1 %collective-permute-start.4 = (bf16[256,2176]{1,0:T(8,128)(2,1)}, bf16[256,2176]{1,0:T(8,128)(2,1)S(1)}, u32[]{:S(2)}, u32[]{:S(2)}) collective-permute-start(bf16[256,2176]{1,0:T(8,128)(2,1)} %get-tuple-element.15), channel_id=1, source_target_pairs={{0,1},{1,0},{2,3},{3,2},{4,5},{5,4},{6,7},{7,6},{8,9},{9,8},{10,11... | collective-permute-start | bytes 3342344 | tf_op jit(solution)/shard_map/ppermute | solution.py:65
  52.3 3.7 %collective-permute-start.14 = (bf16[256,2176]{1,0:T(8,128)(2,1)S(1)}, bf16[256,2176]{1,0:T(8,128)(2,1)S(1)}, u32[]{:S(2)}, u32[]{:S(2)}) collective-permute-start(bf16[256,2176]{1,0:T(8,128)(2,1)S(1)} %get-tuple-element.13), channel_id=1, source_target_pairs={{0,1},{1,0},{2,3},{3,2},{4,5},{5,4},{6,7},{7,6},{8,9},{9,8},{10,11... | collective-permute-start | bytes 3342344 | tf_op jit(solution)/shard_map/ppermute | solution.py:65
  62.3 2.8 %collective-permute-start.15 = (bf16[256,2048]{1,0:T(8,128)(2,1)S(1)}, bf16[256,2048]{1,0:T(8,128)(2,1)S(1)}, u32[]{:S(2)}, u32[]{:S(2)}) collective-permute-start(bf16[256,2048]{1,0:T(8,128)(2,1)S(1)} %split.124), channel_id=1, source_target_pairs={{0,1},{1,0},{2,3},{3,2},{4,5},{5,4},{6,7},{7,6},{8,9},{9,8},{10,11... | collective-permute-start | bytes 3145736 | tf_op jit(solution)/shard_map/ppermute | solution.py:74
  64.8 2.7 %collective-permute-start.5 = (bf16[256,2048]{1,0:T(8,128)(2,1)S(1)}, bf16[256,2048]{1,0:T(8,128)(2,1)S(1)}, u32[]{:S(2)}, u32[]{:S(2)}) collective-permute-start(bf16[256,2048]{1,0:T(8,128)(2,1)S(1)} %split.125), channel_id=1, source_target_pairs={{0,1},{1,0},{2,3},{3,2},{4,5},{5,4},{6,7},{7,6},{8,9},{9,8},{10,11... | collective-permute-start | bytes 3145736 | tf_op jit(solution)/shard_map/ppermute | solution.py:74
  65.5 14.9 %collective-permute-start.16 = (bf16[128,2048]{1,0:T(8,128)(2,1)S(1)}, bf16[128,2048]{1,0:T(8,128)(2,1)S(1)}, u32[]{:S(2)}, u32[]{:S(2)}) collective-permute-start(bf16[128,2048]{1,0:T(8,128)(2,1)S(1)} %split.126), channel_id=1, source_target_pairs={{0,2},{2,0},{1,3},{3,1},{4,6},{6,4},{5,7},{7,5},{8,10},{10,8},{9,1... | collective-permute-start | bytes 1572872 | tf_op jit(solution)/shard_map/ppermute | solution.py:74
  68.0 23.1 %collective-permute-start.6 = (bf16[128,2048]{1,0:T(8,128)(2,1)S(1)}, bf16[128,2048]{1,0:T(8,128)(2,1)S(1)}, u32[]{:S(2)}, u32[]{:S(2)}) collective-permute-start(bf16[128,2048]{1,0:T(8,128)(2,1)S(1)} %split.127), channel_id=1, source_target_pairs={{0,2},{2,0},{1,3},{3,1},{4,6},{6,4},{5,7},{7,5},{8,10},{10,8},{9,1... | collective-permute-start | bytes 1572872 | tf_op jit(solution)/shard_map/ppermute | solution.py:74
  80.6 15.2 %collective-permute-start.19 = (bf16[32,2048]{1,0:T(8,128)(2,1)S(1)}, bf16[32,2048]{1,0:T(8,128)(2,1)S(1)}, u32[]{:S(2)}, u32[]{:S(2)}) collective-permute-start(bf16[32,2048]{1,0:T(8,128)(2,1)S(1)} %get-tuple-element.21), channel_id=1, source_target_pairs={{0,4},{4,8},{8,12},{12,0},{1,5},{5,9},{9,13},{13,1},{2,6},{6,10},{... | collective-permute-start | bytes 393224 | tf_op jit(solution)/shard_map/ppermute | solution.py:74
  84.2 13.1 %collective-permute-start.18 = (bf16[32,2048]{1,0:T(8,128)(2,1)S(1)}, bf16[32,2048]{1,0:T(8,128)(2,1)S(1)}, u32[]{:S(2)}, u32[]{:S(2)}) collective-permute-start(bf16[32,2048]{1,0:T(8,128)(2,1)S(1)} %get-tuple-element.22), channel_id=1, source_target_pairs={{0,8},{4,12},{8,0},{12,4},{1,9},{5,13},{9,1},{13,5},{2,10},{6,14},... | collective-permute-start | bytes 393224 | tf_op jit(solution)/shard_map/ppermute | solution.py:74
  85.2 12.1 %collective-permute-start.17 = (bf16[32,2048]{1,0:T(8,128)(2,1)S(1)}, bf16[32,2048]{1,0:T(8,128)(2,1)S(1)}, u32[]{:S(2)}, u32[]{:S(2)}) collective-permute-start(bf16[32,2048]{1,0:T(8,128)(2,1)S(1)} %get-tuple-element.20), channel_id=1, source_target_pairs={{0,12},{4,0},{8,4},{12,8},{1,13},{5,1},{9,5},{13,9},{2,14},{6,2},{... | collective-permute-start | bytes 393224 | tf_op jit(solution)/shard_map/ppermute | solution.py:74
  91.2 8.4 %collective-permute-start.9 = (bf16[32,2048]{1,0:T(8,128)(2,1)S(1)}, bf16[32,2048]{1,0:T(8,128)(2,1)S(1)}, u32[]{:S(2)}, u32[]{:S(2)}) collective-permute-start(bf16[32,2048]{1,0:T(8,128)(2,1)S(1)} %get-tuple-element.18), channel_id=1, source_target_pairs={{0,4},{4,8},{8,12},{12,0},{1,5},{5,9},{9,13},{13,1},{2,6},{6,10},{... | collective-permute-start | bytes 393224 | tf_op jit(solution)/shard_map/ppermute | solution.py:74
  94.8 9.6 %collective-permute-start.8 = (bf16[32,2048]{1,0:T(8,128)(2,1)S(1)}, bf16[32,2048]{1,0:T(8,128)(2,1)S(1)}, u32[]{:S(2)}, u32[]{:S(2)}) collective-permute-start(bf16[32,2048]{1,0:T(8,128)(2,1)S(1)} %get-tuple-element.19), channel_id=1, source_target_pairs={{0,8},{4,12},{8,0},{12,4},{1,9},{5,13},{9,1},{13,5},{2,10},{6,14},... | collective-permute-start | bytes 393224 | tf_op jit(solution)/shard_map/ppermute | solution.py:74
  95.8 8.7 %collective-permute-start.7 = (bf16[32,2048]{1,0:T(8,128)(2,1)S(1)}, bf16[32,2048]{1,0:T(8,128)(2,1)S(1)}, u32[]{:S(2)}, u32[]{:S(2)}) collective-permute-start(bf16[32,2048]{1,0:T(8,128)(2,1)S(1)} %get-tuple-element.17), channel_id=1, source_target_pairs={{0,12},{4,0},{8,4},{12,8},{1,13},{5,1},{9,5},{13,9},{2,14},{6,2},{... | collective-permute-start | bytes 393224 | tf_op jit(solution)/shard_map/ppermute | solution.py:74

commit v6 on v5

--- a/solution.py
+++ b/solution.py
@@ -114,7 +114,7 @@
     return jnp.concatenate(results, axis=0).astype(jnp.bfloat16)
 
 
-STREAMS = 2
+STREAMS = 4
 
 
 def factor_expert(mesh):

time: 106 us -> 117 us (1.10)
  starting transfers between devices: 29.1 us -> 46.8 us
  waiting for transfers between devices: 48.5 us -> 43.2 us
  local copies, waits for them, and re-layouts: 10.8 us -> 6.1 us
  matrix products: 10.6 us -> 14.4 us
    ppermute x10 -> x20, starting transfers between devices: 13.9 us -> 23.6 us  [scatter_stage(): lax.ppermute(pieces[shift].astype(jnp.bfloat16), axis, pairs)]
    ppermute x10 -> x20, starting transfers between devices: 15.2 us -> 23.2 us  [gather_stage(): got.append(lax.ppermute(block, axis, pairs))]
    ppermute x10 -> x20, waiting for transfers between devices: 25 us -> 20.1 us  [scatter_stage(): lax.ppermute(pieces[shift].astype(jnp.bfloat16), axis, pairs)]
    dot_general x2 -> x4, matrix products: 6.9 us -> 10.2 us  [expert_block(): pair = jnp.dot(rows_in, gate_up, preferred_element_type=jnp.float32)]
    unnamed x13 -> x27, local copies, waits for them, and re-layouts: 5 us -> 3.16 us
    dot_general x2 -> x4, matrix products: 3.69 us -> 4.23 us  [expert_block(): jnp.dot(active, down_proj, preferred_element_type=jnp.float32)]
    ppermute x10 -> x20, waiting for transfers between devices: 23.5 us -> 23.1 us  [gather_stage(): got.append(lax.ppermute(block, axis, pairs))]
  transfers between devices with their start and end apart: 20 -> 40, of which waited for: 10 -> 16; matrix products, arithmetic and copies ran while one was open for 12% -> 14% of each run, Pallas kernels for 0% -> 0%
where the time goes in v6:
time: 117 us
  starting transfers between devices  46.8 us (40%)
  waiting for transfers between devices  43.2 us (37%)
  matrix products  14.4 us (12%)
  local copies, waits for them, and re-layouts  6.1 us (5%)
  other arithmetic  5.47 us (5%)
    ppermute x20, starting transfers between devices, scatter_stage(): lax.ppermute(pieces[shift].astype(jnp.bfloat16), axis, pairs)  23.6 us
    ppermute x20, starting transfers between devices, gather_stage(): got.append(lax.ppermute(block, axis, pairs))  23.2 us
    ppermute x20, waiting for transfers between devices, gather_stage(): got.append(lax.ppermute(block, axis, pairs))  23.1 us
    ppermute x20, waiting for transfers between devices, scatter_stage(): lax.ppermute(pieces[shift].astype(jnp.bfloat16), axis, pairs)  20.1 us
    dot_general x4, matrix products, expert_block(): pair = jnp.dot(rows_in, gate_up, preferred_element_type=jnp.float32)  10.2 us
    dot_general x4, matrix products, expert_block(): jnp.dot(active, down_proj, preferred_element_type=jnp.float32)  4.23 us
    unnamed x27, local copies, waits for them, and re-layouts  3.16 us
  transfers between devices with their start and end apart: 40, of which 16 were waited for; matrix products, arithmetic and copies ran while one was open for 14% of the time, Pallas kernels for 0%

profile of v6, /device:TPU:0, one launch (start us, length us, event | category | flops | bytes accessed | tf_op | source)
XLA Modules:
  0.0 116.5 jit_solution(4558478418393286209)
XLA Ops:
  0.0 0.9 reduce_sum.54
  2.8 1.1 concatenate.54
  4.5 3.1 %collective-permute-start = (bf16[16,2176]{1,0:T(8,128)(2,1)}, bf16[16,2176]{1,0:T(8,128)(2,1)S(1)}, u32[]{:S(2)}, u32[]{:S(2)}) collective-permute-start(bf16[16,2176]{1,0:T(8,128)(2,1)} %get-tuple-element.30), channel_id=1, source_target_pairs={{0,4},{4,8},{8,12},{12,0},{1,5},{5,9},{9,13},{13,1},{2,6},{6,10},{... | collective-permute-start | bytes 208904 | tf_op jit(solution)/shard_map/ppermute | solution.py:65
  7.6 2.6 %collective-permute-start.1 = (bf16[16,2176]{1,0:T(8,128)(2,1)}, bf16[16,2176]{1,0:T(8,128)(2,1)S(1)}, u32[]{:S(2)}, u32[]{:S(2)}) collective-permute-start(bf16[16,2176]{1,0:T(8,128)(2,1)} %get-tuple-element.30), channel_id=1, source_target_pairs={{0,8},{4,12},{8,0},{12,4},{1,9},{5,13},{9,1},{13,5},{2,10},{6,14},... | collective-permute-start | bytes 208904 | tf_op jit(solution)/shard_map/ppermute | solution.py:65
  10.2 1.3 %collective-permute-start.2 = (bf16[16,2176]{1,0:T(8,128)(2,1)}, bf16[16,2176]{1,0:T(8,128)(2,1)S(1)}, u32[]{:S(2)}, u32[]{:S(2)}) collective-permute-start(bf16[16,2176]{1,0:T(8,128)(2,1)} %get-tuple-element.30), channel_id=1, source_target_pairs={{0,12},{4,0},{8,4},{12,8},{1,13},{5,1},{9,5},{13,9},{2,14},{6,2},{... | collective-permute-start | bytes 208904 | tf_op jit(solution)/shard_map/ppermute | solution.py:65
  11.5 0.8 collective-permute-done
  12.4 2.7 %collective-permute-done.1 = bf16[16,2176]{1,0:T(8,128)(2,1)S(1)} collective-permute-done((bf16[16,2176]{1,0:T(8,128)(2,1)}, bf16[16,2176]{1,0:T(8,128)(2,1)S(1)}, u32[]{:S(2)}, u32[]{:S(2)}) %collective-permute-start.1) | collective-permute-done | bytes 69664 | tf_op jit(solution)/shard_map/ppermute | solution.py:65
  15.3 0.9 pad_maximum_fusion
  16.2 1.5 %collective-permute-start.3 = (bf16[64,2176]{1,0:T(8,128)(2,1)S(1)}, bf16[64,2176]{1,0:T(8,128)(2,1)S(1)}, u32[]{:S(2)}, u32[]{:S(2)}) collective-permute-start(bf16[64,2176]{1,0:T(8,128)(2,1)S(1)} %pad_maximum_fusion), channel_id=1, source_target_pairs={{0,2},{2,0},{1,3},{3,1},{4,6},{6,4},{5,7},{7,5},{8,10},{10,8},{9,1... | collective-permute-start | bytes 835592 | tf_op jit(solution)/shard_map/ppermute | solution.py:65
  17.8 0.9 constant_dynamic-update-slice_fusion.19
  18.7 1.8 %collective-permute-start.10 = (bf16[16,2176]{1,0:T(8,128)(2,1)}, bf16[16,2176]{1,0:T(8,128)(2,1)S(1)}, u32[]{:S(2)}, u32[]{:S(2)}) collective-permute-start(bf16[16,2176]{1,0:T(8,128)(2,1)} %get-tuple-element.8), channel_id=1, source_target_pairs={{0,4},{4,8},{8,12},{12,0},{1,5},{5,9},{9,13},{13,1},{2,6},{6,10},{... | collective-permute-start | bytes 208904 | tf_op jit(solution)/shard_map/ppermute | solution.py:65
  20.5 1.9 %collective-permute-start.11 = (bf16[16,2176]{1,0:T(8,128)(2,1)}, bf16[16,2176]{1,0:T(8,128)(2,1)S(1)}, u32[]{:S(2)}, u32[]{:S(2)}) collective-permute-start(bf16[16,2176]{1,0:T(8,128)(2,1)} %get-tuple-element.8), channel_id=1, source_target_pairs={{0,8},{4,12},{8,0},{12,4},{1,9},{5,13},{9,1},{13,5},{2,10},{6,14},... | collective-permute-start | bytes 208904 | tf_op jit(solution)/shard_map/ppermute | solution.py:65
  25.6 2.0 %collective-permute-done.11 = bf16[16,2176]{1,0:T(8,128)(2,1)S(1)} collective-permute-done((bf16[16,2176]{1,0:T(8,128)(2,1)}, bf16[16,2176]{1,0:T(8,128)(2,1)S(1)}, u32[]{:S(2)}, u32[]{:S(2)}) %collective-permute-start.11) | collective-permute-done | bytes 69664 | tf_op jit(solution)/shard_map/ppermute | solution.py:65
  28.2 1.7 %collective-permute-start.20 = (bf16[16,2176]{1,0:T(8,128)(2,1)S(1)}, bf16[16,2176]{1,0:T(8,128)(2,1)S(1)}, u32[]{:S(2)}, u32[]{:S(2)}) collective-permute-start(bf16[16,2176]{1,0:T(8,128)(2,1)S(1)} %copy-done.1), channel_id=1, source_target_pairs={{0,4},{4,8},{8,12},{12,0},{1,5},{5,9},{9,13},{13,1},{2,6},{6,10},{... | collective-permute-start | bytes 208904 | tf_op jit(solution)/shard_map/ppermute | solution.py:65
  29.9 1.4 %collective-permute-start.21 = (bf16[16,2176]{1,0:T(8,128)(2,1)S(1)}, bf16[16,2176]{1,0:T(8,128)(2,1)S(1)}, u32[]{:S(2)}, u32[]{:S(2)}) collective-permute-start(bf16[16,2176]{1,0:T(8,128)(2,1)S(1)} %copy-done.1), channel_id=1, source_target_pairs={{0,8},{4,12},{8,0},{12,4},{1,9},{5,13},{9,1},{13,5},{2,10},{6,14},... | collective-permute-start | bytes 208904 | tf_op jit(solution)/shard_map/ppermute | solution.py:65
  31.3 1.0 collective-permute-start.22
  32.4 2.4 %collective-permute-done.20 = bf16[16,2176]{1,0:T(8,128)(2,1)S(1)} collective-permute-done((bf16[16,2176]{1,0:T(8,128)(2,1)S(1)}, bf16[16,2176]{1,0:T(8,128)(2,1)S(1)}, u32[]{:S(2)}, u32[]{:S(2)}) %collective-permute-start.20) | collective-permute-done | bytes 69664 | tf_op jit(solution)/shard_map/ppermute | solution.py:65
  34.8 2.1 %collective-permute-done.21 = bf16[16,2176]{1,0:T(8,128)(2,1)S(1)} collective-permute-done((bf16[16,2176]{1,0:T(8,128)(2,1)S(1)}, bf16[16,2176]{1,0:T(8,128)(2,1)S(1)}, u32[]{:S(2)}, u32[]{:S(2)}) %collective-permute-start.21) | collective-permute-done | bytes 69664 | tf_op jit(solution)/shard_map/ppermute | solution.py:65
  36.9 1.6 %collective-permute-start.30 = (bf16[16,2176]{1,0:T(8,128)(2,1)S(1)}, bf16[16,2176]{1,0:T(8,128)(2,1)S(1)}, u32[]{:S(2)}, u32[]{:S(2)}) collective-permute-start(bf16[16,2176]{1,0:T(8,128)(2,1)S(1)} %get-tuple-element.10), channel_id=1, source_target_pairs={{0,4},{4,8},{8,12},{12,0},{1,5},{5,9},{9,13},{13,1},{2,6},{6,10},{... | collective-permute-start | bytes 208904 | tf_op jit(solution)/shard_map/ppermute | solution.py:65
  38.4 1.3 %collective-permute-start.31 = (bf16[16,2176]{1,0:T(8,128)(2,1)S(1)}, bf16[16,2176]{1,0:T(8,128)(2,1)S(1)}, u32[]{:S(2)}, u32[]{:S(2)}) collective-permute-start(bf16[16,2176]{1,0:T(8,128)(2,1)S(1)} %get-tuple-element.10), channel_id=1, source_target_pairs={{0,8},{4,12},{8,0},{12,4},{1,9},{5,13},{9,1},{13,5},{2,10},{6,14},... | collective-permute-start | bytes 208904 | tf_op jit(solution)/shard_map/ppermute | solution.py:65
  39.8 1.1 collective-permute-start.32
  40.9 2.8 %collective-permute-done.30 = bf16[16,2176]{1,0:T(8,128)(2,1)S(1)} collective-permute-done((bf16[16,2176]{1,0:T(8,128)(2,1)S(1)}, bf16[16,2176]{1,0:T(8,128)(2,1)S(1)}, u32[]{:S(2)}, u32[]{:S(2)}) %collective-permute-start.30) | collective-permute-done | bytes 69664 | tf_op jit(solution)/shard_map/ppermute | solution.py:65
  44.2 1.3 %collective-permute-done.31 = bf16[16,2176]{1,0:T(8,128)(2,1)S(1)} collective-permute-done((bf16[16,2176]{1,0:T(8,128)(2,1)S(1)}, bf16[16,2176]{1,0:T(8,128)(2,1)S(1)}, u32[]{:S(2)}, u32[]{:S(2)}) %collective-permute-start.31) | collective-permute-done | bytes 69664 | tf_op jit(solution)/shard_map/ppermute | solution.py:65
  46.9 5.2 %collective-permute-done.23 = bf16[64,2176]{1,0:T(8,128)(2,1)S(1)} collective-permute-done((bf16[64,2176]{1,0:T(8,128)(2,1)S(1)}, bf16[64,2176]{1,0:T(8,128)(2,1)S(1)}, u32[]{:S(2)}, u32[]{:S(2)}) %collective-permute-start.23) | collective-permute-done | bytes 278560 | tf_op jit(solution)/shard_map/ppermute | solution.py:65
  52.2 2.9 %collective-permute-done.33 = bf16[64,2176]{1,0:T(8,128)(2,1)S(1)} collective-permute-done((bf16[64,2176]{1,0:T(8,128)(2,1)S(1)}, bf16[64,2176]{1,0:T(8,128)(2,1)S(1)}, u32[]{:S(2)}, u32[]{:S(2)}) %collective-permute-start.33) | collective-permute-done | bytes 278560 | tf_op jit(solution)/shard_map/ppermute | solution.py:65
  55.4 4.7 %fusion.6 = f32[256,1536]{1,0:T(8,128)S(1)} fusion(bf16[1,2048,1536]{2,1,0:T(8,128)(2,1)} %param.10, bf16[256,2176]{1,0:T(8,128)(2,1)S(1)} %constant_dynamic-update-slice_fusion.5), kind=kOutput, calls=%fused_computation.6 | convolution fusion | flops 1610612736 | bytes 8912896 | tf_op jit(solution)/shard_map/dot_general | solution.py:9
  60.2 1.8 %fusion.4 = f32[256,1536]{1,0:T(8,128)S(1)} fusion(bf16[1,2048,1536]{2,1,0:T(8,128)(2,1)S(1)} %bitcast.43, bf16[256,2176]{1,0:T(8,128)(2,1)S(1)} %constant_dynamic-update-slice_fusion.20), kind=kOutput, calls=%fused_computation.4 | convolution fusion | flops 1610612736 | bytes 8912896 | tf_op jit(solution)/shard_map/dot_general | solution.py:9
  62.1 1.8 %fusion.2 = f32[256,1536]{1,0:T(8,128)S(1)} fusion(bf16[1,2048,1536]{2,1,0:T(8,128)(2,1)S(1)} %bitcast.43, bf16[256,2176]{1,0:T(8,128)(2,1)S(1)} %constant_dynamic-update-slice_fusion.35), kind=kOutput, calls=%fused_computation.2 | convolution fusion | flops 1610612736 | bytes 8912896 | tf_op jit(solution)/shard_map/dot_general | solution.py:9
  64.0 1.8 %fusion = f32[256,1536]{1,0:T(8,128)S(1)} fusion(bf16[1,2048,1536]{2,1,0:T(8,128)(2,1)S(1)} %bitcast.43, bf16[256,2176]{1,0:T(8,128)(2,1)S(1)} %constant_dynamic-update-slice_fusion.46), kind=kOutput, calls=%fused_computation | convolution fusion | flops 1610612736 | bytes 8912896 | tf_op jit(solution)/shard_map/dot_general | solution.py:9
  66.4 1.1 fusion.49
  68.1 1.1 fusion.40
  69.3 1.1 fusion.31
  71.0 1.1 fusion.22
  72.9 1.8 %collective-permute-start.26 = (bf16[64,2048]{1,0:T(8,128)(2,1)S(1)}, bf16[64,2048]{1,0:T(8,128)(2,1)S(1)}, u32[]{:S(2)}, u32[]{:S(2)}) collective-permute-start(bf16[64,2048]{1,0:T(8,128)(2,1)S(1)} %split.251), channel_id=1, source_target_pairs={{0,2},{2,0},{1,3},{3,1},{4,6},{6,4},{5,7},{7,5},{8,10},{10,8},{9,1... | collective-permute-start | bytes 786440 | tf_op jit(solution)/shard_map/ppermute | solution.py:74
  75.3 1.8 %collective-permute-start.6 = (bf16[64,2048]{1,0:T(8,128)(2,1)S(1)}, bf16[64,2048]{1,0:T(8,128)(2,1)S(1)}, u32[]{:S(2)}, u32[]{:S(2)}) collective-permute-start(bf16[64,2048]{1,0:T(8,128)(2,1)S(1)} %split.253), channel_id=1, source_target_pairs={{0,2},{2,0},{1,3},{3,1},{4,6},{6,4},{5,7},{7,5},{8,10},{10,8},{9,1... | collective-permute-start | bytes 786440 | tf_op jit(solution)/shard_map/ppermute | solution.py:74
  77.2 4.5 %collective-permute-done.36 = bf16[64,2048]{1,0:T(8,128)(2,1)S(1)} collective-permute-done((bf16[64,2048]{1,0:T(8,128)(2,1)S(1)}, bf16[64,2048]{1,0:T(8,128)(2,1)S(1)}, u32[]{:S(2)}, u32[]{:S(2)}) %collective-permute-start.36) | collective-permute-done | bytes 262176 | tf_op jit(solution)/shard_map/ppermute | solution.py:74
  82.4 1.1 collective-permute-start.38
  83.5 3.7 %collective-permute-done.26 = bf16[64,2048]{1,0:T(8,128)(2,1)S(1)} collective-permute-done((bf16[64,2048]{1,0:T(8,128)(2,1)S(1)}, bf16[64,2048]{1,0:T(8,128)(2,1)S(1)}, u32[]{:S(2)}, u32[]{:S(2)}) %collective-permute-start.26) | collective-permute-done | bytes 262176 | tf_op jit(solution)/shard_map/ppermute | solution.py:74
  87.2 1.2 %collective-permute-start.37 = (bf16[16,2048]{1,0:T(8,128)(2,1)S(1)}, bf16[16,2048]{1,0:T(8,128)(2,1)S(1)}, u32[]{:S(2)}, u32[]{:S(2)}) collective-permute-start(bf16[16,2048]{1,0:T(8,128)(2,1)S(1)} %get-tuple-element.46), channel_id=1, source_target_pairs={{0,12},{4,0},{8,4},{12,8},{1,13},{5,1},{9,5},{13,9},{2,14},{6,2},{... | collective-permute-start | bytes 196616 | tf_op jit(solution)/shard_map/ppermute | solution.py:74
  88.5 4.3 %collective-permute-done.16 = bf16[64,2048]{1,0:T(8,128)(2,1)S(1)} collective-permute-done((bf16[64,2048]{1,0:T(8,128)(2,1)S(1)}, bf16[64,2048]{1,0:T(8,128)(2,1)S(1)}, u32[]{:S(2)}, u32[]{:S(2)}) %collective-permute-start.16) | collective-permute-done | bytes 262176 | tf_op jit(solution)/shard_map/ppermute | solution.py:74
  93.6 4.4 %collective-permute-done.6 = bf16[64,2048]{1,0:T(8,128)(2,1)S(1)} collective-permute-done((bf16[64,2048]{1,0:T(8,128)(2,1)S(1)}, bf16[64,2048]{1,0:T(8,128)(2,1)S(1)}, u32[]{:S(2)}, u32[]{:S(2)}) %collective-permute-start.6) | collective-permute-done | bytes 262176 | tf_op jit(solution)/shard_map/ppermute | solution.py:74
  98.0 0.8 collective-permute-start.28
  98.9 2.2 %collective-permute-start.27 = (bf16[16,2048]{1,0:T(8,128)(2,1)S(1)}, bf16[16,2048]{1,0:T(8,128)(2,1)S(1)}, u32[]{:S(2)}, u32[]{:S(2)}) collective-permute-start(bf16[16,2048]{1,0:T(8,128)(2,1)S(1)} %get-tuple-element.43), channel_id=1, source_target_pairs={{0,12},{4,0},{8,4},{12,8},{1,13},{5,1},{9,5},{13,9},{2,14},{6,2},{... | collective-permute-start | bytes 196616 | tf_op jit(solution)/shard_map/ppermute | solution.py:74
  101.2 1.9 %collective-permute-start.18 = (bf16[16,2048]{1,0:T(8,128)(2,1)S(1)}, bf16[16,2048]{1,0:T(8,128)(2,1)S(1)}, u32[]{:S(2)}, u32[]{:S(2)}) collective-permute-start(bf16[16,2048]{1,0:T(8,128)(2,1)S(1)} %get-tuple-element.42), channel_id=1, source_target_pairs={{0,8},{4,12},{8,0},{12,4},{1,9},{5,13},{9,1},{13,5},{2,10},{6,14},... | collective-permute-start | bytes 196616 | tf_op jit(solution)/shard_map/ppermute | solution.py:74
  103.2 1.9 %collective-permute-start.17 = (bf16[16,2048]{1,0:T(8,128)(2,1)S(1)}, bf16[16,2048]{1,0:T(8,128)(2,1)S(1)}, u32[]{:S(2)}, u32[]{:S(2)}) collective-permute-start(bf16[16,2048]{1,0:T(8,128)(2,1)S(1)} %get-tuple-element.40), channel_id=1, source_target_pairs={{0,12},{4,0},{8,4},{12,8},{1,13},{5,1},{9,5},{13,9},{2,14},{6,2},{... | collective-permute-start | bytes 196616 | tf_op jit(solution)/shard_map/ppermute | solution.py:74
  105.7 2.9 %collective-permute-start.8 = (bf16[16,2048]{1,0:T(8,128)(2,1)S(1)}, bf16[16,2048]{1,0:T(8,128)(2,1)S(1)}, u32[]{:S(2)}, u32[]{:S(2)}) collective-permute-start(bf16[16,2048]{1,0:T(8,128)(2,1)S(1)} %get-tuple-element.39), channel_id=1, source_target_pairs={{0,8},{4,12},{8,0},{12,4},{1,9},{5,13},{9,1},{13,5},{2,10},{6,14},... | collective-permute-start | bytes 196616 | tf_op jit(solution)/shard_map/ppermute | solution.py:74
  108.6 3.9 %collective-permute-start.7 = (bf16[16,2048]{1,0:T(8,128)(2,1)S(1)}, bf16[16,2048]{1,0:T(8,128)(2,1)S(1)}, u32[]{:S(2)}, u32[]{:S(2)}) collective-permute-start(bf16[16,2048]{1,0:T(8,128)(2,1)S(1)} %get-tuple-element.37), channel_id=1, source_target_pairs={{0,12},{4,0},{8,4},{12,8},{1,13},{5,1},{9,5},{13,9},{2,14},{6,2},{... | collective-permute-start | bytes 196616 | tf_op jit(solution)/shard_map/ppermute | solution.py:74
  112.6 3.2 %collective-permute-done.8 = bf16[16,2048]{1,0:T(8,128)(2,1)S(1)} collective-permute-done((bf16[16,2048]{1,0:T(8,128)(2,1)S(1)}, bf16[16,2048]{1,0:T(8,128)(2,1)S(1)}, u32[]{:S(2)}, u32[]{:S(2)}) %collective-permute-start.8) | collective-permute-done | bytes 65568 | tf_op jit(solution)/shard_map/ppermute | solution.py:74
  (119 shorter events, 15.6 us)
Async XLA Ops:
  0.0 66.4 %copy-start = (bf16[1,768,2048]{2,1,0:T(8,128)(2,1)S(1)}, bf16[1,768,2048]{2,1,0:T(8,128)(2,1)}, u32[]{:S(2)}) copy-start(bf16[1,768,2048]{2,1,0:T(8,128)(2,1)} %param.11) | copy-start | bytes 9437188
  4.5 7.8 %collective-permute-start = (bf16[16,2176]{1,0:T(8,128)(2,1)}, bf16[16,2176]{1,0:T(8,128)(2,1)S(1)}, u32[]{:S(2)}, u32[]{:S(2)}) collective-permute-start(bf16[16,2176]{1,0:T(8,128)(2,1)} %get-tuple-element.30), channel_id=1, source_target_pairs={{0,4},{4,8},{8,12},{12,0},{1,5},{5,9},{9,13},{13,1},{2,6},{6,10},{... | collective-permute-start | bytes 208904 | tf_op jit(solution)/shard_map/ppermute | solution.py:65
  7.6 7.5 %collective-permute-start.1 = (bf16[16,2176]{1,0:T(8,128)(2,1)}, bf16[16,2176]{1,0:T(8,128)(2,1)S(1)}, u32[]{:S(2)}, u32[]{:S(2)}) collective-permute-start(bf16[16,2176]{1,0:T(8,128)(2,1)} %get-tuple-element.30), channel_id=1, source_target_pairs={{0,8},{4,12},{8,0},{12,4},{1,9},{5,13},{9,1},{13,5},{2,10},{6,14},... | collective-permute-start | bytes 208904 | tf_op jit(solution)/shard_map/ppermute | solution.py:65
  10.2 5.2 %collective-permute-start.2 = (bf16[16,2176]{1,0:T(8,128)(2,1)}, bf16[16,2176]{1,0:T(8,128)(2,1)S(1)}, u32[]{:S(2)}, u32[]{:S(2)}) collective-permute-start(bf16[16,2176]{1,0:T(8,128)(2,1)} %get-tuple-element.30), channel_id=1, source_target_pairs={{0,12},{4,0},{8,4},{12,8},{1,13},{5,1},{9,5},{13,9},{2,14},{6,2},{... | collective-permute-start | bytes 208904 | tf_op jit(solution)/shard_map/ppermute | solution.py:65
  11.5 16.7 %copy-start.1 = (bf16[16,2176]{1,0:T(8,128)(2,1)S(1)}, bf16[16,2176]{1,0:T(8,128)(2,1)}, u32[]{:S(2)}) copy-start(bf16[16,2176]{1,0:T(8,128)(2,1)} %get-tuple-element.9) | copy-start | bytes 208900
  16.2 29.8 %collective-permute-start.3 = (bf16[64,2176]{1,0:T(8,128)(2,1)S(1)}, bf16[64,2176]{1,0:T(8,128)(2,1)S(1)}, u32[]{:S(2)}, u32[]{:S(2)}) collective-permute-start(bf16[64,2176]{1,0:T(8,128)(2,1)S(1)} %pad_maximum_fusion), channel_id=1, source_target_pairs={{0,2},{2,0},{1,3},{3,1},{4,6},{6,4},{5,7},{7,5},{8,10},{10,8},{9,1... | collective-permute-start | bytes 835592 | tf_op jit(solution)/shard_map/ppermute | solution.py:65
  18.7 6.9 %collective-permute-start.10 = (bf16[16,2176]{1,0:T(8,128)(2,1)}, bf16[16,2176]{1,0:T(8,128)(2,1)S(1)}, u32[]{:S(2)}, u32[]{:S(2)}) collective-permute-start(bf16[16,2176]{1,0:T(8,128)(2,1)} %get-tuple-element.8), channel_id=1, source_target_pairs={{0,4},{4,8},{8,12},{12,0},{1,5},{5,9},{9,13},{13,1},{2,6},{6,10},{... | collective-permute-start | bytes 208904 | tf_op jit(solution)/shard_map/ppermute | solution.py:65
  20.5 7.1 %collective-permute-start.11 = (bf16[16,2176]{1,0:T(8,128)(2,1)}, bf16[16,2176]{1,0:T(8,128)(2,1)S(1)}, u32[]{:S(2)}, u32[]{:S(2)}) collective-permute-start(bf16[16,2176]{1,0:T(8,128)(2,1)} %get-tuple-element.8), channel_id=1, source_target_pairs={{0,8},{4,12},{8,0},{12,4},{1,9},{5,13},{9,1},{13,5},{2,10},{6,14},... | collective-permute-start | bytes 208904 | tf_op jit(solution)/shard_map/ppermute | solution.py:65
  22.4 5.2 %collective-permute-start.12 = (bf16[16,2176]{1,0:T(8,128)(2,1)}, bf16[16,2176]{1,0:T(8,128)(2,1)S(1)}, u32[]{:S(2)}, u32[]{:S(2)}) collective-permute-start(bf16[16,2176]{1,0:T(8,128)(2,1)} %get-tuple-element.8), channel_id=1, source_target_pairs={{0,12},{4,0},{8,4},{12,8},{1,13},{5,1},{9,5},{13,9},{2,14},{6,2},{... | collective-permute-start | bytes 208904 | tf_op jit(solution)/shard_map/ppermute | solution.py:65
  27.6 18.6 %collective-permute-start.13 = (bf16[64,2176]{1,0:T(8,128)(2,1)S(1)}, bf16[64,2176]{1,0:T(8,128)(2,1)S(1)}, u32[]{:S(2)}, u32[]{:S(2)}) collective-permute-start(bf16[64,2176]{1,0:T(8,128)(2,1)S(1)} %get-tuple-element.71), channel_id=1, source_target_pairs={{0,2},{2,0},{1,3},{3,1},{4,6},{6,4},{5,7},{7,5},{8,10},{10,8},{9,1... | collective-permute-start | bytes 835592 | tf_op jit(solution)/shard_map/ppermute | solution.py:65
  28.2 6.5 %collective-permute-start.20 = (bf16[16,2176]{1,0:T(8,128)(2,1)S(1)}, bf16[16,2176]{1,0:T(8,128)(2,1)S(1)}, u32[]{:S(2)}, u32[]{:S(2)}) collective-permute-start(bf16[16,2176]{1,0:T(8,128)(2,1)S(1)} %copy-done.1), channel_id=1, source_target_pairs={{0,4},{4,8},{8,12},{12,0},{1,5},{5,9},{9,13},{13,1},{2,6},{6,10},{... | collective-permute-start | bytes 208904 | tf_op jit(solution)/shard_map/ppermute | solution.py:65
  29.9 6.9 %collective-permute-start.21 = (bf16[16,2176]{1,0:T(8,128)(2,1)S(1)}, bf16[16,2176]{1,0:T(8,128)(2,1)S(1)}, u32[]{:S(2)}, u32[]{:S(2)}) collective-permute-start(bf16[16,2176]{1,0:T(8,128)(2,1)S(1)} %copy-done.1), channel_id=1, source_target_pairs={{0,8},{4,12},{8,0},{12,4},{1,9},{5,13},{9,1},{13,5},{2,10},{6,14},... | collective-permute-start | bytes 208904 | tf_op jit(solution)/shard_map/ppermute | solution.py:65
  31.3 5.5 %collective-permute-start.22 = (bf16[16,2176]{1,0:T(8,128)(2,1)S(1)}, bf16[16,2176]{1,0:T(8,128)(2,1)S(1)}, u32[]{:S(2)}, u32[]{:S(2)}) collective-permute-start(bf16[16,2176]{1,0:T(8,128)(2,1)S(1)} %copy-done.1), channel_id=1, source_target_pairs={{0,12},{4,0},{8,4},{12,8},{1,13},{5,1},{9,5},{13,9},{2,14},{6,2},{... | collective-permute-start | bytes 208904 | tf_op jit(solution)/shard_map/ppermute | solution.py:65
  34.7 11.4 %copy-start.2 = (bf16[256,2176]{1,0:T(8,128)(2,1)S(1)}, bf16[256,2176]{1,0:T(8,128)(2,1)}, u32[]{:S(2)}) copy-start(bf16[256,2176]{1,0:T(8,128)(2,1)} %get-tuple-element.82) | copy-start | bytes 3342340
  34.8 11.4 %copy-start.3 = (bf16[128,2176]{1,0:T(8,128)(2,1)S(1)}, bf16[128,2176]{1,0:T(8,128)(2,1)}, u32[]{:S(2)}) copy-start(bf16[128,2176]{1,0:T(8,128)(2,1)} %get-tuple-element.81) | copy-start | bytes 1671172
  36.9 6.8 %collective-permute-start.30 = (bf16[16,2176]{1,0:T(8,128)(2,1)S(1)}, bf16[16,2176]{1,0:T(8,128)(2,1)S(1)}, u32[]{:S(2)}, u32[]{:S(2)}) collective-permute-start(bf16[16,2176]{1,0:T(8,128)(2,1)S(1)} %get-tuple-element.10), channel_id=1, source_target_pairs={{0,4},{4,8},{8,12},{12,0},{1,5},{5,9},{9,13},{13,1},{2,6},{6,10},{... | collective-permute-start | bytes 208904 | tf_op jit(solution)/shard_map/ppermute | solution.py:65
  38.4 7.1 %collective-permute-start.31 = (bf16[16,2176]{1,0:T(8,128)(2,1)S(1)}, bf16[16,2176]{1,0:T(8,128)(2,1)S(1)}, u32[]{:S(2)}, u32[]{:S(2)}) collective-permute-start(bf16[16,2176]{1,0:T(8,128)(2,1)S(1)} %get-tuple-element.10), channel_id=1, source_target_pairs={{0,8},{4,12},{8,0},{12,4},{1,9},{5,13},{9,1},{13,5},{2,10},{6,14},... | collective-permute-start | bytes 208904 | tf_op jit(solution)/shard_map/ppermute | solution.py:65
  39.8 5.8 %collective-permute-start.32 = (bf16[16,2176]{1,0:T(8,128)(2,1)S(1)}, bf16[16,2176]{1,0:T(8,128)(2,1)S(1)}, u32[]{:S(2)}, u32[]{:S(2)}) collective-permute-start(bf16[16,2176]{1,0:T(8,128)(2,1)S(1)} %get-tuple-element.10), channel_id=1, source_target_pairs={{0,12},{4,0},{8,4},{12,8},{1,13},{5,1},{9,5},{13,9},{2,14},{6,2},{... | collective-permute-start | bytes 208904 | tf_op jit(solution)/shard_map/ppermute | solution.py:65
  43.7 8.4 %collective-permute-start.23 = (bf16[64,2176]{1,0:T(8,128)(2,1)S(1)}, bf16[64,2176]{1,0:T(8,128)(2,1)S(1)}, u32[]{:S(2)}, u32[]{:S(2)}) collective-permute-start(bf16[64,2176]{1,0:T(8,128)(2,1)S(1)} %get-tuple-element.59), channel_id=1, source_target_pairs={{0,2},{2,0},{1,3},{3,1},{4,6},{6,4},{5,7},{7,5},{8,10},{10,8},{9,1... | collective-permute-start | bytes 835592 | tf_op jit(solution)/shard_map/ppermute | solution.py:65
  45.6 9.5 %collective-permute-start.33 = (bf16[64,2176]{1,0:T(8,128)(2,1)S(1)}, bf16[64,2176]{1,0:T(8,128)(2,1)S(1)}, u32[]{:S(2)}, u32[]{:S(2)}) collective-permute-start(bf16[64,2176]{1,0:T(8,128)(2,1)S(1)} %pad_maximum_fusion.1), channel_id=1, source_target_pairs={{0,2},{2,0},{1,3},{3,1},{4,6},{6,4},{5,7},{7,5},{8,10},{10,8},{9,1... | collective-permute-start | bytes 835592 | tf_op jit(solution)/shard_map/ppermute | solution.py:65
  46.2 9.1 %collective-permute-start.4 = (bf16[128,2176]{1,0:T(8,128)(2,1)S(1)}, bf16[128,2176]{1,0:T(8,128)(2,1)S(1)}, u32[]{:S(2)}, u32[]{:S(2)}) collective-permute-start(bf16[128,2176]{1,0:T(8,128)(2,1)S(1)} %get-tuple-element.35), channel_id=1, source_target_pairs={{0,1},{1,0},{2,3},{3,2},{4,5},{5,4},{6,7},{7,6},{8,9},{9,8},{10,11... | collective-permute-start | bytes 1671176 | tf_op jit(solution)/shard_map/ppermute | solution.py:65
  46.3 13.8 %collective-permute-start.14 = (bf16[128,2176]{1,0:T(8,128)(2,1)S(1)}, bf16[128,2176]{1,0:T(8,128)(2,1)S(1)}, u32[]{:S(2)}, u32[]{:S(2)}) collective-permute-start(bf16[128,2176]{1,0:T(8,128)(2,1)S(1)} %get-tuple-element.33), channel_id=1, source_target_pairs={{0,1},{1,0},{2,3},{3,2},{4,5},{5,4},{6,7},{7,6},{8,9},{9,8},{10,11... | collective-permute-start | bytes 1671176 | tf_op jit(solution)/shard_map/ppermute | solution.py:65
  52.2 9.9 %collective-permute-start.24 = (bf16[128,2176]{1,0:T(8,128)(2,1)S(1)}, bf16[128,2176]{1,0:T(8,128)(2,1)S(1)}, u32[]{:S(2)}, u32[]{:S(2)}) collective-permute-start(bf16[128,2176]{1,0:T(8,128)(2,1)S(1)} %get-tuple-element.31), channel_id=1, source_target_pairs={{0,1},{1,0},{2,3},{3,2},{4,5},{5,4},{6,7},{7,6},{8,9},{9,8},{10,11... | collective-permute-start | bytes 1671176 | tf_op jit(solution)/shard_map/ppermute | solution.py:65
  55.1 8.8 %collective-permute-start.34 = (bf16[128,2176]{1,0:T(8,128)(2,1)S(1)}, bf16[128,2176]{1,0:T(8,128)(2,1)S(1)}, u32[]{:S(2)}, u32[]{:S(2)}) collective-permute-start(bf16[128,2176]{1,0:T(8,128)(2,1)S(1)} %get-tuple-element.23), channel_id=1, source_target_pairs={{0,1},{1,0},{2,3},{3,2},{4,5},{5,4},{6,7},{7,6},{8,9},{9,8},{10,11... | collective-permute-start | bytes 1671176 | tf_op jit(solution)/shard_map/ppermute | solution.py:65
  55.3 4.9 %slice-start = ((s8[6291456]{0:T(1024)(128)(4,1)}), s8[4194304]{0:T(1024)(128)(4,1)S(1)}, s32[]{:S(2)}) async-start(s8[6291456]{0:T(1024)(128)(4,1)} %bitcast.42), calls=%async_computation | async-start | bytes 8388608
  55.3 4.8 %slice-start.1 = ((s8[6291456]{0:T(1024)(128)(4,1)}), s8[2097152]{0:T(1024)(128)(4,1)S(1)}, s32[]{:S(2)}) async-start(s8[6291456]{0:T(1024)(128)(4,1)} %bitcast.42), calls=%async_computation.1 | async-start | bytes 4194304
  67.5 4.7 %collective-permute-start.35 = (bf16[128,2048]{1,0:T(8,128)(2,1)S(1)}, bf16[128,2048]{1,0:T(8,128)(2,1)S(1)}, u32[]{:S(2)}, u32[]{:S(2)}) collective-permute-start(bf16[128,2048]{1,0:T(8,128)(2,1)S(1)} %split.246), channel_id=1, source_target_pairs={{0,1},{1,0},{2,3},{3,2},{4,5},{5,4},{6,7},{7,6},{8,9},{9,8},{10,11... | collective-permute-start | bytes 1572872 | tf_op jit(solution)/shard_map/ppermute | solution.py:74
  69.2 3.5 %collective-permute-start.25 = (bf16[128,2048]{1,0:T(8,128)(2,1)S(1)}, bf16[128,2048]{1,0:T(8,128)(2,1)S(1)}, u32[]{:S(2)}, u32[]{:S(2)}) collective-permute-start(bf16[128,2048]{1,0:T(8,128)(2,1)S(1)} %split.247), channel_id=1, source_target_pairs={{0,1},{1,0},{2,3},{3,2},{4,5},{5,4},{6,7},{7,6},{8,9},{9,8},{10,11... | collective-permute-start | bytes 1572872 | tf_op jit(solution)/shard_map/ppermute | solution.py:74
  70.4 4.3 %collective-permute-start.15 = (bf16[128,2048]{1,0:T(8,128)(2,1)S(1)}, bf16[128,2048]{1,0:T(8,128)(2,1)S(1)}, u32[]{:S(2)}, u32[]{:S(2)}) collective-permute-start(bf16[128,2048]{1,0:T(8,128)(2,1)S(1)} %split.248), channel_id=1, source_target_pairs={{0,1},{1,0},{2,3},{3,2},{4,5},{5,4},{6,7},{7,6},{8,9},{9,8},{10,11... | collective-permute-start | bytes 1572872 | tf_op jit(solution)/shard_map/ppermute | solution.py:74
  72.1 3.1 %collective-permute-start.5 = (bf16[128,2048]{1,0:T(8,128)(2,1)S(1)}, bf16[128,2048]{1,0:T(8,128)(2,1)S(1)}, u32[]{:S(2)}, u32[]{:S(2)}) collective-permute-start(bf16[128,2048]{1,0:T(8,128)(2,1)S(1)} %split.249), channel_id=1, source_target_pairs={{0,1},{1,0},{2,3},{3,2},{4,5},{5,4},{6,7},{7,6},{8,9},{9,8},{10,11... | collective-permute-start | bytes 1572872 | tf_op jit(solution)/shard_map/ppermute | solution.py:74
  72.4 9.2 %collective-permute-start.36 = (bf16[64,2048]{1,0:T(8,128)(2,1)S(1)}, bf16[64,2048]{1,0:T(8,128)(2,1)S(1)}, u32[]{:S(2)}, u32[]{:S(2)}) collective-permute-start(bf16[64,2048]{1,0:T(8,128)(2,1)S(1)} %split.250), channel_id=1, source_target_pairs={{0,2},{2,0},{1,3},{3,1},{4,6},{6,4},{5,7},{7,5},{8,10},{10,8},{9,1... | collective-permute-start | bytes 786440 | tf_op jit(solution)/shard_map/ppermute | solution.py:74
  72.9 14.4 %collective-permute-start.26 = (bf16[64,2048]{1,0:T(8,128)(2,1)S(1)}, bf16[64,2048]{1,0:T(8,128)(2,1)S(1)}, u32[]{:S(2)}, u32[]{:S(2)}) collective-permute-start(bf16[64,2048]{1,0:T(8,128)(2,1)S(1)} %split.251), channel_id=1, source_target_pairs={{0,2},{2,0},{1,3},{3,1},{4,6},{6,4},{5,7},{7,5},{8,10},{10,8},{9,1... | collective-permute-start | bytes 786440 | tf_op jit(solution)/shard_map/ppermute | solution.py:74
  74.8 18.0 %collective-permute-start.16 = (bf16[64,2048]{1,0:T(8,128)(2,1)S(1)}, bf16[64,2048]{1,0:T(8,128)(2,1)S(1)}, u32[]{:S(2)}, u32[]{:S(2)}) collective-permute-start(bf16[64,2048]{1,0:T(8,128)(2,1)S(1)} %split.252), channel_id=1, source_target_pairs={{0,2},{2,0},{1,3},{3,1},{4,6},{6,4},{5,7},{7,5},{8,10},{10,8},{9,1... | collective-permute-start | bytes 786440 | tf_op jit(solution)/shard_map/ppermute | solution.py:74
  75.3 22.6 %collective-permute-start.6 = (bf16[64,2048]{1,0:T(8,128)(2,1)S(1)}, bf16[64,2048]{1,0:T(8,128)(2,1)S(1)}, u32[]{:S(2)}, u32[]{:S(2)}) collective-permute-start(bf16[64,2048]{1,0:T(8,128)(2,1)S(1)} %split.253), channel_id=1, source_target_pairs={{0,2},{2,0},{1,3},{3,1},{4,6},{6,4},{5,7},{7,5},{8,10},{10,8},{9,1... | collective-permute-start | bytes 786440 | tf_op jit(solution)/shard_map/ppermute | solution.py:74
  81.7 17.2 %collective-permute-start.39 = (bf16[16,2048]{1,0:T(8,128)(2,1)S(1)}, bf16[16,2048]{1,0:T(8,128)(2,1)S(1)}, u32[]{:S(2)}, u32[]{:S(2)}) collective-permute-start(bf16[16,2048]{1,0:T(8,128)(2,1)S(1)} %get-tuple-element.47), channel_id=1, source_target_pairs={{0,4},{4,8},{8,12},{12,0},{1,5},{5,9},{9,13},{13,1},{2,6},{6,10},{... | collective-permute-start | bytes 196616 | tf_op jit(solution)/shard_map/ppermute | solution.py:74
  82.4 18.8 %collective-permute-start.38 = (bf16[16,2048]{1,0:T(8,128)(2,1)S(1)}, bf16[16,2048]{1,0:T(8,128)(2,1)S(1)}, u32[]{:S(2)}, u32[]{:S(2)}) collective-permute-start(bf16[16,2048]{1,0:T(8,128)(2,1)S(1)} %get-tuple-element.48), channel_id=1, source_target_pairs={{0,8},{4,12},{8,0},{12,4},{1,9},{5,13},{9,1},{13,5},{2,10},{6,14},... | collective-permute-start | bytes 196616 | tf_op jit(solution)/shard_map/ppermute | solution.py:74
  87.2 13.9 %collective-permute-start.37 = (bf16[16,2048]{1,0:T(8,128)(2,1)S(1)}, bf16[16,2048]{1,0:T(8,128)(2,1)S(1)}, u32[]{:S(2)}, u32[]{:S(2)}) collective-permute-start(bf16[16,2048]{1,0:T(8,128)(2,1)S(1)} %get-tuple-element.46), channel_id=1, source_target_pairs={{0,12},{4,0},{8,4},{12,8},{1,13},{5,1},{9,5},{13,9},{2,14},{6,2},{... | collective-permute-start | bytes 196616 | tf_op jit(solution)/shard_map/ppermute | solution.py:74
  92.8 10.3 %collective-permute-start.29 = (bf16[16,2048]{1,0:T(8,128)(2,1)S(1)}, bf16[16,2048]{1,0:T(8,128)(2,1)S(1)}, u32[]{:S(2)}, u32[]{:S(2)}) collective-permute-start(bf16[16,2048]{1,0:T(8,128)(2,1)S(1)} %get-tuple-element.44), channel_id=1, source_target_pairs={{0,4},{4,8},{8,12},{12,0},{1,5},{5,9},{9,13},{13,1},{2,6},{6,10},{... | collective-permute-start | bytes 196616 | tf_op jit(solution)/shard_map/ppermute | solution.py:74
  98.0 7.1 %collective-permute-start.28 = (bf16[16,2048]{1,0:T(8,128)(2,1)S(1)}, bf16[16,2048]{1,0:T(8,128)(2,1)S(1)}, u32[]{:S(2)}, u32[]{:S(2)}) collective-permute-start(bf16[16,2048]{1,0:T(8,128)(2,1)S(1)} %get-tuple-element.45), channel_id=1, source_target_pairs={{0,8},{4,12},{8,0},{12,4},{1,9},{5,13},{9,1},{13,5},{2,10},{6,14},... | collective-permute-start | bytes 196616 | tf_op jit(solution)/shard_map/ppermute | solution.py:74
  98.9 6.8 %collective-permute-start.27 = (bf16[16,2048]{1,0:T(8,128)(2,1)S(1)}, bf16[16,2048]{1,0:T(8,128)(2,1)S(1)}, u32[]{:S(2)}, u32[]{:S(2)}) collective-permute-start(bf16[16,2048]{1,0:T(8,128)(2,1)S(1)} %get-tuple-element.43), channel_id=1, source_target_pairs={{0,12},{4,0},{8,4},{12,8},{1,13},{5,1},{9,5},{13,9},{2,14},{6,2},{... | collective-permute-start | bytes 196616 | tf_op jit(solution)/shard_map/ppermute | solution.py:74
  101.2 7.5 %collective-permute-start.19 = (bf16[16,2048]{1,0:T(8,128)(2,1)S(1)}, bf16[16,2048]{1,0:T(8,128)(2,1)S(1)}, u32[]{:S(2)}, u32[]{:S(2)}) collective-permute-start(bf16[16,2048]{1,0:T(8,128)(2,1)S(1)} %get-tuple-element.41), channel_id=1, source_target_pairs={{0,4},{4,8},{8,12},{12,0},{1,5},{5,9},{9,13},{13,1},{2,6},{6,10},{... | collective-permute-start | bytes 196616 | tf_op jit(solution)/shard_map/ppermute | solution.py:74
  101.2 11.4 %collective-permute-start.18 = (bf16[16,2048]{1,0:T(8,128)(2,1)S(1)}, bf16[16,2048]{1,0:T(8,128)(2,1)S(1)}, u32[]{:S(2)}, u32[]{:S(2)}) collective-permute-start(bf16[16,2048]{1,0:T(8,128)(2,1)S(1)} %get-tuple-element.42), channel_id=1, source_target_pairs={{0,8},{4,12},{8,0},{12,4},{1,9},{5,13},{9,1},{13,5},{2,10},{6,14},... | collective-permute-start | bytes 196616 | tf_op jit(solution)/shard_map/ppermute | solution.py:74
  103.2 9.4 %collective-permute-start.17 = (bf16[16,2048]{1,0:T(8,128)(2,1)S(1)}, bf16[16,2048]{1,0:T(8,128)(2,1)S(1)}, u32[]{:S(2)}, u32[]{:S(2)}) collective-permute-start(bf16[16,2048]{1,0:T(8,128)(2,1)S(1)} %get-tuple-element.40), channel_id=1, source_target_pairs={{0,12},{4,0},{8,4},{12,8},{1,13},{5,1},{9,5},{13,9},{2,14},{6,2},{... | collective-permute-start | bytes 196616 | tf_op jit(solution)/shard_map/ppermute | solution.py:74
  105.1 7.5 %collective-permute-start.9 = (bf16[16,2048]{1,0:T(8,128)(2,1)S(1)}, bf16[16,2048]{1,0:T(8,128)(2,1)S(1)}, u32[]{:S(2)}, u32[]{:S(2)}) collective-permute-start(bf16[16,2048]{1,0:T(8,128)(2,1)S(1)} %get-tuple-element.38), channel_id=1, source_target_pairs={{0,4},{4,8},{8,12},{12,0},{1,5},{5,9},{9,13},{13,1},{2,6},{6,10},{... | collective-permute-start | bytes 196616 | tf_op jit(solution)/shard_map/ppermute | solution.py:74
  105.7 10.1 %collective-permute-start.8 = (bf16[16,2048]{1,0:T(8,128)(2,1)S(1)}, bf16[16,2048]{1,0:T(8,128)(2,1)S(1)}, u32[]{:S(2)}, u32[]{:S(2)}) collective-permute-start(bf16[16,2048]{1,0:T(8,128)(2,1)S(1)} %get-tuple-element.39), channel_id=1, source_target_pairs={{0,8},{4,12},{8,0},{12,4},{1,9},{5,13},{9,1},{13,5},{2,10},{6,14},... | collective-permute-start | bytes 196616 | tf_op jit(solution)/shard_map/ppermute | solution.py:74
  108.6 7.2 %collective-permute-start.7 = (bf16[16,2048]{1,0:T(8,128)(2,1)S(1)}, bf16[16,2048]{1,0:T(8,128)(2,1)S(1)}, u32[]{:S(2)}, u32[]{:S(2)}) collective-permute-start(bf16[16,2048]{1,0:T(8,128)(2,1)S(1)} %get-tuple-element.37), channel_id=1, source_target_pairs={{0,12},{4,0},{8,4},{12,8},{1,13},{5,1},{9,5},{13,9},{2,14},{6,2},{... | collective-permute-start | bytes 196616 | tf_op jit(solution)/shard_map/ppermute | solution.py:74

commit v7 on v5

--- a/solution.py
+++ b/solution.py
@@ -59,6 +59,9 @@
 
 
 def gather_stage(block, axis, size):
+    if size > 2:
+        spread = jnp.broadcast_to(block[None], (size,) + block.shape)
+        return lax.all_to_all(spread, axis, 0, 0, tiled=True).reshape((-1,) + block.shape[1:])
     got = [block]
     for shift in range(1, size):
         pairs = [(i, (i + shift) % size) for i in range(size)]
@@ -67,6 +70,10 @@
 
 
 def scatter_stage(part, axis, size):
+    if size > 2:
+        sent = part.astype(jnp.bfloat16).reshape((size, -1) + part.shape[1:])
+        back = lax.all_to_all(sent, axis, 0, 0, tiled=True)
+        return jnp.sum(back.astype(jnp.float32), axis=0)
     pieces = jnp.split(part, size, axis=0)
     total = pieces[0].astype(jnp.float32)
     for shift in range(1, size):

time: 106 us -> 141 us (1.33)
  blocking collectives: 0 us -> 21.6 us
  waiting for transfers between devices: 48.5 us -> 62.8 us
  starting transfers between devices: 29.1 us -> 16.3 us
  other arithmetic: 6.12 us -> 17.5 us
  local copies, waits for them, and re-layouts: 10.8 us -> 8.46 us
  matrix products: 10.6 us -> 12.9 us
    all_to_all x0 -> x3, waiting for transfers between devices: none -> 23.8 us  [the longest x2 19.1 us: scatter_stage(): back = lax.all_to_all(sent, axis, 0, 0, tiled=True)]
    all_to_all x0 -> x1, blocking collectives: none -> 21.6 us  [gather_stage(): lax.all_to_all(spread, axis, 0, 0, tiled=True)]
    ppermute x10 -> x4, starting transfers between devices: 15.2 us -> 2.1 us  [gather_stage(): got.append(lax.ppermute(block, axis, pairs))]
    all_to_all x0 -> x3, starting transfers between devices: none -> 12.4 us  [the longest x2 8.28 us: scatter_stage(): back = lax.all_to_all(sent, axis, 0, 0, tiled=True)]
    ppermute x10 -> x4, starting transfers between devices: 13.9 us -> 1.77 us  [scatter_stage(): lax.ppermute(pieces[shift].astype(jnp.bfloat16), axis, pairs)]
    ppermute x10 -> x4, waiting for transfers between devices: 25 us -> 18.2 us  [scatter_stage(): lax.ppermute(pieces[shift].astype(jnp.bfloat16), axis, pairs)]
    concatenate x2 -> x4, other arithmetic: 1.27 us -> 6.53 us  [gather_stage(): return jnp.concatenate(got, axis=0)]
    unnamed x13 -> x14, local copies, waits for them, and re-layouts: 5 us -> 0.04 us
  transfers between devices with their start and end apart: 20 -> 11, of which waited for: 10 -> 8; matrix products, arithmetic and copies ran while one was open for 12% -> 20% of each run, Pallas kernels for 0% -> 0%
where the time goes in v7:
time: 141 us; the launch traced here: 140 us
  waiting for transfers between devices  62.8 us (45%)
  blocking collectives  21.6 us (15%)
  other arithmetic  17.5 us (12%)
  starting transfers between devices  16.3 us (12%)
  matrix products  12.9 us (9%)
  local copies, waits for them, and re-layouts  8.46 us (6%)
    all_to_all x1, blocking collectives, gather_stage(): lax.all_to_all(spread, axis, 0, 0, tiled=True)  21.6 us
    ppermute x4, waiting for transfers between devices, gather_stage(): got.append(lax.ppermute(block, axis, pairs))  20.8 us
    all_to_all x2, waiting for transfers between devices, scatter_stage(): back = lax.all_to_all(sent, axis, 0, 0, tiled=True)  19.1 us
    ppermute x4, waiting for transfers between devices, scatter_stage(): lax.ppermute(pieces[shift].astype(jnp.bfloat16), axis, pairs)  18.2 us
    dot_general x2, matrix products, expert_block(): pair = jnp.dot(rows_in, gate_up, preferred_element_type=jnp.float32)  9.23 us
    all_to_all x2, starting transfers between devices, scatter_stage(): back = lax.all_to_all(sent, axis, 0, 0, tiled=True)  8.28 us
    concatenate x4, other arithmetic, gather_stage(): return jnp.concatenate(got, axis=0)  6.53 us
    all_to_all x1, waiting for transfers between devices, gather_stage(): lax.all_to_all(spread, axis, 0, 0, tiled=True)  4.72 us
  transfers between devices with their start and end apart: 11, of which 8 were waited for; matrix products, arithmetic and copies ran while one was open for 20% of the time, Pallas kernels for 0%

profile of v7, /device:TPU:0, one launch (start us, length us, event | category | flops | bytes accessed | tf_op | source)
XLA Modules:
  0.0 139.8 jit_solution(10143043813361077476)
XLA Ops:
  0.0 0.9 reduce_sum.54
  0.9 0.8 broadcast_divide_fusion
  1.7 0.8 select_reduce_fusion
  2.4 0.1 copy.19
  2.5 0.1 copy.20
  2.6 0.1 copy.21
  2.8 1.1 concatenate.24
  3.8 0.7 fusion.35
  4.5 21.6 %all_to_all.20 = bf16[4,32,2176]{2,1,0:T(8,128)(2,1)} all-to-all(bf16[4,32,2176]{2,1,0:T(8,128)(2,1)S(1)} %broadcast_in_dim.21), channel_id=1, replica_groups=mesh['groups'=2,'ez'=4,'ex'=2,'ec'=2] {'ez'}, dimensions={0} | all-to-all | bytes 1114112 | tf_op jit(solution)/shard_map/all_to_all | solution.py:64
  26.1 2.1 %copy.24 = bf16[128,2176]{0,1:T(8,128)(2,1)} copy(bf16[128,2176]{1,0:T(8,128)(2,1)} %bitcast.22) | data formatting | bytes 1114112 | tf_op jit(solution)/shard_map/reshape | solution.py:64
  28.2 1.5 %collective-permute-start = (bf16[128,2176]{0,1:T(8,128)(2,1)}, bf16[128,2176]{0,1:T(8,128)(2,1)}, u32[]{:S(2)}, u32[]{:S(2)}) collective-permute-start(bf16[128,2176]{0,1:T(8,128)(2,1)} %copy.24), channel_id=1, source_target_pairs={{0,2},{2,0},{1,3},{3,1},{4,6},{6,4},{5,7},{7,5},{8,10},{10,8},{9,1... | collective-permute-start | bytes 1671176 | tf_op jit(solution)/shard_map/ppermute | solution.py:68
  29.7 0.8 broadcast_in_dim.22
  30.6 4.2 %all-to-all-start.2 = ((bf16[4,32,2176]{2,1,0:T(8,128)(2,1)}), bf16[4,32,2176]{2,1,0:T(8,128)(2,1)}, u32[]{:S(2)}, u32[]{:S(2)}) async-start(bf16[4,32,2176]{2,1,0:T(8,128)(2,1)} %broadcast_in_dim.22), calls=%async_computation.2 | async-start | bytes 1114112 | tf_op jit(solution)/shard_map/all_to_all | solution.py:64
  34.7 7.4 %collective-permute-done = bf16[128,2176]{0,1:T(8,128)(2,1)} collective-permute-done((bf16[128,2176]{0,1:T(8,128)(2,1)}, bf16[128,2176]{0,1:T(8,128)(2,1)}, u32[]{:S(2)}, u32[]{:S(2)}) %collective-permute-start) | collective-permute-done | bytes 557088 | tf_op jit(solution)/shard_map/ppermute | solution.py:68
  42.1 2.4 %pad_maximum_fusion.2 = bf16[256,2176]{0,1:T(8,128)(2,1)} fusion(bf16[128,2176]{0,1:T(8,128)(2,1)} %collective-permute-done, bf16[128,2176]{0,1:T(8,128)(2,1)} %copy.24), kind=kLoop, calls=%fused_computation.24 | loop fusion | flops 2228224 | bytes 2228224 | tf_op jit(solution)/shard_map/concatenate | solution.py:69
  44.5 4.7 %all-to-all-done.2 = bf16[4,32,2176]{2,1,0:T(8,128)(2,1)} async-done(((bf16[4,32,2176]{2,1,0:T(8,128)(2,1)}), bf16[4,32,2176]{2,1,0:T(8,128)(2,1)}, u32[]{:S(2)}, u32[]{:S(2)}) %all-to-all-start.2) | async-done | bytes 557088 | tf_op jit(solution)/shard_map/all_to_all | solution.py:64
  49.2 2.1 %copy.27 = bf16[128,2176]{0,1:T(8,128)(2,1)} copy(bf16[128,2176]{1,0:T(8,128)(2,1)} %bitcast.4) | data formatting | bytes 1114112 | tf_op jit(solution)/shard_map/reshape | solution.py:64
  51.3 0.5 collective-permute-start.4
  51.8 13.4 %collective-permute-done.4 = bf16[128,2176]{0,1:T(8,128)(2,1)} collective-permute-done((bf16[128,2176]{0,1:T(8,128)(2,1)}, bf16[128,2176]{0,1:T(8,128)(2,1)}, u32[]{:S(2)}, u32[]{:S(2)}) %collective-permute-start.4) | collective-permute-done | bytes 557088 | tf_op jit(solution)/shard_map/ppermute | solution.py:68
  65.3 1.3 pad_maximum_fusion.3
  66.7 1.6 %pad_maximum_fusion = bf16[512,2176]{0,1:T(8,128)(2,1)S(1)} fusion(bf16[256,2176]{0,1:T(8,128)(2,1)} %collective-permute-done.1, bf16[128,2176]{0,1:T(8,128)(2,1)} %collective-permute-done, bf16[128,2176]{0,1:T(8,128)(2,1)S(1)} %copy-done.1), kind=kLoop, calls=%fused_computation.12 | loop fusion | flops 6684672 | bytes 4456448 | tf_op jit(solution)/shard_map/concatenate | solution.py:69
  68.3 0.8 maximum_convert_fusion.1
  69.1 5.7 %fusion.2 = f32[512,1536]{1,0:T(8,128)S(1)} fusion(bf16[1,2048,1536]{2,1,0:T(8,128)(2,1)} %param.10, bf16[512,2176]{0,1:T(8,128)(2,1)S(1)} %pad_maximum_fusion), kind=kOutput, calls=%fused_computation.2 | convolution fusion | flops 3221225472 | bytes 11534336 | tf_op jit(solution)/shard_map/dot_general | solution.py:9
  74.8 0.9 maximum_convert_fusion
  75.8 1.9 %convert_multiply_fusion.1 = f32[512,2048]{1,0:T(8,128)S(1)} fusion(bf16[1,768,2048]{2,1,0:T(8,128)(2,1)S(1)} %copy-done, f32[512]{0:T(512)S(1)} %get-tuple-element.7, f32[512,1536]{1,0:T(8,128)S(1)} %fusion.2), kind=kOutput, calls=%fused_computation.5 | convolution fusion | flops 1616117760 | bytes 10487808 | tf_op jit(solution)/shard_map/dot_general | solution.py:11
  77.6 0.1 split.67
  77.8 0.5 collective-permute-start.2
  78.3 1.3 pad_maximum_fusion.1
  79.6 3.5 %fusion = f32[512,1536]{1,0:T(8,128)S(1)} fusion(bf16[1,2048,1536]{2,1,0:T(8,128)(2,1)S(1)} %bitcast.26, bf16[512,2176]{0,1:T(8,128)(2,1)S(1)} %pad_maximum_fusion.1), kind=kOutput, calls=%fused_computation | convolution fusion | flops 3221225472 | bytes 11534336 | tf_op jit(solution)/shard_map/dot_general | solution.py:9
  83.2 1.8 %convert_multiply_fusion = f32[512,2048]{1,0:T(8,128)S(1)} fusion(bf16[1,768,2048]{2,1,0:T(8,128)(2,1)S(1)} %copy-done, f32[512]{0:T(512)S(1)} %get-tuple-element.8, f32[512,1536]{1,0:T(8,128)S(1)} %fusion), kind=kOutput, calls=%fused_computation.4 | convolution fusion | flops 1616117760 | bytes 10487808 | tf_op jit(solution)/shard_map/dot_general | solution.py:11
  85.0 0.1 split.66
  85.3 0.3 slice_add_fusion.1
  85.7 0.6 collective-permute-start.3
  86.3 1.6 %collective-permute-done.6 = bf16[256,2048]{1,0:T(8,128)(2,1)S(1)} collective-permute-done((bf16[256,2048]{1,0:T(8,128)(2,1)S(1)}, bf16[256,2048]{1,0:T(8,128)(2,1)S(1)}, u32[]{:S(2)}, u32[]{:S(2)}) %collective-permute-start.6) | collective-permute-done | bytes 1048608 | tf_op jit(solution)/shard_map/ppermute | solution.py:81
  87.9 0.3 slice_add_fusion
  88.2 1.0 split.68
  89.2 0.5 collective-permute-start.7
  89.7 10.8 %collective-permute-done.3 = bf16[128,2048]{1,0:T(8,128)(2,1)S(1)} collective-permute-done((bf16[128,2048]{1,0:T(8,128)(2,1)S(1)}, bf16[128,2048]{1,0:T(8,128)(2,1)S(1)}, u32[]{:S(2)}, u32[]{:S(2)}) %collective-permute-start.3) | collective-permute-done | bytes 524320 | tf_op jit(solution)/shard_map/ppermute | solution.py:81
  100.5 0.9 fusion.23
  101.5 4.1 %all-to-all-start.1 = ((bf16[4,32,2048]{2,1,0:T(8,128)(2,1)}), bf16[4,32,2048]{2,1,0:T(8,128)(2,1)}, u32[]{:S(2)}, u32[]{:S(2)}) async-start(bf16[4,32,2048]{2,1,0:T(8,128)(2,1)} %bitcast.23), calls=%async_computation.1 | async-start | bytes 1048576 | tf_op jit(solution)/shard_map/all_to_all | solution.py:75
  105.6 5.8 %collective-permute-done.7 = bf16[128,2048]{1,0:T(8,128)(2,1)} collective-permute-done((bf16[128,2048]{1,0:T(8,128)(2,1)}, bf16[128,2048]{1,0:T(8,128)(2,1)}, u32[]{:S(2)}, u32[]{:S(2)}) %collective-permute-start.7) | collective-permute-done | bytes 524320 | tf_op jit(solution)/shard_map/ppermute | solution.py:81
  111.4 2.3 %fusion.22 = bf16[128,2048]{1,0:T(8,128)(2,1)} fusion(f32[256,2048]{1,0:T(8,128)} %copy-done.3, bf16[128,2048]{1,0:T(8,128)(2,1)} %collective-permute-done.7), kind=kLoop, calls=%fused_computation.28 | loop fusion | flops 786432 | bytes 2097152 | tf_op jit(solution)/shard_map/convert_element_type | solution.py:74
  113.7 6.1 %all-to-all-done.1 = bf16[4,32,2048]{2,1,0:T(8,128)(2,1)} async-done(((bf16[4,32,2048]{2,1,0:T(8,128)(2,1)}), bf16[4,32,2048]{2,1,0:T(8,128)(2,1)}, u32[]{:S(2)}, u32[]{:S(2)}) %all-to-all-start.1) | async-done | bytes 524320 | tf_op jit(solution)/shard_map/all_to_all | solution.py:75
  119.7 4.1 %all-to-all-start.3 = ((bf16[4,32,2048]{2,1,0:T(8,128)(2,1)}), bf16[4,32,2048]{2,1,0:T(8,128)(2,1)}, u32[]{:S(2)}, u32[]{:S(2)}) async-start(bf16[4,32,2048]{2,1,0:T(8,128)(2,1)} %bitcast.24), calls=%async_computation.3 | async-start | bytes 1048576 | tf_op jit(solution)/shard_map/all_to_all | solution.py:75
  123.9 1.1 reduce
  125.0 13.0 %all-to-all-done.3 = bf16[4,32,2048]{2,1,0:T(8,128)(2,1)} async-done(((bf16[4,32,2048]{2,1,0:T(8,128)(2,1)}), bf16[4,32,2048]{2,1,0:T(8,128)(2,1)}, u32[]{:S(2)}, u32[]{:S(2)}) %all-to-all-start.3) | async-done | bytes 524320 | tf_op jit(solution)/shard_map/all_to_all | solution.py:75
  138.0 1.1 reduce.1
  139.1 0.7 pad_maximum_fusion.4
  (27 shorter events, 0.4 us)
Async XLA Ops:
  0.0 75.8 %copy-start = (bf16[1,768,2048]{2,1,0:T(8,128)(2,1)S(1)}, bf16[1,768,2048]{2,1,0:T(8,128)(2,1)}, u32[]{:S(2)}) copy-start(bf16[1,768,2048]{2,1,0:T(8,128)(2,1)} %param.11) | copy-start | bytes 9437188
  4.5 25.2 %copy-start.4 = (bf16[32,2176]{1,0:T(8,128)(2,1)S(1)}, bf16[32,2176]{1,0:T(8,128)(2,1)}, u32[]{:S(2)}) copy-start(bf16[32,2176]{1,0:T(8,128)(2,1)} %get-tuple-element.6) | copy-start | bytes 417796
  28.2 13.9 %collective-permute-start = (bf16[128,2176]{0,1:T(8,128)(2,1)}, bf16[128,2176]{0,1:T(8,128)(2,1)}, u32[]{:S(2)}, u32[]{:S(2)}) collective-permute-start(bf16[128,2176]{0,1:T(8,128)(2,1)} %copy.24), channel_id=1, source_target_pairs={{0,2},{2,0},{1,3},{3,1},{4,6},{6,4},{5,7},{7,5},{8,10},{10,8},{9,1... | collective-permute-start | bytes 1671176 | tf_op jit(solution)/shard_map/ppermute | solution.py:68
  30.6 18.6 %all-to-all-start.2 = ((bf16[4,32,2176]{2,1,0:T(8,128)(2,1)}), bf16[4,32,2176]{2,1,0:T(8,128)(2,1)}, u32[]{:S(2)}, u32[]{:S(2)}) async-start(bf16[4,32,2176]{2,1,0:T(8,128)(2,1)} %broadcast_in_dim.22), calls=%async_computation.2 | async-start | bytes 1114112 | tf_op jit(solution)/shard_map/all_to_all | solution.py:64
  44.5 22.2 %collective-permute-start.1 = (bf16[256,2176]{0,1:T(8,128)(2,1)}, bf16[256,2176]{0,1:T(8,128)(2,1)}, u32[]{:S(2)}, u32[]{:S(2)}) collective-permute-start(bf16[256,2176]{0,1:T(8,128)(2,1)} %pad_maximum_fusion.2), channel_id=1, source_target_pairs={{0,1},{1,0},{2,3},{3,2},{4,5},{5,4},{6,7},{7,6},{8,9},{9,8},{10,11... | collective-permute-start | bytes 3342344 | tf_op jit(solution)/shard_map/ppermute | solution.py:68
  51.3 14.0 %collective-permute-start.4 = (bf16[128,2176]{0,1:T(8,128)(2,1)}, bf16[128,2176]{0,1:T(8,128)(2,1)}, u32[]{:S(2)}, u32[]{:S(2)}) collective-permute-start(bf16[128,2176]{0,1:T(8,128)(2,1)} %copy.27), channel_id=1, source_target_pairs={{0,2},{2,0},{1,3},{3,1},{4,6},{6,4},{5,7},{7,5},{8,10},{10,8},{9,1... | collective-permute-start | bytes 1671176 | tf_op jit(solution)/shard_map/ppermute | solution.py:68
  51.8 14.9 %copy-start.1 = (bf16[128,2176]{0,1:T(8,128)(2,1)S(1)}, bf16[128,2176]{0,1:T(8,128)(2,1)}, u32[]{:S(2)}) copy-start(bf16[128,2176]{0,1:T(8,128)(2,1)} %copy.24) | copy-start | bytes 1671172
  66.6 8.2 %collective-permute-start.5 = (bf16[256,2176]{0,1:T(8,128)(2,1)S(1)}, bf16[256,2176]{0,1:T(8,128)(2,1)S(1)}, u32[]{:S(2)}, u32[]{:S(2)}) collective-permute-start(bf16[256,2176]{0,1:T(8,128)(2,1)S(1)} %pad_maximum_fusion.3), channel_id=1, source_target_pairs={{0,1},{1,0},{2,3},{3,2},{4,5},{5,4},{6,7},{7,6},{8,9},{9,8},{10,11... | collective-permute-start | bytes 3342344 | tf_op jit(solution)/shard_map/ppermute | solution.py:68
  69.0 5.7 %copy-start.2 = (bf16[128,2176]{0,1:T(8,128)(2,1)S(1)}, bf16[128,2176]{0,1:T(8,128)(2,1)}, u32[]{:S(2)}) copy-start(bf16[128,2176]{0,1:T(8,128)(2,1)} %copy.27) | copy-start | bytes 1671172
  74.8 4.8 %slice-start = ((s8[6291456]{0:T(1024)(128)(4,1)}), s8[4194304]{0:T(1024)(128)(4,1)S(1)}, s32[]{:S(2)}) async-start(s8[6291456]{0:T(1024)(128)(4,1)} %bitcast.25), calls=%async_computation.4 | async-start | bytes 8388608
  75.8 3.8 %slice-start.1 = ((s8[6291456]{0:T(1024)(128)(4,1)}), s8[2097152]{0:T(1024)(128)(4,1)S(1)}, s32[]{:S(2)}) async-start(s8[6291456]{0:T(1024)(128)(4,1)} %bitcast.25), calls=%async_computation.5 | async-start | bytes 4194304
  77.8 7.5 %collective-permute-start.2 = (bf16[256,2048]{1,0:T(8,128)(2,1)S(1)}, bf16[256,2048]{1,0:T(8,128)(2,1)S(1)}, u32[]{:S(2)}, u32[]{:S(2)}) collective-permute-start(bf16[256,2048]{1,0:T(8,128)(2,1)S(1)} %split.67), channel_id=1, source_target_pairs={{0,1},{1,0},{2,3},{3,2},{4,5},{5,4},{6,7},{7,6},{8,9},{9,8},{10,11... | collective-permute-start | bytes 3145736 | tf_op jit(solution)/shard_map/ppermute | solution.py:81
  85.2 2.7 %collective-permute-start.6 = (bf16[256,2048]{1,0:T(8,128)(2,1)S(1)}, bf16[256,2048]{1,0:T(8,128)(2,1)S(1)}, u32[]{:S(2)}, u32[]{:S(2)}) collective-permute-start(bf16[256,2048]{1,0:T(8,128)(2,1)S(1)} %split.66), channel_id=1, source_target_pairs={{0,1},{1,0},{2,3},{3,2},{4,5},{5,4},{6,7},{7,6},{8,9},{9,8},{10,11... | collective-permute-start | bytes 3145736 | tf_op jit(solution)/shard_map/ppermute | solution.py:81
  85.7 14.9 %collective-permute-start.3 = (bf16[128,2048]{1,0:T(8,128)(2,1)S(1)}, bf16[128,2048]{1,0:T(8,128)(2,1)S(1)}, u32[]{:S(2)}, u32[]{:S(2)}) collective-permute-start(bf16[128,2048]{1,0:T(8,128)(2,1)S(1)} %split.69), channel_id=1, source_target_pairs={{0,2},{2,0},{1,3},{3,1},{4,6},{6,4},{5,7},{7,5},{8,10},{10,8},{9,1... | collective-permute-start | bytes 1572872 | tf_op jit(solution)/shard_map/ppermute | solution.py:81
  88.2 13.2 %copy-start.3 = (f32[256,2048]{1,0:T(8,128)}, f32[256,2048]{1,0:T(8,128)S(1)}, u32[]{:S(2)}) copy-start(f32[256,2048]{1,0:T(8,128)S(1)} %slice_add_fusion) | copy-start | bytes 6291460
  89.2 22.2 %collective-permute-start.7 = (bf16[128,2048]{1,0:T(8,128)(2,1)}, bf16[128,2048]{1,0:T(8,128)(2,1)}, u32[]{:S(2)}, u32[]{:S(2)}) collective-permute-start(bf16[128,2048]{1,0:T(8,128)(2,1)} %split.68), channel_id=1, source_target_pairs={{0,2},{2,0},{1,3},{3,1},{4,6},{6,4},{5,7},{7,5},{8,10},{10,8},{9,1... | collective-permute-start | bytes 1572872 | tf_op jit(solution)/shard_map/ppermute | solution.py:81
  101.5 18.3 %all-to-all-start.1 = ((bf16[4,32,2048]{2,1,0:T(8,128)(2,1)}), bf16[4,32,2048]{2,1,0:T(8,128)(2,1)}, u32[]{:S(2)}, u32[]{:S(2)}) async-start(bf16[4,32,2048]{2,1,0:T(8,128)(2,1)} %bitcast.23), calls=%async_computation.1 | async-start | bytes 1048576 | tf_op jit(solution)/shard_map/all_to_all | solution.py:75
  119.7 18.2 %all-to-all-start.3 = ((bf16[4,32,2048]{2,1,0:T(8,128)(2,1)}), bf16[4,32,2048]{2,1,0:T(8,128)(2,1)}, u32[]{:S(2)}, u32[]{:S(2)}) async-start(bf16[4,32,2048]{2,1,0:T(8,128)(2,1)} %bitcast.24), calls=%async_computation.3 | async-start | bytes 1048576 | tf_op jit(solution)/shard_map/all_to_all | solution.py:75

commit v8 on v5

--- a/solution.py
+++ b/solution.py
@@ -97,16 +97,17 @@
     results = []
     held = None
     for rows in jnp.split(carried, STREAMS, axis=0):
-        if held is not None:
-            held, rows = lax.optimization_barrier((held, rows))
-        rows = gather_stage(rows, AXES[0], sizes[0])
-        held = rows
-        for axis, size in zip(AXES[1:], sizes[1:]):
+        done = []
+        for stage, (axis, size) in enumerate(zip(AXES, sizes)):
+            if held is not None:
+                _, rows = lax.optimization_barrier((held[(0, 2, 3)[stage]], rows))
             rows = gather_stage(rows, axis, size)
+            done.append(rows)
         tail = rows[:, width_model:width_model + 3 * hosts].astype(jnp.float32)
         gate = tail[:, :hosts] + tail[:, hosts:2 * hosts] + tail[:, 2 * hosts:]
         mine = jnp.sum(gate * pick[None, :], axis=1)
         out = expert_block(rows[:, :width_model], w_in[0], w_down[0], hidden_width)
+        held = done + [out]
         part = out.astype(jnp.float32) * mine[:, None]
         for axis, size in list(zip(AXES, sizes))[::-1]:
             part = scatter_stage(part, axis, size)

time: 106 us -> 122 us (1.15)
  waiting for transfers between devices: 48.5 us -> 71 us
  starting transfers between devices: 29.1 us -> 23.1 us
  local copies, waits for them, and re-layouts: 10.8 us -> 6.17 us
  matrix products: 10.6 us -> 14 us
    ppermute x10, waiting for transfers between devices: 23.5 us -> 41.5 us  [gather_stage(): got.append(lax.ppermute(block, axis, pairs))]
    ppermute x10, starting transfers between devices: 13.9 us -> 9.05 us  [scatter_stage(): lax.ppermute(pieces[shift].astype(jnp.bfloat16), axis, pairs)]
    ppermute x10, waiting for transfers between devices: 25 us -> 29.5 us  [scatter_stage(): lax.ppermute(pieces[shift].astype(jnp.bfloat16), axis, pairs)]
    unnamed x13 -> x12, local copies, waits for them, and re-layouts: 5 us -> 2.65 us
    dot_general x2, matrix products: 6.9 us -> 8.98 us  [expert_block(): pair = jnp.dot(rows_in, gate_up, preferred_element_type=jnp.float32)]
    split x1, local copies, waits for them, and re-layouts: 1.74 us -> 0.04 us  [dense_shards(): jnp.split(carried, STREAMS, axis=0)]
    dot_general x2, matrix products: 3.69 us -> 5.02 us  [expert_block(): jnp.dot(active, down_proj, preferred_element_type=jnp.float32)]
  transfers between devices with their start and end apart: 20 -> 20, of which waited for: 10 -> 13; matrix products, arithmetic and copies ran while one was open for 12% -> 9% of each run, Pallas kernels for 0% -> 0%
where the time goes in v8:
time: 122 us
  waiting for transfers between devices  71 us (58%)
  starting transfers between devices  23.1 us (19%)
  matrix products  14 us (11%)
  other arithmetic  7.29 us (6%)
  local copies, waits for them, and re-layouts  6.17 us (5%)
    ppermute x10, waiting for transfers between devices, gather_stage(): got.append(lax.ppermute(block, axis, pairs))  41.5 us
    ppermute x10, waiting for transfers between devices, scatter_stage(): lax.ppermute(pieces[shift].astype(jnp.bfloat16), axis, pairs)  29.5 us
    ppermute x10, starting transfers between devices, gather_stage(): got.append(lax.ppermute(block, axis, pairs))  14 us
    ppermute x10, starting transfers between devices, scatter_stage(): lax.ppermute(pieces[shift].astype(jnp.bfloat16), axis, pairs)  9.05 us
    dot_general x2, matrix products, expert_block(): pair = jnp.dot(rows_in, gate_up, preferred_element_type=jnp.float32)  8.98 us
    dot_general x2, matrix products, expert_block(): jnp.dot(active, down_proj, preferred_element_type=jnp.float32)  5.02 us
    unnamed x12, local copies, waits for them, and re-layouts  2.65 us
  transfers between devices with their start and end apart: 20, of which 13 were waited for; matrix products, arithmetic and copies ran while one was open for 9% of the time, Pallas kernels for 0%

profile of v8, /device:TPU:0, one launch (start us, length us, event | category | flops | bytes accessed | tf_op | source)
XLA Modules:
  0.0 121.8 jit_solution(11717636811306500625)
XLA Ops:
  0.0 0.9 reduce_sum.36
  0.9 0.8 broadcast_divide_fusion
  1.7 0.8 select_reduce_fusion
  2.8 1.1 concatenate.30
  3.9 5.1 %collective-permute-start.2 = (bf16[32,2176]{1,0:T(8,128)(2,1)S(1)}, bf16[32,2176]{1,0:T(8,128)(2,1)S(1)}, u32[]{:S(2)}, u32[]{:S(2)}) collective-permute-start(bf16[32,2176]{1,0:T(8,128)(2,1)S(1)} %get-tuple-element.28), channel_id=1, source_target_pairs={{0,12},{4,0},{8,4},{12,8},{1,13},{5,1},{9,5},{13,9},{2,14},{6,2},{... | collective-permute-start | bytes 417800 | tf_op jit(solution)/shard_map/ppermute | solution.py:65
  9.0 1.0 collective-permute-start
  10.0 3.1 %collective-permute-done.2 = bf16[32,2176]{1,0:T(8,128)(2,1)S(1)} collective-permute-done((bf16[32,2176]{1,0:T(8,128)(2,1)S(1)}, bf16[32,2176]{1,0:T(8,128)(2,1)S(1)}, u32[]{:S(2)}, u32[]{:S(2)}) %collective-permute-start.2) | collective-permute-done | bytes 139296 | tf_op jit(solution)/shard_map/ppermute | solution.py:65
  13.1 7.7 %collective-permute-done.1 = bf16[32,2176]{1,0:T(8,128)(2,1)S(1)} collective-permute-done((bf16[32,2176]{1,0:T(8,128)(2,1)S(1)}, bf16[32,2176]{1,0:T(8,128)(2,1)S(1)}, u32[]{:S(2)}, u32[]{:S(2)}) %collective-permute-start.1) | collective-permute-done | bytes 139296 | tf_op jit(solution)/shard_map/ppermute | solution.py:65
  20.9 1.6 %collective-permute-start.3 = (bf16[128,2176]{1,0:T(8,128)(2,1)S(1)}, bf16[128,2176]{1,0:T(8,128)(2,1)S(1)}, u32[]{:S(2)}, u32[]{:S(2)}) collective-permute-start(bf16[128,2176]{1,0:T(8,128)(2,1)S(1)} %pad_maximum_fusion.1), channel_id=1, source_target_pairs={{0,2},{2,0},{1,3},{3,1},{4,6},{6,4},{5,7},{7,5},{8,10},{10,8},{9,1... | collective-permute-start | bytes 1671176 | tf_op jit(solution)/shard_map/ppermute | solution.py:65
  22.5 12.4 %collective-permute-done.3 = bf16[128,2176]{1,0:T(8,128)(2,1)S(1)} collective-permute-done((bf16[128,2176]{1,0:T(8,128)(2,1)S(1)}, bf16[128,2176]{1,0:T(8,128)(2,1)S(1)}, u32[]{:S(2)}, u32[]{:S(2)}) %collective-permute-start.3) | collective-permute-done | bytes 557088 | tf_op jit(solution)/shard_map/ppermute | solution.py:65
  35.1 0.6 collective-permute-start.12
  35.7 2.2 %collective-permute-start.11 = (bf16[32,2176]{1,0:T(8,128)(2,1)S(1)}, bf16[32,2176]{1,0:T(8,128)(2,1)S(1)}, u32[]{:S(2)}, u32[]{:S(2)}) collective-permute-start(bf16[32,2176]{1,0:T(8,128)(2,1)S(1)} %get-tuple-element.8), channel_id=1, source_target_pairs={{0,8},{4,12},{8,0},{12,4},{1,9},{5,13},{9,1},{13,5},{2,10},{6,14},... | collective-permute-start | bytes 417800 | tf_op jit(solution)/shard_map/ppermute | solution.py:65
  37.8 1.9 %collective-permute-start.10 = (bf16[32,2176]{1,0:T(8,128)(2,1)S(1)}, bf16[32,2176]{1,0:T(8,128)(2,1)S(1)}, u32[]{:S(2)}, u32[]{:S(2)}) collective-permute-start(bf16[32,2176]{1,0:T(8,128)(2,1)S(1)} %get-tuple-element.8), channel_id=1, source_target_pairs={{0,4},{4,8},{8,12},{12,0},{1,5},{5,9},{9,13},{13,1},{2,6},{6,10},{... | collective-permute-start | bytes 417800 | tf_op jit(solution)/shard_map/ppermute | solution.py:65
  39.8 1.4 %collective-permute-done.12 = bf16[32,2176]{1,0:T(8,128)(2,1)S(1)} collective-permute-done((bf16[32,2176]{1,0:T(8,128)(2,1)S(1)}, bf16[32,2176]{1,0:T(8,128)(2,1)S(1)}, u32[]{:S(2)}, u32[]{:S(2)}) %collective-permute-start.12) | collective-permute-done | bytes 139296 | tf_op jit(solution)/shard_map/ppermute | solution.py:65
  41.2 9.8 %collective-permute-done.11 = bf16[32,2176]{1,0:T(8,128)(2,1)S(1)} collective-permute-done((bf16[32,2176]{1,0:T(8,128)(2,1)S(1)}, bf16[32,2176]{1,0:T(8,128)(2,1)S(1)}, u32[]{:S(2)}, u32[]{:S(2)}) %collective-permute-start.11) | collective-permute-done | bytes 139296 | tf_op jit(solution)/shard_map/ppermute | solution.py:65
  51.2 1.6 %collective-permute-start.13 = (bf16[128,2176]{1,0:T(8,128)(2,1)S(1)}, bf16[128,2176]{1,0:T(8,128)(2,1)S(1)}, u32[]{:S(2)}, u32[]{:S(2)}) collective-permute-start(bf16[128,2176]{1,0:T(8,128)(2,1)S(1)} %pad_maximum_fusion.2), channel_id=1, source_target_pairs={{0,2},{2,0},{1,3},{3,1},{4,6},{6,4},{5,7},{7,5},{8,10},{10,8},{9,1... | collective-permute-start | bytes 1671176 | tf_op jit(solution)/shard_map/ppermute | solution.py:65
  52.8 3.4 %fusion.2 = f32[512,1536]{1,0:T(8,128)S(1)} fusion(bf16[1,2048,1536]{2,1,0:T(8,128)(2,1)S(1)} %copy-done.3, bf16[512,2176]{1,0:T(8,128)(2,1)S(1)} %constant_dynamic-update-slice_fusion.5), kind=kOutput, calls=%fused_computation.2 | convolution fusion | flops 3221225472 | bytes 11534336 | tf_op jit(solution)/shard_map/dot_general | solution.py:9
  56.2 3.2 %fusion.8 = bf16[512,2048]{1,0:T(8,128)(2,1)} fusion(bf16[1,768,2048]{2,1,0:T(8,128)(2,1)S(1)} %copy-done, f32[512,1536]{1,0:T(8,128)S(1)} %fusion.2), kind=kOutput, calls=%fused_computation.10 | convolution fusion | flops 1614020608 | bytes 8388608 | tf_op jit(solution)/shard_map/dot_general | solution.py:11
  59.4 6.3 %collective-permute-done.13 = bf16[128,2176]{1,0:T(8,128)(2,1)S(1)} collective-permute-done((bf16[128,2176]{1,0:T(8,128)(2,1)S(1)}, bf16[128,2176]{1,0:T(8,128)(2,1)S(1)}, u32[]{:S(2)}, u32[]{:S(2)}) %collective-permute-start.13) | collective-permute-done | bytes 557088 | tf_op jit(solution)/shard_map/ppermute | solution.py:65
  65.7 1.1 pad_maximum_fusion
  66.8 0.9 slice_convert_fusion.5
  67.7 1.3 %constant_dynamic-update-slice_fusion.12 = bf16[512,2176]{1,0:T(8,128)(2,1)S(1)} fusion(bf16[256,2176]{1,0:T(8,128)(2,1)} %pad_maximum_fusion), kind=kLoop, calls=%fused_computation.63 | loop fusion | bytes 2228224
  69.1 0.8 collective-permute-done.14
  69.9 1.4 %constant_dynamic-update-slice_fusion.11 = bf16[512,2176]{1,0:T(8,128)(2,1)S(1)} fusion(bf16[512,2176]{1,0:T(8,128)(2,1)S(1)} %constant_dynamic-update-slice_fusion.12, bf16[256,2176]{1,0:T(8,128)(2,1)} %collective-permute-done.14), kind=kLoop, calls=%fused_computation.62 | loop fusion | bytes 2228224 | tf_op jit(solution)/shard_map/concatenate | solution.py:66
  71.3 5.6 %fusion = f32[512,1536]{1,0:T(8,128)S(1)} fusion(bf16[1,2048,1536]{2,1,0:T(8,128)(2,1)} %param.10, bf16[512,2176]{1,0:T(8,128)(2,1)S(1)} %constant_dynamic-update-slice_fusion.11), kind=kOutput, calls=%fused_computation | convolution fusion | flops 3221225472 | bytes 11534336 | tf_op jit(solution)/shard_map/dot_general | solution.py:9
  76.9 0.5 fusion.33
  77.4 1.9 %convert_multiply_fusion = f32[512,2048]{1,0:T(8,128)S(1)} fusion(bf16[1,768,2048]{2,1,0:T(8,128)(2,1)S(1)} %copy-done, f32[512]{0:T(512)S(1)} %get-tuple-element.12, f32[512,1536]{1,0:T(8,128)S(1)} %fusion), kind=kOutput, calls=%fused_computation.4 | convolution fusion | flops 1616117760 | bytes 10487808 | tf_op jit(solution)/shard_map/dot_general | solution.py:11
  79.5 0.2 collective-permute-start.15
  79.7 1.2 %copy-done.1 = bf16[512,2048]{1,0:T(8,128)(2,1)S(1)} copy-done((bf16[512,2048]{1,0:T(8,128)(2,1)S(1)}, bf16[512,2048]{1,0:T(8,128)(2,1)}, u32[]{:S(2)}) %copy-start.1) | copy-done | bytes 2097176
  80.9 0.3 convert_multiply_fusion.1
  81.4 0.2 collective-permute-start.5
  81.6 0.6 collective-permute-done.15
  82.2 0.3 slice_add_fusion
  82.6 1.6 %collective-permute-start.16 = (bf16[128,2048]{1,0:T(8,128)(2,1)S(1)}, bf16[128,2048]{1,0:T(8,128)(2,1)S(1)}, u32[]{:S(2)}, u32[]{:S(2)}) collective-permute-start(bf16[128,2048]{1,0:T(8,128)(2,1)S(1)} %split.126), channel_id=1, source_target_pairs={{0,2},{2,0},{1,3},{3,1},{4,6},{6,4},{5,7},{7,5},{8,10},{10,8},{9,1... | collective-permute-start | bytes 1572872 | tf_op jit(solution)/shard_map/ppermute | solution.py:74
  84.2 0.3 slice_add_fusion.1
  84.6 1.5 %collective-permute-start.6 = (bf16[128,2048]{1,0:T(8,128)(2,1)S(1)}, bf16[128,2048]{1,0:T(8,128)(2,1)S(1)}, u32[]{:S(2)}, u32[]{:S(2)}) collective-permute-start(bf16[128,2048]{1,0:T(8,128)(2,1)S(1)} %split.127), channel_id=1, source_target_pairs={{0,2},{2,0},{1,3},{3,1},{4,6},{6,4},{5,7},{7,5},{8,10},{10,8},{9,1... | collective-permute-start | bytes 1572872 | tf_op jit(solution)/shard_map/ppermute | solution.py:74
  86.1 11.4 %collective-permute-done.16 = bf16[128,2048]{1,0:T(8,128)(2,1)S(1)} collective-permute-done((bf16[128,2048]{1,0:T(8,128)(2,1)S(1)}, bf16[128,2048]{1,0:T(8,128)(2,1)S(1)}, u32[]{:S(2)}, u32[]{:S(2)}) %collective-permute-start.16) | collective-permute-done | bytes 524320 | tf_op jit(solution)/shard_map/ppermute | solution.py:74
  97.5 0.1 fusion.38
  97.7 2.0 %collective-permute-start.19 = (bf16[32,2048]{1,0:T(8,128)(2,1)S(1)}, bf16[32,2048]{1,0:T(8,128)(2,1)S(1)}, u32[]{:S(2)}, u32[]{:S(2)}) collective-permute-start(bf16[32,2048]{1,0:T(8,128)(2,1)S(1)} %get-tuple-element.23), channel_id=1, source_target_pairs={{0,4},{4,8},{8,12},{12,0},{1,5},{5,9},{9,13},{13,1},{2,6},{6,10},{... | collective-permute-start | bytes 393224 | tf_op jit(solution)/shard_map/ppermute | solution.py:74
  99.7 0.7 collective-permute-start.18
  100.5 7.4 %collective-permute-done.6 = bf16[128,2048]{1,0:T(8,128)(2,1)S(1)} collective-permute-done((bf16[128,2048]{1,0:T(8,128)(2,1)S(1)}, bf16[128,2048]{1,0:T(8,128)(2,1)S(1)}, u32[]{:S(2)}, u32[]{:S(2)}) %collective-permute-start.6) | collective-permute-done | bytes 524320 | tf_op jit(solution)/shard_map/ppermute | solution.py:74
  107.9 0.2 fusion.37
  108.1 2.0 %collective-permute-start.9 = (bf16[32,2048]{1,0:T(8,128)(2,1)S(1)}, bf16[32,2048]{1,0:T(8,128)(2,1)S(1)}, u32[]{:S(2)}, u32[]{:S(2)}) collective-permute-start(bf16[32,2048]{1,0:T(8,128)(2,1)S(1)} %get-tuple-element.20), channel_id=1, source_target_pairs={{0,4},{4,8},{8,12},{12,0},{1,5},{5,9},{9,13},{13,1},{2,6},{6,10},{... | collective-permute-start | bytes 393224 | tf_op jit(solution)/shard_map/ppermute | solution.py:74
  110.2 0.7 collective-permute-start.8
  111.0 4.8 %collective-permute-done.7 = bf16[32,2048]{1,0:T(8,128)(2,1)S(1)} collective-permute-done((bf16[32,2048]{1,0:T(8,128)(2,1)S(1)}, bf16[32,2048]{1,0:T(8,128)(2,1)S(1)}, u32[]{:S(2)}, u32[]{:S(2)}) %collective-permute-start.7) | collective-permute-done | bytes 131104 | tf_op jit(solution)/shard_map/ppermute | solution.py:74
  115.7 1.8 %collective-permute-done.9 = bf16[32,2048]{1,0:T(8,128)(2,1)S(1)} collective-permute-done((bf16[32,2048]{1,0:T(8,128)(2,1)S(1)}, bf16[32,2048]{1,0:T(8,128)(2,1)S(1)}, u32[]{:S(2)}, u32[]{:S(2)}) %collective-permute-start.9) | collective-permute-done | bytes 131104 | tf_op jit(solution)/shard_map/ppermute | solution.py:74
  117.6 3.5 %collective-permute-done.8 = bf16[32,2048]{1,0:T(8,128)(2,1)S(1)} collective-permute-done((bf16[32,2048]{1,0:T(8,128)(2,1)S(1)}, bf16[32,2048]{1,0:T(8,128)(2,1)S(1)}, u32[]{:S(2)}, u32[]{:S(2)}) %collective-permute-start.8) | collective-permute-done | bytes 131104 | tf_op jit(solution)/shard_map/ppermute | solution.py:74
  121.1 0.7 pad_maximum_fusion.3
  (42 shorter events, 1.6 us)
Async XLA Ops:
  0.0 56.2 %copy-start = (bf16[1,768,2048]{2,1,0:T(8,128)(2,1)S(1)}, bf16[1,768,2048]{2,1,0:T(8,128)(2,1)}, u32[]{:S(2)}) copy-start(bf16[1,768,2048]{2,1,0:T(8,128)(2,1)} %param.11) | copy-start | bytes 9437188
  3.9 9.2 %collective-permute-start.2 = (bf16[32,2176]{1,0:T(8,128)(2,1)S(1)}, bf16[32,2176]{1,0:T(8,128)(2,1)S(1)}, u32[]{:S(2)}, u32[]{:S(2)}) collective-permute-start(bf16[32,2176]{1,0:T(8,128)(2,1)S(1)} %get-tuple-element.28), channel_id=1, source_target_pairs={{0,12},{4,0},{8,4},{12,8},{1,13},{5,1},{9,5},{13,9},{2,14},{6,2},{... | collective-permute-start | bytes 417800 | tf_op jit(solution)/shard_map/ppermute | solution.py:65
  9.0 11.8 %collective-permute-start.1 = (bf16[32,2176]{1,0:T(8,128)(2,1)S(1)}, bf16[32,2176]{1,0:T(8,128)(2,1)S(1)}, u32[]{:S(2)}, u32[]{:S(2)}) collective-permute-start(bf16[32,2176]{1,0:T(8,128)(2,1)S(1)} %get-tuple-element.28), channel_id=1, source_target_pairs={{0,8},{4,12},{8,0},{12,4},{1,9},{5,13},{9,1},{13,5},{2,10},{6,14},... | collective-permute-start | bytes 417800 | tf_op jit(solution)/shard_map/ppermute | solution.py:65
  9.0 11.8 %collective-permute-start = (bf16[32,2176]{1,0:T(8,128)(2,1)S(1)}, bf16[32,2176]{1,0:T(8,128)(2,1)S(1)}, u32[]{:S(2)}, u32[]{:S(2)}) collective-permute-start(bf16[32,2176]{1,0:T(8,128)(2,1)S(1)} %get-tuple-element.28), channel_id=1, source_target_pairs={{0,4},{4,8},{8,12},{12,0},{1,5},{5,9},{9,13},{13,1},{2,6},{6,10},{... | collective-permute-start | bytes 417800 | tf_op jit(solution)/shard_map/ppermute | solution.py:65
  20.8 31.9 %copy-start.3 = (bf16[1,2048,1536]{2,1,0:T(8,128)(2,1)S(1)}, bf16[1,2048,1536]{2,1,0:T(8,128)(2,1)}, u32[]{:S(2)}) copy-start(bf16[1,2048,1536]{2,1,0:T(8,128)(2,1)} %param.10) | copy-start | bytes 18874372
  20.9 14.0 %collective-permute-start.3 = (bf16[128,2176]{1,0:T(8,128)(2,1)S(1)}, bf16[128,2176]{1,0:T(8,128)(2,1)S(1)}, u32[]{:S(2)}, u32[]{:S(2)}) collective-permute-start(bf16[128,2176]{1,0:T(8,128)(2,1)S(1)} %pad_maximum_fusion.1), channel_id=1, source_target_pairs={{0,2},{2,0},{1,3},{3,1},{4,6},{6,4},{5,7},{7,5},{8,10},{10,8},{9,1... | collective-permute-start | bytes 1671176 | tf_op jit(solution)/shard_map/ppermute | solution.py:65
  35.0 16.0 %collective-permute-start.4 = (bf16[256,2176]{1,0:T(8,128)(2,1)S(1)}, bf16[256,2176]{1,0:T(8,128)(2,1)S(1)}, u32[]{:S(2)}, u32[]{:S(2)}) collective-permute-start(bf16[256,2176]{1,0:T(8,128)(2,1)S(1)} %get-tuple-element.17), channel_id=1, source_target_pairs={{0,1},{1,0},{2,3},{3,2},{4,5},{5,4},{6,7},{7,6},{8,9},{9,8},{10,11... | collective-permute-start | bytes 3342344 | tf_op jit(solution)/shard_map/ppermute | solution.py:65
  35.1 6.1 %collective-permute-start.12 = (bf16[32,2176]{1,0:T(8,128)(2,1)S(1)}, bf16[32,2176]{1,0:T(8,128)(2,1)S(1)}, u32[]{:S(2)}, u32[]{:S(2)}) collective-permute-start(bf16[32,2176]{1,0:T(8,128)(2,1)S(1)} %get-tuple-element.8), channel_id=1, source_target_pairs={{0,12},{4,0},{8,4},{12,8},{1,13},{5,1},{9,5},{13,9},{2,14},{6,2},{... | collective-permute-start | bytes 417800 | tf_op jit(solution)/shard_map/ppermute | solution.py:65
  35.7 15.3 %collective-permute-start.11 = (bf16[32,2176]{1,0:T(8,128)(2,1)S(1)}, bf16[32,2176]{1,0:T(8,128)(2,1)S(1)}, u32[]{:S(2)}, u32[]{:S(2)}) collective-permute-start(bf16[32,2176]{1,0:T(8,128)(2,1)S(1)} %get-tuple-element.8), channel_id=1, source_target_pairs={{0,8},{4,12},{8,0},{12,4},{1,9},{5,13},{9,1},{13,5},{2,10},{6,14},... | collective-permute-start | bytes 417800 | tf_op jit(solution)/shard_map/ppermute | solution.py:65
  37.8 13.2 %collective-permute-start.10 = (bf16[32,2176]{1,0:T(8,128)(2,1)S(1)}, bf16[32,2176]{1,0:T(8,128)(2,1)S(1)}, u32[]{:S(2)}, u32[]{:S(2)}) collective-permute-start(bf16[32,2176]{1,0:T(8,128)(2,1)S(1)} %get-tuple-element.8), channel_id=1, source_target_pairs={{0,4},{4,8},{8,12},{12,0},{1,5},{5,9},{9,13},{13,1},{2,6},{6,10},{... | collective-permute-start | bytes 417800 | tf_op jit(solution)/shard_map/ppermute | solution.py:65
  51.2 5.0 %copy-start.2 = (bf16[512,2176]{1,0:T(8,128)(2,1)}, bf16[512,2176]{1,0:T(8,128)(2,1)S(1)}, u32[]{:S(2)}) copy-start(bf16[512,2176]{1,0:T(8,128)(2,1)S(1)} %constant_dynamic-update-slice_fusion.5) | copy-start | bytes 6684676
  51.2 14.5 %collective-permute-start.13 = (bf16[128,2176]{1,0:T(8,128)(2,1)S(1)}, bf16[128,2176]{1,0:T(8,128)(2,1)S(1)}, u32[]{:S(2)}, u32[]{:S(2)}) collective-permute-start(bf16[128,2176]{1,0:T(8,128)(2,1)S(1)} %pad_maximum_fusion.2), channel_id=1, source_target_pairs={{0,2},{2,0},{1,3},{3,1},{4,6},{6,4},{5,7},{7,5},{8,10},{10,8},{9,1... | collective-permute-start | bytes 1671176 | tf_op jit(solution)/shard_map/ppermute | solution.py:65
  66.8 3.1 %collective-permute-start.14 = (bf16[256,2176]{1,0:T(8,128)(2,1)}, bf16[256,2176]{1,0:T(8,128)(2,1)}, u32[]{:S(2)}, u32[]{:S(2)}) collective-permute-start(bf16[256,2176]{1,0:T(8,128)(2,1)} %pad_maximum_fusion), channel_id=1, source_target_pairs={{0,1},{1,0},{2,3},{3,2},{4,5},{5,4},{6,7},{7,6},{8,9},{9,8},{10,11... | collective-permute-start | bytes 3342344 | tf_op jit(solution)/shard_map/ppermute | solution.py:65
  79.3 1.6 %copy-start.1 = (bf16[512,2048]{1,0:T(8,128)(2,1)S(1)}, bf16[512,2048]{1,0:T(8,128)(2,1)}, u32[]{:S(2)}) copy-start(bf16[512,2048]{1,0:T(8,128)(2,1)} %fusion.8) | copy-start | bytes 6291460
  79.5 2.7 %collective-permute-start.15 = (bf16[256,2048]{1,0:T(8,128)(2,1)S(1)}, bf16[256,2048]{1,0:T(8,128)(2,1)S(1)}, u32[]{:S(2)}, u32[]{:S(2)}) collective-permute-start(bf16[256,2048]{1,0:T(8,128)(2,1)S(1)} %split.124), channel_id=1, source_target_pairs={{0,1},{1,0},{2,3},{3,2},{4,5},{5,4},{6,7},{7,6},{8,9},{9,8},{10,11... | collective-permute-start | bytes 3145736 | tf_op jit(solution)/shard_map/ppermute | solution.py:74
  81.4 2.8 %collective-permute-start.5 = (bf16[256,2048]{1,0:T(8,128)(2,1)S(1)}, bf16[256,2048]{1,0:T(8,128)(2,1)S(1)}, u32[]{:S(2)}, u32[]{:S(2)}) collective-permute-start(bf16[256,2048]{1,0:T(8,128)(2,1)S(1)} %split.125), channel_id=1, source_target_pairs={{0,1},{1,0},{2,3},{3,2},{4,5},{5,4},{6,7},{7,6},{8,9},{9,8},{10,11... | collective-permute-start | bytes 3145736 | tf_op jit(solution)/shard_map/ppermute | solution.py:74
  82.6 14.9 %collective-permute-start.16 = (bf16[128,2048]{1,0:T(8,128)(2,1)S(1)}, bf16[128,2048]{1,0:T(8,128)(2,1)S(1)}, u32[]{:S(2)}, u32[]{:S(2)}) collective-permute-start(bf16[128,2048]{1,0:T(8,128)(2,1)S(1)} %split.126), channel_id=1, source_target_pairs={{0,2},{2,0},{1,3},{3,1},{4,6},{6,4},{5,7},{7,5},{8,10},{10,8},{9,1... | collective-permute-start | bytes 1572872 | tf_op jit(solution)/shard_map/ppermute | solution.py:74
  84.6 23.3 %collective-permute-start.6 = (bf16[128,2048]{1,0:T(8,128)(2,1)S(1)}, bf16[128,2048]{1,0:T(8,128)(2,1)S(1)}, u32[]{:S(2)}, u32[]{:S(2)}) collective-permute-start(bf16[128,2048]{1,0:T(8,128)(2,1)S(1)} %split.127), channel_id=1, source_target_pairs={{0,2},{2,0},{1,3},{3,1},{4,6},{6,4},{5,7},{7,5},{8,10},{10,8},{9,1... | collective-permute-start | bytes 1572872 | tf_op jit(solution)/shard_map/ppermute | solution.py:74
  97.7 12.5 %collective-permute-start.17 = (bf16[32,2048]{1,0:T(8,128)(2,1)S(1)}, bf16[32,2048]{1,0:T(8,128)(2,1)S(1)}, u32[]{:S(2)}, u32[]{:S(2)}) collective-permute-start(bf16[32,2048]{1,0:T(8,128)(2,1)S(1)} %get-tuple-element.22), channel_id=1, source_target_pairs={{0,12},{4,0},{8,4},{12,8},{1,13},{5,1},{9,5},{13,9},{2,14},{6,2},{... | collective-permute-start | bytes 393224 | tf_op jit(solution)/shard_map/ppermute | solution.py:74
  97.7 13.2 %collective-permute-start.19 = (bf16[32,2048]{1,0:T(8,128)(2,1)S(1)}, bf16[32,2048]{1,0:T(8,128)(2,1)S(1)}, u32[]{:S(2)}, u32[]{:S(2)}) collective-permute-start(bf16[32,2048]{1,0:T(8,128)(2,1)S(1)} %get-tuple-element.23), channel_id=1, source_target_pairs={{0,4},{4,8},{8,12},{12,0},{1,5},{5,9},{9,13},{13,1},{2,6},{6,10},{... | collective-permute-start | bytes 393224 | tf_op jit(solution)/shard_map/ppermute | solution.py:74
  99.7 11.2 %collective-permute-start.18 = (bf16[32,2048]{1,0:T(8,128)(2,1)S(1)}, bf16[32,2048]{1,0:T(8,128)(2,1)S(1)}, u32[]{:S(2)}, u32[]{:S(2)}) collective-permute-start(bf16[32,2048]{1,0:T(8,128)(2,1)S(1)} %get-tuple-element.24), channel_id=1, source_target_pairs={{0,8},{4,12},{8,0},{12,4},{1,9},{5,13},{9,1},{13,5},{2,10},{6,14},... | collective-permute-start | bytes 393224 | tf_op jit(solution)/shard_map/ppermute | solution.py:74
  108.1 7.6 %collective-permute-start.7 = (bf16[32,2048]{1,0:T(8,128)(2,1)S(1)}, bf16[32,2048]{1,0:T(8,128)(2,1)S(1)}, u32[]{:S(2)}, u32[]{:S(2)}) collective-permute-start(bf16[32,2048]{1,0:T(8,128)(2,1)S(1)} %get-tuple-element.19), channel_id=1, source_target_pairs={{0,12},{4,0},{8,4},{12,8},{1,13},{5,1},{9,5},{13,9},{2,14},{6,2},{... | collective-permute-start | bytes 393224 | tf_op jit(solution)/shard_map/ppermute | solution.py:74
  108.1 9.4 %collective-permute-start.9 = (bf16[32,2048]{1,0:T(8,128)(2,1)S(1)}, bf16[32,2048]{1,0:T(8,128)(2,1)S(1)}, u32[]{:S(2)}, u32[]{:S(2)}) collective-permute-start(bf16[32,2048]{1,0:T(8,128)(2,1)S(1)} %get-tuple-element.20), channel_id=1, source_target_pairs={{0,4},{4,8},{8,12},{12,0},{1,5},{5,9},{9,13},{13,1},{2,6},{6,10},{... | collective-permute-start | bytes 393224 | tf_op jit(solution)/shard_map/ppermute | solution.py:74
  110.2 10.9 %collective-permute-start.8 = (bf16[32,2048]{1,0:T(8,128)(2,1)S(1)}, bf16[32,2048]{1,0:T(8,128)(2,1)S(1)}, u32[]{:S(2)}, u32[]{:S(2)}) collective-permute-start(bf16[32,2048]{1,0:T(8,128)(2,1)S(1)} %get-tuple-element.21), channel_id=1, source_target_pairs={{0,8},{4,12},{8,0},{12,4},{1,9},{5,13},{9,1},{13,5},{2,10},{6,14},... | collective-permute-start | bytes 393224 | tf_op jit(solution)/shard_map/ppermute | solution.py:74

commit v9 on v5

--- a/solution.py
+++ b/solution.py
@@ -55,7 +55,7 @@
     return mixed.astype(jnp.bfloat16)
 
 
-AXES = ("ez", "ex", "ec")
+AXES = ("ezh", "ezl", "ex", "ec")
 
 
 def gather_stage(block, axis, size):
@@ -80,8 +80,10 @@
     hidden_width = w_down.shape[1]
     experts = host_expert.shape[0]
     sizes = [lax.axis_size(a) for a in AXES]
-    hosts = sizes[0] * sizes[1] * sizes[2]
-    me = (lax.axis_index("ez") * sizes[1] + lax.axis_index("ex")) * sizes[2] + lax.axis_index("ec")
+    hosts = int(np.prod(sizes))
+    me = 0
+    for axis, size in zip(AXES, sizes):
+        me = me * size + lax.axis_index(axis)
     weights = gate_scores / jnp.sum(gate_scores, axis=1, keepdims=True)
     chosen = expert_ids[:, :, None] == host_expert[None, None, :]
     per_host = jnp.sum(jnp.where(chosen, weights[:, :, None], 0.0), axis=1)
@@ -125,9 +127,9 @@
         zs = len({d.coords[2] for d in row})
     except AttributeError:
         return None
-    if cores * xs * zs != row.shape[0]:
+    if cores * xs * zs != row.shape[0] or zs % 2:
         return None
-    return zs, xs, cores
+    return zs // 2, 2, xs, cores
 
 
 def solution(mesh):

time: 106 us -> 118 us (1.11)
  waiting for transfers between devices: 48.5 us -> 69.2 us
  starting transfers between devices: 29.1 us -> 20.3 us
  local copies, waits for them, and re-layouts: 10.8 us -> 7.01 us
  matrix products: 10.6 us -> 12.8 us
  other arithmetic: 6.12 us -> 7.8 us
    ppermute x10 -> x8, waiting for transfers between devices: 25 us -> 35.4 us  [scatter_stage(): lax.ppermute(pieces[shift].astype(jnp.bfloat16), axis, pairs)]
    ppermute x10 -> x8, waiting for transfers between devices: 23.5 us -> 33.8 us  [gather_stage(): got.append(lax.ppermute(block, axis, pairs))]
    ppermute x10 -> x8, starting transfers between devices: 13.9 us -> 8.64 us  [scatter_stage(): lax.ppermute(pieces[shift].astype(jnp.bfloat16), axis, pairs)]
    ppermute x10 -> x8, starting transfers between devices: 15.2 us -> 11.6 us  [gather_stage(): got.append(lax.ppermute(block, axis, pairs))]
    unnamed x13 -> x15, local copies, waits for them, and re-layouts: 5 us -> 2.49 us
    dot_general x2, matrix products: 6.9 us -> 9.13 us  [expert_block(): pair = jnp.dot(rows_in, gate_up, preferred_element_type=jnp.float32)]
    concatenate x2 -> x6, other arithmetic: 1.27 us -> 3 us  [gather_stage(): return jnp.concatenate(got, axis=0)]
    concatenate x4 -> x2, local copies, waits for them, and re-layouts: 1.51 us -> 0.29 us  [gather_stage(): return jnp.concatenate(got, axis=0)]
  transfers between devices with their start and end apart: 20 -> 16, of which waited for: 10 -> 12; matrix products, arithmetic and copies ran while one was open for 12% -> 12% of each run, Pallas kernels for 0% -> 0%
where the time goes in v9:
time: 118 us; the launch traced here: 117 us
  waiting for transfers between devices  69.2 us (59%)
  starting transfers between devices  20.3 us (17%)
  matrix products  12.8 us (11%)
  other arithmetic  7.8 us (7%)
  local copies, waits for them, and re-layouts  7.01 us (6%)
    ppermute x8, waiting for transfers between devices, scatter_stage(): lax.ppermute(pieces[shift].astype(jnp.bfloat16), axis, pairs)  35.4 us
    ppermute x8, waiting for transfers between devices, gather_stage(): got.append(lax.ppermute(block, axis, pairs))  33.8 us
    ppermute x8, starting transfers between devices, gather_stage(): got.append(lax.ppermute(block, axis, pairs))  11.6 us
    dot_general x2, matrix products, expert_block(): pair = jnp.dot(rows_in, gate_up, preferred_element_type=jnp.float32)  9.13 us
    ppermute x8, starting transfers between devices, scatter_stage(): lax.ppermute(pieces[shift].astype(jnp.bfloat16), axis, pairs)  8.64 us
    dot_general x2, matrix products, expert_block(): jnp.dot(active, down_proj, preferred_element_type=jnp.float32)  3.69 us
    concatenate x6, other arithmetic, gather_stage(): return jnp.concatenate(got, axis=0)  3 us
    unnamed x15, local copies, waits for them, and re-layouts  2.49 us
  transfers between devices with their start and end apart: 16, of which 12 were waited for; matrix products, arithmetic and copies ran while one was open for 12% of the time, Pallas kernels for 0%

profile of v9, /device:TPU:0, one launch (start us, length us, event | category | flops | bytes accessed | tf_op | source)
XLA Modules:
  0.0 117.5 jit_solution(4879190873412574403)
XLA Ops:
  0.0 0.9 reduce_sum.36
  0.9 0.8 broadcast_divide_fusion
  1.7 0.8 select_reduce_fusion
  2.4 0.1 copy.10
  2.5 0.1 copy.11
  2.6 0.1 copy.9
  2.8 1.8 %concatenate.40 = bf16[64,2176]{1,0:T(8,128)(2,1)} concatenate(bf16[64,2048]{1,0:T(8,128)(2,1)} %param.6, bf16[64,16]{1,0:T(8,128)(2,1)S(1)} %copy.9, bf16[64,16]{1,0:T(8,128)(2,1)S(1)} %copy.10, bf16[64,16]{1,0:T(8,128)(2,1)S(1)} %copy.11, bf16[64,80]{1,0:T(8,128)(2,1)S(1)} %broadcast_in_dim.16), dimensions={1} | concatenate | bytes 557056 | tf_op jit(solution)/shard_map/concatenate | solution.py:97
  4.5 1.7 %fusion.35 = (bf16[32,2176]{1,0:T(8,128)(2,1)S(1)}, bf16[512,2176]{1,0:T(8,128)(2,1)}, bf16[32,2176]{1,0:T(8,128)(2,1)S(1)}) fusion(bf16[64,2176]{1,0:T(8,128)(2,1)} %concatenate.40), kind=kLoop, calls=%fused_computation.75 | loop fusion | bytes 696320 | tf_op jit(solution)/shard_map/split | solution.py:101
  6.2 4.1 %collective-permute-start = (bf16[32,2176]{1,0:T(8,128)(2,1)S(1)}, bf16[32,2176]{1,0:T(8,128)(2,1)}, u32[]{:S(2)}, u32[]{:S(2)}) collective-permute-start(bf16[32,2176]{1,0:T(8,128)(2,1)S(1)} %get-tuple-element.11), channel_id=1, source_target_pairs={{0,8},{8,0},{1,9},{9,1},{2,10},{10,2},{3,11},{11,3},{4,12},{12,4},... | collective-permute-start | bytes 417800 | tf_op jit(solution)/shard_map/ppermute | solution.py:65
  10.2 6.8 %collective-permute-done = bf16[32,2176]{1,0:T(8,128)(2,1)} collective-permute-done((bf16[32,2176]{1,0:T(8,128)(2,1)S(1)}, bf16[32,2176]{1,0:T(8,128)(2,1)}, u32[]{:S(2)}, u32[]{:S(2)}) %collective-permute-start) | collective-permute-done | bytes 139296 | tf_op jit(solution)/shard_map/ppermute | solution.py:65
  17.0 0.9 pad_maximum_fusion.4
  18.0 4.2 %collective-permute-start.1 = (bf16[64,2176]{1,0:T(8,128)(2,1)S(1)}, bf16[64,2176]{1,0:T(8,128)(2,1)S(1)}, u32[]{:S(2)}, u32[]{:S(2)}) collective-permute-start(bf16[64,2176]{1,0:T(8,128)(2,1)S(1)} %pad_maximum_fusion.4), channel_id=1, source_target_pairs={{0,4},{4,0},{1,5},{5,1},{2,6},{6,2},{3,7},{7,3},{8,12},{12,8},{9,1... | collective-permute-start | bytes 835592 | tf_op jit(solution)/shard_map/ppermute | solution.py:65
  22.2 1.6 %constant_dynamic-update-slice_fusion.3 = bf16[512,2176]{1,0:T(8,128)(2,1)} fusion(bf16[512,2176]{1,0:T(8,128)(2,1)} %get-tuple-element.10, bf16[32,2176]{1,0:T(8,128)(2,1)} %collective-permute-done), kind=kLoop, calls=%fused_computation.59 | loop fusion | bytes 278528
  23.8 3.2 %collective-permute-done.8 = bf16[32,2176]{1,0:T(8,128)(2,1)S(1)} collective-permute-done((bf16[32,2176]{1,0:T(8,128)(2,1)S(1)}, bf16[32,2176]{1,0:T(8,128)(2,1)S(1)}, u32[]{:S(2)}, u32[]{:S(2)}) %collective-permute-start.8) | collective-permute-done | bytes 139296 | tf_op jit(solution)/shard_map/ppermute | solution.py:65
  27.1 4.0 %collective-permute-done.1 = bf16[64,2176]{1,0:T(8,128)(2,1)S(1)} collective-permute-done((bf16[64,2176]{1,0:T(8,128)(2,1)S(1)}, bf16[64,2176]{1,0:T(8,128)(2,1)S(1)}, u32[]{:S(2)}, u32[]{:S(2)}) %collective-permute-start.1) | collective-permute-done | bytes 278560 | tf_op jit(solution)/shard_map/ppermute | solution.py:65
  31.1 0.9 pad_maximum_fusion.2
  32.0 1.6 %collective-permute-start.2 = (bf16[128,2176]{1,0:T(8,128)(2,1)S(1)}, bf16[128,2176]{1,0:T(8,128)(2,1)S(1)}, u32[]{:S(2)}, u32[]{:S(2)}) collective-permute-start(bf16[128,2176]{1,0:T(8,128)(2,1)S(1)} %pad_maximum_fusion.2), channel_id=1, source_target_pairs={{0,2},{2,0},{1,3},{3,1},{4,6},{6,4},{5,7},{7,5},{8,10},{10,8},{9,1... | collective-permute-start | bytes 1671176 | tf_op jit(solution)/shard_map/ppermute | solution.py:65
  33.6 0.7 constant_dynamic-update-slice_fusion.2
  34.3 1.9 %collective-permute-done.9 = bf16[64,2176]{1,0:T(8,128)(2,1)S(1)} collective-permute-done((bf16[64,2176]{1,0:T(8,128)(2,1)S(1)}, bf16[64,2176]{1,0:T(8,128)(2,1)S(1)}, u32[]{:S(2)}, u32[]{:S(2)}) %collective-permute-start.9) | collective-permute-done | bytes 278560 | tf_op jit(solution)/shard_map/ppermute | solution.py:65
  36.2 1.6 %collective-permute-start.10 = (bf16[128,2176]{1,0:T(8,128)(2,1)S(1)}, bf16[128,2176]{1,0:T(8,128)(2,1)S(1)}, u32[]{:S(2)}, u32[]{:S(2)}) collective-permute-start(bf16[128,2176]{1,0:T(8,128)(2,1)S(1)} %pad_maximum_fusion.3), channel_id=1, source_target_pairs={{0,2},{2,0},{1,3},{3,1},{4,6},{6,4},{5,7},{7,5},{8,10},{10,8},{9,1... | collective-permute-start | bytes 1671176 | tf_op jit(solution)/shard_map/ppermute | solution.py:65
  37.8 9.8 %collective-permute-done.2 = bf16[128,2176]{1,0:T(8,128)(2,1)S(1)} collective-permute-done((bf16[128,2176]{1,0:T(8,128)(2,1)S(1)}, bf16[128,2176]{1,0:T(8,128)(2,1)S(1)}, u32[]{:S(2)}, u32[]{:S(2)}) %collective-permute-start.2) | collective-permute-done | bytes 557088 | tf_op jit(solution)/shard_map/ppermute | solution.py:65
  47.6 1.0 pad_maximum_fusion
  48.8 8.1 %collective-permute-done.10 = bf16[128,2176]{1,0:T(8,128)(2,1)S(1)} collective-permute-done((bf16[128,2176]{1,0:T(8,128)(2,1)S(1)}, bf16[128,2176]{1,0:T(8,128)(2,1)S(1)}, u32[]{:S(2)}, u32[]{:S(2)}) %collective-permute-start.10) | collective-permute-done | bytes 557088 | tf_op jit(solution)/shard_map/ppermute | solution.py:65
  57.2 0.1 constant_dynamic-update-slice_fusion
  57.4 5.7 %fusion.2 = f32[512,1536]{1,0:T(8,128)S(1)} fusion(bf16[1,2048,1536]{2,1,0:T(8,128)(2,1)} %param.10, bf16[512,2176]{1,0:T(8,128)(2,1)S(1)} %constant_dynamic-update-slice_fusion), kind=kOutput, calls=%fused_computation.2 | convolution fusion | flops 3221225472 | bytes 11534336 | tf_op jit(solution)/shard_map/dot_general | solution.py:9
  63.1 0.1 constant_dynamic-update-slice_fusion.5
  63.3 3.4 %fusion = f32[512,1536]{1,0:T(8,128)S(1)} fusion(bf16[1,2048,1536]{2,1,0:T(8,128)(2,1)S(1)} %bitcast.19, bf16[512,2176]{1,0:T(8,128)(2,1)S(1)} %constant_dynamic-update-slice_fusion.5), kind=kOutput, calls=%fused_computation | convolution fusion | flops 3221225472 | bytes 11534336 | tf_op jit(solution)/shard_map/dot_general | solution.py:9
  66.7 0.5 fusion.31
  67.3 1.8 %convert_multiply_fusion.1 = f32[512,2048]{1,0:T(8,128)S(1)} fusion(bf16[1,768,2048]{2,1,0:T(8,128)(2,1)S(1)} %copy-done, f32[512]{0:T(512)S(1)} %get-tuple-element.7, f32[512,1536]{1,0:T(8,128)S(1)} %fusion.2), kind=kOutput, calls=%fused_computation.5 | convolution fusion | flops 1616117760 | bytes 10487808 | tf_op jit(solution)/shard_map/dot_general | solution.py:11
  69.1 0.1 split.120
  69.3 0.6 collective-permute-start.4
  69.8 1.8 %convert_multiply_fusion = f32[512,2048]{1,0:T(8,128)S(1)} fusion(bf16[1,768,2048]{2,1,0:T(8,128)(2,1)S(1)} %copy-done, f32[512]{0:T(512)S(1)} %get-tuple-element.8, f32[512,1536]{1,0:T(8,128)S(1)} %fusion), kind=kOutput, calls=%fused_computation.4 | convolution fusion | flops 1616117760 | bytes 10487808 | tf_op jit(solution)/shard_map/dot_general | solution.py:11
  71.7 0.1 split.119
  71.9 0.2 collective-permute-done.4
  72.1 0.3 slice_add_fusion.1
  72.5 1.6 %collective-permute-start.5 = (bf16[128,2048]{1,0:T(8,128)(2,1)S(1)}, bf16[128,2048]{1,0:T(8,128)(2,1)S(1)}, u32[]{:S(2)}, u32[]{:S(2)}) collective-permute-start(bf16[128,2048]{1,0:T(8,128)(2,1)S(1)} %split.122), channel_id=1, source_target_pairs={{0,2},{2,0},{1,3},{3,1},{4,6},{6,4},{5,7},{7,5},{8,10},{10,8},{9,1... | collective-permute-start | bytes 1572872 | tf_op jit(solution)/shard_map/ppermute | solution.py:74
  74.1 0.4 collective-permute-done.12
  74.5 0.3 slice_add_fusion
  75.0 1.6 %collective-permute-start.13 = (bf16[128,2048]{1,0:T(8,128)(2,1)S(1)}, bf16[128,2048]{1,0:T(8,128)(2,1)S(1)}, u32[]{:S(2)}, u32[]{:S(2)}) collective-permute-start(bf16[128,2048]{1,0:T(8,128)(2,1)S(1)} %split.121), channel_id=1, source_target_pairs={{0,2},{2,0},{1,3},{3,1},{4,6},{6,4},{5,7},{7,5},{8,10},{10,8},{9,1... | collective-permute-start | bytes 1572872 | tf_op jit(solution)/shard_map/ppermute | solution.py:74
  76.5 10.8 %collective-permute-done.5 = bf16[128,2048]{1,0:T(8,128)(2,1)S(1)} collective-permute-done((bf16[128,2048]{1,0:T(8,128)(2,1)S(1)}, bf16[128,2048]{1,0:T(8,128)(2,1)S(1)}, u32[]{:S(2)}, u32[]{:S(2)}) %collective-permute-start.5) | collective-permute-done | bytes 524320 | tf_op jit(solution)/shard_map/ppermute | solution.py:74
  87.4 0.1 slice_add_fusion.3
  87.6 10.4 %collective-permute-done.13 = bf16[128,2048]{1,0:T(8,128)(2,1)S(1)} collective-permute-done((bf16[128,2048]{1,0:T(8,128)(2,1)S(1)}, bf16[128,2048]{1,0:T(8,128)(2,1)S(1)}, u32[]{:S(2)}, u32[]{:S(2)}) %collective-permute-start.13) | collective-permute-done | bytes 524320 | tf_op jit(solution)/shard_map/ppermute | solution.py:74
  98.0 0.1 slice_add_fusion.2
  98.4 3.6 %collective-permute-start.7 = (bf16[32,2048]{1,0:T(8,128)(2,1)S(1)}, bf16[32,2048]{1,0:T(8,128)(2,1)S(1)}, u32[]{:S(2)}, u32[]{:S(2)}) collective-permute-start(bf16[32,2048]{1,0:T(8,128)(2,1)S(1)} %split.126), channel_id=1, source_target_pairs={{0,8},{8,0},{1,9},{9,1},{2,10},{10,2},{3,11},{11,3},{4,12},{12,4},... | collective-permute-start | bytes 393224 | tf_op jit(solution)/shard_map/ppermute | solution.py:74
  101.9 6.8 %collective-permute-done.14 = bf16[64,2048]{1,0:T(8,128)(2,1)S(1)} collective-permute-done((bf16[64,2048]{1,0:T(8,128)(2,1)S(1)}, bf16[64,2048]{1,0:T(8,128)(2,1)S(1)}, u32[]{:S(2)}, u32[]{:S(2)}) %collective-permute-start.14) | collective-permute-done | bytes 262176 | tf_op jit(solution)/shard_map/ppermute | solution.py:74
  108.9 1.1 collective-permute-start.15
  110.0 6.7 %collective-permute-done.15 = bf16[32,2048]{1,0:T(8,128)(2,1)S(1)} collective-permute-done((bf16[32,2048]{1,0:T(8,128)(2,1)S(1)}, bf16[32,2048]{1,0:T(8,128)(2,1)S(1)}, u32[]{:S(2)}, u32[]{:S(2)}) %collective-permute-start.15) | collective-permute-done | bytes 131104 | tf_op jit(solution)/shard_map/ppermute | solution.py:74
  116.8 0.7 pad_maximum_fusion.6
  (43 shorter events, 1.3 us)
Async XLA Ops:
  0.0 67.3 %copy-start = (bf16[1,768,2048]{2,1,0:T(8,128)(2,1)S(1)}, bf16[1,768,2048]{2,1,0:T(8,128)(2,1)}, u32[]{:S(2)}) copy-start(bf16[1,768,2048]{2,1,0:T(8,128)(2,1)} %param.11) | copy-start | bytes 9437188
  6.2 10.8 %collective-permute-start = (bf16[32,2176]{1,0:T(8,128)(2,1)S(1)}, bf16[32,2176]{1,0:T(8,128)(2,1)}, u32[]{:S(2)}, u32[]{:S(2)}) collective-permute-start(bf16[32,2176]{1,0:T(8,128)(2,1)S(1)} %get-tuple-element.11), channel_id=1, source_target_pairs={{0,8},{8,0},{1,9},{9,1},{2,10},{10,2},{3,11},{11,3},{4,12},{12,4},... | collective-permute-start | bytes 417800 | tf_op jit(solution)/shard_map/ppermute | solution.py:65
  17.9 9.1 %collective-permute-start.8 = (bf16[32,2176]{1,0:T(8,128)(2,1)S(1)}, bf16[32,2176]{1,0:T(8,128)(2,1)S(1)}, u32[]{:S(2)}, u32[]{:S(2)}) collective-permute-start(bf16[32,2176]{1,0:T(8,128)(2,1)S(1)} %get-tuple-element.6), channel_id=1, source_target_pairs={{0,8},{8,0},{1,9},{9,1},{2,10},{10,2},{3,11},{11,3},{4,12},{12,4},... | collective-permute-start | bytes 417800 | tf_op jit(solution)/shard_map/ppermute | solution.py:65
  18.0 13.1 %collective-permute-start.1 = (bf16[64,2176]{1,0:T(8,128)(2,1)S(1)}, bf16[64,2176]{1,0:T(8,128)(2,1)S(1)}, u32[]{:S(2)}, u32[]{:S(2)}) collective-permute-start(bf16[64,2176]{1,0:T(8,128)(2,1)S(1)} %pad_maximum_fusion.4), channel_id=1, source_target_pairs={{0,4},{4,0},{1,5},{5,1},{2,6},{6,2},{3,7},{7,3},{8,12},{12,8},{9,1... | collective-permute-start | bytes 835592 | tf_op jit(solution)/shard_map/ppermute | solution.py:65
  27.0 9.2 %collective-permute-start.9 = (bf16[64,2176]{1,0:T(8,128)(2,1)S(1)}, bf16[64,2176]{1,0:T(8,128)(2,1)S(1)}, u32[]{:S(2)}, u32[]{:S(2)}) collective-permute-start(bf16[64,2176]{1,0:T(8,128)(2,1)S(1)} %pad_maximum_fusion.5), channel_id=1, source_target_pairs={{0,4},{4,0},{1,5},{5,1},{2,6},{6,2},{3,7},{7,3},{8,12},{12,8},{9,1... | collective-permute-start | bytes 835592 | tf_op jit(solution)/shard_map/ppermute | solution.py:65
  32.0 15.6 %collective-permute-start.2 = (bf16[128,2176]{1,0:T(8,128)(2,1)S(1)}, bf16[128,2176]{1,0:T(8,128)(2,1)S(1)}, u32[]{:S(2)}, u32[]{:S(2)}) collective-permute-start(bf16[128,2176]{1,0:T(8,128)(2,1)S(1)} %pad_maximum_fusion.2), channel_id=1, source_target_pairs={{0,2},{2,0},{1,3},{3,1},{4,6},{6,4},{5,7},{7,5},{8,10},{10,8},{9,1... | collective-permute-start | bytes 1671176 | tf_op jit(solution)/shard_map/ppermute | solution.py:65
  34.3 14.4 %copy-start.1 = (bf16[512,2176]{1,0:T(8,128)(2,1)S(1)}, bf16[512,2176]{1,0:T(8,128)(2,1)}, u32[]{:S(2)}) copy-start(bf16[512,2176]{1,0:T(8,128)(2,1)} %constant_dynamic-update-slice_fusion.2) | copy-start | bytes 6684676
  36.2 20.7 %collective-permute-start.10 = (bf16[128,2176]{1,0:T(8,128)(2,1)S(1)}, bf16[128,2176]{1,0:T(8,128)(2,1)S(1)}, u32[]{:S(2)}, u32[]{:S(2)}) collective-permute-start(bf16[128,2176]{1,0:T(8,128)(2,1)S(1)} %pad_maximum_fusion.3), channel_id=1, source_target_pairs={{0,2},{2,0},{1,3},{3,1},{4,6},{6,4},{5,7},{7,5},{8,10},{10,8},{9,1... | collective-permute-start | bytes 1671176 | tf_op jit(solution)/shard_map/ppermute | solution.py:65
  48.6 8.6 %collective-permute-start.3 = (bf16[256,2176]{1,0:T(8,128)(2,1)S(1)}, bf16[256,2176]{1,0:T(8,128)(2,1)S(1)}, u32[]{:S(2)}, u32[]{:S(2)}) collective-permute-start(bf16[256,2176]{1,0:T(8,128)(2,1)S(1)} %pad_maximum_fusion), channel_id=1, source_target_pairs={{0,1},{1,0},{2,3},{3,2},{4,5},{5,4},{6,7},{7,6},{8,9},{9,8},{10,11... | collective-permute-start | bytes 3342344 | tf_op jit(solution)/shard_map/ppermute | solution.py:65
  57.0 6.1 %collective-permute-start.11 = (bf16[256,2176]{1,0:T(8,128)(2,1)S(1)}, bf16[256,2176]{1,0:T(8,128)(2,1)S(1)}, u32[]{:S(2)}, u32[]{:S(2)}) collective-permute-start(bf16[256,2176]{1,0:T(8,128)(2,1)S(1)} %pad_maximum_fusion.1), channel_id=1, source_target_pairs={{0,1},{1,0},{2,3},{3,2},{4,5},{5,4},{6,7},{7,6},{8,9},{9,8},{10,11... | collective-permute-start | bytes 3342344 | tf_op jit(solution)/shard_map/ppermute | solution.py:65
  57.2 6.1 %slice-start = ((s8[6291456]{0:T(1024)(128)(4,1)}), s8[4194304]{0:T(1024)(128)(4,1)S(1)}, s32[]{:S(2)}) async-start(s8[6291456]{0:T(1024)(128)(4,1)} %bitcast.18), calls=%async_computation | async-start | bytes 8388608
  57.4 5.9 %slice-start.1 = ((s8[6291456]{0:T(1024)(128)(4,1)}), s8[2097152]{0:T(1024)(128)(4,1)S(1)}, s32[]{:S(2)}) async-start(s8[6291456]{0:T(1024)(128)(4,1)} %bitcast.18), calls=%async_computation.1 | async-start | bytes 4194304
  69.3 2.8 %collective-permute-start.4 = (bf16[256,2048]{1,0:T(8,128)(2,1)S(1)}, bf16[256,2048]{1,0:T(8,128)(2,1)S(1)}, u32[]{:S(2)}, u32[]{:S(2)}) collective-permute-start(bf16[256,2048]{1,0:T(8,128)(2,1)S(1)} %split.120), channel_id=1, source_target_pairs={{0,1},{1,0},{2,3},{3,2},{4,5},{5,4},{6,7},{7,6},{8,9},{9,8},{10,11... | collective-permute-start | bytes 3145736 | tf_op jit(solution)/shard_map/ppermute | solution.py:74
  71.8 2.7 %collective-permute-start.12 = (bf16[256,2048]{1,0:T(8,128)(2,1)S(1)}, bf16[256,2048]{1,0:T(8,128)(2,1)S(1)}, u32[]{:S(2)}, u32[]{:S(2)}) collective-permute-start(bf16[256,2048]{1,0:T(8,128)(2,1)S(1)} %split.119), channel_id=1, source_target_pairs={{0,1},{1,0},{2,3},{3,2},{4,5},{5,4},{6,7},{7,6},{8,9},{9,8},{10,11... | collective-permute-start | bytes 3145736 | tf_op jit(solution)/shard_map/ppermute | solution.py:74
  72.5 14.9 %collective-permute-start.5 = (bf16[128,2048]{1,0:T(8,128)(2,1)S(1)}, bf16[128,2048]{1,0:T(8,128)(2,1)S(1)}, u32[]{:S(2)}, u32[]{:S(2)}) collective-permute-start(bf16[128,2048]{1,0:T(8,128)(2,1)S(1)} %split.122), channel_id=1, source_target_pairs={{0,2},{2,0},{1,3},{3,1},{4,6},{6,4},{5,7},{7,5},{8,10},{10,8},{9,1... | collective-permute-start | bytes 1572872 | tf_op jit(solution)/shard_map/ppermute | solution.py:74
  75.0 23.1 %collective-permute-start.13 = (bf16[128,2048]{1,0:T(8,128)(2,1)S(1)}, bf16[128,2048]{1,0:T(8,128)(2,1)S(1)}, u32[]{:S(2)}, u32[]{:S(2)}) collective-permute-start(bf16[128,2048]{1,0:T(8,128)(2,1)S(1)} %split.121), channel_id=1, source_target_pairs={{0,2},{2,0},{1,3},{3,1},{4,6},{6,4},{5,7},{7,5},{8,10},{10,8},{9,1... | collective-permute-start | bytes 1572872 | tf_op jit(solution)/shard_map/ppermute | solution.py:74
  87.5 10.7 %collective-permute-start.6 = (bf16[64,2048]{1,0:T(8,128)(2,1)S(1)}, bf16[64,2048]{1,0:T(8,128)(2,1)S(1)}, u32[]{:S(2)}, u32[]{:S(2)}) collective-permute-start(bf16[64,2048]{1,0:T(8,128)(2,1)S(1)} %split.124), channel_id=1, source_target_pairs={{0,4},{4,0},{1,5},{5,1},{2,6},{6,2},{3,7},{7,3},{8,12},{12,8},{9,1... | collective-permute-start | bytes 786440 | tf_op jit(solution)/shard_map/ppermute | solution.py:74
  98.2 10.6 %collective-permute-start.14 = (bf16[64,2048]{1,0:T(8,128)(2,1)S(1)}, bf16[64,2048]{1,0:T(8,128)(2,1)S(1)}, u32[]{:S(2)}, u32[]{:S(2)}) collective-permute-start(bf16[64,2048]{1,0:T(8,128)(2,1)S(1)} %split.123), channel_id=1, source_target_pairs={{0,4},{4,0},{1,5},{5,1},{2,6},{6,2},{3,7},{7,3},{8,12},{12,8},{9,1... | collective-permute-start | bytes 786440 | tf_op jit(solution)/shard_map/ppermute | solution.py:74
  98.4 11.7 %collective-permute-start.7 = (bf16[32,2048]{1,0:T(8,128)(2,1)S(1)}, bf16[32,2048]{1,0:T(8,128)(2,1)S(1)}, u32[]{:S(2)}, u32[]{:S(2)}) collective-permute-start(bf16[32,2048]{1,0:T(8,128)(2,1)S(1)} %split.126), channel_id=1, source_target_pairs={{0,8},{8,0},{1,9},{9,1},{2,10},{10,2},{3,11},{11,3},{4,12},{12,4},... | collective-permute-start | bytes 393224 | tf_op jit(solution)/shard_map/ppermute | solution.py:74
  108.9 7.8 %collective-permute-start.15 = (bf16[32,2048]{1,0:T(8,128)(2,1)S(1)}, bf16[32,2048]{1,0:T(8,128)(2,1)S(1)}, u32[]{:S(2)}, u32[]{:S(2)}) collective-permute-start(bf16[32,2048]{1,0:T(8,128)(2,1)S(1)} %split.125), channel_id=1, source_target_pairs={{0,8},{8,0},{1,9},{9,1},{2,10},{10,2},{3,11},{11,3},{4,12},{12,4},... | collective-permute-start | bytes 393224 | tf_op jit(solution)/shard_map/ppermute | solution.py:74

commit v10 on v8

--- a/solution.py
+++ b/solution.py
@@ -97,20 +97,23 @@
     results = []
     held = None
     for rows in jnp.split(carried, STREAMS, axis=0):
-        done = []
+        done = [None] * (2 * len(AXES))
         for stage, (axis, size) in enumerate(zip(AXES, sizes)):
             if held is not None:
-                _, rows = lax.optimization_barrier((held[(0, 2, 3)[stage]], rows))
+                _, rows = lax.optimization_barrier((held[stage], rows))
             rows = gather_stage(rows, axis, size)
-            done.append(rows)
+            done[stage] = rows
         tail = rows[:, width_model:width_model + 3 * hosts].astype(jnp.float32)
         gate = tail[:, :hosts] + tail[:, hosts:2 * hosts] + tail[:, 2 * hosts:]
         mine = jnp.sum(gate * pick[None, :], axis=1)
         out = expert_block(rows[:, :width_model], w_in[0], w_down[0], hidden_width)
-        held = done + [out]
         part = out.astype(jnp.float32) * mine[:, None]
-        for axis, size in list(zip(AXES, sizes))[::-1]:
+        for stage, (axis, size) in list(enumerate(zip(AXES, sizes)))[::-1]:
+            if held is not None:
+                _, part = lax.optimization_barrier((held[len(AXES) + stage], part))
             part = scatter_stage(part, axis, size)
+            done[len(AXES) + stage] = part
+        held = done
         results.append(part)
     return jnp.concatenate(results, axis=0).astype(jnp.bfloat16)
 

time: 122 us -> 113 us (0.926)
  waiting for transfers between devices: 71 us -> 59.7 us
  starting transfers between devices: 23.1 us -> 25.7 us
  matrix products: 14 us -> 12.7 us
    ppermute x10, waiting for transfers between devices: 41.5 us -> 30.3 us  [gather_stage(): got.append(lax.ppermute(block, axis, pairs))]
    ppermute x10, starting transfers between devices: 9.05 us -> 11.5 us  [scatter_stage(): lax.ppermute(pieces[shift].astype(jnp.bfloat16), axis, pairs)]
    dot_general x2, matrix products: 5.02 us -> 3.7 us  [expert_block(): jnp.dot(active, down_proj, preferred_element_type=jnp.float32)]
    unnamed x12 -> x14, local copies, waits for them, and re-layouts: 2.65 us -> 2.12 us
  transfers between devices with their start and end apart: 20 -> 20, of which waited for: 13 -> 11; matrix products, arithmetic and copies ran while one was open for 9% -> 15% of each run, Pallas kernels for 0% -> 0%
where the time goes in v10:
time: 113 us
  waiting for transfers between devices  59.7 us (53%)
  starting transfers between devices  25.7 us (23%)
  matrix products  12.7 us (11%)
  other arithmetic  7.1 us (6%)
  local copies, waits for them, and re-layouts  7.07 us (6%)
    ppermute x10, waiting for transfers between devices, gather_stage(): got.append(lax.ppermute(block, axis, pairs))  30.3 us
    ppermute x10, waiting for transfers between devices, scatter_stage(): lax.ppermute(pieces[shift].astype(jnp.bfloat16), axis, pairs)  29.4 us
    ppermute x10, starting transfers between devices, gather_stage(): got.append(lax.ppermute(block, axis, pairs))  14.2 us
    ppermute x10, starting transfers between devices, scatter_stage(): lax.ppermute(pieces[shift].astype(jnp.bfloat16), axis, pairs)  11.5 us
    dot_general x2, matrix products, expert_block(): pair = jnp.dot(rows_in, gate_up, preferred_element_type=jnp.float32)  9.02 us
    dot_general x2, matrix products, expert_block(): jnp.dot(active, down_proj, preferred_element_type=jnp.float32)  3.7 us
    concatenate x3, local copies, waits for them, and re-layouts, gather_stage(): return jnp.concatenate(got, axis=0)  2.44 us
  transfers between devices with their start and end apart: 20, of which 11 were waited for; matrix products, arithmetic and copies ran while one was open for 15% of the time, Pallas kernels for 0%

profile of v10, /device:TPU:0, one launch (start us, length us, event | category | flops | bytes accessed | tf_op | source)
XLA Modules:
  0.0 112.6 jit_solution(8000786222226398446)
XLA Ops:
  0.0 0.9 reduce_sum.36
  0.9 0.8 broadcast_divide_fusion
  1.7 0.8 select_reduce_fusion
  2.8 1.1 concatenate.30
  3.8 0.7 fusion.38
  4.5 3.1 %collective-permute-start = (bf16[32,2176]{1,0:T(8,128)(2,1)S(1)}, bf16[32,2176]{1,0:T(8,128)(2,1)S(1)}, u32[]{:S(2)}, u32[]{:S(2)}) collective-permute-start(bf16[32,2176]{1,0:T(8,128)(2,1)S(1)} %get-tuple-element.32), channel_id=1, source_target_pairs={{0,4},{4,8},{8,12},{12,0},{1,5},{5,9},{9,13},{13,1},{2,6},{6,10},{... | collective-permute-start | bytes 417800 | tf_op jit(solution)/shard_map/ppermute | solution.py:65
  7.6 2.6 %collective-permute-start.1 = (bf16[32,2176]{1,0:T(8,128)(2,1)S(1)}, bf16[32,2176]{1,0:T(8,128)(2,1)S(1)}, u32[]{:S(2)}, u32[]{:S(2)}) collective-permute-start(bf16[32,2176]{1,0:T(8,128)(2,1)S(1)} %get-tuple-element.32), channel_id=1, source_target_pairs={{0,8},{4,12},{8,0},{12,4},{1,9},{5,13},{9,1},{13,5},{2,10},{6,14},... | collective-permute-start | bytes 417800 | tf_op jit(solution)/shard_map/ppermute | solution.py:65
  10.2 1.3 %collective-permute-start.2 = (bf16[32,2176]{1,0:T(8,128)(2,1)S(1)}, bf16[32,2176]{1,0:T(8,128)(2,1)S(1)}, u32[]{:S(2)}, u32[]{:S(2)}) collective-permute-start(bf16[32,2176]{1,0:T(8,128)(2,1)S(1)} %get-tuple-element.32), channel_id=1, source_target_pairs={{0,12},{4,0},{8,4},{12,8},{1,13},{5,1},{9,5},{13,9},{2,14},{6,2},{... | collective-permute-start | bytes 417800 | tf_op jit(solution)/shard_map/ppermute | solution.py:65
  11.5 2.7 %collective-permute-done = bf16[32,2176]{1,0:T(8,128)(2,1)S(1)} collective-permute-done((bf16[32,2176]{1,0:T(8,128)(2,1)S(1)}, bf16[32,2176]{1,0:T(8,128)(2,1)S(1)}, u32[]{:S(2)}, u32[]{:S(2)}) %collective-permute-start) | collective-permute-done | bytes 139296 | tf_op jit(solution)/shard_map/ppermute | solution.py:65
  14.2 5.1 %collective-permute-done.1 = bf16[32,2176]{1,0:T(8,128)(2,1)S(1)} collective-permute-done((bf16[32,2176]{1,0:T(8,128)(2,1)S(1)}, bf16[32,2176]{1,0:T(8,128)(2,1)S(1)}, u32[]{:S(2)}, u32[]{:S(2)}) %collective-permute-start.1) | collective-permute-done | bytes 139296 | tf_op jit(solution)/shard_map/ppermute | solution.py:65
  19.4 1.6 %collective-permute-start.3 = (bf16[128,2176]{1,0:T(8,128)(2,1)S(1)}, bf16[128,2176]{1,0:T(8,128)(2,1)S(1)}, u32[]{:S(2)}, u32[]{:S(2)}) collective-permute-start(bf16[128,2176]{1,0:T(8,128)(2,1)S(1)} %pad_maximum_fusion.1), channel_id=1, source_target_pairs={{0,2},{2,0},{1,3},{3,1},{4,6},{6,4},{5,7},{7,5},{8,10},{10,8},{9,1... | collective-permute-start | bytes 1671176 | tf_op jit(solution)/shard_map/ppermute | solution.py:65
  20.9 4.5 %collective-permute-start.12 = (bf16[32,2176]{1,0:T(8,128)(2,1)S(1)}, bf16[32,2176]{1,0:T(8,128)(2,1)S(1)}, u32[]{:S(2)}, u32[]{:S(2)}) collective-permute-start(bf16[32,2176]{1,0:T(8,128)(2,1)S(1)} %get-tuple-element.11), channel_id=1, source_target_pairs={{0,12},{4,0},{8,4},{12,8},{1,13},{5,1},{9,5},{13,9},{2,14},{6,2},{... | collective-permute-start | bytes 417800 | tf_op jit(solution)/shard_map/ppermute | solution.py:65
  25.4 0.4 collective-permute-start.11
  25.8 0.2 collective-permute-start.10
  26.0 0.7 constant_dynamic-update-slice_fusion.3
  26.7 0.7 constant_dynamic-update-slice_fusion.2
  27.4 0.7 constant_dynamic-update-slice_fusion.1
  28.0 5.9 %collective-permute-done.3 = bf16[128,2176]{1,0:T(8,128)(2,1)S(1)} collective-permute-done((bf16[128,2176]{1,0:T(8,128)(2,1)S(1)}, bf16[128,2176]{1,0:T(8,128)(2,1)S(1)}, u32[]{:S(2)}, u32[]{:S(2)}) %collective-permute-start.3) | collective-permute-done | bytes 557088 | tf_op jit(solution)/shard_map/ppermute | solution.py:65
  33.9 0.9 constant_dynamic-update-slice_fusion
  34.8 3.3 %collective-permute-done.11 = bf16[32,2176]{1,0:T(8,128)(2,1)S(1)} collective-permute-done((bf16[32,2176]{1,0:T(8,128)(2,1)S(1)}, bf16[32,2176]{1,0:T(8,128)(2,1)S(1)}, u32[]{:S(2)}, u32[]{:S(2)}) %collective-permute-start.11) | collective-permute-done | bytes 139296 | tf_op jit(solution)/shard_map/ppermute | solution.py:65
  38.1 0.9 pad_maximum_fusion.2
  38.9 0.5 collective-permute-start.13
  39.5 13.4 %collective-permute-done.13 = bf16[128,2176]{1,0:T(8,128)(2,1)} collective-permute-done((bf16[128,2176]{1,0:T(8,128)(2,1)}, bf16[128,2176]{1,0:T(8,128)(2,1)}, u32[]{:S(2)}, u32[]{:S(2)}) %collective-permute-start.13) | collective-permute-done | bytes 557088 | tf_op jit(solution)/shard_map/ppermute | solution.py:65
  52.8 1.3 %pad_maximum_fusion = bf16[256,2176]{1,0:T(8,128)(2,1)S(1)} fusion(bf16[128,2176]{1,0:T(8,128)(2,1)} %collective-permute-done.13, bf16[128,2176]{1,0:T(8,128)(2,1)} %pad_maximum_fusion.2), kind=kLoop, calls=%fused_computation.22 | loop fusion | flops 2228224 | bytes 2228224 | tf_op jit(solution)/shard_map/concatenate | solution.py:66
  54.2 1.4 %constant_dynamic-update-slice_fusion.5 = bf16[512,2176]{1,0:T(8,128)(2,1)S(1)} fusion(bf16[512,2176]{1,0:T(8,128)(2,1)S(1)} %copy-done.2, bf16[256,2176]{1,0:T(8,128)(2,1)} %collective-permute-done.4), kind=kLoop, calls=%fused_computation.52 | loop fusion | bytes 2228224 | tf_op jit(solution)/shard_map/concatenate | solution.py:66
  55.8 5.6 %fusion.2 = f32[512,1536]{1,0:T(8,128)S(1)} fusion(bf16[1,2048,1536]{2,1,0:T(8,128)(2,1)} %param.10, bf16[512,2176]{1,0:T(8,128)(2,1)S(1)} %constant_dynamic-update-slice_fusion.5), kind=kOutput, calls=%fused_computation.2 | convolution fusion | flops 3221225472 | bytes 11534336 | tf_op jit(solution)/shard_map/dot_general | solution.py:9
  61.5 0.5 fusion.27
  62.1 1.9 %convert_multiply_fusion.1 = f32[512,2048]{1,0:T(8,128)S(1)} fusion(bf16[1,768,2048]{2,1,0:T(8,128)(2,1)S(1)} %copy-done, f32[512]{0:T(512)S(1)} %get-tuple-element.18, f32[512,1536]{1,0:T(8,128)S(1)} %fusion.2), kind=kOutput, calls=%fused_computation.5 | convolution fusion | flops 1616117760 | bytes 10487808 | tf_op jit(solution)/shard_map/dot_general | solution.py:11
  64.1 0.6 collective-permute-start.5
  64.7 3.4 %fusion = f32[512,1536]{1,0:T(8,128)S(1)} fusion(bf16[1,2048,1536]{2,1,0:T(8,128)(2,1)S(1)} %bitcast.19, bf16[512,2176]{1,0:T(8,128)(2,1)S(1)} %constant_dynamic-update-slice_fusion.11), kind=kOutput, calls=%fused_computation | convolution fusion | flops 3221225472 | bytes 11534336 | tf_op jit(solution)/shard_map/dot_general | solution.py:9
  68.1 0.3 slice_add_fusion
  68.6 0.6 collective-permute-start.6
  69.2 1.9 %convert_multiply_fusion = f32[512,2048]{1,0:T(8,128)S(1)} fusion(bf16[1,768,2048]{2,1,0:T(8,128)(2,1)S(1)} %copy-done, f32[512]{0:T(512)S(1)} %get-tuple-element.17, f32[512,1536]{1,0:T(8,128)S(1)} %fusion), kind=kOutput, calls=%fused_computation.4 | convolution fusion | flops 1616117760 | bytes 10487808 | tf_op jit(solution)/shard_map/dot_general | solution.py:11
  71.3 11.5 %collective-permute-done.6 = bf16[128,2048]{1,0:T(8,128)(2,1)S(1)} collective-permute-done((bf16[128,2048]{1,0:T(8,128)(2,1)S(1)}, bf16[128,2048]{1,0:T(8,128)(2,1)S(1)}, u32[]{:S(2)}, u32[]{:S(2)}) %collective-permute-start.6) | collective-permute-done | bytes 524320 | tf_op jit(solution)/shard_map/ppermute | solution.py:74
  83.0 1.8 %collective-permute-start.9 = (bf16[32,2048]{1,0:T(8,128)(2,1)S(1)}, bf16[32,2048]{1,0:T(8,128)(2,1)S(1)}, u32[]{:S(2)}, u32[]{:S(2)}) collective-permute-start(bf16[32,2048]{1,0:T(8,128)(2,1)S(1)} %get-tuple-element.27), channel_id=1, source_target_pairs={{0,4},{4,8},{8,12},{12,0},{1,5},{5,9},{9,13},{13,1},{2,6},{6,10},{... | collective-permute-start | bytes 393224 | tf_op jit(solution)/shard_map/ppermute | solution.py:74
  84.8 0.6 collective-permute-start.8
  85.4 1.8 %collective-permute-start.7 = (bf16[32,2048]{1,0:T(8,128)(2,1)S(1)}, bf16[32,2048]{1,0:T(8,128)(2,1)S(1)}, u32[]{:S(2)}, u32[]{:S(2)}) collective-permute-start(bf16[32,2048]{1,0:T(8,128)(2,1)S(1)} %get-tuple-element.26), channel_id=1, source_target_pairs={{0,12},{4,0},{8,4},{12,8},{1,13},{5,1},{9,5},{13,9},{2,14},{6,2},{... | collective-permute-start | bytes 393224 | tf_op jit(solution)/shard_map/ppermute | solution.py:74
  87.2 0.3 convert_add_fusion
  87.6 1.6 %collective-permute-start.16 = (bf16[128,2048]{1,0:T(8,128)(2,1)S(1)}, bf16[128,2048]{1,0:T(8,128)(2,1)S(1)}, u32[]{:S(2)}, u32[]{:S(2)}) collective-permute-start(bf16[128,2048]{1,0:T(8,128)(2,1)S(1)} %split.115), channel_id=1, source_target_pairs={{0,2},{2,0},{1,3},{3,1},{4,6},{6,4},{5,7},{7,5},{8,10},{10,8},{9,1... | collective-permute-start | bytes 1572872 | tf_op jit(solution)/shard_map/ppermute | solution.py:74
  89.2 2.1 %collective-permute-done.9 = bf16[32,2048]{1,0:T(8,128)(2,1)S(1)} collective-permute-done((bf16[32,2048]{1,0:T(8,128)(2,1)S(1)}, bf16[32,2048]{1,0:T(8,128)(2,1)S(1)}, u32[]{:S(2)}, u32[]{:S(2)}) %collective-permute-start.9) | collective-permute-done | bytes 131104 | tf_op jit(solution)/shard_map/ppermute | solution.py:74
  91.3 4.2 %collective-permute-done.8 = bf16[32,2048]{1,0:T(8,128)(2,1)S(1)} collective-permute-done((bf16[32,2048]{1,0:T(8,128)(2,1)S(1)}, bf16[32,2048]{1,0:T(8,128)(2,1)S(1)}, u32[]{:S(2)}, u32[]{:S(2)}) %collective-permute-start.8) | collective-permute-done | bytes 131104 | tf_op jit(solution)/shard_map/ppermute | solution.py:74
  95.5 4.9 %collective-permute-done.16 = bf16[128,2048]{1,0:T(8,128)(2,1)S(1)} collective-permute-done((bf16[128,2048]{1,0:T(8,128)(2,1)S(1)}, bf16[128,2048]{1,0:T(8,128)(2,1)S(1)}, u32[]{:S(2)}, u32[]{:S(2)}) %collective-permute-start.16) | collective-permute-done | bytes 524320 | tf_op jit(solution)/shard_map/ppermute | solution.py:74
  100.7 0.3 collective-permute-start.19
  101.0 2.0 %collective-permute-start.18 = (bf16[32,2048]{1,0:T(8,128)(2,1)S(1)}, bf16[32,2048]{1,0:T(8,128)(2,1)S(1)}, u32[]{:S(2)}, u32[]{:S(2)}) collective-permute-start(bf16[32,2048]{1,0:T(8,128)(2,1)S(1)} %get-tuple-element.25), channel_id=1, source_target_pairs={{0,8},{4,12},{8,0},{12,4},{1,9},{5,13},{9,1},{13,5},{2,10},{6,14},... | collective-permute-start | bytes 393224 | tf_op jit(solution)/shard_map/ppermute | solution.py:74
  103.0 2.1 %collective-permute-start.17 = (bf16[32,2048]{1,0:T(8,128)(2,1)S(1)}, bf16[32,2048]{1,0:T(8,128)(2,1)S(1)}, u32[]{:S(2)}, u32[]{:S(2)}) collective-permute-start(bf16[32,2048]{1,0:T(8,128)(2,1)S(1)} %get-tuple-element.23), channel_id=1, source_target_pairs={{0,12},{4,0},{8,4},{12,8},{1,13},{5,1},{9,5},{13,9},{2,14},{6,2},{... | collective-permute-start | bytes 393224 | tf_op jit(solution)/shard_map/ppermute | solution.py:74
  105.1 3.8 %collective-permute-done.19 = bf16[32,2048]{1,0:T(8,128)(2,1)S(1)} collective-permute-done((bf16[32,2048]{1,0:T(8,128)(2,1)S(1)}, bf16[32,2048]{1,0:T(8,128)(2,1)S(1)}, u32[]{:S(2)}, u32[]{:S(2)}) %collective-permute-start.19) | collective-permute-done | bytes 131104 | tf_op jit(solution)/shard_map/ppermute | solution.py:74
  108.9 2.9 %collective-permute-done.18 = bf16[32,2048]{1,0:T(8,128)(2,1)S(1)} collective-permute-done((bf16[32,2048]{1,0:T(8,128)(2,1)S(1)}, bf16[32,2048]{1,0:T(8,128)(2,1)S(1)}, u32[]{:S(2)}, u32[]{:S(2)}) %collective-permute-start.18) | collective-permute-done | bytes 131104 | tf_op jit(solution)/shard_map/ppermute | solution.py:74
  111.9 0.7 pad_maximum_fusion.3
  (45 shorter events, 1.8 us)
Async XLA Ops:
  0.0 62.1 %copy-start = (bf16[1,768,2048]{2,1,0:T(8,128)(2,1)S(1)}, bf16[1,768,2048]{2,1,0:T(8,128)(2,1)}, u32[]{:S(2)}) copy-start(bf16[1,768,2048]{2,1,0:T(8,128)(2,1)} %param.11) | copy-start | bytes 9437188
  4.5 9.7 %collective-permute-start = (bf16[32,2176]{1,0:T(8,128)(2,1)S(1)}, bf16[32,2176]{1,0:T(8,128)(2,1)S(1)}, u32[]{:S(2)}, u32[]{:S(2)}) collective-permute-start(bf16[32,2176]{1,0:T(8,128)(2,1)S(1)} %get-tuple-element.32), channel_id=1, source_target_pairs={{0,4},{4,8},{8,12},{12,0},{1,5},{5,9},{9,13},{13,1},{2,6},{6,10},{... | collective-permute-start | bytes 417800 | tf_op jit(solution)/shard_map/ppermute | solution.py:65
  7.6 11.8 %collective-permute-start.1 = (bf16[32,2176]{1,0:T(8,128)(2,1)S(1)}, bf16[32,2176]{1,0:T(8,128)(2,1)S(1)}, u32[]{:S(2)}, u32[]{:S(2)}) collective-permute-start(bf16[32,2176]{1,0:T(8,128)(2,1)S(1)} %get-tuple-element.32), channel_id=1, source_target_pairs={{0,8},{4,12},{8,0},{12,4},{1,9},{5,13},{9,1},{13,5},{2,10},{6,14},... | collective-permute-start | bytes 417800 | tf_op jit(solution)/shard_map/ppermute | solution.py:65
  10.2 9.2 %collective-permute-start.2 = (bf16[32,2176]{1,0:T(8,128)(2,1)S(1)}, bf16[32,2176]{1,0:T(8,128)(2,1)S(1)}, u32[]{:S(2)}, u32[]{:S(2)}) collective-permute-start(bf16[32,2176]{1,0:T(8,128)(2,1)S(1)} %get-tuple-element.32), channel_id=1, source_target_pairs={{0,12},{4,0},{8,4},{12,8},{1,13},{5,1},{9,5},{13,9},{2,14},{6,2},{... | collective-permute-start | bytes 417800 | tf_op jit(solution)/shard_map/ppermute | solution.py:65
  19.4 14.5 %collective-permute-start.3 = (bf16[128,2176]{1,0:T(8,128)(2,1)S(1)}, bf16[128,2176]{1,0:T(8,128)(2,1)S(1)}, u32[]{:S(2)}, u32[]{:S(2)}) collective-permute-start(bf16[128,2176]{1,0:T(8,128)(2,1)S(1)} %pad_maximum_fusion.1), channel_id=1, source_target_pairs={{0,2},{2,0},{1,3},{3,1},{4,6},{6,4},{5,7},{7,5},{8,10},{10,8},{9,1... | collective-permute-start | bytes 1671176 | tf_op jit(solution)/shard_map/ppermute | solution.py:65
  20.9 13.9 %collective-permute-start.12 = (bf16[32,2176]{1,0:T(8,128)(2,1)S(1)}, bf16[32,2176]{1,0:T(8,128)(2,1)S(1)}, u32[]{:S(2)}, u32[]{:S(2)}) collective-permute-start(bf16[32,2176]{1,0:T(8,128)(2,1)S(1)} %get-tuple-element.11), channel_id=1, source_target_pairs={{0,12},{4,0},{8,4},{12,8},{1,13},{5,1},{9,5},{13,9},{2,14},{6,2},{... | collective-permute-start | bytes 417800 | tf_op jit(solution)/shard_map/ppermute | solution.py:65
  25.4 12.6 %collective-permute-start.11 = (bf16[32,2176]{1,0:T(8,128)(2,1)S(1)}, bf16[32,2176]{1,0:T(8,128)(2,1)S(1)}, u32[]{:S(2)}, u32[]{:S(2)}) collective-permute-start(bf16[32,2176]{1,0:T(8,128)(2,1)S(1)} %get-tuple-element.11), channel_id=1, source_target_pairs={{0,8},{4,12},{8,0},{12,4},{1,9},{5,13},{9,1},{13,5},{2,10},{6,14},... | collective-permute-start | bytes 417800 | tf_op jit(solution)/shard_map/ppermute | solution.py:65
  25.8 12.2 %collective-permute-start.10 = (bf16[32,2176]{1,0:T(8,128)(2,1)S(1)}, bf16[32,2176]{1,0:T(8,128)(2,1)S(1)}, u32[]{:S(2)}, u32[]{:S(2)}) collective-permute-start(bf16[32,2176]{1,0:T(8,128)(2,1)S(1)} %get-tuple-element.11), channel_id=1, source_target_pairs={{0,4},{4,8},{8,12},{12,0},{1,5},{5,9},{9,13},{13,1},{2,6},{6,10},{... | collective-permute-start | bytes 417800 | tf_op jit(solution)/shard_map/ppermute | solution.py:65
  34.8 4.2 %copy-start.1 = (bf16[512,2176]{1,0:T(8,128)(2,1)}, bf16[512,2176]{1,0:T(8,128)(2,1)S(1)}, u32[]{:S(2)}) copy-start(bf16[512,2176]{1,0:T(8,128)(2,1)S(1)} %get-tuple-element.22) | copy-start | bytes 6684676
  34.8 19.4 %collective-permute-start.4 = (bf16[256,2176]{1,0:T(8,128)(2,1)}, bf16[256,2176]{1,0:T(8,128)(2,1)}, u32[]{:S(2)}, u32[]{:S(2)}) collective-permute-start(bf16[256,2176]{1,0:T(8,128)(2,1)} %get-tuple-element.21), channel_id=1, source_target_pairs={{0,1},{1,0},{2,3},{3,2},{4,5},{5,4},{6,7},{7,6},{8,9},{9,8},{10,11... | collective-permute-start | bytes 3342344 | tf_op jit(solution)/shard_map/ppermute | solution.py:65
  38.9 13.9 %collective-permute-start.13 = (bf16[128,2176]{1,0:T(8,128)(2,1)}, bf16[128,2176]{1,0:T(8,128)(2,1)}, u32[]{:S(2)}, u32[]{:S(2)}) collective-permute-start(bf16[128,2176]{1,0:T(8,128)(2,1)} %pad_maximum_fusion.2), channel_id=1, source_target_pairs={{0,2},{2,0},{1,3},{3,1},{4,6},{6,4},{5,7},{7,5},{8,10},{10,8},{9,1... | collective-permute-start | bytes 1671176 | tf_op jit(solution)/shard_map/ppermute | solution.py:65
  39.5 14.7 %copy-start.2 = (bf16[512,2176]{1,0:T(8,128)(2,1)S(1)}, bf16[512,2176]{1,0:T(8,128)(2,1)}, u32[]{:S(2)}) copy-start(bf16[512,2176]{1,0:T(8,128)(2,1)} %copy-done.1) | copy-start | bytes 6684676
  55.6 5.7 %collective-permute-start.14 = (bf16[256,2176]{1,0:T(8,128)(2,1)S(1)}, bf16[256,2176]{1,0:T(8,128)(2,1)S(1)}, u32[]{:S(2)}, u32[]{:S(2)}) collective-permute-start(bf16[256,2176]{1,0:T(8,128)(2,1)S(1)} %pad_maximum_fusion), channel_id=1, source_target_pairs={{0,1},{1,0},{2,3},{3,2},{4,5},{5,4},{6,7},{7,6},{8,9},{9,8},{10,11... | collective-permute-start | bytes 3342344 | tf_op jit(solution)/shard_map/ppermute | solution.py:65
  61.5 3.1 %slice-start = ((s8[6291456]{0:T(1024)(128)(4,1)}), s8[4194304]{0:T(1024)(128)(4,1)S(1)}, s32[]{:S(2)}) async-start(s8[6291456]{0:T(1024)(128)(4,1)} %bitcast.18), calls=%async_computation | async-start | bytes 8388608
  62.1 2.6 %slice-start.1 = ((s8[6291456]{0:T(1024)(128)(4,1)}), s8[2097152]{0:T(1024)(128)(4,1)S(1)}, s32[]{:S(2)}) async-start(s8[6291456]{0:T(1024)(128)(4,1)} %bitcast.18), calls=%async_computation.1 | async-start | bytes 4194304
  64.1 4.0 %collective-permute-start.5 = (bf16[256,2048]{1,0:T(8,128)(2,1)S(1)}, bf16[256,2048]{1,0:T(8,128)(2,1)S(1)}, u32[]{:S(2)}, u32[]{:S(2)}) collective-permute-start(bf16[256,2048]{1,0:T(8,128)(2,1)S(1)} %split.114), channel_id=1, source_target_pairs={{0,1},{1,0},{2,3},{3,2},{4,5},{5,4},{6,7},{7,6},{8,9},{9,8},{10,11... | collective-permute-start | bytes 3145736 | tf_op jit(solution)/shard_map/ppermute | solution.py:74
  68.6 14.3 %collective-permute-start.6 = (bf16[128,2048]{1,0:T(8,128)(2,1)S(1)}, bf16[128,2048]{1,0:T(8,128)(2,1)S(1)}, u32[]{:S(2)}, u32[]{:S(2)}) collective-permute-start(bf16[128,2048]{1,0:T(8,128)(2,1)S(1)} %split.116), channel_id=1, source_target_pairs={{0,2},{2,0},{1,3},{3,1},{4,6},{6,4},{5,7},{7,5},{8,10},{10,8},{9,1... | collective-permute-start | bytes 1572872 | tf_op jit(solution)/shard_map/ppermute | solution.py:74
  71.2 16.1 %collective-permute-start.15 = (bf16[256,2048]{1,0:T(8,128)(2,1)S(1)}, bf16[256,2048]{1,0:T(8,128)(2,1)S(1)}, u32[]{:S(2)}, u32[]{:S(2)}) collective-permute-start(bf16[256,2048]{1,0:T(8,128)(2,1)S(1)} %split.113), channel_id=1, source_target_pairs={{0,1},{1,0},{2,3},{3,2},{4,5},{5,4},{6,7},{7,6},{8,9},{9,8},{10,11... | collective-permute-start | bytes 3145736 | tf_op jit(solution)/shard_map/ppermute | solution.py:74
  83.0 8.3 %collective-permute-start.9 = (bf16[32,2048]{1,0:T(8,128)(2,1)S(1)}, bf16[32,2048]{1,0:T(8,128)(2,1)S(1)}, u32[]{:S(2)}, u32[]{:S(2)}) collective-permute-start(bf16[32,2048]{1,0:T(8,128)(2,1)S(1)} %get-tuple-element.27), channel_id=1, source_target_pairs={{0,4},{4,8},{8,12},{12,0},{1,5},{5,9},{9,13},{13,1},{2,6},{6,10},{... | collective-permute-start | bytes 393224 | tf_op jit(solution)/shard_map/ppermute | solution.py:74
  84.8 10.7 %collective-permute-start.8 = (bf16[32,2048]{1,0:T(8,128)(2,1)S(1)}, bf16[32,2048]{1,0:T(8,128)(2,1)S(1)}, u32[]{:S(2)}, u32[]{:S(2)}) collective-permute-start(bf16[32,2048]{1,0:T(8,128)(2,1)S(1)} %get-tuple-element.28), channel_id=1, source_target_pairs={{0,8},{4,12},{8,0},{12,4},{1,9},{5,13},{9,1},{13,5},{2,10},{6,14},... | collective-permute-start | bytes 393224 | tf_op jit(solution)/shard_map/ppermute | solution.py:74
  85.4 10.1 %collective-permute-start.7 = (bf16[32,2048]{1,0:T(8,128)(2,1)S(1)}, bf16[32,2048]{1,0:T(8,128)(2,1)S(1)}, u32[]{:S(2)}, u32[]{:S(2)}) collective-permute-start(bf16[32,2048]{1,0:T(8,128)(2,1)S(1)} %get-tuple-element.26), channel_id=1, source_target_pairs={{0,12},{4,0},{8,4},{12,8},{1,13},{5,1},{9,5},{13,9},{2,14},{6,2},{... | collective-permute-start | bytes 393224 | tf_op jit(solution)/shard_map/ppermute | solution.py:74
  87.6 12.8 %collective-permute-start.16 = (bf16[128,2048]{1,0:T(8,128)(2,1)S(1)}, bf16[128,2048]{1,0:T(8,128)(2,1)S(1)}, u32[]{:S(2)}, u32[]{:S(2)}) collective-permute-start(bf16[128,2048]{1,0:T(8,128)(2,1)S(1)} %split.115), channel_id=1, source_target_pairs={{0,2},{2,0},{1,3},{3,1},{4,6},{6,4},{5,7},{7,5},{8,10},{10,8},{9,1... | collective-permute-start | bytes 1572872 | tf_op jit(solution)/shard_map/ppermute | solution.py:74
  100.7 8.2 %collective-permute-start.19 = (bf16[32,2048]{1,0:T(8,128)(2,1)S(1)}, bf16[32,2048]{1,0:T(8,128)(2,1)S(1)}, u32[]{:S(2)}, u32[]{:S(2)}) collective-permute-start(bf16[32,2048]{1,0:T(8,128)(2,1)S(1)} %get-tuple-element.24), channel_id=1, source_target_pairs={{0,4},{4,8},{8,12},{12,0},{1,5},{5,9},{9,13},{13,1},{2,6},{6,10},{... | collective-permute-start | bytes 393224 | tf_op jit(solution)/shard_map/ppermute | solution.py:74
  101.0 10.8 %collective-permute-start.18 = (bf16[32,2048]{1,0:T(8,128)(2,1)S(1)}, bf16[32,2048]{1,0:T(8,128)(2,1)S(1)}, u32[]{:S(2)}, u32[]{:S(2)}) collective-permute-start(bf16[32,2048]{1,0:T(8,128)(2,1)S(1)} %get-tuple-element.25), channel_id=1, source_target_pairs={{0,8},{4,12},{8,0},{12,4},{1,9},{5,13},{9,1},{13,5},{2,10},{6,14},... | collective-permute-start | bytes 393224 | tf_op jit(solution)/shard_map/ppermute | solution.py:74
  103.0 8.8 %collective-permute-start.17 = (bf16[32,2048]{1,0:T(8,128)(2,1)S(1)}, bf16[32,2048]{1,0:T(8,128)(2,1)S(1)}, u32[]{:S(2)}, u32[]{:S(2)}) collective-permute-start(bf16[32,2048]{1,0:T(8,128)(2,1)S(1)} %get-tuple-element.23), channel_id=1, source_target_pairs={{0,12},{4,0},{8,4},{12,8},{1,13},{5,1},{9,5},{13,9},{2,14},{6,2},{... | collective-permute-start | bytes 393224 | tf_op jit(solution)/shard_map/ppermute | solution.py:74

commit v11 on v5

--- a/solution.py
+++ b/solution.py
@@ -95,13 +95,8 @@
     carried = jnp.concatenate([tokens, meta], axis=1)
     pick = (jnp.arange(hosts, dtype=jnp.int32) == me).astype(jnp.float32)
     results = []
-    held = None
     for rows in jnp.split(carried, STREAMS, axis=0):
-        if held is not None:
-            held, rows = lax.optimization_barrier((held, rows))
-        rows = gather_stage(rows, AXES[0], sizes[0])
-        held = rows
-        for axis, size in zip(AXES[1:], sizes[1:]):
+        for axis, size in zip(AXES, sizes):
             rows = gather_stage(rows, axis, size)
         tail = rows[:, width_model:width_model + 3 * hosts].astype(jnp.float32)
         gate = tail[:, :hosts] + tail[:, hosts:2 * hosts] + tail[:, 2 * hosts:]

time: 106 us -> 117 us (1.10)
  starting transfers between devices: 29.1 us -> 40.3 us
  waiting for transfers between devices: 48.5 us -> 43.9 us
  local copies, waits for them, and re-layouts: 10.8 us -> 14 us
  matrix products: 10.6 us -> 12.8 us
    ppermute x10, starting transfers between devices: 13.9 us -> 24.7 us  [scatter_stage(): lax.ppermute(pieces[shift].astype(jnp.bfloat16), axis, pairs)]
    concatenate x4, local copies, waits for them, and re-layouts: 1.51 us -> 5.87 us  [gather_stage(): return jnp.concatenate(got, axis=0)]
    ppermute x10, waiting for transfers between devices: 25 us -> 22.5 us  [scatter_stage(): lax.ppermute(pieces[shift].astype(jnp.bfloat16), axis, pairs)]
    dot_general x2, matrix products: 6.9 us -> 9.13 us  [expert_block(): pair = jnp.dot(rows_in, gate_up, preferred_element_type=jnp.float32)]
    ppermute x10, waiting for transfers between devices: 23.5 us -> 21.4 us  [gather_stage(): got.append(lax.ppermute(block, axis, pairs))]
    split x1 -> x0, local copies, waits for them, and re-layouts: 1.74 us -> none  [dense_shards(): jnp.split(carried, STREAMS, axis=0)]
    unnamed x13 -> x21, local copies, waits for them, and re-layouts: 5 us -> 6.33 us
    concatenate x2, other arithmetic: 1.27 us -> 0.08 us  [gather_stage(): return jnp.concatenate(got, axis=0)]
  transfers between devices with their start and end apart: 20 -> 20, of which waited for: 10 -> 12; matrix products, arithmetic and copies ran while one was open for 12% -> 11% of each run, Pallas kernels for 0% -> 0%
where the time goes in v11:
time: 117 us
  waiting for transfers between devices  43.9 us (38%)
  starting transfers between devices  40.3 us (34%)
  local copies, waits for them, and re-layouts  14 us (12%)
  matrix products  12.8 us (11%)
  other arithmetic  5.84 us (5%)
    ppermute x10, starting transfers between devices, scatter_stage(): lax.ppermute(pieces[shift].astype(jnp.bfloat16), axis, pairs)  24.7 us
    ppermute x10, waiting for transfers between devices, scatter_stage(): lax.ppermute(pieces[shift].astype(jnp.bfloat16), axis, pairs)  22.5 us
    ppermute x10, waiting for transfers between devices, gather_stage(): got.append(lax.ppermute(block, axis, pairs))  21.4 us
    ppermute x10, starting transfers between devices, gather_stage(): got.append(lax.ppermute(block, axis, pairs))  15.5 us
    dot_general x2, matrix products, expert_block(): pair = jnp.dot(rows_in, gate_up, preferred_element_type=jnp.float32)  9.13 us
    unnamed x21, local copies, waits for them, and re-layouts  6.33 us
    concatenate x4, local copies, waits for them, and re-layouts, gather_stage(): return jnp.concatenate(got, axis=0)  5.87 us
    dot_general x2, matrix products, expert_block(): jnp.dot(active, down_proj, preferred_element_type=jnp.float32)  3.69 us
  transfers between devices with their start and end apart: 20, of which 12 were waited for; matrix products, arithmetic and copies ran while one was open for 11% of the time, Pallas kernels for 0%

profile of v11, /device:TPU:0, one launch (start us, length us, event | category | flops | bytes accessed | tf_op | source)
XLA Modules:
  0.0 117.2 jit_solution(16121809861615578162)
XLA Ops:
  0.0 0.9 reduce_sum.36
  0.9 0.8 broadcast_divide_fusion
  1.7 0.8 select_reduce_fusion
  2.8 1.1 concatenate.32
  3.8 0.8 constant_dynamic-update-slice_fusion.15
  4.6 3.1 %collective-permute-start.10 = (bf16[32,2176]{1,0:T(8,128)(2,1)S(1)}, bf16[32,2176]{1,0:T(8,128)(2,1)S(1)}, u32[]{:S(2)}, u32[]{:S(2)}) collective-permute-start(bf16[32,2176]{1,0:T(8,128)(2,1)S(1)} %get-tuple-element.25), channel_id=1, source_target_pairs={{0,4},{4,8},{8,12},{12,0},{1,5},{5,9},{9,13},{13,1},{2,6},{6,10},{... | collective-permute-start | bytes 417800 | tf_op jit(solution)/shard_map/ppermute | solution.py:65
  7.7 2.6 %collective-permute-start.11 = (bf16[32,2176]{1,0:T(8,128)(2,1)S(1)}, bf16[32,2176]{1,0:T(8,128)(2,1)S(1)}, u32[]{:S(2)}, u32[]{:S(2)}) collective-permute-start(bf16[32,2176]{1,0:T(8,128)(2,1)S(1)} %get-tuple-element.25), channel_id=1, source_target_pairs={{0,8},{4,12},{8,0},{12,4},{1,9},{5,13},{9,1},{13,5},{2,10},{6,14},... | collective-permute-start | bytes 417800 | tf_op jit(solution)/shard_map/ppermute | solution.py:65
  10.3 1.3 %collective-permute-start.12 = (bf16[32,2176]{1,0:T(8,128)(2,1)S(1)}, bf16[32,2176]{1,0:T(8,128)(2,1)S(1)}, u32[]{:S(2)}, u32[]{:S(2)}) collective-permute-start(bf16[32,2176]{1,0:T(8,128)(2,1)S(1)} %get-tuple-element.25), channel_id=1, source_target_pairs={{0,12},{4,0},{8,4},{12,8},{1,13},{5,1},{9,5},{13,9},{2,14},{6,2},{... | collective-permute-start | bytes 417800 | tf_op jit(solution)/shard_map/ppermute | solution.py:65
  11.6 0.7 collective-permute-start
  12.3 0.3 collective-permute-start.1
  12.7 1.7 %collective-permute-done.10 = bf16[32,2176]{1,0:T(8,128)(2,1)S(1)} collective-permute-done((bf16[32,2176]{1,0:T(8,128)(2,1)S(1)}, bf16[32,2176]{1,0:T(8,128)(2,1)S(1)}, u32[]{:S(2)}, u32[]{:S(2)}) %collective-permute-start.10) | collective-permute-done | bytes 139296 | tf_op jit(solution)/shard_map/ppermute | solution.py:65
  14.3 2.5 %collective-permute-start.2 = (bf16[32,2176]{1,0:T(8,128)(2,1)S(1)}, bf16[32,2176]{1,0:T(8,128)(2,1)S(1)}, u32[]{:S(2)}, u32[]{:S(2)}) collective-permute-start(bf16[32,2176]{1,0:T(8,128)(2,1)S(1)} %get-tuple-element.26), channel_id=1, source_target_pairs={{0,12},{4,0},{8,4},{12,8},{1,13},{5,1},{9,5},{13,9},{2,14},{6,2},{... | collective-permute-start | bytes 417800 | tf_op jit(solution)/shard_map/ppermute | solution.py:65
  16.8 3.5 %collective-permute-done.11 = bf16[32,2176]{1,0:T(8,128)(2,1)S(1)} collective-permute-done((bf16[32,2176]{1,0:T(8,128)(2,1)S(1)}, bf16[32,2176]{1,0:T(8,128)(2,1)S(1)}, u32[]{:S(2)}, u32[]{:S(2)}) %collective-permute-start.11) | collective-permute-done | bytes 139296 | tf_op jit(solution)/shard_map/ppermute | solution.py:65
  20.4 2.2 %collective-permute-done.12 = bf16[32,2176]{1,0:T(8,128)(2,1)S(1)} collective-permute-done((bf16[32,2176]{1,0:T(8,128)(2,1)S(1)}, bf16[32,2176]{1,0:T(8,128)(2,1)S(1)}, u32[]{:S(2)}, u32[]{:S(2)}) %collective-permute-start.12) | collective-permute-done | bytes 139296 | tf_op jit(solution)/shard_map/ppermute | solution.py:65
  22.6 3.5 %collective-permute-start.13 = (bf16[128,2176]{1,0:T(8,128)(2,1)S(1)}, bf16[128,2176]{1,0:T(8,128)(2,1)S(1)}, u32[]{:S(2)}, u32[]{:S(2)}) collective-permute-start(bf16[128,2176]{1,0:T(8,128)(2,1)S(1)} %pad_maximum_fusion.1), channel_id=1, source_target_pairs={{0,2},{2,0},{1,3},{3,1},{4,6},{6,4},{5,7},{7,5},{8,10},{10,8},{9,1... | collective-permute-start | bytes 1671176 | tf_op jit(solution)/shard_map/ppermute | solution.py:65
  26.1 5.3 %collective-permute-done.1 = bf16[32,2176]{1,0:T(8,128)(2,1)S(1)} collective-permute-done((bf16[32,2176]{1,0:T(8,128)(2,1)S(1)}, bf16[32,2176]{1,0:T(8,128)(2,1)S(1)}, u32[]{:S(2)}, u32[]{:S(2)}) %collective-permute-start.1) | collective-permute-done | bytes 139296 | tf_op jit(solution)/shard_map/ppermute | solution.py:65
  31.5 1.6 %collective-permute-start.3 = (bf16[128,2176]{1,0:T(8,128)(2,1)S(1)}, bf16[128,2176]{1,0:T(8,128)(2,1)S(1)}, u32[]{:S(2)}, u32[]{:S(2)}) collective-permute-start(bf16[128,2176]{1,0:T(8,128)(2,1)S(1)} %pad_maximum_fusion), channel_id=1, source_target_pairs={{0,2},{2,0},{1,3},{3,1},{4,6},{6,4},{5,7},{7,5},{8,10},{10,8},{9,1... | collective-permute-start | bytes 1671176 | tf_op jit(solution)/shard_map/ppermute | solution.py:65
  33.0 0.7 constant_dynamic-update-slice_fusion.14
  33.7 0.7 constant_dynamic-update-slice_fusion.13
  34.4 0.7 constant_dynamic-update-slice_fusion.12
  35.1 0.7 constant_dynamic-update-slice_fusion.3
  35.7 0.7 constant_dynamic-update-slice_fusion.2
  36.4 1.0 constant_dynamic-update-slice_fusion.11
  37.4 0.7 constant_dynamic-update-slice_fusion.1
  38.1 8.7 %collective-permute-done.3 = bf16[128,2176]{1,0:T(8,128)(2,1)S(1)} collective-permute-done((bf16[128,2176]{1,0:T(8,128)(2,1)S(1)}, bf16[128,2176]{1,0:T(8,128)(2,1)S(1)}, u32[]{:S(2)}, u32[]{:S(2)}) %collective-permute-start.3) | collective-permute-done | bytes 557088 | tf_op jit(solution)/shard_map/ppermute | solution.py:65
  46.8 0.9 constant_dynamic-update-slice_fusion
  47.7 1.4 %copy-done.1 = bf16[512,2176]{1,0:T(8,128)(2,1)} copy-done((bf16[512,2176]{1,0:T(8,128)(2,1)}, bf16[512,2176]{1,0:T(8,128)(2,1)S(1)}, u32[]{:S(2)}) %copy-start.1) | copy-done | bytes 2228248
  49.1 2.5 %constant_dynamic-update-slice_fusion.16 = bf16[512,2176]{1,0:T(8,128)(2,1)} fusion(bf16[512,2176]{1,0:T(8,128)(2,1)} %copy-done.3, bf16[256,2176]{1,0:T(8,128)(2,1)} %collective-permute-done.14), kind=kLoop, calls=%fused_computation.66 | loop fusion | bytes 2228224 | tf_op jit(solution)/shard_map/concatenate | solution.py:66
  51.5 0.9 slice_convert_fusion.4
  52.5 1.5 %constant_dynamic-update-slice_fusion.5 = bf16[512,2176]{1,0:T(8,128)(2,1)S(1)} fusion(bf16[512,2176]{1,0:T(8,128)(2,1)S(1)} %copy-done.2, bf16[256,2176]{1,0:T(8,128)(2,1)} %collective-permute-done.4), kind=kLoop, calls=%fused_computation.55 | loop fusion | bytes 2228224 | tf_op jit(solution)/shard_map/concatenate | solution.py:66
  54.1 5.7 %fusion.2 = f32[512,1536]{1,0:T(8,128)S(1)} fusion(bf16[1,2048,1536]{2,1,0:T(8,128)(2,1)} %param.10, bf16[512,2176]{1,0:T(8,128)(2,1)S(1)} %constant_dynamic-update-slice_fusion.5), kind=kOutput, calls=%fused_computation.2 | convolution fusion | flops 3221225472 | bytes 11534336 | tf_op jit(solution)/shard_map/dot_general | solution.py:9
  59.8 3.4 %fusion = f32[512,1536]{1,0:T(8,128)S(1)} fusion(bf16[1,2048,1536]{2,1,0:T(8,128)(2,1)S(1)} %bitcast.19, bf16[512,2176]{1,0:T(8,128)(2,1)S(1)} %copy-done.4), kind=kOutput, calls=%fused_computation | convolution fusion | flops 3221225472 | bytes 11534336 | tf_op jit(solution)/shard_map/dot_general | solution.py:9
  63.3 0.5 fusion.35
  63.8 1.8 %convert_multiply_fusion.1 = f32[512,2048]{1,0:T(8,128)S(1)} fusion(bf16[1,768,2048]{2,1,0:T(8,128)(2,1)S(1)} %copy-done, f32[512]{0:T(512)S(1)} %get-tuple-element.5, f32[512,1536]{1,0:T(8,128)S(1)} %fusion.2), kind=kOutput, calls=%fused_computation.5 | convolution fusion | flops 1616117760 | bytes 10487808 | tf_op jit(solution)/shard_map/dot_general | solution.py:11
  65.8 0.6 collective-permute-start.5
  66.4 1.8 %convert_multiply_fusion = f32[512,2048]{1,0:T(8,128)S(1)} fusion(bf16[1,768,2048]{2,1,0:T(8,128)(2,1)S(1)} %copy-done, f32[512]{0:T(512)S(1)} %get-tuple-element.6, f32[512,1536]{1,0:T(8,128)S(1)} %fusion), kind=kOutput, calls=%fused_computation.4 | convolution fusion | flops 1616117760 | bytes 10487808 | tf_op jit(solution)/shard_map/dot_general | solution.py:11
  68.7 0.3 slice_add_fusion.1
  69.1 1.8 %collective-permute-start.6 = (bf16[128,2048]{1,0:T(8,128)(2,1)S(1)}, bf16[128,2048]{1,0:T(8,128)(2,1)S(1)}, u32[]{:S(2)}, u32[]{:S(2)}) collective-permute-start(bf16[128,2048]{1,0:T(8,128)(2,1)S(1)} %split.129), channel_id=1, source_target_pairs={{0,2},{2,0},{1,3},{3,1},{4,6},{6,4},{5,7},{7,5},{8,10},{10,8},{9,1... | collective-permute-start | bytes 1572872 | tf_op jit(solution)/shard_map/ppermute | solution.py:74
  71.1 0.3 slice_add_fusion
  71.5 1.8 %collective-permute-start.16 = (bf16[128,2048]{1,0:T(8,128)(2,1)S(1)}, bf16[128,2048]{1,0:T(8,128)(2,1)S(1)}, u32[]{:S(2)}, u32[]{:S(2)}) collective-permute-start(bf16[128,2048]{1,0:T(8,128)(2,1)S(1)} %split.128), channel_id=1, source_target_pairs={{0,2},{2,0},{1,3},{3,1},{4,6},{6,4},{5,7},{7,5},{8,10},{10,8},{9,1... | collective-permute-start | bytes 1572872 | tf_op jit(solution)/shard_map/ppermute | solution.py:74
  73.3 10.6 %collective-permute-done.6 = bf16[128,2048]{1,0:T(8,128)(2,1)S(1)} collective-permute-done((bf16[128,2048]{1,0:T(8,128)(2,1)S(1)}, bf16[128,2048]{1,0:T(8,128)(2,1)S(1)}, u32[]{:S(2)}, u32[]{:S(2)}) %collective-permute-start.6) | collective-permute-done | bytes 524320 | tf_op jit(solution)/shard_map/ppermute | solution.py:74
  84.1 6.0 %collective-permute-start.7 = (bf16[32,2048]{1,0:T(8,128)(2,1)S(1)}, bf16[32,2048]{1,0:T(8,128)(2,1)S(1)}, u32[]{:S(2)}, u32[]{:S(2)}) collective-permute-start(bf16[32,2048]{1,0:T(8,128)(2,1)S(1)} %get-tuple-element.15), channel_id=1, source_target_pairs={{0,12},{4,0},{8,4},{12,8},{1,13},{5,1},{9,5},{13,9},{2,14},{6,2},{... | collective-permute-start | bytes 393224 | tf_op jit(solution)/shard_map/ppermute | solution.py:74
  90.1 4.3 %collective-permute-start.8 = (bf16[32,2048]{1,0:T(8,128)(2,1)S(1)}, bf16[32,2048]{1,0:T(8,128)(2,1)S(1)}, u32[]{:S(2)}, u32[]{:S(2)}) collective-permute-start(bf16[32,2048]{1,0:T(8,128)(2,1)S(1)} %get-tuple-element.17), channel_id=1, source_target_pairs={{0,8},{4,12},{8,0},{12,4},{1,9},{5,13},{9,1},{13,5},{2,10},{6,14},... | collective-permute-start | bytes 393224 | tf_op jit(solution)/shard_map/ppermute | solution.py:74
  94.8 6.0 %collective-permute-start.17 = (bf16[32,2048]{1,0:T(8,128)(2,1)S(1)}, bf16[32,2048]{1,0:T(8,128)(2,1)S(1)}, u32[]{:S(2)}, u32[]{:S(2)}) collective-permute-start(bf16[32,2048]{1,0:T(8,128)(2,1)S(1)} %get-tuple-element.18), channel_id=1, source_target_pairs={{0,12},{4,0},{8,4},{12,8},{1,13},{5,1},{9,5},{13,9},{2,14},{6,2},{... | collective-permute-start | bytes 393224 | tf_op jit(solution)/shard_map/ppermute | solution.py:74
  100.8 4.3 %collective-permute-start.18 = (bf16[32,2048]{1,0:T(8,128)(2,1)S(1)}, bf16[32,2048]{1,0:T(8,128)(2,1)S(1)}, u32[]{:S(2)}, u32[]{:S(2)}) collective-permute-start(bf16[32,2048]{1,0:T(8,128)(2,1)S(1)} %get-tuple-element.20), channel_id=1, source_target_pairs={{0,8},{4,12},{8,0},{12,4},{1,9},{5,13},{9,1},{13,5},{2,10},{6,14},... | collective-permute-start | bytes 393224 | tf_op jit(solution)/shard_map/ppermute | solution.py:74
  105.3 2.8 %collective-permute-done.17 = bf16[32,2048]{1,0:T(8,128)(2,1)S(1)} collective-permute-done((bf16[32,2048]{1,0:T(8,128)(2,1)S(1)}, bf16[32,2048]{1,0:T(8,128)(2,1)S(1)}, u32[]{:S(2)}, u32[]{:S(2)}) %collective-permute-start.17) | collective-permute-done | bytes 131104 | tf_op jit(solution)/shard_map/ppermute | solution.py:74
  108.1 8.3 %collective-permute-done.18 = bf16[32,2048]{1,0:T(8,128)(2,1)S(1)} collective-permute-done((bf16[32,2048]{1,0:T(8,128)(2,1)S(1)}, bf16[32,2048]{1,0:T(8,128)(2,1)S(1)}, u32[]{:S(2)}, u32[]{:S(2)}) %collective-permute-start.18) | collective-permute-done | bytes 131104 | tf_op jit(solution)/shard_map/ppermute | solution.py:74
  116.5 0.7 pad_maximum_fusion.2
  (50 shorter events, 2.2 us)
Async XLA Ops:
  0.0 63.8 %copy-start = (bf16[1,768,2048]{2,1,0:T(8,128)(2,1)S(1)}, bf16[1,768,2048]{2,1,0:T(8,128)(2,1)}, u32[]{:S(2)}) copy-start(bf16[1,768,2048]{2,1,0:T(8,128)(2,1)} %param.11) | copy-start | bytes 9437188
  4.6 9.7 %collective-permute-start.10 = (bf16[32,2176]{1,0:T(8,128)(2,1)S(1)}, bf16[32,2176]{1,0:T(8,128)(2,1)S(1)}, u32[]{:S(2)}, u32[]{:S(2)}) collective-permute-start(bf16[32,2176]{1,0:T(8,128)(2,1)S(1)} %get-tuple-element.25), channel_id=1, source_target_pairs={{0,4},{4,8},{8,12},{12,0},{1,5},{5,9},{9,13},{13,1},{2,6},{6,10},{... | collective-permute-start | bytes 417800 | tf_op jit(solution)/shard_map/ppermute | solution.py:65
  7.7 12.7 %collective-permute-start.11 = (bf16[32,2176]{1,0:T(8,128)(2,1)S(1)}, bf16[32,2176]{1,0:T(8,128)(2,1)S(1)}, u32[]{:S(2)}, u32[]{:S(2)}) collective-permute-start(bf16[32,2176]{1,0:T(8,128)(2,1)S(1)} %get-tuple-element.25), channel_id=1, source_target_pairs={{0,8},{4,12},{8,0},{12,4},{1,9},{5,13},{9,1},{13,5},{2,10},{6,14},... | collective-permute-start | bytes 417800 | tf_op jit(solution)/shard_map/ppermute | solution.py:65
  10.3 12.3 %collective-permute-start.12 = (bf16[32,2176]{1,0:T(8,128)(2,1)S(1)}, bf16[32,2176]{1,0:T(8,128)(2,1)S(1)}, u32[]{:S(2)}, u32[]{:S(2)}) collective-permute-start(bf16[32,2176]{1,0:T(8,128)(2,1)S(1)} %get-tuple-element.25), channel_id=1, source_target_pairs={{0,12},{4,0},{8,4},{12,8},{1,13},{5,1},{9,5},{13,9},{2,14},{6,2},{... | collective-permute-start | bytes 417800 | tf_op jit(solution)/shard_map/ppermute | solution.py:65
  11.6 14.5 %collective-permute-start = (bf16[32,2176]{1,0:T(8,128)(2,1)S(1)}, bf16[32,2176]{1,0:T(8,128)(2,1)S(1)}, u32[]{:S(2)}, u32[]{:S(2)}) collective-permute-start(bf16[32,2176]{1,0:T(8,128)(2,1)S(1)} %get-tuple-element.26), channel_id=1, source_target_pairs={{0,4},{4,8},{8,12},{12,0},{1,5},{5,9},{9,13},{13,1},{2,6},{6,10},{... | collective-permute-start | bytes 417800 | tf_op jit(solution)/shard_map/ppermute | solution.py:65
  12.3 19.1 %collective-permute-start.1 = (bf16[32,2176]{1,0:T(8,128)(2,1)S(1)}, bf16[32,2176]{1,0:T(8,128)(2,1)S(1)}, u32[]{:S(2)}, u32[]{:S(2)}) collective-permute-start(bf16[32,2176]{1,0:T(8,128)(2,1)S(1)} %get-tuple-element.26), channel_id=1, source_target_pairs={{0,8},{4,12},{8,0},{12,4},{1,9},{5,13},{9,1},{13,5},{2,10},{6,14},... | collective-permute-start | bytes 417800 | tf_op jit(solution)/shard_map/ppermute | solution.py:65
  14.3 17.1 %collective-permute-start.2 = (bf16[32,2176]{1,0:T(8,128)(2,1)S(1)}, bf16[32,2176]{1,0:T(8,128)(2,1)S(1)}, u32[]{:S(2)}, u32[]{:S(2)}) collective-permute-start(bf16[32,2176]{1,0:T(8,128)(2,1)S(1)} %get-tuple-element.26), channel_id=1, source_target_pairs={{0,12},{4,0},{8,4},{12,8},{1,13},{5,1},{9,5},{13,9},{2,14},{6,2},{... | collective-permute-start | bytes 417800 | tf_op jit(solution)/shard_map/ppermute | solution.py:65
  22.6 13.8 %collective-permute-start.13 = (bf16[128,2176]{1,0:T(8,128)(2,1)S(1)}, bf16[128,2176]{1,0:T(8,128)(2,1)S(1)}, u32[]{:S(2)}, u32[]{:S(2)}) collective-permute-start(bf16[128,2176]{1,0:T(8,128)(2,1)S(1)} %pad_maximum_fusion.1), channel_id=1, source_target_pairs={{0,2},{2,0},{1,3},{3,1},{4,6},{6,4},{5,7},{7,5},{8,10},{10,8},{9,1... | collective-permute-start | bytes 1671176 | tf_op jit(solution)/shard_map/ppermute | solution.py:65
  31.5 15.3 %collective-permute-start.3 = (bf16[128,2176]{1,0:T(8,128)(2,1)S(1)}, bf16[128,2176]{1,0:T(8,128)(2,1)S(1)}, u32[]{:S(2)}, u32[]{:S(2)}) collective-permute-start(bf16[128,2176]{1,0:T(8,128)(2,1)S(1)} %pad_maximum_fusion), channel_id=1, source_target_pairs={{0,2},{2,0},{1,3},{3,1},{4,6},{6,4},{5,7},{7,5},{8,10},{10,8},{9,1... | collective-permute-start | bytes 1671176 | tf_op jit(solution)/shard_map/ppermute | solution.py:65
  37.4 11.7 %copy-start.3 = (bf16[512,2176]{1,0:T(8,128)(2,1)}, bf16[512,2176]{1,0:T(8,128)(2,1)S(1)}, u32[]{:S(2)}) copy-start(bf16[512,2176]{1,0:T(8,128)(2,1)S(1)} %get-tuple-element.12) | copy-start | bytes 6684676
  37.4 11.7 %collective-permute-start.14 = (bf16[256,2176]{1,0:T(8,128)(2,1)}, bf16[256,2176]{1,0:T(8,128)(2,1)}, u32[]{:S(2)}, u32[]{:S(2)}) collective-permute-start(bf16[256,2176]{1,0:T(8,128)(2,1)} %get-tuple-element.11), channel_id=1, source_target_pairs={{0,1},{1,0},{2,3},{3,2},{4,5},{5,4},{6,7},{7,6},{8,9},{9,8},{10,11... | collective-permute-start | bytes 3342344 | tf_op jit(solution)/shard_map/ppermute | solution.py:65
  47.7 1.4 %copy-start.1 = (bf16[512,2176]{1,0:T(8,128)(2,1)}, bf16[512,2176]{1,0:T(8,128)(2,1)S(1)}, u32[]{:S(2)}) copy-start(bf16[512,2176]{1,0:T(8,128)(2,1)S(1)} %get-tuple-element.14) | copy-start | bytes 6684676
  49.0 3.4 %collective-permute-start.4 = (bf16[256,2176]{1,0:T(8,128)(2,1)}, bf16[256,2176]{1,0:T(8,128)(2,1)}, u32[]{:S(2)}, u32[]{:S(2)}) collective-permute-start(bf16[256,2176]{1,0:T(8,128)(2,1)} %get-tuple-element.13), channel_id=1, source_target_pairs={{0,1},{1,0},{2,3},{3,2},{4,5},{5,4},{6,7},{7,6},{8,9},{9,8},{10,11... | collective-permute-start | bytes 3342344 | tf_op jit(solution)/shard_map/ppermute | solution.py:65
  49.0 3.4 %copy-start.2 = (bf16[512,2176]{1,0:T(8,128)(2,1)S(1)}, bf16[512,2176]{1,0:T(8,128)(2,1)}, u32[]{:S(2)}) copy-start(bf16[512,2176]{1,0:T(8,128)(2,1)} %copy-done.1) | copy-start | bytes 6684676
  52.5 7.3 %slice-start = ((s8[6291456]{0:T(1024)(128)(4,1)}), s8[4194304]{0:T(1024)(128)(4,1)S(1)}, s32[]{:S(2)}) async-start(s8[6291456]{0:T(1024)(128)(4,1)} %bitcast.18), calls=%async_computation | async-start | bytes 8388608
  54.1 5.8 %copy-start.4 = (bf16[512,2176]{1,0:T(8,128)(2,1)S(1)}, bf16[512,2176]{1,0:T(8,128)(2,1)}, u32[]{:S(2)}) copy-start(bf16[512,2176]{1,0:T(8,128)(2,1)} %constant_dynamic-update-slice_fusion.16) | copy-start | bytes 6684676
  54.1 5.8 %slice-start.1 = ((s8[6291456]{0:T(1024)(128)(4,1)}), s8[2097152]{0:T(1024)(128)(4,1)S(1)}, s32[]{:S(2)}) async-start(s8[6291456]{0:T(1024)(128)(4,1)} %bitcast.18), calls=%async_computation.1 | async-start | bytes 4194304
  65.8 2.9 %collective-permute-start.5 = (bf16[256,2048]{1,0:T(8,128)(2,1)S(1)}, bf16[256,2048]{1,0:T(8,128)(2,1)S(1)}, u32[]{:S(2)}, u32[]{:S(2)}) collective-permute-start(bf16[256,2048]{1,0:T(8,128)(2,1)S(1)} %split.127), channel_id=1, source_target_pairs={{0,1},{1,0},{2,3},{3,2},{4,5},{5,4},{6,7},{7,6},{8,9},{9,8},{10,11... | collective-permute-start | bytes 3145736 | tf_op jit(solution)/shard_map/ppermute | solution.py:74
  68.4 2.7 %collective-permute-start.15 = (bf16[256,2048]{1,0:T(8,128)(2,1)S(1)}, bf16[256,2048]{1,0:T(8,128)(2,1)S(1)}, u32[]{:S(2)}, u32[]{:S(2)}) collective-permute-start(bf16[256,2048]{1,0:T(8,128)(2,1)S(1)} %split.126), channel_id=1, source_target_pairs={{0,1},{1,0},{2,3},{3,2},{4,5},{5,4},{6,7},{7,6},{8,9},{9,8},{10,11... | collective-permute-start | bytes 3145736 | tf_op jit(solution)/shard_map/ppermute | solution.py:74
  69.1 14.9 %collective-permute-start.6 = (bf16[128,2048]{1,0:T(8,128)(2,1)S(1)}, bf16[128,2048]{1,0:T(8,128)(2,1)S(1)}, u32[]{:S(2)}, u32[]{:S(2)}) collective-permute-start(bf16[128,2048]{1,0:T(8,128)(2,1)S(1)} %split.129), channel_id=1, source_target_pairs={{0,2},{2,0},{1,3},{3,1},{4,6},{6,4},{5,7},{7,5},{8,10},{10,8},{9,1... | collective-permute-start | bytes 1572872 | tf_op jit(solution)/shard_map/ppermute | solution.py:74
  71.5 23.1 %collective-permute-start.16 = (bf16[128,2048]{1,0:T(8,128)(2,1)S(1)}, bf16[128,2048]{1,0:T(8,128)(2,1)S(1)}, u32[]{:S(2)}, u32[]{:S(2)}) collective-permute-start(bf16[128,2048]{1,0:T(8,128)(2,1)S(1)} %split.128), channel_id=1, source_target_pairs={{0,2},{2,0},{1,3},{3,1},{4,6},{6,4},{5,7},{7,5},{8,10},{10,8},{9,1... | collective-permute-start | bytes 1572872 | tf_op jit(solution)/shard_map/ppermute | solution.py:74
  84.1 20.9 %collective-permute-start.7 = (bf16[32,2048]{1,0:T(8,128)(2,1)S(1)}, bf16[32,2048]{1,0:T(8,128)(2,1)S(1)}, u32[]{:S(2)}, u32[]{:S(2)}) collective-permute-start(bf16[32,2048]{1,0:T(8,128)(2,1)S(1)} %get-tuple-element.15), channel_id=1, source_target_pairs={{0,12},{4,0},{8,4},{12,8},{1,13},{5,1},{9,5},{13,9},{2,14},{6,2},{... | collective-permute-start | bytes 393224 | tf_op jit(solution)/shard_map/ppermute | solution.py:74
  90.1 15.1 %collective-permute-start.8 = (bf16[32,2048]{1,0:T(8,128)(2,1)S(1)}, bf16[32,2048]{1,0:T(8,128)(2,1)S(1)}, u32[]{:S(2)}, u32[]{:S(2)}) collective-permute-start(bf16[32,2048]{1,0:T(8,128)(2,1)S(1)} %get-tuple-element.17), channel_id=1, source_target_pairs={{0,8},{4,12},{8,0},{12,4},{1,9},{5,13},{9,1},{13,5},{2,10},{6,14},... | collective-permute-start | bytes 393224 | tf_op jit(solution)/shard_map/ppermute | solution.py:74
  94.4 10.8 %collective-permute-start.9 = (bf16[32,2048]{1,0:T(8,128)(2,1)S(1)}, bf16[32,2048]{1,0:T(8,128)(2,1)S(1)}, u32[]{:S(2)}, u32[]{:S(2)}) collective-permute-start(bf16[32,2048]{1,0:T(8,128)(2,1)S(1)} %get-tuple-element.16), channel_id=1, source_target_pairs={{0,4},{4,8},{8,12},{12,0},{1,5},{5,9},{9,13},{13,1},{2,6},{6,10},{... | collective-permute-start | bytes 393224 | tf_op jit(solution)/shard_map/ppermute | solution.py:74
  94.8 13.3 %collective-permute-start.17 = (bf16[32,2048]{1,0:T(8,128)(2,1)S(1)}, bf16[32,2048]{1,0:T(8,128)(2,1)S(1)}, u32[]{:S(2)}, u32[]{:S(2)}) collective-permute-start(bf16[32,2048]{1,0:T(8,128)(2,1)S(1)} %get-tuple-element.18), channel_id=1, source_target_pairs={{0,12},{4,0},{8,4},{12,8},{1,13},{5,1},{9,5},{13,9},{2,14},{6,2},{... | collective-permute-start | bytes 393224 | tf_op jit(solution)/shard_map/ppermute | solution.py:74
  100.8 15.6 %collective-permute-start.18 = (bf16[32,2048]{1,0:T(8,128)(2,1)S(1)}, bf16[32,2048]{1,0:T(8,128)(2,1)S(1)}, u32[]{:S(2)}, u32[]{:S(2)}) collective-permute-start(bf16[32,2048]{1,0:T(8,128)(2,1)S(1)} %get-tuple-element.20), channel_id=1, source_target_pairs={{0,8},{4,12},{8,0},{12,4},{1,9},{5,13},{9,1},{13,5},{2,10},{6,14},... | collective-permute-start | bytes 393224 | tf_op jit(solution)/shard_map/ppermute | solution.py:74
  105.1 11.3 %collective-permute-start.19 = (bf16[32,2048]{1,0:T(8,128)(2,1)S(1)}, bf16[32,2048]{1,0:T(8,128)(2,1)S(1)}, u32[]{:S(2)}, u32[]{:S(2)}) collective-permute-start(bf16[32,2048]{1,0:T(8,128)(2,1)S(1)} %get-tuple-element.19), channel_id=1, source_target_pairs={{0,4},{4,8},{8,12},{12,0},{1,5},{5,9},{9,13},{13,1},{2,6},{6,10},{... | collective-permute-start | bytes 393224 | tf_op jit(solution)/shard_map/ppermute | solution.py:74

commit v12 on v11

--- a/solution.py
+++ b/solution.py
@@ -94,22 +94,32 @@
     meta = meta.astype(jnp.bfloat16)
     carried = jnp.concatenate([tokens, meta], axis=1)
     pick = (jnp.arange(hosts, dtype=jnp.int32) == me).astype(jnp.float32)
-    results = []
-    for rows in jnp.split(carried, STREAMS, axis=0):
-        for axis, size in zip(AXES, sizes):
-            rows = gather_stage(rows, axis, size)
-        tail = rows[:, width_model:width_model + 3 * hosts].astype(jnp.float32)
-        gate = tail[:, :hosts] + tail[:, hosts:2 * hosts] + tail[:, 2 * hosts:]
-        mine = jnp.sum(gate * pick[None, :], axis=1)
-        out = expert_block(rows[:, :width_model], w_in[0], w_down[0], hidden_width)
-        part = out.astype(jnp.float32) * mine[:, None]
-        for axis, size in list(zip(AXES, sizes))[::-1]:
-            part = scatter_stage(part, axis, size)
-        results.append(part)
-    return jnp.concatenate(results, axis=0).astype(jnp.bfloat16)
-
-
-STREAMS = 2
+    z_blocks = [carried] + [
+        lax.ppermute(carried, AXES[0], [(i, (i + shift) % sizes[0]) for i in range(sizes[0])])
+        for shift in range(1, sizes[0])
+    ]
+    swap = [(i, (i + 1) % sizes[1]) for i in range(sizes[1])]
+    x_blocks = [lax.ppermute(block, AXES[1], swap) for block in z_blocks]
+    rows = jnp.concatenate(z_blocks + x_blocks, axis=0)
+    rows = gather_stage(rows, AXES[2], sizes[2])
+    tail = rows[:, width_model:width_model + 3 * hosts].astype(jnp.float32)
+    gate = tail[:, :hosts] + tail[:, hosts:2 * hosts] + tail[:, 2 * hosts:]
+    mine = jnp.sum(gate * pick[None, :], axis=1)
+    out = expert_block(rows[:, :width_model], w_in[0], w_down[0], hidden_width)
+    part = out.astype(jnp.float32) * mine[:, None]
+    part = scatter_stage(part, AXES[2], sizes[2])
+    own, other = jnp.split(part, 2, axis=0)
+    own_blocks = jnp.split(own, sizes[0], axis=0)
+    other_blocks = jnp.split(other, sizes[0], axis=0)
+    total = None
+    for shift in range(sizes[0]):
+        block = own_blocks[shift] + lax.ppermute(
+            other_blocks[shift].astype(jnp.bfloat16), AXES[1], swap).astype(jnp.float32)
+        if shift:
+            pairs = [(i, (i - shift) % sizes[0]) for i in range(sizes[0])]
+            block = lax.ppermute(block.astype(jnp.bfloat16), AXES[0], pairs).astype(jnp.float32)
+        total = block if total is None else total + block
+    return total.astype(jnp.bfloat16)
 
 
 def factor_expert(mesh):

time: 117 us -> 123 us (1.051)
  waiting for transfers between devices: 43.9 us -> 73.8 us
  starting transfers between devices: 40.3 us -> 16.6 us
    ppermute x0 -> x14, waiting for transfers between devices: none -> 65.1 us  [the longest x3 21.1 us: dense_shards(): lax.ppermute(carried, AXES[0], [(i, (i + shift) % sizes[0]) for i in rang...]
    ppermute x10 -> x1, starting transfers between devices: 24.7 us -> 0.21 us  [scatter_stage(): lax.ppermute(pieces[shift].astype(jnp.bfloat16), axis, pairs)]
    ppermute x10 -> x1, waiting for transfers between devices: 22.5 us -> 4.02 us  [scatter_stage(): lax.ppermute(pieces[shift].astype(jnp.bfloat16), axis, pairs)]
    ppermute x10 -> x1, waiting for transfers between devices: 21.4 us -> 4.68 us  [gather_stage(): got.append(lax.ppermute(block, axis, pairs))]
    ppermute x0 -> x14, starting transfers between devices: none -> 16.4 us  [the longest x4 5.59 us: dense_shards(): x_blocks = [lax.ppermute(block, AXES[1], swap) for block in z_blocks]]
    ppermute x10 -> x1, starting transfers between devices: 15.5 us -> 0.01 us  [gather_stage(): got.append(lax.ppermute(block, axis, pairs))]
    concatenate x4 -> x1, local copies, waits for them, and re-layouts: 5.87 us -> 3.16 us  [gather_stage(): return jnp.concatenate(got, axis=0)]
    unnamed x21 -> x11, local copies, waits for them, and re-layouts: 6.33 us -> 7.37 us
  transfers between devices with their start and end apart: 20 -> 16, of which waited for: 12 -> 11; matrix products, arithmetic and copies ran while one was open for 11% -> 4% of each run, Pallas kernels for 0% -> 0%
where the time goes in v12:
time: 123 us
  waiting for transfers between devices  73.8 us (60%)
  starting transfers between devices  16.6 us (13%)
  matrix products  13.5 us (11%)
  local copies, waits for them, and re-layouts  13 us (11%)
  other arithmetic  6.12 us (5%)
    ppermute x3, waiting for transfers between devices, dense_shards(): lax.ppermute(carried, AXES[0], [(i, (i + shift) % sizes[0]) for i in rang...  21.1 us
    ppermute x4, waiting for transfers between devices, dense_shards(): lax.ppermute(other_blocks[shift].astype(jnp.bfloat16), AXES[1], swap)  18.9 us
    ppermute x3, waiting for transfers between devices, dense_shards(): lax.ppermute(block.astype(jnp.bfloat16), AXES[0], pairs).astype(jnp.float32)  16.9 us
    dot_general x1, matrix products, expert_block(): pair = jnp.dot(rows_in, gate_up, preferred_element_type=jnp.float32)  10 us
    ppermute x4, waiting for transfers between devices, dense_shards(): x_blocks = [lax.ppermute(block, AXES[1], swap) for block in z_blocks]  8.2 us
    unnamed x11, local copies, waits for them, and re-layouts  7.37 us
    ppermute x4, starting transfers between devices, dense_shards(): x_blocks = [lax.ppermute(block, AXES[1], swap) for block in z_blocks]  5.59 us
    ppermute x1, waiting for transfers between devices, gather_stage(): got.append(lax.ppermute(block, axis, pairs))  4.68 us
  transfers between devices with their start and end apart: 16, of which 11 were waited for; matrix products, arithmetic and copies ran while one was open for 4% of the time, Pallas kernels for 0%

profile of v12, /device:TPU:0, one launch (start us, length us, event | category | flops | bytes accessed | tf_op | source)
XLA Modules:
  0.0 123.2 jit_solution(7575160118819206096)
XLA Ops:
  0.0 0.9 reduce_sum.27
  0.9 0.8 broadcast_divide_fusion
  1.7 0.8 select_reduce_fusion
  2.4 0.1 copy.11
  2.5 0.1 copy.10
  2.6 0.1 copy.9
  2.8 1.1 concatenate.13
  3.8 3.0 %collective-permute-start.3 = (bf16[64,2176]{1,0:T(8,128)(2,1)S(1)}, bf16[64,2176]{1,0:T(8,128)(2,1)S(1)}, u32[]{:S(2)}, u32[]{:S(2)}) collective-permute-start(bf16[64,2176]{1,0:T(8,128)(2,1)S(1)} %concatenate.13), channel_id=1, source_target_pairs={{0,2},{2,0},{1,3},{3,1},{4,6},{6,4},{5,7},{7,5},{8,10},{10,8},{9,1... | collective-permute-start | bytes 835592 | tf_op jit(solution)/shard_map/ppermute | solution.py:102
  6.8 3.6 %collective-permute-start.2 = (bf16[64,2176]{1,0:T(8,128)(2,1)S(1)}, bf16[64,2176]{1,0:T(8,128)(2,1)S(1)}, u32[]{:S(2)}, u32[]{:S(2)}) collective-permute-start(bf16[64,2176]{1,0:T(8,128)(2,1)S(1)} %concatenate.13), channel_id=1, source_target_pairs={{0,12},{4,0},{8,4},{12,8},{1,13},{5,1},{9,5},{13,9},{2,14},{6,2},{... | collective-permute-start | bytes 835592 | tf_op jit(solution)/shard_map/ppermute | solution.py:98
  10.4 1.0 collective-permute-start
  11.5 0.8 constant_dynamic-update-slice_fusion.7
  12.2 5.3 %collective-permute-done.2 = bf16[64,2176]{1,0:T(8,128)(2,1)S(1)} collective-permute-done((bf16[64,2176]{1,0:T(8,128)(2,1)S(1)}, bf16[64,2176]{1,0:T(8,128)(2,1)S(1)}, u32[]{:S(2)}, u32[]{:S(2)}) %collective-permute-start.2) | collective-permute-done | bytes 278560 | tf_op jit(solution)/shard_map/ppermute | solution.py:98
  17.5 0.5 collective-permute-start.6
  18.1 15.8 %collective-permute-done.1 = bf16[64,2176]{1,0:T(8,128)(2,1)S(1)} collective-permute-done((bf16[64,2176]{1,0:T(8,128)(2,1)S(1)}, bf16[64,2176]{1,0:T(8,128)(2,1)S(1)}, u32[]{:S(2)}, u32[]{:S(2)}) %collective-permute-start.1) | collective-permute-done | bytes 278560 | tf_op jit(solution)/shard_map/ppermute | solution.py:98
  33.9 0.5 collective-permute-start.5
  34.4 1.5 %collective-permute-start.4 = (bf16[64,2176]{1,0:T(8,128)(2,1)S(1)}, bf16[64,2176]{1,0:T(8,128)(2,1)S(1)}, u32[]{:S(2)}, u32[]{:S(2)}) collective-permute-start(bf16[64,2176]{1,0:T(8,128)(2,1)S(1)} %collective-permute-done), channel_id=1, source_target_pairs={{0,2},{2,0},{1,3},{3,1},{4,6},{6,4},{5,7},{7,5},{8,10},{10,8},{9,1... | collective-permute-start | bytes 835592 | tf_op jit(solution)/shard_map/ppermute | solution.py:102
  35.9 0.8 constant_dynamic-update-slice_fusion.6
  36.7 0.7 constant_dynamic-update-slice_fusion.5
  37.4 0.7 constant_dynamic-update-slice_fusion.4
  38.1 0.8 constant_dynamic-update-slice_fusion.3
  38.9 8.2 %collective-permute-done.4 = bf16[64,2176]{1,0:T(8,128)(2,1)S(1)} collective-permute-done((bf16[64,2176]{1,0:T(8,128)(2,1)S(1)}, bf16[64,2176]{1,0:T(8,128)(2,1)S(1)}, u32[]{:S(2)}, u32[]{:S(2)}) %collective-permute-start.4) | collective-permute-done | bytes 278560 | tf_op jit(solution)/shard_map/ppermute | solution.py:102
  47.1 0.8 constant_dynamic-update-slice_fusion.2
  47.9 0.8 constant_dynamic-update-slice_fusion.1
  48.7 0.8 constant_dynamic-update-slice_fusion
  49.4 2.1 %copy-done.1 = bf16[1024,2176]{1,0:T(8,128)(2,1)} copy-done((bf16[1024,2176]{1,0:T(8,128)(2,1)}, bf16[1024,2176]{1,0:T(8,128)(2,1)S(1)}, u32[]{:S(2)}) %copy-start.1) | copy-done | bytes 4456472
  51.5 4.7 %collective-permute-done.7 = bf16[512,2176]{1,0:T(8,128)(2,1)} collective-permute-done((bf16[512,2176]{1,0:T(8,128)(2,1)}, bf16[512,2176]{1,0:T(8,128)(2,1)}, u32[]{:S(2)}, u32[]{:S(2)}) %collective-permute-start.7) | collective-permute-done | bytes 2228256 | tf_op jit(solution)/shard_map/ppermute | solution.py:65
  56.2 3.2 %constant_dynamic-update-slice_fusion.8 = bf16[1024,2176]{1,0:T(8,128)(2,1)} fusion(bf16[1024,2176]{1,0:T(8,128)(2,1)} %copy-done.1, bf16[512,2176]{1,0:T(8,128)(2,1)} %collective-permute-done.7), kind=kLoop, calls=%fused_computation.35 | loop fusion | bytes 4456448 | tf_op jit(solution)/shard_map/concatenate | solution.py:66
  59.3 1.0 slice_convert_fusion.1
  60.3 10.0 %fusion = f32[1024,1536]{1,0:T(8,128)S(1)} fusion(bf16[1,2048,1536]{2,1,0:T(8,128)(2,1)} %param.10, bf16[1024,2176]{1,0:T(8,128)(2,1)} %constant_dynamic-update-slice_fusion.8), kind=kOutput, calls=%fused_computation.1 | convolution fusion | flops 6442450944 | bytes 16777216 | tf_op jit(solution)/shard_map/dot_general | solution.py:9
  70.3 0.5 fusion.15
  70.9 3.5 %convert_multiply_fusion = f32[1024,2048]{1,0:T(8,128)S(1)} fusion(f32[1024]{0:T(1024)S(1)} %fusion.15, bf16[1,768,2048]{2,1,0:T(8,128)(2,1)S(1)} %copy-done, f32[1024,1536]{1,0:T(8,128)S(1)} %fusion), kind=kOutput, calls=%fused_computation | convolution fusion | flops 3232235520 | bytes 17829888 | tf_op jit(solution)/shard_map/dot_general | solution.py:11
  74.4 0.3 split.77
  74.7 0.2 collective-permute-start.8
  75.0 4.0 %collective-permute-done.8 = bf16[512,2048]{1,0:T(8,128)(2,1)S(1)} collective-permute-done((bf16[512,2048]{1,0:T(8,128)(2,1)S(1)}, bf16[512,2048]{1,0:T(8,128)(2,1)S(1)}, u32[]{:S(2)}, u32[]{:S(2)}) %collective-permute-start.8) | collective-permute-done | bytes 2097184 | tf_op jit(solution)/shard_map/ppermute | solution.py:74
  79.0 1.1 fusion.18
  80.2 0.6 collective-permute-start.14
  80.8 1.5 %collective-permute-start.12 = (bf16[64,2048]{1,0:T(8,128)(2,1)S(1)}, bf16[64,2048]{1,0:T(8,128)(2,1)S(1)}, u32[]{:S(2)}, u32[]{:S(2)}) collective-permute-start(bf16[64,2048]{1,0:T(8,128)(2,1)S(1)} %get-tuple-element.12), channel_id=1, source_target_pairs={{0,2},{2,0},{1,3},{3,1},{4,6},{6,4},{5,7},{7,5},{8,10},{10,8},{9,1... | collective-permute-start | bytes 786440 | tf_op jit(solution)/shard_map/ppermute | solution.py:116
  82.3 0.5 collective-permute-start.10
  82.8 1.5 %collective-permute-start.9 = (bf16[64,2048]{1,0:T(8,128)(2,1)S(1)}, bf16[64,2048]{1,0:T(8,128)(2,1)S(1)}, u32[]{:S(2)}, u32[]{:S(2)}) collective-permute-start(bf16[64,2048]{1,0:T(8,128)(2,1)S(1)} %get-tuple-element.10), channel_id=1, source_target_pairs={{0,2},{2,0},{1,3},{3,1},{4,6},{6,4},{5,7},{7,5},{8,10},{10,8},{9,1... | collective-permute-start | bytes 786440 | tf_op jit(solution)/shard_map/ppermute | solution.py:116
  84.3 5.1 %collective-permute-done.14 = bf16[64,2048]{1,0:T(8,128)(2,1)S(1)} collective-permute-done((bf16[64,2048]{1,0:T(8,128)(2,1)S(1)}, bf16[64,2048]{1,0:T(8,128)(2,1)S(1)}, u32[]{:S(2)}, u32[]{:S(2)}) %collective-permute-start.14) | collective-permute-done | bytes 262176 | tf_op jit(solution)/shard_map/ppermute | solution.py:116
  89.4 5.6 %collective-permute-done.12 = bf16[64,2048]{1,0:T(8,128)(2,1)S(1)} collective-permute-done((bf16[64,2048]{1,0:T(8,128)(2,1)S(1)}, bf16[64,2048]{1,0:T(8,128)(2,1)S(1)}, u32[]{:S(2)}, u32[]{:S(2)}) %collective-permute-start.12) | collective-permute-done | bytes 262176 | tf_op jit(solution)/shard_map/ppermute | solution.py:116
  95.0 5.6 %collective-permute-done.10 = bf16[64,2048]{1,0:T(8,128)(2,1)S(1)} collective-permute-done((bf16[64,2048]{1,0:T(8,128)(2,1)S(1)}, bf16[64,2048]{1,0:T(8,128)(2,1)S(1)}, u32[]{:S(2)}, u32[]{:S(2)}) %collective-permute-start.10) | collective-permute-done | bytes 262176 | tf_op jit(solution)/shard_map/ppermute | solution.py:116
  100.6 0.2 fusion.9
  101.0 1.9 %collective-permute-start.15 = (bf16[64,2048]{1,0:T(8,128)(2,1)S(1)}, bf16[64,2048]{1,0:T(8,128)(2,1)S(1)}, u32[]{:S(2)}, u32[]{:S(2)}) collective-permute-start(bf16[64,2048]{1,0:T(8,128)(2,1)S(1)} %get-tuple-element.9), channel_id=1, source_target_pairs={{0,4},{4,8},{8,12},{12,0},{1,5},{5,9},{9,13},{13,1},{2,6},{6,10},{... | collective-permute-start | bytes 786440 | tf_op jit(solution)/shard_map/ppermute | solution.py:120
  102.9 2.5 %collective-permute-done.9 = bf16[64,2048]{1,0:T(8,128)(2,1)S(1)} collective-permute-done((bf16[64,2048]{1,0:T(8,128)(2,1)S(1)}, bf16[64,2048]{1,0:T(8,128)(2,1)S(1)}, u32[]{:S(2)}, u32[]{:S(2)}) %collective-permute-start.9) | collective-permute-done | bytes 262176 | tf_op jit(solution)/shard_map/ppermute | solution.py:116
  105.4 4.0 %collective-permute-done.11 = bf16[64,2048]{1,0:T(8,128)(2,1)S(1)} collective-permute-done((bf16[64,2048]{1,0:T(8,128)(2,1)S(1)}, bf16[64,2048]{1,0:T(8,128)(2,1)S(1)}, u32[]{:S(2)}, u32[]{:S(2)}) %collective-permute-start.11) | collective-permute-done | bytes 262176 | tf_op jit(solution)/shard_map/ppermute | solution.py:120
  109.4 12.9 %collective-permute-done.13 = bf16[64,2048]{1,0:T(8,128)(2,1)S(1)} collective-permute-done((bf16[64,2048]{1,0:T(8,128)(2,1)S(1)}, bf16[64,2048]{1,0:T(8,128)(2,1)S(1)}, u32[]{:S(2)}, u32[]{:S(2)}) %collective-permute-start.13) | collective-permute-done | bytes 262176 | tf_op jit(solution)/shard_map/ppermute | solution.py:120
  122.4 0.9 fusion.13
  (16 shorter events, 0.3 us)
Async XLA Ops:
  0.0 70.9 %copy-start = (bf16[1,768,2048]{2,1,0:T(8,128)(2,1)S(1)}, bf16[1,768,2048]{2,1,0:T(8,128)(2,1)}, u32[]{:S(2)}) copy-start(bf16[1,768,2048]{2,1,0:T(8,128)(2,1)} %param.11) | copy-start | bytes 9437188
  3.8 34.3 %collective-permute-start.3 = (bf16[64,2176]{1,0:T(8,128)(2,1)S(1)}, bf16[64,2176]{1,0:T(8,128)(2,1)S(1)}, u32[]{:S(2)}, u32[]{:S(2)}) collective-permute-start(bf16[64,2176]{1,0:T(8,128)(2,1)S(1)} %concatenate.13), channel_id=1, source_target_pairs={{0,2},{2,0},{1,3},{3,1},{4,6},{6,4},{5,7},{7,5},{8,10},{10,8},{9,1... | collective-permute-start | bytes 835592 | tf_op jit(solution)/shard_map/ppermute | solution.py:102
  6.8 10.7 %collective-permute-start.2 = (bf16[64,2176]{1,0:T(8,128)(2,1)S(1)}, bf16[64,2176]{1,0:T(8,128)(2,1)S(1)}, u32[]{:S(2)}, u32[]{:S(2)}) collective-permute-start(bf16[64,2176]{1,0:T(8,128)(2,1)S(1)} %concatenate.13), channel_id=1, source_target_pairs={{0,12},{4,0},{8,4},{12,8},{1,13},{5,1},{9,5},{13,9},{2,14},{6,2},{... | collective-permute-start | bytes 835592 | tf_op jit(solution)/shard_map/ppermute | solution.py:98
  10.4 23.4 %collective-permute-start.1 = (bf16[64,2176]{1,0:T(8,128)(2,1)S(1)}, bf16[64,2176]{1,0:T(8,128)(2,1)S(1)}, u32[]{:S(2)}, u32[]{:S(2)}) collective-permute-start(bf16[64,2176]{1,0:T(8,128)(2,1)S(1)} %concatenate.13), channel_id=1, source_target_pairs={{0,8},{4,12},{8,0},{12,4},{1,9},{5,13},{9,1},{13,5},{2,10},{6,14},... | collective-permute-start | bytes 835592 | tf_op jit(solution)/shard_map/ppermute | solution.py:98
  10.4 24.0 %collective-permute-start = (bf16[64,2176]{1,0:T(8,128)(2,1)S(1)}, bf16[64,2176]{1,0:T(8,128)(2,1)S(1)}, u32[]{:S(2)}, u32[]{:S(2)}) collective-permute-start(bf16[64,2176]{1,0:T(8,128)(2,1)S(1)} %concatenate.13), channel_id=1, source_target_pairs={{0,4},{4,8},{8,12},{12,0},{1,5},{5,9},{9,13},{13,1},{2,6},{6,10},{... | collective-permute-start | bytes 835592 | tf_op jit(solution)/shard_map/ppermute | solution.py:98
  17.5 31.1 %collective-permute-start.6 = (bf16[64,2176]{1,0:T(8,128)(2,1)S(1)}, bf16[64,2176]{1,0:T(8,128)(2,1)S(1)}, u32[]{:S(2)}, u32[]{:S(2)}) collective-permute-start(bf16[64,2176]{1,0:T(8,128)(2,1)S(1)} %collective-permute-done.2), channel_id=1, source_target_pairs={{0,2},{2,0},{1,3},{3,1},{4,6},{6,4},{5,7},{7,5},{8,10},{10,8},{9,1... | collective-permute-start | bytes 835592 | tf_op jit(solution)/shard_map/ppermute | solution.py:102
  33.9 14.0 %collective-permute-start.5 = (bf16[64,2176]{1,0:T(8,128)(2,1)S(1)}, bf16[64,2176]{1,0:T(8,128)(2,1)S(1)}, u32[]{:S(2)}, u32[]{:S(2)}) collective-permute-start(bf16[64,2176]{1,0:T(8,128)(2,1)S(1)} %collective-permute-done.1), channel_id=1, source_target_pairs={{0,2},{2,0},{1,3},{3,1},{4,6},{6,4},{5,7},{7,5},{8,10},{10,8},{9,1... | collective-permute-start | bytes 835592 | tf_op jit(solution)/shard_map/ppermute | solution.py:102
  34.4 12.7 %collective-permute-start.4 = (bf16[64,2176]{1,0:T(8,128)(2,1)S(1)}, bf16[64,2176]{1,0:T(8,128)(2,1)S(1)}, u32[]{:S(2)}, u32[]{:S(2)}) collective-permute-start(bf16[64,2176]{1,0:T(8,128)(2,1)S(1)} %collective-permute-done), channel_id=1, source_target_pairs={{0,2},{2,0},{1,3},{3,1},{4,6},{6,4},{5,7},{7,5},{8,10},{10,8},{9,1... | collective-permute-start | bytes 835592 | tf_op jit(solution)/shard_map/ppermute | solution.py:102
  49.4 2.1 %copy-start.1 = (bf16[1024,2176]{1,0:T(8,128)(2,1)}, bf16[1024,2176]{1,0:T(8,128)(2,1)S(1)}, u32[]{:S(2)}) copy-start(bf16[1024,2176]{1,0:T(8,128)(2,1)S(1)} %get-tuple-element.15) | copy-start | bytes 13369348
  51.5 4.7 %collective-permute-start.7 = (bf16[512,2176]{1,0:T(8,128)(2,1)}, bf16[512,2176]{1,0:T(8,128)(2,1)}, u32[]{:S(2)}, u32[]{:S(2)}) collective-permute-start(bf16[512,2176]{1,0:T(8,128)(2,1)} %get-tuple-element.14), channel_id=1, source_target_pairs={{0,1},{1,0},{2,3},{3,2},{4,5},{5,4},{6,7},{7,6},{8,9},{9,8},{10,11... | collective-permute-start | bytes 6684680 | tf_op jit(solution)/shard_map/ppermute | solution.py:65
  74.7 4.2 %collective-permute-start.8 = (bf16[512,2048]{1,0:T(8,128)(2,1)S(1)}, bf16[512,2048]{1,0:T(8,128)(2,1)S(1)}, u32[]{:S(2)}, u32[]{:S(2)}) collective-permute-start(bf16[512,2048]{1,0:T(8,128)(2,1)S(1)} %split.77), channel_id=1, source_target_pairs={{0,1},{1,0},{2,3},{3,2},{4,5},{5,4},{6,7},{7,6},{8,9},{9,8},{10,11... | collective-permute-start | bytes 6291464 | tf_op jit(solution)/shard_map/ppermute | solution.py:74
  80.2 9.2 %collective-permute-start.14 = (bf16[64,2048]{1,0:T(8,128)(2,1)S(1)}, bf16[64,2048]{1,0:T(8,128)(2,1)S(1)}, u32[]{:S(2)}, u32[]{:S(2)}) collective-permute-start(bf16[64,2048]{1,0:T(8,128)(2,1)S(1)} %get-tuple-element.11), channel_id=1, source_target_pairs={{0,2},{2,0},{1,3},{3,1},{4,6},{6,4},{5,7},{7,5},{8,10},{10,8},{9,1... | collective-permute-start | bytes 786440 | tf_op jit(solution)/shard_map/ppermute | solution.py:116
  80.8 14.3 %collective-permute-start.12 = (bf16[64,2048]{1,0:T(8,128)(2,1)S(1)}, bf16[64,2048]{1,0:T(8,128)(2,1)S(1)}, u32[]{:S(2)}, u32[]{:S(2)}) collective-permute-start(bf16[64,2048]{1,0:T(8,128)(2,1)S(1)} %get-tuple-element.12), channel_id=1, source_target_pairs={{0,2},{2,0},{1,3},{3,1},{4,6},{6,4},{5,7},{7,5},{8,10},{10,8},{9,1... | collective-permute-start | bytes 786440 | tf_op jit(solution)/shard_map/ppermute | solution.py:116
  82.3 18.4 %collective-permute-start.10 = (bf16[64,2048]{1,0:T(8,128)(2,1)S(1)}, bf16[64,2048]{1,0:T(8,128)(2,1)S(1)}, u32[]{:S(2)}, u32[]{:S(2)}) collective-permute-start(bf16[64,2048]{1,0:T(8,128)(2,1)S(1)} %get-tuple-element.13), channel_id=1, source_target_pairs={{0,2},{2,0},{1,3},{3,1},{4,6},{6,4},{5,7},{7,5},{8,10},{10,8},{9,1... | collective-permute-start | bytes 786440 | tf_op jit(solution)/shard_map/ppermute | solution.py:116
  82.8 22.7 %collective-permute-start.9 = (bf16[64,2048]{1,0:T(8,128)(2,1)S(1)}, bf16[64,2048]{1,0:T(8,128)(2,1)S(1)}, u32[]{:S(2)}, u32[]{:S(2)}) collective-permute-start(bf16[64,2048]{1,0:T(8,128)(2,1)S(1)} %get-tuple-element.10), channel_id=1, source_target_pairs={{0,2},{2,0},{1,3},{3,1},{4,6},{6,4},{5,7},{7,5},{8,10},{10,8},{9,1... | collective-permute-start | bytes 786440 | tf_op jit(solution)/shard_map/ppermute | solution.py:116
  100.9 8.6 %collective-permute-start.11 = (bf16[64,2048]{1,0:T(8,128)(2,1)S(1)}, bf16[64,2048]{1,0:T(8,128)(2,1)S(1)}, u32[]{:S(2)}, u32[]{:S(2)}) collective-permute-start(bf16[64,2048]{1,0:T(8,128)(2,1)S(1)} %get-tuple-element.7), channel_id=1, source_target_pairs={{0,12},{4,0},{8,4},{12,8},{1,13},{5,1},{9,5},{13,9},{2,14},{6,2},{... | collective-permute-start | bytes 786440 | tf_op jit(solution)/shard_map/ppermute | solution.py:120
  100.9 21.4 %collective-permute-start.13 = (bf16[64,2048]{1,0:T(8,128)(2,1)S(1)}, bf16[64,2048]{1,0:T(8,128)(2,1)S(1)}, u32[]{:S(2)}, u32[]{:S(2)}) collective-permute-start(bf16[64,2048]{1,0:T(8,128)(2,1)S(1)} %get-tuple-element.8), channel_id=1, source_target_pairs={{0,8},{4,12},{8,0},{12,4},{1,9},{5,13},{9,1},{13,5},{2,10},{6,14},... | collective-permute-start | bytes 786440 | tf_op jit(solution)/shard_map/ppermute | solution.py:120
  101.0 21.4 %collective-permute-start.15 = (bf16[64,2048]{1,0:T(8,128)(2,1)S(1)}, bf16[64,2048]{1,0:T(8,128)(2,1)S(1)}, u32[]{:S(2)}, u32[]{:S(2)}) collective-permute-start(bf16[64,2048]{1,0:T(8,128)(2,1)S(1)} %get-tuple-element.9), channel_id=1, source_target_pairs={{0,4},{4,8},{8,12},{12,0},{1,5},{5,9},{9,13},{13,1},{2,6},{6,10},{... | collective-permute-start | bytes 786440 | tf_op jit(solution)/shard_map/ppermute | solution.py:120

commit v13 on v5

--- a/solution.py
+++ b/solution.py
@@ -99,10 +99,10 @@
     for rows in jnp.split(carried, STREAMS, axis=0):
         if held is not None:
             held, rows = lax.optimization_barrier((held, rows))
-        rows = gather_stage(rows, AXES[0], sizes[0])
-        held = rows
-        for axis, size in zip(AXES[1:], sizes[1:]):
+        for stage, (axis, size) in enumerate(zip(AXES, sizes)):
             rows = gather_stage(rows, axis, size)
+            if stage == 1:
+                held = rows
         tail = rows[:, width_model:width_model + 3 * hosts].astype(jnp.float32)
         gate = tail[:, :hosts] + tail[:, hosts:2 * hosts] + tail[:, 2 * hosts:]
         mine = jnp.sum(gate * pick[None, :], axis=1)

time: 106 us -> 121 us (1.14)
  waiting for transfers between devices: 48.5 us -> 60.9 us
  starting transfers between devices: 29.1 us -> 31.9 us
    ppermute x10, waiting for transfers between devices: 23.5 us -> 36.9 us  [gather_stage(): got.append(lax.ppermute(block, axis, pairs))]
    ppermute x10, starting transfers between devices: 13.9 us -> 15.8 us  [scatter_stage(): lax.ppermute(pieces[shift].astype(jnp.bfloat16), axis, pairs)]
  transfers between devices with their start and end apart: 20 -> 20, of which waited for: 10 -> 12; matrix products, arithmetic and copies ran while one was open for 12% -> 10% of each run, Pallas kernels for 0% -> 0%
where the time goes in v13:
time: 121 us
  waiting for transfers between devices  60.9 us (50%)
  starting transfers between devices  31.9 us (26%)
  local copies, waits for them, and re-layouts  10.8 us (9%)
  matrix products  10.6 us (9%)
  other arithmetic  6.12 us (5%)
    ppermute x10, waiting for transfers between devices, gather_stage(): got.append(lax.ppermute(block, axis, pairs))  36.9 us
    ppermute x10, waiting for transfers between devices, scatter_stage(): lax.ppermute(pieces[shift].astype(jnp.bfloat16), axis, pairs)  23.9 us
    ppermute x10, starting transfers between devices, gather_stage(): got.append(lax.ppermute(block, axis, pairs))  16.1 us
    ppermute x10, starting transfers between devices, scatter_stage(): lax.ppermute(pieces[shift].astype(jnp.bfloat16), axis, pairs)  15.8 us
    dot_general x2, matrix products, expert_block(): pair = jnp.dot(rows_in, gate_up, preferred_element_type=jnp.float32)  6.9 us
    unnamed x13, local copies, waits for them, and re-layouts  5 us
    dot_general x2, matrix products, expert_block(): jnp.dot(active, down_proj, preferred_element_type=jnp.float32)  3.68 us
  transfers between devices with their start and end apart: 20, of which 12 were waited for; matrix products, arithmetic and copies ran while one was open for 10% of the time, Pallas kernels for 0%

profile of v13, /device:TPU:0, one launch (start us, length us, event | category | flops | bytes accessed | tf_op | source)
XLA Modules:
  0.0 120.5 jit_solution(2931300179043835691)
XLA Ops:
  0.0 0.9 reduce_sum.36
  0.9 0.8 broadcast_divide_fusion
  1.7 0.8 select_reduce_fusion
  2.8 1.7 %concatenate.32 = bf16[64,2176]{1,0:T(8,128)(2,1)} concatenate(bf16[64,2048]{1,0:T(8,128)(2,1)} %param.6, bf16[64,16]{1,0:T(8,128)(2,1)S(1)} %copy.9, bf16[64,16]{1,0:T(8,128)(2,1)S(1)} %copy.10, bf16[64,16]{1,0:T(8,128)(2,1)S(1)} %copy.11, bf16[64,80]{1,0:T(8,128)(2,1)S(1)} %broadcast_in_dim.16), dimensions={1} | concatenate | bytes 557056 | tf_op jit(solution)/shard_map/concatenate | solution.py:95
  4.5 1.7 %fusion.43 = (bf16[32,2176]{1,0:T(8,128)(2,1)S(1)}, bf16[256,2176]{1,0:T(8,128)(2,1)}, bf16[512,2176]{1,0:T(8,128)(2,1)}, bf16[32,2176]{1,0:T(8,128)(2,1)S(1)}) fusion(bf16[64,2176]{1,0:T(8,128)(2,1)} %concatenate.32), kind=kLoop, calls=%fused_computation.85 | loop fusion | bytes 835584 | tf_op jit(solution)/shard_map/split | solution.py:99
  6.2 3.1 %collective-permute-start = (bf16[32,2176]{1,0:T(8,128)(2,1)S(1)}, bf16[32,2176]{1,0:T(8,128)(2,1)}, u32[]{:S(2)}, u32[]{:S(2)}) collective-permute-start(bf16[32,2176]{1,0:T(8,128)(2,1)S(1)} %get-tuple-element.26), channel_id=1, source_target_pairs={{0,4},{4,8},{8,12},{12,0},{1,5},{5,9},{9,13},{13,1},{2,6},{6,10},{... | collective-permute-start | bytes 417800 | tf_op jit(solution)/shard_map/ppermute | solution.py:65
  9.3 2.6 %collective-permute-start.1 = (bf16[32,2176]{1,0:T(8,128)(2,1)S(1)}, bf16[32,2176]{1,0:T(8,128)(2,1)}, u32[]{:S(2)}, u32[]{:S(2)}) collective-permute-start(bf16[32,2176]{1,0:T(8,128)(2,1)S(1)} %get-tuple-element.26), channel_id=1, source_target_pairs={{0,8},{4,12},{8,0},{12,4},{1,9},{5,13},{9,1},{13,5},{2,10},{6,14},... | collective-permute-start | bytes 417800 | tf_op jit(solution)/shard_map/ppermute | solution.py:65
  11.9 1.3 %collective-permute-start.2 = (bf16[32,2176]{1,0:T(8,128)(2,1)S(1)}, bf16[32,2176]{1,0:T(8,128)(2,1)}, u32[]{:S(2)}, u32[]{:S(2)}) collective-permute-start(bf16[32,2176]{1,0:T(8,128)(2,1)S(1)} %get-tuple-element.26), channel_id=1, source_target_pairs={{0,12},{4,0},{8,4},{12,8},{1,13},{5,1},{9,5},{13,9},{2,14},{6,2},{... | collective-permute-start | bytes 417800 | tf_op jit(solution)/shard_map/ppermute | solution.py:65
  13.2 2.8 %collective-permute-done = bf16[32,2176]{1,0:T(8,128)(2,1)} collective-permute-done((bf16[32,2176]{1,0:T(8,128)(2,1)S(1)}, bf16[32,2176]{1,0:T(8,128)(2,1)}, u32[]{:S(2)}, u32[]{:S(2)}) %collective-permute-start) | collective-permute-done | bytes 139296 | tf_op jit(solution)/shard_map/ppermute | solution.py:65
  16.0 5.1 %collective-permute-done.1 = bf16[32,2176]{1,0:T(8,128)(2,1)} collective-permute-done((bf16[32,2176]{1,0:T(8,128)(2,1)S(1)}, bf16[32,2176]{1,0:T(8,128)(2,1)}, u32[]{:S(2)}, u32[]{:S(2)}) %collective-permute-start.1) | collective-permute-done | bytes 139296 | tf_op jit(solution)/shard_map/ppermute | solution.py:65
  21.2 1.2 %pad_maximum_fusion = bf16[128,2176]{1,0:T(8,128)(2,1)S(1)} fusion(bf16[32,2176]{1,0:T(8,128)(2,1)} %collective-permute-done.2, bf16[32,2176]{1,0:T(8,128)(2,1)} %collective-permute-done.1, bf16[32,2176]{1,0:T(8,128)(2,1)} %collective-permute-done, bf16[32,2176]{1,0:T(8,128)(2,1)S(1)} %get-tuple-element.26), kind=kLoop, calls=%fused_computation.28 | loop fusion | flops 2228224 | bytes 1114112 | tf_op jit(solution)/shard_map/concatenate | solution.py:66
  22.4 1.6 %collective-permute-start.3 = (bf16[128,2176]{1,0:T(8,128)(2,1)S(1)}, bf16[128,2176]{1,0:T(8,128)(2,1)S(1)}, u32[]{:S(2)}, u32[]{:S(2)}) collective-permute-start(bf16[128,2176]{1,0:T(8,128)(2,1)S(1)} %pad_maximum_fusion), channel_id=1, source_target_pairs={{0,2},{2,0},{1,3},{3,1},{4,6},{6,4},{5,7},{7,5},{8,10},{10,8},{9,1... | collective-permute-start | bytes 1671176 | tf_op jit(solution)/shard_map/ppermute | solution.py:65
  23.9 1.6 %constant_dynamic-update-slice_fusion.3 = (bf16[256,2176]{1,0:T(8,128)(2,1)}, bf16[512,2176]{1,0:T(8,128)(2,1)}) fusion(bf16[256,2176]{1,0:T(8,128)(2,1)} %get-tuple-element.24, bf16[32,2176]{1,0:T(8,128)(2,1)} %collective-permute-done, bf16[512,2176]{1,0:T(8,128)(2,1)} %get-tuple-element.25), kind=kLoop, calls=%fused_computation.53 | loop fusion | bytes 417792
  25.6 1.6 %constant_dynamic-update-slice_fusion.2 = (bf16[256,2176]{1,0:T(8,128)(2,1)}, bf16[512,2176]{1,0:T(8,128)(2,1)}) fusion(bf16[256,2176]{1,0:T(8,128)(2,1)} %get-tuple-element.39, bf16[32,2176]{1,0:T(8,128)(2,1)} %collective-permute-done.1, bf16[512,2176]{1,0:T(8,128)(2,1)} %get-tuple-element.40), kind=kLoop, calls=%fused_computation.52 | loop fusion | bytes 417792
  27.2 1.6 %constant_dynamic-update-slice_fusion.1 = (bf16[256,2176]{1,0:T(8,128)(2,1)}, bf16[512,2176]{1,0:T(8,128)(2,1)}) fusion(bf16[256,2176]{1,0:T(8,128)(2,1)} %get-tuple-element.37, bf16[32,2176]{1,0:T(8,128)(2,1)} %collective-permute-done.2, bf16[512,2176]{1,0:T(8,128)(2,1)} %get-tuple-element.38), kind=kLoop, calls=%fused_computation.51 | loop fusion | bytes 417792
  28.8 8.1 %collective-permute-done.3 = bf16[128,2176]{1,0:T(8,128)(2,1)S(1)} collective-permute-done((bf16[128,2176]{1,0:T(8,128)(2,1)S(1)}, bf16[128,2176]{1,0:T(8,128)(2,1)S(1)}, u32[]{:S(2)}, u32[]{:S(2)}) %collective-permute-start.3) | collective-permute-done | bytes 557088 | tf_op jit(solution)/shard_map/ppermute | solution.py:65
  36.9 1.1 constant_dynamic-update-slice_fusion
  38.0 3.5 %collective-permute-start.10 = (bf16[32,2176]{1,0:T(8,128)(2,1)S(1)}, bf16[32,2176]{1,0:T(8,128)(2,1)S(1)}, u32[]{:S(2)}, u32[]{:S(2)}) collective-permute-start(bf16[32,2176]{1,0:T(8,128)(2,1)S(1)} %get-tuple-element.6), channel_id=1, source_target_pairs={{0,4},{4,8},{8,12},{12,0},{1,5},{5,9},{9,13},{13,1},{2,6},{6,10},{... | collective-permute-start | bytes 417800 | tf_op jit(solution)/shard_map/ppermute | solution.py:65
  41.5 0.6 collective-permute-start.11
  42.1 1.8 %collective-permute-start.12 = (bf16[32,2176]{1,0:T(8,128)(2,1)S(1)}, bf16[32,2176]{1,0:T(8,128)(2,1)S(1)}, u32[]{:S(2)}, u32[]{:S(2)}) collective-permute-start(bf16[32,2176]{1,0:T(8,128)(2,1)S(1)} %get-tuple-element.6), channel_id=1, source_target_pairs={{0,12},{4,0},{8,4},{12,8},{1,13},{5,1},{9,5},{13,9},{2,14},{6,2},{... | collective-permute-start | bytes 417800 | tf_op jit(solution)/shard_map/ppermute | solution.py:65
  43.9 2.5 %collective-permute-done.10 = bf16[32,2176]{1,0:T(8,128)(2,1)S(1)} collective-permute-done((bf16[32,2176]{1,0:T(8,128)(2,1)S(1)}, bf16[32,2176]{1,0:T(8,128)(2,1)S(1)}, u32[]{:S(2)}, u32[]{:S(2)}) %collective-permute-start.10) | collective-permute-done | bytes 139296 | tf_op jit(solution)/shard_map/ppermute | solution.py:65
  46.4 5.5 %collective-permute-done.11 = bf16[32,2176]{1,0:T(8,128)(2,1)S(1)} collective-permute-done((bf16[32,2176]{1,0:T(8,128)(2,1)S(1)}, bf16[32,2176]{1,0:T(8,128)(2,1)S(1)}, u32[]{:S(2)}, u32[]{:S(2)}) %collective-permute-start.11) | collective-permute-done | bytes 139296 | tf_op jit(solution)/shard_map/ppermute | solution.py:65
  52.0 1.6 %collective-permute-start.13 = (bf16[128,2176]{1,0:T(8,128)(2,1)S(1)}, bf16[128,2176]{1,0:T(8,128)(2,1)S(1)}, u32[]{:S(2)}, u32[]{:S(2)}) collective-permute-start(bf16[128,2176]{1,0:T(8,128)(2,1)S(1)} %pad_maximum_fusion.1), channel_id=1, source_target_pairs={{0,2},{2,0},{1,3},{3,1},{4,6},{6,4},{5,7},{7,5},{8,10},{10,8},{9,1... | collective-permute-start | bytes 1671176 | tf_op jit(solution)/shard_map/ppermute | solution.py:65
  53.6 12.9 %collective-permute-done.13 = bf16[128,2176]{1,0:T(8,128)(2,1)S(1)} collective-permute-done((bf16[128,2176]{1,0:T(8,128)(2,1)S(1)}, bf16[128,2176]{1,0:T(8,128)(2,1)S(1)}, u32[]{:S(2)}, u32[]{:S(2)}) %collective-permute-start.13) | collective-permute-done | bytes 557088 | tf_op jit(solution)/shard_map/ppermute | solution.py:65
  67.0 3.4 %fusion.2 = f32[512,1536]{1,0:T(8,128)S(1)} fusion(bf16[1,2048,1536]{2,1,0:T(8,128)(2,1)S(1)} %copy-done.2, bf16[512,2176]{1,0:T(8,128)(2,1)S(1)} %constant_dynamic-update-slice_fusion.5), kind=kOutput, calls=%fused_computation.2 | convolution fusion | flops 3221225472 | bytes 11534336 | tf_op jit(solution)/shard_map/dot_general | solution.py:9
  70.6 3.4 %fusion = f32[512,1536]{1,0:T(8,128)S(1)} fusion(bf16[1,2048,1536]{2,1,0:T(8,128)(2,1)S(1)} %copy-done.2, bf16[512,2176]{1,0:T(8,128)(2,1)S(1)} %constant_dynamic-update-slice_fusion.16), kind=kOutput, calls=%fused_computation | convolution fusion | flops 3221225472 | bytes 11534336 | tf_op jit(solution)/shard_map/dot_general | solution.py:9
  74.1 0.5 fusion.35
  74.6 1.8 %convert_multiply_fusion = f32[512,2048]{1,0:T(8,128)S(1)} fusion(bf16[1,768,2048]{2,1,0:T(8,128)(2,1)S(1)} %copy-done, f32[512]{0:T(512)S(1)} %get-tuple-element.8, f32[512,1536]{1,0:T(8,128)S(1)} %fusion), kind=kOutput, calls=%fused_computation.4 | convolution fusion | flops 1616117760 | bytes 10487808 | tf_op jit(solution)/shard_map/dot_general | solution.py:11
  76.6 0.5 collective-permute-start.15
  77.2 1.8 %convert_multiply_fusion.1 = f32[512,2048]{1,0:T(8,128)S(1)} fusion(bf16[1,768,2048]{2,1,0:T(8,128)(2,1)S(1)} %copy-done, f32[512]{0:T(512)S(1)} %get-tuple-element.7, f32[512,1536]{1,0:T(8,128)S(1)} %fusion.2), kind=kOutput, calls=%fused_computation.5 | convolution fusion | flops 1616117760 | bytes 10487808 | tf_op jit(solution)/shard_map/dot_general | solution.py:11
  79.3 0.2 collective-permute-done.15
  79.5 0.3 slice_add_fusion
  79.9 1.6 %collective-permute-start.16 = (bf16[128,2048]{1,0:T(8,128)(2,1)S(1)}, bf16[128,2048]{1,0:T(8,128)(2,1)S(1)}, u32[]{:S(2)}, u32[]{:S(2)}) collective-permute-start(bf16[128,2048]{1,0:T(8,128)(2,1)S(1)} %split.126), channel_id=1, source_target_pairs={{0,2},{2,0},{1,3},{3,1},{4,6},{6,4},{5,7},{7,5},{8,10},{10,8},{9,1... | collective-permute-start | bytes 1572872 | tf_op jit(solution)/shard_map/ppermute | solution.py:74
  81.5 0.4 collective-permute-done.5
  81.9 0.3 slice_add_fusion.1
  82.3 1.6 %collective-permute-start.6 = (bf16[128,2048]{1,0:T(8,128)(2,1)S(1)}, bf16[128,2048]{1,0:T(8,128)(2,1)S(1)}, u32[]{:S(2)}, u32[]{:S(2)}) collective-permute-start(bf16[128,2048]{1,0:T(8,128)(2,1)S(1)} %split.127), channel_id=1, source_target_pairs={{0,2},{2,0},{1,3},{3,1},{4,6},{6,4},{5,7},{7,5},{8,10},{10,8},{9,1... | collective-permute-start | bytes 1572872 | tf_op jit(solution)/shard_map/ppermute | solution.py:74
  83.9 10.9 %collective-permute-done.16 = bf16[128,2048]{1,0:T(8,128)(2,1)S(1)} collective-permute-done((bf16[128,2048]{1,0:T(8,128)(2,1)S(1)}, bf16[128,2048]{1,0:T(8,128)(2,1)S(1)}, u32[]{:S(2)}, u32[]{:S(2)}) %collective-permute-start.16) | collective-permute-done | bytes 524320 | tf_op jit(solution)/shard_map/ppermute | solution.py:74
  94.9 3.6 %collective-permute-start.19 = (bf16[32,2048]{1,0:T(8,128)(2,1)S(1)}, bf16[32,2048]{1,0:T(8,128)(2,1)S(1)}, u32[]{:S(2)}, u32[]{:S(2)}) collective-permute-start(bf16[32,2048]{1,0:T(8,128)(2,1)S(1)} %get-tuple-element.21), channel_id=1, source_target_pairs={{0,4},{4,8},{8,12},{12,0},{1,5},{5,9},{9,13},{13,1},{2,6},{6,10},{... | collective-permute-start | bytes 393224 | tf_op jit(solution)/shard_map/ppermute | solution.py:74
  98.5 2.2 %collective-permute-start.18 = (bf16[32,2048]{1,0:T(8,128)(2,1)S(1)}, bf16[32,2048]{1,0:T(8,128)(2,1)S(1)}, u32[]{:S(2)}, u32[]{:S(2)}) collective-permute-start(bf16[32,2048]{1,0:T(8,128)(2,1)S(1)} %get-tuple-element.22), channel_id=1, source_target_pairs={{0,8},{4,12},{8,0},{12,4},{1,9},{5,13},{9,1},{13,5},{2,10},{6,14},... | collective-permute-start | bytes 393224 | tf_op jit(solution)/shard_map/ppermute | solution.py:74
  100.8 0.2 collective-permute-start.17
  101.0 4.4 %collective-permute-done.6 = bf16[128,2048]{1,0:T(8,128)(2,1)S(1)} collective-permute-done((bf16[128,2048]{1,0:T(8,128)(2,1)S(1)}, bf16[128,2048]{1,0:T(8,128)(2,1)S(1)}, u32[]{:S(2)}, u32[]{:S(2)}) %collective-permute-start.6) | collective-permute-done | bytes 524320 | tf_op jit(solution)/shard_map/ppermute | solution.py:74
  105.4 0.2 fusion.39
  105.6 3.6 %collective-permute-start.9 = (bf16[32,2048]{1,0:T(8,128)(2,1)S(1)}, bf16[32,2048]{1,0:T(8,128)(2,1)S(1)}, u32[]{:S(2)}, u32[]{:S(2)}) collective-permute-start(bf16[32,2048]{1,0:T(8,128)(2,1)S(1)} %get-tuple-element.18), channel_id=1, source_target_pairs={{0,4},{4,8},{8,12},{12,0},{1,5},{5,9},{9,13},{13,1},{2,6},{6,10},{... | collective-permute-start | bytes 393224 | tf_op jit(solution)/shard_map/ppermute | solution.py:74
  109.2 2.2 %collective-permute-start.8 = (bf16[32,2048]{1,0:T(8,128)(2,1)S(1)}, bf16[32,2048]{1,0:T(8,128)(2,1)S(1)}, u32[]{:S(2)}, u32[]{:S(2)}) collective-permute-start(bf16[32,2048]{1,0:T(8,128)(2,1)S(1)} %get-tuple-element.19), channel_id=1, source_target_pairs={{0,8},{4,12},{8,0},{12,4},{1,9},{5,13},{9,1},{13,5},{2,10},{6,14},... | collective-permute-start | bytes 393224 | tf_op jit(solution)/shard_map/ppermute | solution.py:74
  111.4 0.2 collective-permute-start.7
  111.7 3.6 %collective-permute-done.9 = bf16[32,2048]{1,0:T(8,128)(2,1)S(1)} collective-permute-done((bf16[32,2048]{1,0:T(8,128)(2,1)S(1)}, bf16[32,2048]{1,0:T(8,128)(2,1)S(1)}, u32[]{:S(2)}, u32[]{:S(2)}) %collective-permute-start.9) | collective-permute-done | bytes 131104 | tf_op jit(solution)/shard_map/ppermute | solution.py:74
  115.3 4.4 %collective-permute-done.8 = bf16[32,2048]{1,0:T(8,128)(2,1)S(1)} collective-permute-done((bf16[32,2048]{1,0:T(8,128)(2,1)S(1)}, bf16[32,2048]{1,0:T(8,128)(2,1)S(1)}, u32[]{:S(2)}, u32[]{:S(2)}) %collective-permute-start.8) | collective-permute-done | bytes 131104 | tf_op jit(solution)/shard_map/ppermute | solution.py:74
  119.8 0.7 pad_maximum_fusion.2
  (42 shorter events, 1.9 us)
Async XLA Ops:
  0.0 74.6 %copy-start = (bf16[1,768,2048]{2,1,0:T(8,128)(2,1)S(1)}, bf16[1,768,2048]{2,1,0:T(8,128)(2,1)}, u32[]{:S(2)}) copy-start(bf16[1,768,2048]{2,1,0:T(8,128)(2,1)} %param.11) | copy-start | bytes 9437188
  6.2 9.8 %collective-permute-start = (bf16[32,2176]{1,0:T(8,128)(2,1)S(1)}, bf16[32,2176]{1,0:T(8,128)(2,1)}, u32[]{:S(2)}, u32[]{:S(2)}) collective-permute-start(bf16[32,2176]{1,0:T(8,128)(2,1)S(1)} %get-tuple-element.26), channel_id=1, source_target_pairs={{0,4},{4,8},{8,12},{12,0},{1,5},{5,9},{9,13},{13,1},{2,6},{6,10},{... | collective-permute-start | bytes 417800 | tf_op jit(solution)/shard_map/ppermute | solution.py:65
  9.3 11.9 %collective-permute-start.1 = (bf16[32,2176]{1,0:T(8,128)(2,1)S(1)}, bf16[32,2176]{1,0:T(8,128)(2,1)}, u32[]{:S(2)}, u32[]{:S(2)}) collective-permute-start(bf16[32,2176]{1,0:T(8,128)(2,1)S(1)} %get-tuple-element.26), channel_id=1, source_target_pairs={{0,8},{4,12},{8,0},{12,4},{1,9},{5,13},{9,1},{13,5},{2,10},{6,14},... | collective-permute-start | bytes 417800 | tf_op jit(solution)/shard_map/ppermute | solution.py:65
  11.9 9.3 %collective-permute-start.2 = (bf16[32,2176]{1,0:T(8,128)(2,1)S(1)}, bf16[32,2176]{1,0:T(8,128)(2,1)}, u32[]{:S(2)}, u32[]{:S(2)}) collective-permute-start(bf16[32,2176]{1,0:T(8,128)(2,1)S(1)} %get-tuple-element.26), channel_id=1, source_target_pairs={{0,12},{4,0},{8,4},{12,8},{1,13},{5,1},{9,5},{13,9},{2,14},{6,2},{... | collective-permute-start | bytes 417800 | tf_op jit(solution)/shard_map/ppermute | solution.py:65
  21.2 45.8 %copy-start.2 = (bf16[1,2048,1536]{2,1,0:T(8,128)(2,1)S(1)}, bf16[1,2048,1536]{2,1,0:T(8,128)(2,1)}, u32[]{:S(2)}) copy-start(bf16[1,2048,1536]{2,1,0:T(8,128)(2,1)} %param.10) | copy-start | bytes 18874372
  22.4 14.5 %collective-permute-start.3 = (bf16[128,2176]{1,0:T(8,128)(2,1)S(1)}, bf16[128,2176]{1,0:T(8,128)(2,1)S(1)}, u32[]{:S(2)}, u32[]{:S(2)}) collective-permute-start(bf16[128,2176]{1,0:T(8,128)(2,1)S(1)} %pad_maximum_fusion), channel_id=1, source_target_pairs={{0,2},{2,0},{1,3},{3,1},{4,6},{6,4},{5,7},{7,5},{8,10},{10,8},{9,1... | collective-permute-start | bytes 1671176 | tf_op jit(solution)/shard_map/ppermute | solution.py:65
  38.0 28.8 %collective-permute-start.4 = (bf16[256,2176]{1,0:T(8,128)(2,1)}, bf16[256,2176]{1,0:T(8,128)(2,1)S(1)}, u32[]{:S(2)}, u32[]{:S(2)}) collective-permute-start(bf16[256,2176]{1,0:T(8,128)(2,1)} %get-tuple-element.15), channel_id=1, source_target_pairs={{0,1},{1,0},{2,3},{3,2},{4,5},{5,4},{6,7},{7,6},{8,9},{9,8},{10,11... | collective-permute-start | bytes 3342344 | tf_op jit(solution)/shard_map/ppermute | solution.py:65
  38.0 8.4 %collective-permute-start.10 = (bf16[32,2176]{1,0:T(8,128)(2,1)S(1)}, bf16[32,2176]{1,0:T(8,128)(2,1)S(1)}, u32[]{:S(2)}, u32[]{:S(2)}) collective-permute-start(bf16[32,2176]{1,0:T(8,128)(2,1)S(1)} %get-tuple-element.6), channel_id=1, source_target_pairs={{0,4},{4,8},{8,12},{12,0},{1,5},{5,9},{9,13},{13,1},{2,6},{6,10},{... | collective-permute-start | bytes 417800 | tf_op jit(solution)/shard_map/ppermute | solution.py:65
  41.5 10.4 %collective-permute-start.11 = (bf16[32,2176]{1,0:T(8,128)(2,1)S(1)}, bf16[32,2176]{1,0:T(8,128)(2,1)S(1)}, u32[]{:S(2)}, u32[]{:S(2)}) collective-permute-start(bf16[32,2176]{1,0:T(8,128)(2,1)S(1)} %get-tuple-element.6), channel_id=1, source_target_pairs={{0,8},{4,12},{8,0},{12,4},{1,9},{5,13},{9,1},{13,5},{2,10},{6,14},... | collective-permute-start | bytes 417800 | tf_op jit(solution)/shard_map/ppermute | solution.py:65
  42.1 9.8 %collective-permute-start.12 = (bf16[32,2176]{1,0:T(8,128)(2,1)S(1)}, bf16[32,2176]{1,0:T(8,128)(2,1)S(1)}, u32[]{:S(2)}, u32[]{:S(2)}) collective-permute-start(bf16[32,2176]{1,0:T(8,128)(2,1)S(1)} %get-tuple-element.6), channel_id=1, source_target_pairs={{0,12},{4,0},{8,4},{12,8},{1,13},{5,1},{9,5},{13,9},{2,14},{6,2},{... | collective-permute-start | bytes 417800 | tf_op jit(solution)/shard_map/ppermute | solution.py:65
  43.9 22.9 %copy-start.1 = (bf16[512,2176]{1,0:T(8,128)(2,1)S(1)}, bf16[512,2176]{1,0:T(8,128)(2,1)}, u32[]{:S(2)}) copy-start(bf16[512,2176]{1,0:T(8,128)(2,1)} %get-tuple-element.16) | copy-start | bytes 6684676
  52.0 14.6 %collective-permute-start.13 = (bf16[128,2176]{1,0:T(8,128)(2,1)S(1)}, bf16[128,2176]{1,0:T(8,128)(2,1)S(1)}, u32[]{:S(2)}, u32[]{:S(2)}) collective-permute-start(bf16[128,2176]{1,0:T(8,128)(2,1)S(1)} %pad_maximum_fusion.1), channel_id=1, source_target_pairs={{0,2},{2,0},{1,3},{3,1},{4,6},{6,4},{5,7},{7,5},{8,10},{10,8},{9,1... | collective-permute-start | bytes 1671176 | tf_op jit(solution)/shard_map/ppermute | solution.py:65
  66.7 3.7 %collective-permute-start.14 = (bf16[256,2176]{1,0:T(8,128)(2,1)S(1)}, bf16[256,2176]{1,0:T(8,128)(2,1)S(1)}, u32[]{:S(2)}, u32[]{:S(2)}) collective-permute-start(bf16[256,2176]{1,0:T(8,128)(2,1)S(1)} %get-tuple-element.13), channel_id=1, source_target_pairs={{0,1},{1,0},{2,3},{3,2},{4,5},{5,4},{6,7},{7,6},{8,9},{9,8},{10,11... | collective-permute-start | bytes 3342344 | tf_op jit(solution)/shard_map/ppermute | solution.py:65
  76.6 2.8 %collective-permute-start.15 = (bf16[256,2048]{1,0:T(8,128)(2,1)S(1)}, bf16[256,2048]{1,0:T(8,128)(2,1)S(1)}, u32[]{:S(2)}, u32[]{:S(2)}) collective-permute-start(bf16[256,2048]{1,0:T(8,128)(2,1)S(1)} %split.124), channel_id=1, source_target_pairs={{0,1},{1,0},{2,3},{3,2},{4,5},{5,4},{6,7},{7,6},{8,9},{9,8},{10,11... | collective-permute-start | bytes 3145736 | tf_op jit(solution)/shard_map/ppermute | solution.py:74
  79.2 2.7 %collective-permute-start.5 = (bf16[256,2048]{1,0:T(8,128)(2,1)S(1)}, bf16[256,2048]{1,0:T(8,128)(2,1)S(1)}, u32[]{:S(2)}, u32[]{:S(2)}) collective-permute-start(bf16[256,2048]{1,0:T(8,128)(2,1)S(1)} %split.125), channel_id=1, source_target_pairs={{0,1},{1,0},{2,3},{3,2},{4,5},{5,4},{6,7},{7,6},{8,9},{9,8},{10,11... | collective-permute-start | bytes 3145736 | tf_op jit(solution)/shard_map/ppermute | solution.py:74
  79.9 14.9 %collective-permute-start.16 = (bf16[128,2048]{1,0:T(8,128)(2,1)S(1)}, bf16[128,2048]{1,0:T(8,128)(2,1)S(1)}, u32[]{:S(2)}, u32[]{:S(2)}) collective-permute-start(bf16[128,2048]{1,0:T(8,128)(2,1)S(1)} %split.126), channel_id=1, source_target_pairs={{0,2},{2,0},{1,3},{3,1},{4,6},{6,4},{5,7},{7,5},{8,10},{10,8},{9,1... | collective-permute-start | bytes 1572872 | tf_op jit(solution)/shard_map/ppermute | solution.py:74
  82.3 23.1 %collective-permute-start.6 = (bf16[128,2048]{1,0:T(8,128)(2,1)S(1)}, bf16[128,2048]{1,0:T(8,128)(2,1)S(1)}, u32[]{:S(2)}, u32[]{:S(2)}) collective-permute-start(bf16[128,2048]{1,0:T(8,128)(2,1)S(1)} %split.127), channel_id=1, source_target_pairs={{0,2},{2,0},{1,3},{3,1},{4,6},{6,4},{5,7},{7,5},{8,10},{10,8},{9,1... | collective-permute-start | bytes 1572872 | tf_op jit(solution)/shard_map/ppermute | solution.py:74
  94.9 16.5 %collective-permute-start.19 = (bf16[32,2048]{1,0:T(8,128)(2,1)S(1)}, bf16[32,2048]{1,0:T(8,128)(2,1)S(1)}, u32[]{:S(2)}, u32[]{:S(2)}) collective-permute-start(bf16[32,2048]{1,0:T(8,128)(2,1)S(1)} %get-tuple-element.21), channel_id=1, source_target_pairs={{0,4},{4,8},{8,12},{12,0},{1,5},{5,9},{9,13},{13,1},{2,6},{6,10},{... | collective-permute-start | bytes 393224 | tf_op jit(solution)/shard_map/ppermute | solution.py:74
  98.5 13.1 %collective-permute-start.18 = (bf16[32,2048]{1,0:T(8,128)(2,1)S(1)}, bf16[32,2048]{1,0:T(8,128)(2,1)S(1)}, u32[]{:S(2)}, u32[]{:S(2)}) collective-permute-start(bf16[32,2048]{1,0:T(8,128)(2,1)S(1)} %get-tuple-element.22), channel_id=1, source_target_pairs={{0,8},{4,12},{8,0},{12,4},{1,9},{5,13},{9,1},{13,5},{2,10},{6,14},... | collective-permute-start | bytes 393224 | tf_op jit(solution)/shard_map/ppermute | solution.py:74
  100.8 10.9 %collective-permute-start.17 = (bf16[32,2048]{1,0:T(8,128)(2,1)S(1)}, bf16[32,2048]{1,0:T(8,128)(2,1)S(1)}, u32[]{:S(2)}, u32[]{:S(2)}) collective-permute-start(bf16[32,2048]{1,0:T(8,128)(2,1)S(1)} %get-tuple-element.20), channel_id=1, source_target_pairs={{0,12},{4,0},{8,4},{12,8},{1,13},{5,1},{9,5},{13,9},{2,14},{6,2},{... | collective-permute-start | bytes 393224 | tf_op jit(solution)/shard_map/ppermute | solution.py:74
  105.6 9.7 %collective-permute-start.9 = (bf16[32,2048]{1,0:T(8,128)(2,1)S(1)}, bf16[32,2048]{1,0:T(8,128)(2,1)S(1)}, u32[]{:S(2)}, u32[]{:S(2)}) collective-permute-start(bf16[32,2048]{1,0:T(8,128)(2,1)S(1)} %get-tuple-element.18), channel_id=1, source_target_pairs={{0,4},{4,8},{8,12},{12,0},{1,5},{5,9},{9,13},{13,1},{2,6},{6,10},{... | collective-permute-start | bytes 393224 | tf_op jit(solution)/shard_map/ppermute | solution.py:74
  109.2 10.5 %collective-permute-start.8 = (bf16[32,2048]{1,0:T(8,128)(2,1)S(1)}, bf16[32,2048]{1,0:T(8,128)(2,1)S(1)}, u32[]{:S(2)}, u32[]{:S(2)}) collective-permute-start(bf16[32,2048]{1,0:T(8,128)(2,1)S(1)} %get-tuple-element.19), channel_id=1, source_target_pairs={{0,8},{4,12},{8,0},{12,4},{1,9},{5,13},{9,1},{13,5},{2,10},{6,14},... | collective-permute-start | bytes 393224 | tf_op jit(solution)/shard_map/ppermute | solution.py:74
  111.4 8.3 %collective-permute-start.7 = (bf16[32,2048]{1,0:T(8,128)(2,1)S(1)}, bf16[32,2048]{1,0:T(8,128)(2,1)S(1)}, u32[]{:S(2)}, u32[]{:S(2)}) collective-permute-start(bf16[32,2048]{1,0:T(8,128)(2,1)S(1)} %get-tuple-element.17), channel_id=1, source_target_pairs={{0,12},{4,0},{8,4},{12,8},{1,13},{5,1},{9,5},{13,9},{2,14},{6,2},{... | collective-permute-start | bytes 393224 | tf_op jit(solution)/shard_map/ppermute | solution.py:74

commit v14 on v11

--- a/solution.py
+++ b/solution.py
@@ -95,15 +95,18 @@
     carried = jnp.concatenate([tokens, meta], axis=1)
     pick = (jnp.arange(hosts, dtype=jnp.int32) == me).astype(jnp.float32)
     results = []
-    for rows in jnp.split(carried, STREAMS, axis=0):
-        for axis, size in zip(AXES, sizes):
+    for number, rows in enumerate(jnp.split(carried, STREAMS, axis=0)):
+        order = list(zip(AXES, sizes))
+        if number % 2:
+            order = [order[1], order[0]] + order[2:]
+        for axis, size in order:
             rows = gather_stage(rows, axis, size)
         tail = rows[:, width_model:width_model + 3 * hosts].astype(jnp.float32)
         gate = tail[:, :hosts] + tail[:, hosts:2 * hosts] + tail[:, 2 * hosts:]
         mine = jnp.sum(gate * pick[None, :], axis=1)
         out = expert_block(rows[:, :width_model], w_in[0], w_down[0], hidden_width)
         part = out.astype(jnp.float32) * mine[:, None]
-        for axis, size in list(zip(AXES, sizes))[::-1]:
+        for axis, size in order[::-1]:
             part = scatter_stage(part, axis, size)
         results.append(part)
     return jnp.concatenate(results, axis=0).astype(jnp.bfloat16)

time: 117 us -> 108 us (0.923)
  starting transfers between devices: 40.3 us -> 28.2 us
  waiting for transfers between devices: 43.9 us -> 51 us
  local copies, waits for them, and re-layouts: 14 us -> 8.75 us
  other arithmetic: 5.84 us -> 7.05 us
    ppermute x10, starting transfers between devices: 24.7 us -> 14.2 us  [scatter_stage(): lax.ppermute(pieces[shift].astype(jnp.bfloat16), axis, pairs)]
    ppermute x10, waiting for transfers between devices: 22.5 us -> 30.8 us  [scatter_stage(): lax.ppermute(pieces[shift].astype(jnp.bfloat16), axis, pairs)]
    concatenate x4, local copies, waits for them, and re-layouts: 5.87 us -> 1.28 us  [gather_stage(): return jnp.concatenate(got, axis=0)]
    concatenate x2, other arithmetic: 0.08 us -> 2.16 us  [gather_stage(): return jnp.concatenate(got, axis=0)]
    ppermute x10, starting transfers between devices: 15.5 us -> 13.9 us  [gather_stage(): got.append(lax.ppermute(block, axis, pairs))]
    ppermute x10, waiting for transfers between devices: 21.4 us -> 20.2 us  [gather_stage(): got.append(lax.ppermute(block, axis, pairs))]
    unnamed x21 -> x19, local copies, waits for them, and re-layouts: 6.33 us -> 5.66 us
  transfers between devices with their start and end apart: 20 -> 20, of which waited for: 12 -> 7; matrix products, arithmetic and copies ran while one was open for 11% -> 19% of each run, Pallas kernels for 0% -> 0%
where the time goes in v14:
time: 108 us
  waiting for transfers between devices  51 us (47%)
  starting transfers between devices  28.2 us (26%)
  matrix products  12.7 us (12%)
  local copies, waits for them, and re-layouts  8.75 us (8%)
  other arithmetic  7.05 us (7%)
    ppermute x10, waiting for transfers between devices, scatter_stage(): lax.ppermute(pieces[shift].astype(jnp.bfloat16), axis, pairs)  30.8 us
    ppermute x10, waiting for transfers between devices, gather_stage(): got.append(lax.ppermute(block, axis, pairs))  20.2 us
    ppermute x10, starting transfers between devices, scatter_stage(): lax.ppermute(pieces[shift].astype(jnp.bfloat16), axis, pairs)  14.2 us
    ppermute x10, starting transfers between devices, gather_stage(): got.append(lax.ppermute(block, axis, pairs))  13.9 us
    dot_general x2, matrix products, expert_block(): pair = jnp.dot(rows_in, gate_up, preferred_element_type=jnp.float32)  8.99 us
    unnamed x19, local copies, waits for them, and re-layouts  5.66 us
    dot_general x2, matrix products, expert_block(): jnp.dot(active, down_proj, preferred_element_type=jnp.float32)  3.69 us
    concatenate x2, other arithmetic, gather_stage(): return jnp.concatenate(got, axis=0)  2.16 us
  transfers between devices with their start and end apart: 20, of which 7 were waited for; matrix products, arithmetic and copies ran while one was open for 19% of the time, Pallas kernels for 0%

profile of v14, /device:TPU:0, one launch (start us, length us, event | category | flops | bytes accessed | tf_op | source)
XLA Modules:
  0.0 107.9 jit_solution(14576944859546200424)
XLA Ops:
  0.0 0.9 reduce_sum.36
  0.9 0.8 broadcast_divide_fusion
  1.7 0.8 select_reduce_fusion
  2.8 1.1 concatenate.32
  3.8 0.9 constant_dynamic-update-slice_fusion.15
  4.7 3.0 %collective-permute-start.10 = (bf16[32,2176]{1,0:T(8,128)(2,1)}, bf16[32,2176]{1,0:T(8,128)(2,1)}, u32[]{:S(2)}, u32[]{:S(2)}) collective-permute-start(bf16[32,2176]{1,0:T(8,128)(2,1)} %get-tuple-element.29), channel_id=1, source_target_pairs={{0,2},{2,0},{1,3},{3,1},{4,6},{6,4},{5,7},{7,5},{8,10},{10,8},{9,1... | collective-permute-start | bytes 417800 | tf_op jit(solution)/shard_map/ppermute | solution.py:65
  7.7 1.6 %collective-permute-start = (bf16[32,2176]{1,0:T(8,128)(2,1)}, bf16[32,2176]{1,0:T(8,128)(2,1)}, u32[]{:S(2)}, u32[]{:S(2)}) collective-permute-start(bf16[32,2176]{1,0:T(8,128)(2,1)} %get-tuple-element.30), channel_id=1, source_target_pairs={{0,4},{4,8},{8,12},{12,0},{1,5},{5,9},{9,13},{13,1},{2,6},{6,10},{... | collective-permute-start | bytes 417800 | tf_op jit(solution)/shard_map/ppermute | solution.py:65
  9.3 2.6 %collective-permute-start.1 = (bf16[32,2176]{1,0:T(8,128)(2,1)}, bf16[32,2176]{1,0:T(8,128)(2,1)S(1)}, u32[]{:S(2)}, u32[]{:S(2)}) collective-permute-start(bf16[32,2176]{1,0:T(8,128)(2,1)} %get-tuple-element.30), channel_id=1, source_target_pairs={{0,8},{4,12},{8,0},{12,4},{1,9},{5,13},{9,1},{13,5},{2,10},{6,14},... | collective-permute-start | bytes 417800 | tf_op jit(solution)/shard_map/ppermute | solution.py:65
  11.9 1.3 %collective-permute-start.2 = (bf16[32,2176]{1,0:T(8,128)(2,1)}, bf16[32,2176]{1,0:T(8,128)(2,1)S(1)}, u32[]{:S(2)}, u32[]{:S(2)}) collective-permute-start(bf16[32,2176]{1,0:T(8,128)(2,1)} %get-tuple-element.30), channel_id=1, source_target_pairs={{0,12},{4,0},{8,4},{12,8},{1,13},{5,1},{9,5},{13,9},{2,14},{6,2},{... | collective-permute-start | bytes 417800 | tf_op jit(solution)/shard_map/ppermute | solution.py:65
  13.2 1.1 %pad_maximum_fusion.1 = bf16[64,2176]{1,0:T(8,128)(2,1)S(1)} fusion(bf16[32,2176]{1,0:T(8,128)(2,1)} %collective-permute-done.10, bf16[32,2176]{1,0:T(8,128)(2,1)} %get-tuple-element.29), kind=kLoop, calls=%fused_computation.30 | loop fusion | flops 557056 | bytes 557056 | tf_op jit(solution)/shard_map/concatenate | solution.py:66
  14.4 0.7 collective-permute-start.11
  15.1 2.0 %collective-permute-start.12 = (bf16[64,2176]{1,0:T(8,128)(2,1)S(1)}, bf16[64,2176]{1,0:T(8,128)(2,1)S(1)}, u32[]{:S(2)}, u32[]{:S(2)}) collective-permute-start(bf16[64,2176]{1,0:T(8,128)(2,1)S(1)} %pad_maximum_fusion.1), channel_id=1, source_target_pairs={{0,8},{4,12},{8,0},{12,4},{1,9},{5,13},{9,1},{13,5},{2,10},{6,14},... | collective-permute-start | bytes 835592 | tf_op jit(solution)/shard_map/ppermute | solution.py:65
  17.2 1.4 %collective-permute-start.13 = (bf16[64,2176]{1,0:T(8,128)(2,1)S(1)}, bf16[64,2176]{1,0:T(8,128)(2,1)S(1)}, u32[]{:S(2)}, u32[]{:S(2)}) collective-permute-start(bf16[64,2176]{1,0:T(8,128)(2,1)S(1)} %pad_maximum_fusion.1), channel_id=1, source_target_pairs={{0,12},{4,0},{8,4},{12,8},{1,13},{5,1},{9,5},{13,9},{2,14},{6,2},{... | collective-permute-start | bytes 835592 | tf_op jit(solution)/shard_map/ppermute | solution.py:65
  18.5 13.1 %collective-permute-done.1 = bf16[32,2176]{1,0:T(8,128)(2,1)S(1)} collective-permute-done((bf16[32,2176]{1,0:T(8,128)(2,1)}, bf16[32,2176]{1,0:T(8,128)(2,1)S(1)}, u32[]{:S(2)}, u32[]{:S(2)}) %collective-permute-start.1) | collective-permute-done | bytes 139296 | tf_op jit(solution)/shard_map/ppermute | solution.py:65
  31.7 1.0 pad_maximum_fusion
  32.7 0.8 collective-permute-start.3
  33.5 1.6 %constant_dynamic-update-slice_fusion.14 = (bf16[256,2176]{1,0:T(8,128)(2,1)}, bf16[512,2176]{1,0:T(8,128)(2,1)}) fusion(bf16[256,2176]{1,0:T(8,128)(2,1)} %get-tuple-element.25, bf16[32,2176]{1,0:T(8,128)(2,1)} %collective-permute-done.10, bf16[512,2176]{1,0:T(8,128)(2,1)} %get-tuple-element.28), kind=kLoop, calls=%fused_computation.64 | loop fusion | bytes 417792
  35.2 0.9 constant_dynamic-update-slice_fusion.13
  36.0 5.9 %collective-permute-done.12 = bf16[64,2176]{1,0:T(8,128)(2,1)S(1)} collective-permute-done((bf16[64,2176]{1,0:T(8,128)(2,1)S(1)}, bf16[64,2176]{1,0:T(8,128)(2,1)S(1)}, u32[]{:S(2)}, u32[]{:S(2)}) %collective-permute-start.12) | collective-permute-done | bytes 278560 | tf_op jit(solution)/shard_map/ppermute | solution.py:65
  41.9 0.8 constant_dynamic-update-slice_fusion.12
  42.7 0.9 constant_dynamic-update-slice_fusion.11
  43.6 1.1 %constant_dynamic-update-slice_fusion.3 = (bf16[256,2176]{1,0:T(8,128)(2,1)S(1)}, bf16[512,2176]{1,0:T(8,128)(2,1)S(1)}) fusion(bf16[256,2176]{1,0:T(8,128)(2,1)S(1)} %copy-done.3, bf16[32,2176]{1,0:T(8,128)(2,1)} %collective-permute-done, bf16[512,2176]{1,0:T(8,128)(2,1)S(1)} %copy-done.1), kind=kLoop, calls=%fused_computation.53 | loop fusion | bytes 417792
  44.9 0.5 collective-permute-start.4
  45.4 1.2 %collective-permute-done.14 = bf16[256,2176]{1,0:T(8,128)(2,1)S(1)} collective-permute-done((bf16[256,2176]{1,0:T(8,128)(2,1)}, bf16[256,2176]{1,0:T(8,128)(2,1)S(1)}, u32[]{:S(2)}, u32[]{:S(2)}) %collective-permute-start.14) | collective-permute-done | bytes 1114144 | tf_op jit(solution)/shard_map/ppermute | solution.py:65
  46.6 0.1 constant_dynamic-update-slice_fusion.16
  46.7 5.5 %fusion = f32[512,1536]{1,0:T(8,128)S(1)} fusion(bf16[1,2048,1536]{2,1,0:T(8,128)(2,1)} %param.10, bf16[512,2176]{1,0:T(8,128)(2,1)S(1)} %constant_dynamic-update-slice_fusion.16), kind=kOutput, calls=%fused_computation | convolution fusion | flops 3221225472 | bytes 11534336 | tf_op jit(solution)/shard_map/dot_general | solution.py:9
  52.3 0.1 constant_dynamic-update-slice_fusion.5
  52.5 0.5 fusion.35
  53.1 1.8 %convert_multiply_fusion = f32[512,2048]{1,0:T(8,128)S(1)} fusion(bf16[1,768,2048]{2,1,0:T(8,128)(2,1)S(1)} %copy-done, f32[512]{0:T(512)S(1)} %get-tuple-element.6, f32[512,1536]{1,0:T(8,128)S(1)} %fusion), kind=kOutput, calls=%fused_computation.4 | convolution fusion | flops 1616117760 | bytes 10487808 | tf_op jit(solution)/shard_map/dot_general | solution.py:11
  55.1 0.2 collective-permute-start.15
  55.3 0.2 slice-done.1
  55.5 3.4 %fusion.2 = f32[512,1536]{1,0:T(8,128)S(1)} fusion(bf16[1,2048,1536]{2,1,0:T(8,128)(2,1)S(1)} %bitcast.19, bf16[512,2176]{1,0:T(8,128)(2,1)S(1)} %constant_dynamic-update-slice_fusion.5), kind=kOutput, calls=%fused_computation.2 | convolution fusion | flops 3221225472 | bytes 11534336 | tf_op jit(solution)/shard_map/dot_general | solution.py:9
  58.9 1.8 %convert_multiply_fusion.1 = f32[512,2048]{1,0:T(8,128)S(1)} fusion(bf16[1,768,2048]{2,1,0:T(8,128)(2,1)S(1)} %copy-done, f32[512]{0:T(512)S(1)} %get-tuple-element.5, f32[512,1536]{1,0:T(8,128)S(1)} %fusion.2), kind=kOutput, calls=%fused_computation.5 | convolution fusion | flops 1616117760 | bytes 10487808 | tf_op jit(solution)/shard_map/dot_general | solution.py:11
  60.9 0.2 collective-permute-start.5
  61.2 0.4 fusion.40
  61.7 7.5 %collective-permute-start.16 = (bf16[64,2048]{1,0:T(8,128)(2,1)S(1)}, bf16[64,2048]{1,0:T(8,128)(2,1)S(1)}, u32[]{:S(2)}, u32[]{:S(2)}) collective-permute-start(bf16[64,2048]{1,0:T(8,128)(2,1)S(1)} %get-tuple-element.11), channel_id=1, source_target_pairs={{0,12},{4,0},{8,4},{12,8},{1,13},{5,1},{9,5},{13,9},{2,14},{6,2},{... | collective-permute-start | bytes 786440 | tf_op jit(solution)/shard_map/ppermute | solution.py:74
  69.2 0.6 collective-permute-start.18
  69.9 0.3 slice_add_fusion.1
  70.3 0.6 collective-permute-start.6
  70.9 5.1 %collective-permute-done.16 = bf16[64,2048]{1,0:T(8,128)(2,1)S(1)} collective-permute-done((bf16[64,2048]{1,0:T(8,128)(2,1)S(1)}, bf16[64,2048]{1,0:T(8,128)(2,1)S(1)}, u32[]{:S(2)}, u32[]{:S(2)}) %collective-permute-start.16) | collective-permute-done | bytes 262176 | tf_op jit(solution)/shard_map/ppermute | solution.py:74
  76.0 16.4 %collective-permute-done.17 = bf16[64,2048]{1,0:T(8,128)(2,1)S(1)} collective-permute-done((bf16[64,2048]{1,0:T(8,128)(2,1)S(1)}, bf16[64,2048]{1,0:T(8,128)(2,1)S(1)}, u32[]{:S(2)}, u32[]{:S(2)}) %collective-permute-start.17) | collective-permute-done | bytes 262176 | tf_op jit(solution)/shard_map/ppermute | solution.py:74
  92.6 0.6 collective-permute-start.19
  93.2 0.2 fusion.39
  93.4 2.4 %collective-permute-start.8 = (bf16[32,2048]{1,0:T(8,128)(2,1)S(1)}, bf16[32,2048]{1,0:T(8,128)(2,1)S(1)}, u32[]{:S(2)}, u32[]{:S(2)}) collective-permute-start(bf16[32,2048]{1,0:T(8,128)(2,1)S(1)} %get-tuple-element.18), channel_id=1, source_target_pairs={{0,8},{4,12},{8,0},{12,4},{1,9},{5,13},{9,1},{13,5},{2,10},{6,14},... | collective-permute-start | bytes 393224 | tf_op jit(solution)/shard_map/ppermute | solution.py:74
  95.9 1.9 %collective-permute-start.9 = (bf16[32,2048]{1,0:T(8,128)(2,1)S(1)}, bf16[32,2048]{1,0:T(8,128)(2,1)S(1)}, u32[]{:S(2)}, u32[]{:S(2)}) collective-permute-start(bf16[32,2048]{1,0:T(8,128)(2,1)S(1)} %get-tuple-element.17), channel_id=1, source_target_pairs={{0,4},{4,8},{8,12},{12,0},{1,5},{5,9},{9,13},{13,1},{2,6},{6,10},{... | collective-permute-start | bytes 393224 | tf_op jit(solution)/shard_map/ppermute | solution.py:74
  97.9 1.2 %collective-permute-done.7 = bf16[32,2048]{1,0:T(8,128)(2,1)S(1)} collective-permute-done((bf16[32,2048]{1,0:T(8,128)(2,1)S(1)}, bf16[32,2048]{1,0:T(8,128)(2,1)S(1)}, u32[]{:S(2)}, u32[]{:S(2)}) %collective-permute-start.7) | collective-permute-done | bytes 131104 | tf_op jit(solution)/shard_map/ppermute | solution.py:74
  99.1 8.0 %collective-permute-done.8 = bf16[32,2048]{1,0:T(8,128)(2,1)S(1)} collective-permute-done((bf16[32,2048]{1,0:T(8,128)(2,1)S(1)}, bf16[32,2048]{1,0:T(8,128)(2,1)S(1)}, u32[]{:S(2)}, u32[]{:S(2)}) %collective-permute-start.8) | collective-permute-done | bytes 131104 | tf_op jit(solution)/shard_map/ppermute | solution.py:74
  107.2 0.7 pad_maximum_fusion.2
  (48 shorter events, 1.3 us)
Async XLA Ops:
  0.0 53.0 %copy-start = (bf16[1,768,2048]{2,1,0:T(8,128)(2,1)S(1)}, bf16[1,768,2048]{2,1,0:T(8,128)(2,1)}, u32[]{:S(2)}) copy-start(bf16[1,768,2048]{2,1,0:T(8,128)(2,1)} %param.11) | copy-start | bytes 9437188
  4.7 8.5 %collective-permute-start.10 = (bf16[32,2176]{1,0:T(8,128)(2,1)}, bf16[32,2176]{1,0:T(8,128)(2,1)}, u32[]{:S(2)}, u32[]{:S(2)}) collective-permute-start(bf16[32,2176]{1,0:T(8,128)(2,1)} %get-tuple-element.29), channel_id=1, source_target_pairs={{0,2},{2,0},{1,3},{3,1},{4,6},{6,4},{5,7},{7,5},{8,10},{10,8},{9,1... | collective-permute-start | bytes 417800 | tf_op jit(solution)/shard_map/ppermute | solution.py:65
  7.7 9.5 %collective-permute-start = (bf16[32,2176]{1,0:T(8,128)(2,1)}, bf16[32,2176]{1,0:T(8,128)(2,1)}, u32[]{:S(2)}, u32[]{:S(2)}) collective-permute-start(bf16[32,2176]{1,0:T(8,128)(2,1)} %get-tuple-element.30), channel_id=1, source_target_pairs={{0,4},{4,8},{8,12},{12,0},{1,5},{5,9},{9,13},{13,1},{2,6},{6,10},{... | collective-permute-start | bytes 417800 | tf_op jit(solution)/shard_map/ppermute | solution.py:65
  9.3 22.4 %collective-permute-start.1 = (bf16[32,2176]{1,0:T(8,128)(2,1)}, bf16[32,2176]{1,0:T(8,128)(2,1)S(1)}, u32[]{:S(2)}, u32[]{:S(2)}) collective-permute-start(bf16[32,2176]{1,0:T(8,128)(2,1)} %get-tuple-element.30), channel_id=1, source_target_pairs={{0,8},{4,12},{8,0},{12,4},{1,9},{5,13},{9,1},{13,5},{2,10},{6,14},... | collective-permute-start | bytes 417800 | tf_op jit(solution)/shard_map/ppermute | solution.py:65
  11.9 19.8 %collective-permute-start.2 = (bf16[32,2176]{1,0:T(8,128)(2,1)}, bf16[32,2176]{1,0:T(8,128)(2,1)S(1)}, u32[]{:S(2)}, u32[]{:S(2)}) collective-permute-start(bf16[32,2176]{1,0:T(8,128)(2,1)} %get-tuple-element.30), channel_id=1, source_target_pairs={{0,12},{4,0},{8,4},{12,8},{1,13},{5,1},{9,5},{13,9},{2,14},{6,2},{... | collective-permute-start | bytes 417800 | tf_op jit(solution)/shard_map/ppermute | solution.py:65
  13.2 30.4 %copy-start.1 = (bf16[512,2176]{1,0:T(8,128)(2,1)S(1)}, bf16[512,2176]{1,0:T(8,128)(2,1)}, u32[]{:S(2)}) copy-start(bf16[512,2176]{1,0:T(8,128)(2,1)} %get-tuple-element.27) | copy-start | bytes 6684676
  13.2 30.4 %copy-start.3 = (bf16[256,2176]{1,0:T(8,128)(2,1)S(1)}, bf16[256,2176]{1,0:T(8,128)(2,1)}, u32[]{:S(2)}) copy-start(bf16[256,2176]{1,0:T(8,128)(2,1)} %get-tuple-element.26) | copy-start | bytes 3342340
  14.4 20.8 %collective-permute-start.11 = (bf16[64,2176]{1,0:T(8,128)(2,1)S(1)}, bf16[64,2176]{1,0:T(8,128)(2,1)S(1)}, u32[]{:S(2)}, u32[]{:S(2)}) collective-permute-start(bf16[64,2176]{1,0:T(8,128)(2,1)S(1)} %pad_maximum_fusion.1), channel_id=1, source_target_pairs={{0,4},{4,8},{8,12},{12,0},{1,5},{5,9},{9,13},{13,1},{2,6},{6,10},{... | collective-permute-start | bytes 835592 | tf_op jit(solution)/shard_map/ppermute | solution.py:65
  15.1 26.8 %collective-permute-start.12 = (bf16[64,2176]{1,0:T(8,128)(2,1)S(1)}, bf16[64,2176]{1,0:T(8,128)(2,1)S(1)}, u32[]{:S(2)}, u32[]{:S(2)}) collective-permute-start(bf16[64,2176]{1,0:T(8,128)(2,1)S(1)} %pad_maximum_fusion.1), channel_id=1, source_target_pairs={{0,8},{4,12},{8,0},{12,4},{1,9},{5,13},{9,1},{13,5},{2,10},{6,14},... | collective-permute-start | bytes 835592 | tf_op jit(solution)/shard_map/ppermute | solution.py:65
  17.2 25.6 %collective-permute-start.13 = (bf16[64,2176]{1,0:T(8,128)(2,1)S(1)}, bf16[64,2176]{1,0:T(8,128)(2,1)S(1)}, u32[]{:S(2)}, u32[]{:S(2)}) collective-permute-start(bf16[64,2176]{1,0:T(8,128)(2,1)S(1)} %pad_maximum_fusion.1), channel_id=1, source_target_pairs={{0,12},{4,0},{8,4},{12,8},{1,13},{5,1},{9,5},{13,9},{2,14},{6,2},{... | collective-permute-start | bytes 835592 | tf_op jit(solution)/shard_map/ppermute | solution.py:65
  32.7 12.1 %collective-permute-start.3 = (bf16[128,2176]{1,0:T(8,128)(2,1)S(1)}, bf16[128,2176]{1,0:T(8,128)(2,1)S(1)}, u32[]{:S(2)}, u32[]{:S(2)}) collective-permute-start(bf16[128,2176]{1,0:T(8,128)(2,1)S(1)} %pad_maximum_fusion), channel_id=1, source_target_pairs={{0,2},{2,0},{1,3},{3,1},{4,6},{6,4},{5,7},{7,5},{8,10},{10,8},{9,1... | collective-permute-start | bytes 1671176 | tf_op jit(solution)/shard_map/ppermute | solution.py:65
  43.6 3.0 %copy-start.2 = (bf16[512,2176]{1,0:T(8,128)(2,1)S(1)}, bf16[512,2176]{1,0:T(8,128)(2,1)}, u32[]{:S(2)}) copy-start(bf16[512,2176]{1,0:T(8,128)(2,1)} %get-tuple-element.20) | copy-start | bytes 6684676
  43.6 3.0 %collective-permute-start.14 = (bf16[256,2176]{1,0:T(8,128)(2,1)}, bf16[256,2176]{1,0:T(8,128)(2,1)S(1)}, u32[]{:S(2)}, u32[]{:S(2)}) collective-permute-start(bf16[256,2176]{1,0:T(8,128)(2,1)} %get-tuple-element.19), channel_id=1, source_target_pairs={{0,1},{1,0},{2,3},{3,2},{4,5},{5,4},{6,7},{7,6},{8,9},{9,8},{10,11... | collective-permute-start | bytes 3342344 | tf_op jit(solution)/shard_map/ppermute | solution.py:65
  44.9 7.4 %collective-permute-start.4 = (bf16[256,2176]{1,0:T(8,128)(2,1)S(1)}, bf16[256,2176]{1,0:T(8,128)(2,1)S(1)}, u32[]{:S(2)}, u32[]{:S(2)}) collective-permute-start(bf16[256,2176]{1,0:T(8,128)(2,1)S(1)} %get-tuple-element.14), channel_id=1, source_target_pairs={{0,1},{1,0},{2,3},{3,2},{4,5},{5,4},{6,7},{7,6},{8,9},{9,8},{10,11... | collective-permute-start | bytes 3342344 | tf_op jit(solution)/shard_map/ppermute | solution.py:65
  52.5 2.8 %slice-start = ((s8[6291456]{0:T(1024)(128)(4,1)}), s8[4194304]{0:T(1024)(128)(4,1)S(1)}, s32[]{:S(2)}) async-start(s8[6291456]{0:T(1024)(128)(4,1)} %bitcast.18), calls=%async_computation | async-start | bytes 8388608
  53.0 2.5 %slice-start.1 = ((s8[6291456]{0:T(1024)(128)(4,1)}), s8[2097152]{0:T(1024)(128)(4,1)S(1)}, s32[]{:S(2)}) async-start(s8[6291456]{0:T(1024)(128)(4,1)} %bitcast.18), calls=%async_computation.1 | async-start | bytes 4194304
  55.1 6.1 %collective-permute-start.15 = (bf16[256,2048]{1,0:T(8,128)(2,1)S(1)}, bf16[256,2048]{1,0:T(8,128)(2,1)S(1)}, u32[]{:S(2)}, u32[]{:S(2)}) collective-permute-start(bf16[256,2048]{1,0:T(8,128)(2,1)S(1)} %split.126), channel_id=1, source_target_pairs={{0,1},{1,0},{2,3},{3,2},{4,5},{5,4},{6,7},{7,6},{8,9},{9,8},{10,11... | collective-permute-start | bytes 3145736 | tf_op jit(solution)/shard_map/ppermute | solution.py:74
  60.9 8.9 %collective-permute-start.5 = (bf16[256,2048]{1,0:T(8,128)(2,1)S(1)}, bf16[256,2048]{1,0:T(8,128)(2,1)S(1)}, u32[]{:S(2)}, u32[]{:S(2)}) collective-permute-start(bf16[256,2048]{1,0:T(8,128)(2,1)S(1)} %split.127), channel_id=1, source_target_pairs={{0,1},{1,0},{2,3},{3,2},{4,5},{5,4},{6,7},{7,6},{8,9},{9,8},{10,11... | collective-permute-start | bytes 3145736 | tf_op jit(solution)/shard_map/ppermute | solution.py:74
  61.7 14.3 %collective-permute-start.16 = (bf16[64,2048]{1,0:T(8,128)(2,1)S(1)}, bf16[64,2048]{1,0:T(8,128)(2,1)S(1)}, u32[]{:S(2)}, u32[]{:S(2)}) collective-permute-start(bf16[64,2048]{1,0:T(8,128)(2,1)S(1)} %get-tuple-element.11), channel_id=1, source_target_pairs={{0,12},{4,0},{8,4},{12,8},{1,13},{5,1},{9,5},{13,9},{2,14},{6,2},{... | collective-permute-start | bytes 786440 | tf_op jit(solution)/shard_map/ppermute | solution.py:74
  69.2 23.2 %collective-permute-start.17 = (bf16[64,2048]{1,0:T(8,128)(2,1)S(1)}, bf16[64,2048]{1,0:T(8,128)(2,1)S(1)}, u32[]{:S(2)}, u32[]{:S(2)}) collective-permute-start(bf16[64,2048]{1,0:T(8,128)(2,1)S(1)} %get-tuple-element.13), channel_id=1, source_target_pairs={{0,8},{4,12},{8,0},{12,4},{1,9},{5,13},{9,1},{13,5},{2,10},{6,14},... | collective-permute-start | bytes 786440 | tf_op jit(solution)/shard_map/ppermute | solution.py:74
  69.2 23.2 %collective-permute-start.18 = (bf16[64,2048]{1,0:T(8,128)(2,1)S(1)}, bf16[64,2048]{1,0:T(8,128)(2,1)S(1)}, u32[]{:S(2)}, u32[]{:S(2)}) collective-permute-start(bf16[64,2048]{1,0:T(8,128)(2,1)S(1)} %get-tuple-element.12), channel_id=1, source_target_pairs={{0,4},{4,8},{8,12},{12,0},{1,5},{5,9},{9,13},{13,1},{2,6},{6,10},{... | collective-permute-start | bytes 786440 | tf_op jit(solution)/shard_map/ppermute | solution.py:74
  70.3 22.9 %collective-permute-start.6 = (bf16[128,2048]{1,0:T(8,128)(2,1)S(1)}, bf16[128,2048]{1,0:T(8,128)(2,1)S(1)}, u32[]{:S(2)}, u32[]{:S(2)}) collective-permute-start(bf16[128,2048]{1,0:T(8,128)(2,1)S(1)} %split.128), channel_id=1, source_target_pairs={{0,2},{2,0},{1,3},{3,1},{4,6},{6,4},{5,7},{7,5},{8,10},{10,8},{9,1... | collective-permute-start | bytes 1572872 | tf_op jit(solution)/shard_map/ppermute | solution.py:74
  92.6 5.3 %collective-permute-start.19 = (bf16[32,2048]{1,0:T(8,128)(2,1)S(1)}, bf16[32,2048]{1,0:T(8,128)(2,1)S(1)}, u32[]{:S(2)}, u32[]{:S(2)}) collective-permute-start(bf16[32,2048]{1,0:T(8,128)(2,1)S(1)} %split.129), channel_id=1, source_target_pairs={{0,2},{2,0},{1,3},{3,1},{4,6},{6,4},{5,7},{7,5},{8,10},{10,8},{9,1... | collective-permute-start | bytes 393224 | tf_op jit(solution)/shard_map/ppermute | solution.py:74
  93.4 5.7 %collective-permute-start.7 = (bf16[32,2048]{1,0:T(8,128)(2,1)S(1)}, bf16[32,2048]{1,0:T(8,128)(2,1)S(1)}, u32[]{:S(2)}, u32[]{:S(2)}) collective-permute-start(bf16[32,2048]{1,0:T(8,128)(2,1)S(1)} %get-tuple-element.16), channel_id=1, source_target_pairs={{0,12},{4,0},{8,4},{12,8},{1,13},{5,1},{9,5},{13,9},{2,14},{6,2},{... | collective-permute-start | bytes 393224 | tf_op jit(solution)/shard_map/ppermute | solution.py:74
  93.4 13.7 %collective-permute-start.8 = (bf16[32,2048]{1,0:T(8,128)(2,1)S(1)}, bf16[32,2048]{1,0:T(8,128)(2,1)S(1)}, u32[]{:S(2)}, u32[]{:S(2)}) collective-permute-start(bf16[32,2048]{1,0:T(8,128)(2,1)S(1)} %get-tuple-element.18), channel_id=1, source_target_pairs={{0,8},{4,12},{8,0},{12,4},{1,9},{5,13},{9,1},{13,5},{2,10},{6,14},... | collective-permute-start | bytes 393224 | tf_op jit(solution)/shard_map/ppermute | solution.py:74
  95.9 11.2 %collective-permute-start.9 = (bf16[32,2048]{1,0:T(8,128)(2,1)S(1)}, bf16[32,2048]{1,0:T(8,128)(2,1)S(1)}, u32[]{:S(2)}, u32[]{:S(2)}) collective-permute-start(bf16[32,2048]{1,0:T(8,128)(2,1)S(1)} %get-tuple-element.17), channel_id=1, source_target_pairs={{0,4},{4,8},{8,12},{12,0},{1,5},{5,9},{9,13},{13,1},{2,6},{6,10},{... | collective-permute-start | bytes 393224 | tf_op jit(solution)/shard_map/ppermute | solution.py:74

commit v15 on v14

--- a/solution.py
+++ b/solution.py
@@ -106,8 +106,16 @@
         mine = jnp.sum(gate * pick[None, :], axis=1)
         out = expert_block(rows[:, :width_model], w_in[0], w_down[0], hidden_width)
         part = out.astype(jnp.float32) * mine[:, None]
-        for axis, size in order[::-1]:
-            part = scatter_stage(part, axis, size)
+        if number % 2:
+            part = scatter_stage(part, AXES[2], sizes[2])
+            split = part.reshape((sizes[0], sizes[1], -1) + part.shape[1:])
+            total = split[:, 0]
+            swap = [(i, (i + 1) % sizes[1]) for i in range(sizes[1])]
+            total = total + lax.ppermute(split[:, 1].astype(jnp.bfloat16), AXES[1], swap).astype(jnp.float32)
+            part = scatter_stage(total.reshape((-1,) + part.shape[1:]), AXES[0], sizes[0])
+        else:
+            for axis, size in order[::-1]:
+                part = scatter_stage(part, axis, size)
         results.append(part)
     return jnp.concatenate(results, axis=0).astype(jnp.bfloat16)
 

time: 108 us -> 107 us (level)
  waiting for transfers between devices: 51 us -> 46.2 us
  starting transfers between devices: 28.2 us -> 32.3 us
    ppermute x10 -> x9, waiting for transfers between devices: 30.8 us -> 24 us  [scatter_stage(): lax.ppermute(pieces[shift].astype(jnp.bfloat16), axis, pairs)]
    ppermute x10 -> x9, starting transfers between devices: 14.2 us -> 17.6 us  [scatter_stage(): lax.ppermute(pieces[shift].astype(jnp.bfloat16), axis, pairs)]
    ppermute x0 -> x1, waiting for transfers between devices: none -> 2.03 us  [dense_shards(): lax.ppermute(split[:, 1].astype(jnp.bfloat16), AXES[1], swap)]
  transfers between devices with their start and end apart: 20 -> 20, of which waited for: 7 -> 9; matrix products, arithmetic and copies ran while one was open for 19% -> 15% of each run, Pallas kernels for 0% -> 0%
where the time goes in v15:
time: 107 us
  waiting for transfers between devices  46.2 us (43%)
  starting transfers between devices  32.3 us (30%)
  matrix products  12.8 us (12%)
  local copies, waits for them, and re-layouts  8.53 us (8%)
  other arithmetic  6.87 us (6%)
    ppermute x9, waiting for transfers between devices, scatter_stage(): lax.ppermute(pieces[shift].astype(jnp.bfloat16), axis, pairs)  24 us
    ppermute x10, waiting for transfers between devices, gather_stage(): got.append(lax.ppermute(block, axis, pairs))  20.2 us
    ppermute x9, starting transfers between devices, scatter_stage(): lax.ppermute(pieces[shift].astype(jnp.bfloat16), axis, pairs)  17.6 us
    ppermute x10, starting transfers between devices, gather_stage(): got.append(lax.ppermute(block, axis, pairs))  14.1 us
    dot_general x2, matrix products, expert_block(): pair = jnp.dot(rows_in, gate_up, preferred_element_type=jnp.float32)  9.14 us
    unnamed x19, local copies, waits for them, and re-layouts  5.43 us
    dot_general x2, matrix products, expert_block(): jnp.dot(active, down_proj, preferred_element_type=jnp.float32)  3.68 us
  transfers between devices with their start and end apart: 20, of which 9 were waited for; matrix products, arithmetic and copies ran while one was open for 15% of the time, Pallas kernels for 0%

profile of v15, /device:TPU:0, one launch (start us, length us, event | category | flops | bytes accessed | tf_op | source)
XLA Modules:
  0.0 107.0 jit_solution(11043907625193936603)
XLA Ops:
  0.0 0.9 reduce_sum.36
  0.9 0.8 broadcast_divide_fusion
  1.7 0.8 select_reduce_fusion
  2.8 1.1 concatenate.32
  3.8 0.9 constant_dynamic-update-slice_fusion.15
  4.7 3.0 %collective-permute-start.10 = (bf16[32,2176]{1,0:T(8,128)(2,1)}, bf16[32,2176]{1,0:T(8,128)(2,1)}, u32[]{:S(2)}, u32[]{:S(2)}) collective-permute-start(bf16[32,2176]{1,0:T(8,128)(2,1)} %get-tuple-element.29), channel_id=1, source_target_pairs={{0,2},{2,0},{1,3},{3,1},{4,6},{6,4},{5,7},{7,5},{8,10},{10,8},{9,1... | collective-permute-start | bytes 417800 | tf_op jit(solution)/shard_map/ppermute | solution.py:65
  7.7 1.6 %collective-permute-start = (bf16[32,2176]{1,0:T(8,128)(2,1)}, bf16[32,2176]{1,0:T(8,128)(2,1)}, u32[]{:S(2)}, u32[]{:S(2)}) collective-permute-start(bf16[32,2176]{1,0:T(8,128)(2,1)} %get-tuple-element.30), channel_id=1, source_target_pairs={{0,4},{4,8},{8,12},{12,0},{1,5},{5,9},{9,13},{13,1},{2,6},{6,10},{... | collective-permute-start | bytes 417800 | tf_op jit(solution)/shard_map/ppermute | solution.py:65
  9.3 2.6 %collective-permute-start.1 = (bf16[32,2176]{1,0:T(8,128)(2,1)}, bf16[32,2176]{1,0:T(8,128)(2,1)S(1)}, u32[]{:S(2)}, u32[]{:S(2)}) collective-permute-start(bf16[32,2176]{1,0:T(8,128)(2,1)} %get-tuple-element.30), channel_id=1, source_target_pairs={{0,8},{4,12},{8,0},{12,4},{1,9},{5,13},{9,1},{13,5},{2,10},{6,14},... | collective-permute-start | bytes 417800 | tf_op jit(solution)/shard_map/ppermute | solution.py:65
  11.9 1.3 %collective-permute-start.2 = (bf16[32,2176]{1,0:T(8,128)(2,1)}, bf16[32,2176]{1,0:T(8,128)(2,1)S(1)}, u32[]{:S(2)}, u32[]{:S(2)}) collective-permute-start(bf16[32,2176]{1,0:T(8,128)(2,1)} %get-tuple-element.30), channel_id=1, source_target_pairs={{0,12},{4,0},{8,4},{12,8},{1,13},{5,1},{9,5},{13,9},{2,14},{6,2},{... | collective-permute-start | bytes 417800 | tf_op jit(solution)/shard_map/ppermute | solution.py:65
  13.2 1.0 pad_maximum_fusion.1
  14.2 0.7 collective-permute-start.11
  15.0 2.2 %collective-permute-start.12 = (bf16[64,2176]{1,0:T(8,128)(2,1)S(1)}, bf16[64,2176]{1,0:T(8,128)(2,1)S(1)}, u32[]{:S(2)}, u32[]{:S(2)}) collective-permute-start(bf16[64,2176]{1,0:T(8,128)(2,1)S(1)} %pad_maximum_fusion.1), channel_id=1, source_target_pairs={{0,8},{4,12},{8,0},{12,4},{1,9},{5,13},{9,1},{13,5},{2,10},{6,14},... | collective-permute-start | bytes 835592 | tf_op jit(solution)/shard_map/ppermute | solution.py:65
  17.2 1.3 %collective-permute-start.13 = (bf16[64,2176]{1,0:T(8,128)(2,1)S(1)}, bf16[64,2176]{1,0:T(8,128)(2,1)S(1)}, u32[]{:S(2)}, u32[]{:S(2)}) collective-permute-start(bf16[64,2176]{1,0:T(8,128)(2,1)S(1)} %pad_maximum_fusion.1), channel_id=1, source_target_pairs={{0,12},{4,0},{8,4},{12,8},{1,13},{5,1},{9,5},{13,9},{2,14},{6,2},{... | collective-permute-start | bytes 835592 | tf_op jit(solution)/shard_map/ppermute | solution.py:65
  18.5 13.2 %collective-permute-done.1 = bf16[32,2176]{1,0:T(8,128)(2,1)S(1)} collective-permute-done((bf16[32,2176]{1,0:T(8,128)(2,1)}, bf16[32,2176]{1,0:T(8,128)(2,1)S(1)}, u32[]{:S(2)}, u32[]{:S(2)}) %collective-permute-start.1) | collective-permute-done | bytes 139296 | tf_op jit(solution)/shard_map/ppermute | solution.py:65
  31.7 1.0 pad_maximum_fusion
  32.7 0.8 collective-permute-start.3
  33.5 1.6 %constant_dynamic-update-slice_fusion.14 = (bf16[256,2176]{1,0:T(8,128)(2,1)}, bf16[512,2176]{1,0:T(8,128)(2,1)}) fusion(bf16[256,2176]{1,0:T(8,128)(2,1)} %get-tuple-element.25, bf16[32,2176]{1,0:T(8,128)(2,1)} %collective-permute-done.10, bf16[512,2176]{1,0:T(8,128)(2,1)} %get-tuple-element.28), kind=kLoop, calls=%fused_computation.70 | loop fusion | bytes 417792
  35.2 0.9 constant_dynamic-update-slice_fusion.13
  36.0 5.9 %collective-permute-done.12 = bf16[64,2176]{1,0:T(8,128)(2,1)S(1)} collective-permute-done((bf16[64,2176]{1,0:T(8,128)(2,1)S(1)}, bf16[64,2176]{1,0:T(8,128)(2,1)S(1)}, u32[]{:S(2)}, u32[]{:S(2)}) %collective-permute-start.12) | collective-permute-done | bytes 278560 | tf_op jit(solution)/shard_map/ppermute | solution.py:65
  41.9 0.8 constant_dynamic-update-slice_fusion.12
  42.7 0.9 constant_dynamic-update-slice_fusion.11
  43.6 1.1 %constant_dynamic-update-slice_fusion.3 = (bf16[256,2176]{1,0:T(8,128)(2,1)S(1)}, bf16[512,2176]{1,0:T(8,128)(2,1)S(1)}) fusion(bf16[256,2176]{1,0:T(8,128)(2,1)S(1)} %copy-done.3, bf16[32,2176]{1,0:T(8,128)(2,1)} %collective-permute-done, bf16[512,2176]{1,0:T(8,128)(2,1)S(1)} %copy-done.1), kind=kLoop, calls=%fused_computation.59 | loop fusion | bytes 417792
  44.9 0.5 collective-permute-start.4
  45.4 1.2 %collective-permute-done.14 = bf16[256,2176]{1,0:T(8,128)(2,1)S(1)} collective-permute-done((bf16[256,2176]{1,0:T(8,128)(2,1)}, bf16[256,2176]{1,0:T(8,128)(2,1)S(1)}, u32[]{:S(2)}, u32[]{:S(2)}) %collective-permute-start.14) | collective-permute-done | bytes 1114144 | tf_op jit(solution)/shard_map/ppermute | solution.py:65
  46.8 5.7 %fusion = f32[512,1536]{1,0:T(8,128)S(1)} fusion(bf16[1,2048,1536]{2,1,0:T(8,128)(2,1)} %param.10, bf16[512,2176]{1,0:T(8,128)(2,1)S(1)} %constant_dynamic-update-slice_fusion.16), kind=kOutput, calls=%fused_computation | convolution fusion | flops 3221225472 | bytes 11534336 | tf_op jit(solution)/shard_map/dot_general | solution.py:9
  52.5 0.1 constant_dynamic-update-slice_fusion.5
  52.7 3.4 %fusion.2 = f32[512,1536]{1,0:T(8,128)S(1)} fusion(bf16[1,2048,1536]{2,1,0:T(8,128)(2,1)S(1)} %bitcast.45, bf16[512,2176]{1,0:T(8,128)(2,1)S(1)} %constant_dynamic-update-slice_fusion.5), kind=kOutput, calls=%fused_computation.2 | convolution fusion | flops 3221225472 | bytes 11534336 | tf_op jit(solution)/shard_map/dot_general | solution.py:9
  56.1 0.5 fusion.38
  56.7 1.8 %convert_multiply_fusion.1 = f32[512,2048]{1,0:T(8,128)S(1)} fusion(bf16[1,768,2048]{2,1,0:T(8,128)(2,1)S(1)} %copy-done, f32[512]{0:T(512)S(1)} %get-tuple-element.5, f32[512,1536]{1,0:T(8,128)S(1)} %fusion.2), kind=kOutput, calls=%fused_computation.5 | convolution fusion | flops 1616117760 | bytes 10487808 | tf_op jit(solution)/shard_map/dot_general | solution.py:11
  58.7 0.2 collective-permute-start.5
  58.9 1.8 %convert_multiply_fusion = f32[512,2048]{1,0:T(8,128)S(1)} fusion(bf16[1,768,2048]{2,1,0:T(8,128)(2,1)S(1)} %copy-done, f32[512]{0:T(512)S(1)} %get-tuple-element.6, f32[512,1536]{1,0:T(8,128)S(1)} %fusion), kind=kOutput, calls=%fused_computation.4 | convolution fusion | flops 1616117760 | bytes 10487808 | tf_op jit(solution)/shard_map/dot_general | solution.py:11
  60.9 0.4 collective-permute-start.15
  61.4 0.3 slice_add_fusion.1
  61.8 0.6 collective-permute-start.6
  62.4 1.2 %collective-permute-done.15 = bf16[256,2048]{1,0:T(8,128)(2,1)S(1)} collective-permute-done((bf16[256,2048]{1,0:T(8,128)(2,1)S(1)}, bf16[256,2048]{1,0:T(8,128)(2,1)S(1)}, u32[]{:S(2)}, u32[]{:S(2)}) %collective-permute-start.15) | collective-permute-done | bytes 1048608 | tf_op jit(solution)/shard_map/ppermute | solution.py:74
  63.6 0.3 slice_add_fusion
  64.0 0.6 collective-permute-start.16
  64.6 12.1 %collective-permute-done.6 = bf16[128,2048]{1,0:T(8,128)(2,1)S(1)} collective-permute-done((bf16[128,2048]{1,0:T(8,128)(2,1)S(1)}, bf16[128,2048]{1,0:T(8,128)(2,1)S(1)}, u32[]{:S(2)}, u32[]{:S(2)}) %collective-permute-start.6) | collective-permute-done | bytes 524320 | tf_op jit(solution)/shard_map/ppermute | solution.py:74
  76.7 0.1 fusion.42
  76.9 7.5 %collective-permute-start.7 = (bf16[32,2048]{1,0:T(8,128)(2,1)S(1)}, bf16[32,2048]{1,0:T(8,128)(2,1)S(1)}, u32[]{:S(2)}, u32[]{:S(2)}) collective-permute-start(bf16[32,2048]{1,0:T(8,128)(2,1)S(1)} %get-tuple-element.13), channel_id=1, source_target_pairs={{0,12},{4,0},{8,4},{12,8},{1,13},{5,1},{9,5},{13,9},{2,14},{6,2},{... | collective-permute-start | bytes 393224 | tf_op jit(solution)/shard_map/ppermute | solution.py:74
  84.4 0.6 collective-permute-start.9
  85.1 2.0 %collective-permute-done.16 = bf16[4,32,2048]{2,1,0:T(8,128)(2,1)S(1)} collective-permute-done((bf16[4,32,2048]{2,1,0:T(8,128)(2,1)S(1)}, bf16[4,32,2048]{2,1,0:T(8,128)(2,1)S(1)}, u32[]{:S(2)}, u32[]{:S(2)}) %collective-permute-start.16) | collective-permute-done | bytes 524320 | tf_op jit(solution)/shard_map/ppermute | solution.py:114
  87.1 0.2 fusion.43
  87.3 7.5 %collective-permute-start.17 = (bf16[32,2048]{1,0:T(8,128)(2,1)S(1)}, bf16[32,2048]{1,0:T(8,128)(2,1)S(1)}, u32[]{:S(2)}, u32[]{:S(2)}) collective-permute-start(bf16[32,2048]{1,0:T(8,128)(2,1)S(1)} %get-tuple-element.16), channel_id=1, source_target_pairs={{0,12},{4,0},{8,4},{12,8},{1,13},{5,1},{9,5},{13,9},{2,14},{6,2},{... | collective-permute-start | bytes 393224 | tf_op jit(solution)/shard_map/ppermute | solution.py:74
  94.9 0.6 collective-permute-start.19
  95.6 3.2 %collective-permute-done.17 = bf16[32,2048]{1,0:T(8,128)(2,1)S(1)} collective-permute-done((bf16[32,2048]{1,0:T(8,128)(2,1)S(1)}, bf16[32,2048]{1,0:T(8,128)(2,1)S(1)}, u32[]{:S(2)}, u32[]{:S(2)}) %collective-permute-start.17) | collective-permute-done | bytes 131104 | tf_op jit(solution)/shard_map/ppermute | solution.py:74
  98.7 7.5 %collective-permute-done.18 = bf16[32,2048]{1,0:T(8,128)(2,1)S(1)} collective-permute-done((bf16[32,2048]{1,0:T(8,128)(2,1)S(1)}, bf16[32,2048]{1,0:T(8,128)(2,1)S(1)}, u32[]{:S(2)}, u32[]{:S(2)}) %collective-permute-start.18) | collective-permute-done | bytes 131104 | tf_op jit(solution)/shard_map/ppermute | solution.py:74
  106.3 0.7 pad_maximum_fusion.2
  (48 shorter events, 1.4 us)
Async XLA Ops:
  0.0 56.7 %copy-start = (bf16[1,768,2048]{2,1,0:T(8,128)(2,1)S(1)}, bf16[1,768,2048]{2,1,0:T(8,128)(2,1)}, u32[]{:S(2)}) copy-start(bf16[1,768,2048]{2,1,0:T(8,128)(2,1)} %param.11) | copy-start | bytes 9437188
  4.7 8.5 %collective-permute-start.10 = (bf16[32,2176]{1,0:T(8,128)(2,1)}, bf16[32,2176]{1,0:T(8,128)(2,1)}, u32[]{:S(2)}, u32[]{:S(2)}) collective-permute-start(bf16[32,2176]{1,0:T(8,128)(2,1)} %get-tuple-element.29), channel_id=1, source_target_pairs={{0,2},{2,0},{1,3},{3,1},{4,6},{6,4},{5,7},{7,5},{8,10},{10,8},{9,1... | collective-permute-start | bytes 417800 | tf_op jit(solution)/shard_map/ppermute | solution.py:65
  7.7 9.5 %collective-permute-start = (bf16[32,2176]{1,0:T(8,128)(2,1)}, bf16[32,2176]{1,0:T(8,128)(2,1)}, u32[]{:S(2)}, u32[]{:S(2)}) collective-permute-start(bf16[32,2176]{1,0:T(8,128)(2,1)} %get-tuple-element.30), channel_id=1, source_target_pairs={{0,4},{4,8},{8,12},{12,0},{1,5},{5,9},{9,13},{13,1},{2,6},{6,10},{... | collective-permute-start | bytes 417800 | tf_op jit(solution)/shard_map/ppermute | solution.py:65
  9.3 22.4 %collective-permute-start.1 = (bf16[32,2176]{1,0:T(8,128)(2,1)}, bf16[32,2176]{1,0:T(8,128)(2,1)S(1)}, u32[]{:S(2)}, u32[]{:S(2)}) collective-permute-start(bf16[32,2176]{1,0:T(8,128)(2,1)} %get-tuple-element.30), channel_id=1, source_target_pairs={{0,8},{4,12},{8,0},{12,4},{1,9},{5,13},{9,1},{13,5},{2,10},{6,14},... | collective-permute-start | bytes 417800 | tf_op jit(solution)/shard_map/ppermute | solution.py:65
  11.9 19.8 %collective-permute-start.2 = (bf16[32,2176]{1,0:T(8,128)(2,1)}, bf16[32,2176]{1,0:T(8,128)(2,1)S(1)}, u32[]{:S(2)}, u32[]{:S(2)}) collective-permute-start(bf16[32,2176]{1,0:T(8,128)(2,1)} %get-tuple-element.30), channel_id=1, source_target_pairs={{0,12},{4,0},{8,4},{12,8},{1,13},{5,1},{9,5},{13,9},{2,14},{6,2},{... | collective-permute-start | bytes 417800 | tf_op jit(solution)/shard_map/ppermute | solution.py:65
  14.2 29.4 %copy-start.1 = (bf16[512,2176]{1,0:T(8,128)(2,1)S(1)}, bf16[512,2176]{1,0:T(8,128)(2,1)}, u32[]{:S(2)}) copy-start(bf16[512,2176]{1,0:T(8,128)(2,1)} %get-tuple-element.27) | copy-start | bytes 6684676
  14.2 29.4 %copy-start.3 = (bf16[256,2176]{1,0:T(8,128)(2,1)S(1)}, bf16[256,2176]{1,0:T(8,128)(2,1)}, u32[]{:S(2)}) copy-start(bf16[256,2176]{1,0:T(8,128)(2,1)} %get-tuple-element.26) | copy-start | bytes 3342340
  14.2 20.9 %collective-permute-start.11 = (bf16[64,2176]{1,0:T(8,128)(2,1)S(1)}, bf16[64,2176]{1,0:T(8,128)(2,1)S(1)}, u32[]{:S(2)}, u32[]{:S(2)}) collective-permute-start(bf16[64,2176]{1,0:T(8,128)(2,1)S(1)} %pad_maximum_fusion.1), channel_id=1, source_target_pairs={{0,4},{4,8},{8,12},{12,0},{1,5},{5,9},{9,13},{13,1},{2,6},{6,10},{... | collective-permute-start | bytes 835592 | tf_op jit(solution)/shard_map/ppermute | solution.py:65
  15.0 26.9 %collective-permute-start.12 = (bf16[64,2176]{1,0:T(8,128)(2,1)S(1)}, bf16[64,2176]{1,0:T(8,128)(2,1)S(1)}, u32[]{:S(2)}, u32[]{:S(2)}) collective-permute-start(bf16[64,2176]{1,0:T(8,128)(2,1)S(1)} %pad_maximum_fusion.1), channel_id=1, source_target_pairs={{0,8},{4,12},{8,0},{12,4},{1,9},{5,13},{9,1},{13,5},{2,10},{6,14},... | collective-permute-start | bytes 835592 | tf_op jit(solution)/shard_map/ppermute | solution.py:65
  17.2 25.6 %collective-permute-start.13 = (bf16[64,2176]{1,0:T(8,128)(2,1)S(1)}, bf16[64,2176]{1,0:T(8,128)(2,1)S(1)}, u32[]{:S(2)}, u32[]{:S(2)}) collective-permute-start(bf16[64,2176]{1,0:T(8,128)(2,1)S(1)} %pad_maximum_fusion.1), channel_id=1, source_target_pairs={{0,12},{4,0},{8,4},{12,8},{1,13},{5,1},{9,5},{13,9},{2,14},{6,2},{... | collective-permute-start | bytes 835592 | tf_op jit(solution)/shard_map/ppermute | solution.py:65
  32.7 12.1 %collective-permute-start.3 = (bf16[128,2176]{1,0:T(8,128)(2,1)S(1)}, bf16[128,2176]{1,0:T(8,128)(2,1)S(1)}, u32[]{:S(2)}, u32[]{:S(2)}) collective-permute-start(bf16[128,2176]{1,0:T(8,128)(2,1)S(1)} %pad_maximum_fusion), channel_id=1, source_target_pairs={{0,2},{2,0},{1,3},{3,1},{4,6},{6,4},{5,7},{7,5},{8,10},{10,8},{9,1... | collective-permute-start | bytes 1671176 | tf_op jit(solution)/shard_map/ppermute | solution.py:65
  43.6 3.0 %copy-start.2 = (bf16[512,2176]{1,0:T(8,128)(2,1)S(1)}, bf16[512,2176]{1,0:T(8,128)(2,1)}, u32[]{:S(2)}) copy-start(bf16[512,2176]{1,0:T(8,128)(2,1)} %get-tuple-element.20) | copy-start | bytes 6684676
  43.6 3.0 %collective-permute-start.14 = (bf16[256,2176]{1,0:T(8,128)(2,1)}, bf16[256,2176]{1,0:T(8,128)(2,1)S(1)}, u32[]{:S(2)}, u32[]{:S(2)}) collective-permute-start(bf16[256,2176]{1,0:T(8,128)(2,1)} %get-tuple-element.19), channel_id=1, source_target_pairs={{0,1},{1,0},{2,3},{3,2},{4,5},{5,4},{6,7},{7,6},{8,9},{9,8},{10,11... | collective-permute-start | bytes 3342344 | tf_op jit(solution)/shard_map/ppermute | solution.py:65
  44.9 7.5 %collective-permute-start.4 = (bf16[256,2176]{1,0:T(8,128)(2,1)S(1)}, bf16[256,2176]{1,0:T(8,128)(2,1)S(1)}, u32[]{:S(2)}, u32[]{:S(2)}) collective-permute-start(bf16[256,2176]{1,0:T(8,128)(2,1)S(1)} %get-tuple-element.11), channel_id=1, source_target_pairs={{0,1},{1,0},{2,3},{3,2},{4,5},{5,4},{6,7},{7,6},{8,9},{9,8},{10,11... | collective-permute-start | bytes 3342344 | tf_op jit(solution)/shard_map/ppermute | solution.py:65
  46.7 5.9 %slice-start = ((s8[6291456]{0:T(1024)(128)(4,1)}), s8[4194304]{0:T(1024)(128)(4,1)S(1)}, s32[]{:S(2)}) async-start(s8[6291456]{0:T(1024)(128)(4,1)} %bitcast.44), calls=%async_computation | async-start | bytes 8388608
  46.8 5.9 %slice-start.1 = ((s8[6291456]{0:T(1024)(128)(4,1)}), s8[2097152]{0:T(1024)(128)(4,1)S(1)}, s32[]{:S(2)}) async-start(s8[6291456]{0:T(1024)(128)(4,1)} %bitcast.44), calls=%async_computation.1 | async-start | bytes 4194304
  58.7 2.7 %collective-permute-start.5 = (bf16[256,2048]{1,0:T(8,128)(2,1)S(1)}, bf16[256,2048]{1,0:T(8,128)(2,1)S(1)}, u32[]{:S(2)}, u32[]{:S(2)}) collective-permute-start(bf16[256,2048]{1,0:T(8,128)(2,1)S(1)} %split.119), channel_id=1, source_target_pairs={{0,1},{1,0},{2,3},{3,2},{4,5},{5,4},{6,7},{7,6},{8,9},{9,8},{10,11... | collective-permute-start | bytes 3145736 | tf_op jit(solution)/shard_map/ppermute | solution.py:74
  60.9 2.7 %collective-permute-start.15 = (bf16[256,2048]{1,0:T(8,128)(2,1)S(1)}, bf16[256,2048]{1,0:T(8,128)(2,1)S(1)}, u32[]{:S(2)}, u32[]{:S(2)}) collective-permute-start(bf16[256,2048]{1,0:T(8,128)(2,1)S(1)} %split.118), channel_id=1, source_target_pairs={{0,1},{1,0},{2,3},{3,2},{4,5},{5,4},{6,7},{7,6},{8,9},{9,8},{10,11... | collective-permute-start | bytes 3145736 | tf_op jit(solution)/shard_map/ppermute | solution.py:74
  61.8 14.9 %collective-permute-start.6 = (bf16[128,2048]{1,0:T(8,128)(2,1)S(1)}, bf16[128,2048]{1,0:T(8,128)(2,1)S(1)}, u32[]{:S(2)}, u32[]{:S(2)}) collective-permute-start(bf16[128,2048]{1,0:T(8,128)(2,1)S(1)} %split.120), channel_id=1, source_target_pairs={{0,2},{2,0},{1,3},{3,1},{4,6},{6,4},{5,7},{7,5},{8,10},{10,8},{9,1... | collective-permute-start | bytes 1572872 | tf_op jit(solution)/shard_map/ppermute | solution.py:74
  64.0 23.1 %collective-permute-start.16 = (bf16[4,32,2048]{2,1,0:T(8,128)(2,1)S(1)}, bf16[4,32,2048]{2,1,0:T(8,128)(2,1)S(1)}, u32[]{:S(2)}, u32[]{:S(2)}) collective-permute-start(bf16[4,32,2048]{2,1,0:T(8,128)(2,1)S(1)} %fusion.27), channel_id=1, source_target_pairs={{0,2},{2,0},{1,3},{3,1},{4,6},{6,4},{5,7},{7,5},{8,10},{10,8},{9,1... | collective-permute-start | bytes 1572872 | tf_op jit(solution)/shard_map/ppermute | solution.py:114
  76.9 18.0 %collective-permute-start.7 = (bf16[32,2048]{1,0:T(8,128)(2,1)S(1)}, bf16[32,2048]{1,0:T(8,128)(2,1)S(1)}, u32[]{:S(2)}, u32[]{:S(2)}) collective-permute-start(bf16[32,2048]{1,0:T(8,128)(2,1)S(1)} %get-tuple-element.13), channel_id=1, source_target_pairs={{0,12},{4,0},{8,4},{12,8},{1,13},{5,1},{9,5},{13,9},{2,14},{6,2},{... | collective-permute-start | bytes 393224 | tf_op jit(solution)/shard_map/ppermute | solution.py:74
  84.4 11.1 %collective-permute-start.8 = (bf16[32,2048]{1,0:T(8,128)(2,1)S(1)}, bf16[32,2048]{1,0:T(8,128)(2,1)S(1)}, u32[]{:S(2)}, u32[]{:S(2)}) collective-permute-start(bf16[32,2048]{1,0:T(8,128)(2,1)S(1)} %get-tuple-element.15), channel_id=1, source_target_pairs={{0,8},{4,12},{8,0},{12,4},{1,9},{5,13},{9,1},{13,5},{2,10},{6,14},... | collective-permute-start | bytes 393224 | tf_op jit(solution)/shard_map/ppermute | solution.py:74
  84.4 11.1 %collective-permute-start.9 = (bf16[32,2048]{1,0:T(8,128)(2,1)S(1)}, bf16[32,2048]{1,0:T(8,128)(2,1)S(1)}, u32[]{:S(2)}, u32[]{:S(2)}) collective-permute-start(bf16[32,2048]{1,0:T(8,128)(2,1)S(1)} %get-tuple-element.14), channel_id=1, source_target_pairs={{0,4},{4,8},{8,12},{12,0},{1,5},{5,9},{9,13},{13,1},{2,6},{6,10},{... | collective-permute-start | bytes 393224 | tf_op jit(solution)/shard_map/ppermute | solution.py:74
  87.3 11.4 %collective-permute-start.17 = (bf16[32,2048]{1,0:T(8,128)(2,1)S(1)}, bf16[32,2048]{1,0:T(8,128)(2,1)S(1)}, u32[]{:S(2)}, u32[]{:S(2)}) collective-permute-start(bf16[32,2048]{1,0:T(8,128)(2,1)S(1)} %get-tuple-element.16), channel_id=1, source_target_pairs={{0,12},{4,0},{8,4},{12,8},{1,13},{5,1},{9,5},{13,9},{2,14},{6,2},{... | collective-permute-start | bytes 393224 | tf_op jit(solution)/shard_map/ppermute | solution.py:74
  94.9 11.4 %collective-permute-start.18 = (bf16[32,2048]{1,0:T(8,128)(2,1)S(1)}, bf16[32,2048]{1,0:T(8,128)(2,1)S(1)}, u32[]{:S(2)}, u32[]{:S(2)}) collective-permute-start(bf16[32,2048]{1,0:T(8,128)(2,1)S(1)} %get-tuple-element.18), channel_id=1, source_target_pairs={{0,8},{4,12},{8,0},{12,4},{1,9},{5,13},{9,1},{13,5},{2,10},{6,14},... | collective-permute-start | bytes 393224 | tf_op jit(solution)/shard_map/ppermute | solution.py:74
  94.9 11.4 %collective-permute-start.19 = (bf16[32,2048]{1,0:T(8,128)(2,1)S(1)}, bf16[32,2048]{1,0:T(8,128)(2,1)S(1)}, u32[]{:S(2)}, u32[]{:S(2)}) collective-permute-start(bf16[32,2048]{1,0:T(8,128)(2,1)S(1)} %get-tuple-element.17), channel_id=1, source_target_pairs={{0,4},{4,8},{8,12},{12,0},{1,5},{5,9},{9,13},{13,1},{2,6},{6,10},{... | collective-permute-start | bytes 393224 | tf_op jit(solution)/shard_map/ppermute | solution.py:74

commit v16 on v15

--- a/solution.py
+++ b/solution.py
@@ -108,6 +108,7 @@
         part = out.astype(jnp.float32) * mine[:, None]
         if number % 2:
             part = scatter_stage(part, AXES[2], sizes[2])
+            _, part = lax.optimization_barrier((x_back, part))
             split = part.reshape((sizes[0], sizes[1], -1) + part.shape[1:])
             total = split[:, 0]
             swap = [(i, (i + 1) % sizes[1]) for i in range(sizes[1])]
@@ -116,6 +117,8 @@
         else:
             for axis, size in order[::-1]:
                 part = scatter_stage(part, axis, size)
+                if axis == AXES[1]:
+                    x_back = part
         results.append(part)
     return jnp.concatenate(results, axis=0).astype(jnp.bfloat16)
 

time: 107 us -> 109 us (1.019)
  waiting for transfers between devices: 46.2 us -> 47.7 us
    ppermute x1, waiting for transfers between devices: 2.03 us -> 4.35 us  [dense_shards(): lax.ppermute(split[:, 1].astype(jnp.bfloat16), AXES[1], swap)]
where the time goes in v16:
time: 109 us
  waiting for transfers between devices  47.7 us (44%)
  starting transfers between devices  32.3 us (30%)
  matrix products  12.8 us (12%)
  local copies, waits for them, and re-layouts  8.53 us (8%)
  other arithmetic  6.86 us (6%)
    ppermute x9, waiting for transfers between devices, scatter_stage(): lax.ppermute(pieces[shift].astype(jnp.bfloat16), axis, pairs)  23.2 us
    ppermute x10, waiting for transfers between devices, gather_stage(): got.append(lax.ppermute(block, axis, pairs))  20.2 us
    ppermute x9, starting transfers between devices, scatter_stage(): lax.ppermute(pieces[shift].astype(jnp.bfloat16), axis, pairs)  17.6 us
    ppermute x10, starting transfers between devices, gather_stage(): got.append(lax.ppermute(block, axis, pairs))  14.1 us
    dot_general x2, matrix products, expert_block(): pair = jnp.dot(rows_in, gate_up, preferred_element_type=jnp.float32)  9.14 us
    unnamed x19, local copies, waits for them, and re-layouts  5.43 us
    ppermute x1, waiting for transfers between devices, dense_shards(): lax.ppermute(split[:, 1].astype(jnp.bfloat16), AXES[1], swap)  4.35 us
    dot_general x2, matrix products, expert_block(): jnp.dot(active, down_proj, preferred_element_type=jnp.float32)  3.68 us
  transfers between devices with their start and end apart: 20, of which 9 were waited for; matrix products, arithmetic and copies ran while one was open for 15% of the time, Pallas kernels for 0%

profile of v16, /device:TPU:0, one launch (start us, length us, event | category | flops | bytes accessed | tf_op | source)
XLA Modules:
  0.0 108.5 jit_solution(7973867424046649637)
XLA Ops:
  0.0 0.9 reduce_sum.36
  0.9 0.8 broadcast_divide_fusion
  1.7 0.8 select_reduce_fusion
  2.8 1.1 concatenate.32
  3.8 0.9 constant_dynamic-update-slice_fusion.4
  4.7 3.0 %collective-permute-start.10 = (bf16[32,2176]{1,0:T(8,128)(2,1)}, bf16[32,2176]{1,0:T(8,128)(2,1)}, u32[]{:S(2)}, u32[]{:S(2)}) collective-permute-start(bf16[32,2176]{1,0:T(8,128)(2,1)} %get-tuple-element.25), channel_id=1, source_target_pairs={{0,2},{2,0},{1,3},{3,1},{4,6},{6,4},{5,7},{7,5},{8,10},{10,8},{9,1... | collective-permute-start | bytes 417800 | tf_op jit(solution)/shard_map/ppermute | solution.py:65
  7.7 1.6 %collective-permute-start = (bf16[32,2176]{1,0:T(8,128)(2,1)}, bf16[32,2176]{1,0:T(8,128)(2,1)}, u32[]{:S(2)}, u32[]{:S(2)}) collective-permute-start(bf16[32,2176]{1,0:T(8,128)(2,1)} %get-tuple-element.26), channel_id=1, source_target_pairs={{0,4},{4,8},{8,12},{12,0},{1,5},{5,9},{9,13},{13,1},{2,6},{6,10},{... | collective-permute-start | bytes 417800 | tf_op jit(solution)/shard_map/ppermute | solution.py:65
  9.3 2.6 %collective-permute-start.1 = (bf16[32,2176]{1,0:T(8,128)(2,1)}, bf16[32,2176]{1,0:T(8,128)(2,1)S(1)}, u32[]{:S(2)}, u32[]{:S(2)}) collective-permute-start(bf16[32,2176]{1,0:T(8,128)(2,1)} %get-tuple-element.26), channel_id=1, source_target_pairs={{0,8},{4,12},{8,0},{12,4},{1,9},{5,13},{9,1},{13,5},{2,10},{6,14},... | collective-permute-start | bytes 417800 | tf_op jit(solution)/shard_map/ppermute | solution.py:65
  11.9 1.3 %collective-permute-start.2 = (bf16[32,2176]{1,0:T(8,128)(2,1)}, bf16[32,2176]{1,0:T(8,128)(2,1)S(1)}, u32[]{:S(2)}, u32[]{:S(2)}) collective-permute-start(bf16[32,2176]{1,0:T(8,128)(2,1)} %get-tuple-element.26), channel_id=1, source_target_pairs={{0,12},{4,0},{8,4},{12,8},{1,13},{5,1},{9,5},{13,9},{2,14},{6,2},{... | collective-permute-start | bytes 417800 | tf_op jit(solution)/shard_map/ppermute | solution.py:65
  13.2 1.0 pad_maximum_fusion.1
  14.2 0.7 collective-permute-start.11
  15.0 2.2 %collective-permute-start.12 = (bf16[64,2176]{1,0:T(8,128)(2,1)S(1)}, bf16[64,2176]{1,0:T(8,128)(2,1)S(1)}, u32[]{:S(2)}, u32[]{:S(2)}) collective-permute-start(bf16[64,2176]{1,0:T(8,128)(2,1)S(1)} %pad_maximum_fusion.1), channel_id=1, source_target_pairs={{0,8},{4,12},{8,0},{12,4},{1,9},{5,13},{9,1},{13,5},{2,10},{6,14},... | collective-permute-start | bytes 835592 | tf_op jit(solution)/shard_map/ppermute | solution.py:65
  17.2 1.3 %collective-permute-start.13 = (bf16[64,2176]{1,0:T(8,128)(2,1)S(1)}, bf16[64,2176]{1,0:T(8,128)(2,1)S(1)}, u32[]{:S(2)}, u32[]{:S(2)}) collective-permute-start(bf16[64,2176]{1,0:T(8,128)(2,1)S(1)} %pad_maximum_fusion.1), channel_id=1, source_target_pairs={{0,12},{4,0},{8,4},{12,8},{1,13},{5,1},{9,5},{13,9},{2,14},{6,2},{... | collective-permute-start | bytes 835592 | tf_op jit(solution)/shard_map/ppermute | solution.py:65
  18.5 13.2 %collective-permute-done.1 = bf16[32,2176]{1,0:T(8,128)(2,1)S(1)} collective-permute-done((bf16[32,2176]{1,0:T(8,128)(2,1)}, bf16[32,2176]{1,0:T(8,128)(2,1)S(1)}, u32[]{:S(2)}, u32[]{:S(2)}) %collective-permute-start.1) | collective-permute-done | bytes 139296 | tf_op jit(solution)/shard_map/ppermute | solution.py:65
  31.7 1.0 pad_maximum_fusion
  32.7 0.8 collective-permute-start.3
  33.5 1.6 %constant_dynamic-update-slice_fusion.14 = (bf16[256,2176]{1,0:T(8,128)(2,1)}, bf16[512,2176]{1,0:T(8,128)(2,1)}) fusion(bf16[256,2176]{1,0:T(8,128)(2,1)} %get-tuple-element.23, bf16[32,2176]{1,0:T(8,128)(2,1)} %collective-permute-done.10, bf16[512,2176]{1,0:T(8,128)(2,1)} %get-tuple-element.24), kind=kLoop, calls=%fused_computation.70 | loop fusion | bytes 417792
  35.2 0.9 constant_dynamic-update-slice_fusion.13
  36.0 5.9 %collective-permute-done.12 = bf16[64,2176]{1,0:T(8,128)(2,1)S(1)} collective-permute-done((bf16[64,2176]{1,0:T(8,128)(2,1)S(1)}, bf16[64,2176]{1,0:T(8,128)(2,1)S(1)}, u32[]{:S(2)}, u32[]{:S(2)}) %collective-permute-start.12) | collective-permute-done | bytes 278560 | tf_op jit(solution)/shard_map/ppermute | solution.py:65
  41.9 0.8 constant_dynamic-update-slice_fusion.12
  42.7 0.9 constant_dynamic-update-slice_fusion.11
  43.6 1.1 constant_dynamic-update-slice_fusion.3
  44.9 0.5 collective-permute-start.4
  45.4 1.2 %collective-permute-done.14 = bf16[256,2176]{1,0:T(8,128)(2,1)S(1)} collective-permute-done((bf16[256,2176]{1,0:T(8,128)(2,1)}, bf16[256,2176]{1,0:T(8,128)(2,1)S(1)}, u32[]{:S(2)}, u32[]{:S(2)}) %collective-permute-start.14) | collective-permute-done | bytes 1114144 | tf_op jit(solution)/shard_map/ppermute | solution.py:65
  46.8 5.7 %fusion = f32[512,1536]{1,0:T(8,128)S(1)} fusion(bf16[1,2048,1536]{2,1,0:T(8,128)(2,1)} %param.10, bf16[512,2176]{1,0:T(8,128)(2,1)S(1)} %constant_dynamic-update-slice_fusion.16), kind=kOutput, calls=%fused_computation | convolution fusion | flops 3221225472 | bytes 11534336 | tf_op jit(solution)/shard_map/dot_general | solution.py:9
  52.5 0.1 constant_dynamic-update-slice_fusion.5
  52.7 3.4 %fusion.2 = f32[512,1536]{1,0:T(8,128)S(1)} fusion(bf16[1,2048,1536]{2,1,0:T(8,128)(2,1)S(1)} %bitcast.45, bf16[512,2176]{1,0:T(8,128)(2,1)S(1)} %constant_dynamic-update-slice_fusion.5), kind=kOutput, calls=%fused_computation.2 | convolution fusion | flops 3221225472 | bytes 11534336 | tf_op jit(solution)/shard_map/dot_general | solution.py:9
  56.1 0.5 fusion.33
  56.7 1.8 %convert_multiply_fusion.1 = f32[512,2048]{1,0:T(8,128)S(1)} fusion(bf16[1,768,2048]{2,1,0:T(8,128)(2,1)S(1)} %copy-done, f32[512]{0:T(512)S(1)} %get-tuple-element.8, f32[512,1536]{1,0:T(8,128)S(1)} %fusion.2), kind=kOutput, calls=%fused_computation.5 | convolution fusion | flops 1616117760 | bytes 10487808 | tf_op jit(solution)/shard_map/dot_general | solution.py:11
  58.7 0.2 collective-permute-start.5
  58.9 1.8 %convert_multiply_fusion = f32[512,2048]{1,0:T(8,128)S(1)} fusion(bf16[1,768,2048]{2,1,0:T(8,128)(2,1)S(1)} %copy-done, f32[512]{0:T(512)S(1)} %get-tuple-element.7, f32[512,1536]{1,0:T(8,128)S(1)} %fusion), kind=kOutput, calls=%fused_computation.4 | convolution fusion | flops 1616117760 | bytes 10487808 | tf_op jit(solution)/shard_map/dot_general | solution.py:11
  60.9 0.4 collective-permute-start.15
  61.4 0.3 slice_add_fusion.1
  61.8 0.6 collective-permute-start.6
  62.4 1.2 %collective-permute-done.15 = bf16[256,2048]{1,0:T(8,128)(2,1)S(1)} collective-permute-done((bf16[256,2048]{1,0:T(8,128)(2,1)S(1)}, bf16[256,2048]{1,0:T(8,128)(2,1)S(1)}, u32[]{:S(2)}, u32[]{:S(2)}) %collective-permute-start.15) | collective-permute-done | bytes 1048608 | tf_op jit(solution)/shard_map/ppermute | solution.py:74
  63.6 0.3 slice_add_fusion
  64.0 11.9 %collective-permute-done.6 = bf16[128,2048]{1,0:T(8,128)(2,1)S(1)} collective-permute-done((bf16[128,2048]{1,0:T(8,128)(2,1)S(1)}, bf16[128,2048]{1,0:T(8,128)(2,1)S(1)}, u32[]{:S(2)}, u32[]{:S(2)}) %collective-permute-start.6) | collective-permute-done | bytes 524320 | tf_op jit(solution)/shard_map/ppermute | solution.py:74
  76.1 0.6 collective-permute-start.16
  76.7 7.6 %collective-permute-start.7 = (bf16[32,2048]{1,0:T(8,128)(2,1)S(1)}, bf16[32,2048]{1,0:T(8,128)(2,1)S(1)}, u32[]{:S(2)}, u32[]{:S(2)}) collective-permute-start(bf16[32,2048]{1,0:T(8,128)(2,1)S(1)} %get-tuple-element.15), channel_id=1, source_target_pairs={{0,12},{4,0},{8,4},{12,8},{1,13},{5,1},{9,5},{13,9},{2,14},{6,2},{... | collective-permute-start | bytes 393224 | tf_op jit(solution)/shard_map/ppermute | solution.py:74
  84.3 0.6 collective-permute-start.9
  84.9 4.4 %collective-permute-done.16 = bf16[4,32,2048]{2,1,0:T(8,128)(2,1)S(1)} collective-permute-done((bf16[4,32,2048]{2,1,0:T(8,128)(2,1)S(1)}, bf16[4,32,2048]{2,1,0:T(8,128)(2,1)S(1)}, u32[]{:S(2)}, u32[]{:S(2)}) %collective-permute-start.16) | collective-permute-done | bytes 524320 | tf_op jit(solution)/shard_map/ppermute | solution.py:115
  89.3 0.2 fusion.43
  89.5 7.6 %collective-permute-start.17 = (bf16[32,2048]{1,0:T(8,128)(2,1)S(1)}, bf16[32,2048]{1,0:T(8,128)(2,1)S(1)}, u32[]{:S(2)}, u32[]{:S(2)}) collective-permute-start(bf16[32,2048]{1,0:T(8,128)(2,1)S(1)} %get-tuple-element.18), channel_id=1, source_target_pairs={{0,12},{4,0},{8,4},{12,8},{1,13},{5,1},{9,5},{13,9},{2,14},{6,2},{... | collective-permute-start | bytes 393224 | tf_op jit(solution)/shard_map/ppermute | solution.py:74
  97.0 0.2 collective-permute-start.18
  97.3 0.4 collective-permute-start.19
  97.7 3.2 %collective-permute-done.17 = bf16[32,2048]{1,0:T(8,128)(2,1)S(1)} collective-permute-done((bf16[32,2048]{1,0:T(8,128)(2,1)S(1)}, bf16[32,2048]{1,0:T(8,128)(2,1)S(1)}, u32[]{:S(2)}, u32[]{:S(2)}) %collective-permute-start.17) | collective-permute-done | bytes 131104 | tf_op jit(solution)/shard_map/ppermute | solution.py:74
  100.9 6.8 %collective-permute-done.18 = bf16[32,2048]{1,0:T(8,128)(2,1)S(1)} collective-permute-done((bf16[32,2048]{1,0:T(8,128)(2,1)S(1)}, bf16[32,2048]{1,0:T(8,128)(2,1)S(1)}, u32[]{:S(2)}, u32[]{:S(2)}) %collective-permute-start.18) | collective-permute-done | bytes 131104 | tf_op jit(solution)/shard_map/ppermute | solution.py:74
  107.8 0.7 pad_maximum_fusion.2
  (48 shorter events, 1.6 us)
Async XLA Ops:
  0.0 56.7 %copy-start = (bf16[1,768,2048]{2,1,0:T(8,128)(2,1)S(1)}, bf16[1,768,2048]{2,1,0:T(8,128)(2,1)}, u32[]{:S(2)}) copy-start(bf16[1,768,2048]{2,1,0:T(8,128)(2,1)} %param.11) | copy-start | bytes 9437188
  4.7 8.5 %collective-permute-start.10 = (bf16[32,2176]{1,0:T(8,128)(2,1)}, bf16[32,2176]{1,0:T(8,128)(2,1)}, u32[]{:S(2)}, u32[]{:S(2)}) collective-permute-start(bf16[32,2176]{1,0:T(8,128)(2,1)} %get-tuple-element.25), channel_id=1, source_target_pairs={{0,2},{2,0},{1,3},{3,1},{4,6},{6,4},{5,7},{7,5},{8,10},{10,8},{9,1... | collective-permute-start | bytes 417800 | tf_op jit(solution)/shard_map/ppermute | solution.py:65
  7.7 9.5 %collective-permute-start = (bf16[32,2176]{1,0:T(8,128)(2,1)}, bf16[32,2176]{1,0:T(8,128)(2,1)}, u32[]{:S(2)}, u32[]{:S(2)}) collective-permute-start(bf16[32,2176]{1,0:T(8,128)(2,1)} %get-tuple-element.26), channel_id=1, source_target_pairs={{0,4},{4,8},{8,12},{12,0},{1,5},{5,9},{9,13},{13,1},{2,6},{6,10},{... | collective-permute-start | bytes 417800 | tf_op jit(solution)/shard_map/ppermute | solution.py:65
  9.3 22.4 %collective-permute-start.1 = (bf16[32,2176]{1,0:T(8,128)(2,1)}, bf16[32,2176]{1,0:T(8,128)(2,1)S(1)}, u32[]{:S(2)}, u32[]{:S(2)}) collective-permute-start(bf16[32,2176]{1,0:T(8,128)(2,1)} %get-tuple-element.26), channel_id=1, source_target_pairs={{0,8},{4,12},{8,0},{12,4},{1,9},{5,13},{9,1},{13,5},{2,10},{6,14},... | collective-permute-start | bytes 417800 | tf_op jit(solution)/shard_map/ppermute | solution.py:65
  11.9 19.8 %collective-permute-start.2 = (bf16[32,2176]{1,0:T(8,128)(2,1)}, bf16[32,2176]{1,0:T(8,128)(2,1)S(1)}, u32[]{:S(2)}, u32[]{:S(2)}) collective-permute-start(bf16[32,2176]{1,0:T(8,128)(2,1)} %get-tuple-element.26), channel_id=1, source_target_pairs={{0,12},{4,0},{8,4},{12,8},{1,13},{5,1},{9,5},{13,9},{2,14},{6,2},{... | collective-permute-start | bytes 417800 | tf_op jit(solution)/shard_map/ppermute | solution.py:65
  14.2 29.4 %copy-start.1 = (bf16[512,2176]{1,0:T(8,128)(2,1)S(1)}, bf16[512,2176]{1,0:T(8,128)(2,1)}, u32[]{:S(2)}) copy-start(bf16[512,2176]{1,0:T(8,128)(2,1)} %get-tuple-element.22) | copy-start | bytes 6684676
  14.2 29.4 %copy-start.3 = (bf16[256,2176]{1,0:T(8,128)(2,1)S(1)}, bf16[256,2176]{1,0:T(8,128)(2,1)}, u32[]{:S(2)}) copy-start(bf16[256,2176]{1,0:T(8,128)(2,1)} %get-tuple-element.21) | copy-start | bytes 3342340
  14.2 20.9 %collective-permute-start.11 = (bf16[64,2176]{1,0:T(8,128)(2,1)S(1)}, bf16[64,2176]{1,0:T(8,128)(2,1)S(1)}, u32[]{:S(2)}, u32[]{:S(2)}) collective-permute-start(bf16[64,2176]{1,0:T(8,128)(2,1)S(1)} %pad_maximum_fusion.1), channel_id=1, source_target_pairs={{0,4},{4,8},{8,12},{12,0},{1,5},{5,9},{9,13},{13,1},{2,6},{6,10},{... | collective-permute-start | bytes 835592 | tf_op jit(solution)/shard_map/ppermute | solution.py:65
  15.0 26.9 %collective-permute-start.12 = (bf16[64,2176]{1,0:T(8,128)(2,1)S(1)}, bf16[64,2176]{1,0:T(8,128)(2,1)S(1)}, u32[]{:S(2)}, u32[]{:S(2)}) collective-permute-start(bf16[64,2176]{1,0:T(8,128)(2,1)S(1)} %pad_maximum_fusion.1), channel_id=1, source_target_pairs={{0,8},{4,12},{8,0},{12,4},{1,9},{5,13},{9,1},{13,5},{2,10},{6,14},... | collective-permute-start | bytes 835592 | tf_op jit(solution)/shard_map/ppermute | solution.py:65
  17.2 25.6 %collective-permute-start.13 = (bf16[64,2176]{1,0:T(8,128)(2,1)S(1)}, bf16[64,2176]{1,0:T(8,128)(2,1)S(1)}, u32[]{:S(2)}, u32[]{:S(2)}) collective-permute-start(bf16[64,2176]{1,0:T(8,128)(2,1)S(1)} %pad_maximum_fusion.1), channel_id=1, source_target_pairs={{0,12},{4,0},{8,4},{12,8},{1,13},{5,1},{9,5},{13,9},{2,14},{6,2},{... | collective-permute-start | bytes 835592 | tf_op jit(solution)/shard_map/ppermute | solution.py:65
  32.7 12.1 %collective-permute-start.3 = (bf16[128,2176]{1,0:T(8,128)(2,1)S(1)}, bf16[128,2176]{1,0:T(8,128)(2,1)S(1)}, u32[]{:S(2)}, u32[]{:S(2)}) collective-permute-start(bf16[128,2176]{1,0:T(8,128)(2,1)S(1)} %pad_maximum_fusion), channel_id=1, source_target_pairs={{0,2},{2,0},{1,3},{3,1},{4,6},{6,4},{5,7},{7,5},{8,10},{10,8},{9,1... | collective-permute-start | bytes 1671176 | tf_op jit(solution)/shard_map/ppermute | solution.py:65
  43.6 3.0 %copy-start.2 = (bf16[512,2176]{1,0:T(8,128)(2,1)S(1)}, bf16[512,2176]{1,0:T(8,128)(2,1)}, u32[]{:S(2)}) copy-start(bf16[512,2176]{1,0:T(8,128)(2,1)} %get-tuple-element.28) | copy-start | bytes 6684676
  43.6 3.0 %collective-permute-start.14 = (bf16[256,2176]{1,0:T(8,128)(2,1)}, bf16[256,2176]{1,0:T(8,128)(2,1)S(1)}, u32[]{:S(2)}, u32[]{:S(2)}) collective-permute-start(bf16[256,2176]{1,0:T(8,128)(2,1)} %get-tuple-element.27), channel_id=1, source_target_pairs={{0,1},{1,0},{2,3},{3,2},{4,5},{5,4},{6,7},{7,6},{8,9},{9,8},{10,11... | collective-permute-start | bytes 3342344 | tf_op jit(solution)/shard_map/ppermute | solution.py:65
  44.9 7.6 %collective-permute-start.4 = (bf16[256,2176]{1,0:T(8,128)(2,1)S(1)}, bf16[256,2176]{1,0:T(8,128)(2,1)S(1)}, u32[]{:S(2)}, u32[]{:S(2)}) collective-permute-start(bf16[256,2176]{1,0:T(8,128)(2,1)S(1)} %get-tuple-element.13), channel_id=1, source_target_pairs={{0,1},{1,0},{2,3},{3,2},{4,5},{5,4},{6,7},{7,6},{8,9},{9,8},{10,11... | collective-permute-start | bytes 3342344 | tf_op jit(solution)/shard_map/ppermute | solution.py:65
  46.7 5.9 %slice-start = ((s8[6291456]{0:T(1024)(128)(4,1)}), s8[4194304]{0:T(1024)(128)(4,1)S(1)}, s32[]{:S(2)}) async-start(s8[6291456]{0:T(1024)(128)(4,1)} %bitcast.44), calls=%async_computation | async-start | bytes 8388608
  46.8 5.9 %slice-start.1 = ((s8[6291456]{0:T(1024)(128)(4,1)}), s8[2097152]{0:T(1024)(128)(4,1)S(1)}, s32[]{:S(2)}) async-start(s8[6291456]{0:T(1024)(128)(4,1)} %bitcast.44), calls=%async_computation.1 | async-start | bytes 4194304
  58.7 2.7 %collective-permute-start.5 = (bf16[256,2048]{1,0:T(8,128)(2,1)S(1)}, bf16[256,2048]{1,0:T(8,128)(2,1)S(1)}, u32[]{:S(2)}, u32[]{:S(2)}) collective-permute-start(bf16[256,2048]{1,0:T(8,128)(2,1)S(1)} %split.119), channel_id=1, source_target_pairs={{0,1},{1,0},{2,3},{3,2},{4,5},{5,4},{6,7},{7,6},{8,9},{9,8},{10,11... | collective-permute-start | bytes 3145736 | tf_op jit(solution)/shard_map/ppermute | solution.py:74
  60.9 2.7 %collective-permute-start.15 = (bf16[256,2048]{1,0:T(8,128)(2,1)S(1)}, bf16[256,2048]{1,0:T(8,128)(2,1)S(1)}, u32[]{:S(2)}, u32[]{:S(2)}) collective-permute-start(bf16[256,2048]{1,0:T(8,128)(2,1)S(1)} %split.118), channel_id=1, source_target_pairs={{0,1},{1,0},{2,3},{3,2},{4,5},{5,4},{6,7},{7,6},{8,9},{9,8},{10,11... | collective-permute-start | bytes 3145736 | tf_op jit(solution)/shard_map/ppermute | solution.py:74
  61.8 14.0 %collective-permute-start.6 = (bf16[128,2048]{1,0:T(8,128)(2,1)S(1)}, bf16[128,2048]{1,0:T(8,128)(2,1)S(1)}, u32[]{:S(2)}, u32[]{:S(2)}) collective-permute-start(bf16[128,2048]{1,0:T(8,128)(2,1)S(1)} %split.120), channel_id=1, source_target_pairs={{0,2},{2,0},{1,3},{3,1},{4,6},{6,4},{5,7},{7,5},{8,10},{10,8},{9,1... | collective-permute-start | bytes 1572872 | tf_op jit(solution)/shard_map/ppermute | solution.py:74
  76.1 13.2 %collective-permute-start.16 = (bf16[4,32,2048]{2,1,0:T(8,128)(2,1)S(1)}, bf16[4,32,2048]{2,1,0:T(8,128)(2,1)S(1)}, u32[]{:S(2)}, u32[]{:S(2)}) collective-permute-start(bf16[4,32,2048]{2,1,0:T(8,128)(2,1)S(1)} %fusion.27), channel_id=1, source_target_pairs={{0,2},{2,0},{1,3},{3,1},{4,6},{6,4},{5,7},{7,5},{8,10},{10,8},{9,1... | collective-permute-start | bytes 1572872 | tf_op jit(solution)/shard_map/ppermute | solution.py:115
  76.7 20.5 %collective-permute-start.7 = (bf16[32,2048]{1,0:T(8,128)(2,1)S(1)}, bf16[32,2048]{1,0:T(8,128)(2,1)S(1)}, u32[]{:S(2)}, u32[]{:S(2)}) collective-permute-start(bf16[32,2048]{1,0:T(8,128)(2,1)S(1)} %get-tuple-element.15), channel_id=1, source_target_pairs={{0,12},{4,0},{8,4},{12,8},{1,13},{5,1},{9,5},{13,9},{2,14},{6,2},{... | collective-permute-start | bytes 393224 | tf_op jit(solution)/shard_map/ppermute | solution.py:74
  84.3 13.4 %collective-permute-start.8 = (bf16[32,2048]{1,0:T(8,128)(2,1)S(1)}, bf16[32,2048]{1,0:T(8,128)(2,1)S(1)}, u32[]{:S(2)}, u32[]{:S(2)}) collective-permute-start(bf16[32,2048]{1,0:T(8,128)(2,1)S(1)} %get-tuple-element.17), channel_id=1, source_target_pairs={{0,8},{4,12},{8,0},{12,4},{1,9},{5,13},{9,1},{13,5},{2,10},{6,14},... | collective-permute-start | bytes 393224 | tf_op jit(solution)/shard_map/ppermute | solution.py:74
  84.3 13.4 %collective-permute-start.9 = (bf16[32,2048]{1,0:T(8,128)(2,1)S(1)}, bf16[32,2048]{1,0:T(8,128)(2,1)S(1)}, u32[]{:S(2)}, u32[]{:S(2)}) collective-permute-start(bf16[32,2048]{1,0:T(8,128)(2,1)S(1)} %get-tuple-element.16), channel_id=1, source_target_pairs={{0,4},{4,8},{8,12},{12,0},{1,5},{5,9},{9,13},{13,1},{2,6},{6,10},{... | collective-permute-start | bytes 393224 | tf_op jit(solution)/shard_map/ppermute | solution.py:74
  89.5 11.4 %collective-permute-start.17 = (bf16[32,2048]{1,0:T(8,128)(2,1)S(1)}, bf16[32,2048]{1,0:T(8,128)(2,1)S(1)}, u32[]{:S(2)}, u32[]{:S(2)}) collective-permute-start(bf16[32,2048]{1,0:T(8,128)(2,1)S(1)} %get-tuple-element.18), channel_id=1, source_target_pairs={{0,12},{4,0},{8,4},{12,8},{1,13},{5,1},{9,5},{13,9},{2,14},{6,2},{... | collective-permute-start | bytes 393224 | tf_op jit(solution)/shard_map/ppermute | solution.py:74
  97.0 10.7 %collective-permute-start.18 = (bf16[32,2048]{1,0:T(8,128)(2,1)S(1)}, bf16[32,2048]{1,0:T(8,128)(2,1)S(1)}, u32[]{:S(2)}, u32[]{:S(2)}) collective-permute-start(bf16[32,2048]{1,0:T(8,128)(2,1)S(1)} %get-tuple-element.20), channel_id=1, source_target_pairs={{0,8},{4,12},{8,0},{12,4},{1,9},{5,13},{9,1},{13,5},{2,10},{6,14},... | collective-permute-start | bytes 393224 | tf_op jit(solution)/shard_map/ppermute | solution.py:74
  97.3 10.5 %collective-permute-start.19 = (bf16[32,2048]{1,0:T(8,128)(2,1)S(1)}, bf16[32,2048]{1,0:T(8,128)(2,1)S(1)}, u32[]{:S(2)}, u32[]{:S(2)}) collective-permute-start(bf16[32,2048]{1,0:T(8,128)(2,1)S(1)} %get-tuple-element.19), channel_id=1, source_target_pairs={{0,4},{4,8},{8,12},{12,0},{1,5},{5,9},{9,13},{13,1},{2,6},{6,10},{... | collective-permute-start | bytes 393224 | tf_op jit(solution)/shard_map/ppermute | solution.py:74

commit v17 on v5

--- a/solution.py
+++ b/solution.py
@@ -94,6 +94,8 @@
     meta = meta.astype(jnp.bfloat16)
     carried = jnp.concatenate([tokens, meta], axis=1)
     pick = (jnp.arange(hosts, dtype=jnp.int32) == me).astype(jnp.float32)
+    partner = me + 1 - 2 * lax.axis_index(AXES[2])
+    pick_other = (jnp.arange(hosts, dtype=jnp.int32) == partner).astype(jnp.float32)
     results = []
     held = None
     for rows in jnp.split(carried, STREAMS, axis=0):
@@ -107,8 +109,13 @@
         gate = tail[:, :hosts] + tail[:, hosts:2 * hosts] + tail[:, 2 * hosts:]
         mine = jnp.sum(gate * pick[None, :], axis=1)
         out = expert_block(rows[:, :width_model], w_in[0], w_down[0], hidden_width)
-        part = out.astype(jnp.float32) * mine[:, None]
-        for axis, size in list(zip(AXES, sizes))[::-1]:
+        theirs = jnp.sum(gate * pick_other[None, :], axis=1)
+        kept, sent = jnp.split(out, 2, axis=0)
+        pairs = [(i, (i + 1) % sizes[2]) for i in range(sizes[2])]
+        back = lax.ppermute(sent, AXES[2], pairs).astype(jnp.float32)
+        half = kept.shape[0]
+        part = kept.astype(jnp.float32) * mine[:half, None] + back * theirs[:half, None]
+        for axis, size in list(zip(AXES[:2], sizes[:2]))[::-1]:
             part = scatter_stage(part, axis, size)
         results.append(part)
     return jnp.concatenate(results, axis=0).astype(jnp.bfloat16)

time: 106 us -> 109 us (1.028)
  waiting for transfers between devices: 48.5 us -> 53.3 us
  starting transfers between devices: 29.1 us -> 27.2 us
    ppermute x10 -> x8, waiting for transfers between devices: 25 us -> 29 us  [scatter_stage(): lax.ppermute(pieces[shift].astype(jnp.bfloat16), axis, pairs)]
    ppermute x10 -> x8, starting transfers between devices: 13.9 us -> 11.5 us  [scatter_stage(): lax.ppermute(pieces[shift].astype(jnp.bfloat16), axis, pairs)]
    unnamed x13 -> x14, local copies, waits for them, and re-layouts: 5 us -> 6.75 us
    split x1 -> x2, local copies, waits for them, and re-layouts: 1.74 us -> 0.17 us  [dense_shards(): kept, sent = jnp.split(out, 2, axis=0)]
  transfers between devices with their start and end apart: 20 -> 20, of which waited for: 10 -> 10; matrix products, arithmetic and copies ran while one was open for 12% -> 18% of each run, Pallas kernels for 0% -> 0%
where the time goes in v17:
time: 109 us; the launch traced here: 108 us
  waiting for transfers between devices  53.3 us (49%)
  starting transfers between devices  27.2 us (25%)
  local copies, waits for them, and re-layouts  10.6 us (10%)
  matrix products  10.5 us (10%)
  other arithmetic  6.44 us (6%)
    ppermute x8, waiting for transfers between devices, scatter_stage(): lax.ppermute(pieces[shift].astype(jnp.bfloat16), axis, pairs)  29 us
    ppermute x10, waiting for transfers between devices, gather_stage(): got.append(lax.ppermute(block, axis, pairs))  23.5 us
    ppermute x10, starting transfers between devices, gather_stage(): got.append(lax.ppermute(block, axis, pairs))  15 us
    ppermute x8, starting transfers between devices, scatter_stage(): lax.ppermute(pieces[shift].astype(jnp.bfloat16), axis, pairs)  11.5 us
    dot_general x2, matrix products, expert_block(): pair = jnp.dot(rows_in, gate_up, preferred_element_type=jnp.float32)  6.81 us
    unnamed x14, local copies, waits for them, and re-layouts  6.75 us
    dot_general x2, matrix products, expert_block(): jnp.dot(active, down_proj, preferred_element_type=jnp.float32)  3.69 us
  transfers between devices with their start and end apart: 20, of which 10 were waited for; matrix products, arithmetic and copies ran while one was open for 18% of the time, Pallas kernels for 0%

profile of v17, /device:TPU:0, one launch (start us, length us, event | category | flops | bytes accessed | tf_op | source)
XLA Modules:
  0.0 108.4 jit_solution(6272123700794081209)
XLA Ops:
  0.0 0.9 reduce_sum.54
  0.9 0.8 broadcast_divide_fusion
  1.7 0.8 select_reduce_fusion
  2.8 1.7 %concatenate.32 = bf16[64,2176]{1,0:T(8,128)(2,1)} concatenate(bf16[64,2048]{1,0:T(8,128)(2,1)} %param.6, bf16[64,16]{1,0:T(8,128)(2,1)S(1)} %copy.9, bf16[64,16]{1,0:T(8,128)(2,1)S(1)} %copy.10, bf16[64,16]{1,0:T(8,128)(2,1)S(1)} %copy.11, bf16[64,80]{1,0:T(8,128)(2,1)S(1)} %broadcast_in_dim.16), dimensions={1} | concatenate | bytes 557056 | tf_op jit(solution)/shard_map/concatenate | solution.py:95
  4.5 1.7 %constant_dynamic-update-slice_fusion.4 = (bf16[256,2176]{1,0:T(8,128)(2,1)}, bf16[512,2176]{1,0:T(8,128)(2,1)}, bf16[32,2176]{1,0:T(8,128)(2,1)S(1)}, bf16[32,2176]{1,0:T(8,128)(2,1)S(1)}) fusion(bf16[64,2176]{1,0:T(8,128)(2,1)} %concatenate.32), kind=kLoop, calls=%fused_computation.50 | loop fusion | bytes 835584
  6.2 3.1 %collective-permute-start = (bf16[32,2176]{1,0:T(8,128)(2,1)S(1)}, bf16[32,2176]{1,0:T(8,128)(2,1)}, u32[]{:S(2)}, u32[]{:S(2)}) collective-permute-start(bf16[32,2176]{1,0:T(8,128)(2,1)S(1)} %get-tuple-element.30), channel_id=1, source_target_pairs={{0,4},{4,8},{8,12},{12,0},{1,5},{5,9},{9,13},{13,1},{2,6},{6,10},{... | collective-permute-start | bytes 417800 | tf_op jit(solution)/shard_map/ppermute | solution.py:65
  9.3 2.6 %collective-permute-start.1 = (bf16[32,2176]{1,0:T(8,128)(2,1)S(1)}, bf16[32,2176]{1,0:T(8,128)(2,1)}, u32[]{:S(2)}, u32[]{:S(2)}) collective-permute-start(bf16[32,2176]{1,0:T(8,128)(2,1)S(1)} %get-tuple-element.30), channel_id=1, source_target_pairs={{0,8},{4,12},{8,0},{12,4},{1,9},{5,13},{9,1},{13,5},{2,10},{6,14},... | collective-permute-start | bytes 417800 | tf_op jit(solution)/shard_map/ppermute | solution.py:65
  11.9 1.3 %collective-permute-start.2 = (bf16[32,2176]{1,0:T(8,128)(2,1)S(1)}, bf16[32,2176]{1,0:T(8,128)(2,1)}, u32[]{:S(2)}, u32[]{:S(2)}) collective-permute-start(bf16[32,2176]{1,0:T(8,128)(2,1)S(1)} %get-tuple-element.30), channel_id=1, source_target_pairs={{0,12},{4,0},{8,4},{12,8},{1,13},{5,1},{9,5},{13,9},{2,14},{6,2},{... | collective-permute-start | bytes 417800 | tf_op jit(solution)/shard_map/ppermute | solution.py:65
  13.2 2.8 %collective-permute-done = bf16[32,2176]{1,0:T(8,128)(2,1)} collective-permute-done((bf16[32,2176]{1,0:T(8,128)(2,1)S(1)}, bf16[32,2176]{1,0:T(8,128)(2,1)}, u32[]{:S(2)}, u32[]{:S(2)}) %collective-permute-start) | collective-permute-done | bytes 139296 | tf_op jit(solution)/shard_map/ppermute | solution.py:65
  16.0 5.1 %collective-permute-done.1 = bf16[32,2176]{1,0:T(8,128)(2,1)} collective-permute-done((bf16[32,2176]{1,0:T(8,128)(2,1)S(1)}, bf16[32,2176]{1,0:T(8,128)(2,1)}, u32[]{:S(2)}, u32[]{:S(2)}) %collective-permute-start.1) | collective-permute-done | bytes 139296 | tf_op jit(solution)/shard_map/ppermute | solution.py:65
  21.1 1.2 %pad_maximum_fusion = bf16[128,2176]{1,0:T(8,128)(2,1)S(1)} fusion(bf16[32,2176]{1,0:T(8,128)(2,1)} %collective-permute-done.2, bf16[32,2176]{1,0:T(8,128)(2,1)} %collective-permute-done.1, bf16[32,2176]{1,0:T(8,128)(2,1)} %collective-permute-done, bf16[32,2176]{1,0:T(8,128)(2,1)S(1)} %get-tuple-element.30), kind=kLoop, calls=%fused_computation.24 | loop fusion | flops 2228224 | bytes 1114112 | tf_op jit(solution)/shard_map/concatenate | solution.py:66
  22.4 1.6 %collective-permute-start.3 = (bf16[128,2176]{1,0:T(8,128)(2,1)S(1)}, bf16[128,2176]{1,0:T(8,128)(2,1)S(1)}, u32[]{:S(2)}, u32[]{:S(2)}) collective-permute-start(bf16[128,2176]{1,0:T(8,128)(2,1)S(1)} %pad_maximum_fusion), channel_id=1, source_target_pairs={{0,2},{2,0},{1,3},{3,1},{4,6},{6,4},{5,7},{7,5},{8,10},{10,8},{9,1... | collective-permute-start | bytes 1671176 | tf_op jit(solution)/shard_map/ppermute | solution.py:65
  23.9 3.5 %collective-permute-start.10 = (bf16[32,2176]{1,0:T(8,128)(2,1)S(1)}, bf16[32,2176]{1,0:T(8,128)(2,1)S(1)}, u32[]{:S(2)}, u32[]{:S(2)}) collective-permute-start(bf16[32,2176]{1,0:T(8,128)(2,1)S(1)} %get-tuple-element.6), channel_id=1, source_target_pairs={{0,4},{4,8},{8,12},{12,0},{1,5},{5,9},{9,13},{13,1},{2,6},{6,10},{... | collective-permute-start | bytes 417800 | tf_op jit(solution)/shard_map/ppermute | solution.py:65
  27.4 1.6 %collective-permute-start.11 = (bf16[32,2176]{1,0:T(8,128)(2,1)S(1)}, bf16[32,2176]{1,0:T(8,128)(2,1)S(1)}, u32[]{:S(2)}, u32[]{:S(2)}) collective-permute-start(bf16[32,2176]{1,0:T(8,128)(2,1)S(1)} %get-tuple-element.6), channel_id=1, source_target_pairs={{0,8},{4,12},{8,0},{12,4},{1,9},{5,13},{9,1},{13,5},{2,10},{6,14},... | collective-permute-start | bytes 417800 | tf_op jit(solution)/shard_map/ppermute | solution.py:65
  29.0 0.7 collective-permute-start.12
  29.8 1.6 %constant_dynamic-update-slice_fusion.3 = (bf16[256,2176]{1,0:T(8,128)(2,1)}, bf16[512,2176]{1,0:T(8,128)(2,1)}) fusion(bf16[256,2176]{1,0:T(8,128)(2,1)} %get-tuple-element.27, bf16[32,2176]{1,0:T(8,128)(2,1)} %collective-permute-done, bf16[512,2176]{1,0:T(8,128)(2,1)} %get-tuple-element.28), kind=kLoop, calls=%fused_computation.49 | loop fusion | bytes 417792
  31.4 1.6 %constant_dynamic-update-slice_fusion.2 = (bf16[256,2176]{1,0:T(8,128)(2,1)}, bf16[512,2176]{1,0:T(8,128)(2,1)}) fusion(bf16[256,2176]{1,0:T(8,128)(2,1)} %get-tuple-element.35, bf16[32,2176]{1,0:T(8,128)(2,1)} %collective-permute-done.1, bf16[512,2176]{1,0:T(8,128)(2,1)} %get-tuple-element.36), kind=kLoop, calls=%fused_computation.48 | loop fusion | bytes 417792
  33.0 1.6 %constant_dynamic-update-slice_fusion.1 = (bf16[256,2176]{1,0:T(8,128)(2,1)}, bf16[512,2176]{1,0:T(8,128)(2,1)}) fusion(bf16[256,2176]{1,0:T(8,128)(2,1)} %get-tuple-element.33, bf16[32,2176]{1,0:T(8,128)(2,1)} %collective-permute-done.2, bf16[512,2176]{1,0:T(8,128)(2,1)} %get-tuple-element.34), kind=kLoop, calls=%fused_computation.47 | loop fusion | bytes 417792
  34.7 2.8 %collective-permute-done.11 = bf16[32,2176]{1,0:T(8,128)(2,1)S(1)} collective-permute-done((bf16[32,2176]{1,0:T(8,128)(2,1)S(1)}, bf16[32,2176]{1,0:T(8,128)(2,1)S(1)}, u32[]{:S(2)}, u32[]{:S(2)}) %collective-permute-start.11) | collective-permute-done | bytes 139296 | tf_op jit(solution)/shard_map/ppermute | solution.py:65
  37.6 0.6 collective-permute-start.13
  38.2 1.1 constant_dynamic-update-slice_fusion
  39.4 12.8 %collective-permute-done.13 = bf16[128,2176]{1,0:T(8,128)(2,1)S(1)} collective-permute-done((bf16[128,2176]{1,0:T(8,128)(2,1)S(1)}, bf16[128,2176]{1,0:T(8,128)(2,1)S(1)}, u32[]{:S(2)}, u32[]{:S(2)}) %collective-permute-start.13) | collective-permute-done | bytes 557088 | tf_op jit(solution)/shard_map/ppermute | solution.py:65
  52.1 0.1 constant_dynamic-update-slice_fusion.11
  52.3 0.1 constant_dynamic-update-slice_fusion.5
  52.5 3.4 %fusion.2 = f32[512,1536]{1,0:T(8,128)S(1)} fusion(bf16[1,2048,1536]{2,1,0:T(8,128)(2,1)S(1)} %copy-done.2, bf16[512,2176]{1,0:T(8,128)(2,1)S(1)} %constant_dynamic-update-slice_fusion.5), kind=kOutput, calls=%fused_computation.2 | convolution fusion | flops 3221225472 | bytes 11534336 | tf_op jit(solution)/shard_map/dot_general | solution.py:9
  55.9 1.8 %fusion.8 = bf16[512,2048]{1,0:T(8,128)(2,1)S(1)} fusion(bf16[1,768,2048]{2,1,0:T(8,128)(2,1)S(1)} %copy-done, f32[512,1536]{1,0:T(8,128)S(1)} %fusion.2), kind=kOutput, calls=%fused_computation.8 | convolution fusion | flops 1614020608 | bytes 8388608 | tf_op jit(solution)/shard_map/dot_general | solution.py:11
  57.9 0.5 collective-permute-start.5
  58.4 0.1 constant_dynamic-update-slice_fusion.16
  58.6 3.4 %fusion = f32[512,1536]{1,0:T(8,128)S(1)} fusion(bf16[1,2048,1536]{2,1,0:T(8,128)(2,1)S(1)} %copy-done.2, bf16[512,2176]{1,0:T(8,128)(2,1)S(1)} %constant_dynamic-update-slice_fusion.16), kind=kOutput, calls=%fused_computation | convolution fusion | flops 3221225472 | bytes 11534336 | tf_op jit(solution)/shard_map/dot_general | solution.py:9
  62.0 1.8 %fusion.11 = bf16[512,2048]{1,0:T(8,128)(2,1)S(1)} fusion(bf16[1,768,2048]{2,1,0:T(8,128)(2,1)S(1)} %copy-done, f32[512,1536]{1,0:T(8,128)S(1)} %fusion), kind=kOutput, calls=%fused_computation.9 | convolution fusion | flops 1614020608 | bytes 8388608 | tf_op jit(solution)/shard_map/dot_general | solution.py:11
  64.1 0.7 multiply_reduce_fusion.1
  64.8 0.4 multiply_add_fusion.1
  65.3 0.6 collective-permute-start.6
  65.9 0.8 collective-permute-done.15
  66.6 0.4 multiply_add_fusion
  67.1 0.8 collective-permute-start.16
  67.9 12.2 %collective-permute-done.6 = bf16[128,2048]{1,0:T(8,128)(2,1)S(1)} collective-permute-done((bf16[128,2048]{1,0:T(8,128)(2,1)S(1)}, bf16[128,2048]{1,0:T(8,128)(2,1)S(1)}, u32[]{:S(2)}, u32[]{:S(2)}) %collective-permute-start.6) | collective-permute-done | bytes 524320 | tf_op jit(solution)/shard_map/ppermute | solution.py:74
  80.1 0.2 fusion.31
  80.4 4.0 %collective-permute-start.7 = (bf16[32,2048]{1,0:T(8,128)(2,1)S(1)}, bf16[32,2048]{1,0:T(8,128)(2,1)S(1)}, u32[]{:S(2)}, u32[]{:S(2)}) collective-permute-start(bf16[32,2048]{1,0:T(8,128)(2,1)S(1)} %get-tuple-element.21), channel_id=1, source_target_pairs={{0,12},{4,0},{8,4},{12,8},{1,13},{5,1},{9,5},{13,9},{2,14},{6,2},{... | collective-permute-start | bytes 393224 | tf_op jit(solution)/shard_map/ppermute | solution.py:74
  84.4 1.0 collective-permute-start.8
  85.4 5.4 %collective-permute-done.16 = bf16[128,2048]{1,0:T(8,128)(2,1)S(1)} collective-permute-done((bf16[128,2048]{1,0:T(8,128)(2,1)S(1)}, bf16[128,2048]{1,0:T(8,128)(2,1)S(1)}, u32[]{:S(2)}, u32[]{:S(2)}) %collective-permute-start.16) | collective-permute-done | bytes 524320 | tf_op jit(solution)/shard_map/ppermute | solution.py:74
  90.9 0.2 fusion.32
  91.1 4.0 %collective-permute-start.17 = (bf16[32,2048]{1,0:T(8,128)(2,1)S(1)}, bf16[32,2048]{1,0:T(8,128)(2,1)S(1)}, u32[]{:S(2)}, u32[]{:S(2)}) collective-permute-start(bf16[32,2048]{1,0:T(8,128)(2,1)S(1)} %get-tuple-element.24), channel_id=1, source_target_pairs={{0,12},{4,0},{8,4},{12,8},{1,13},{5,1},{9,5},{13,9},{2,14},{6,2},{... | collective-permute-start | bytes 393224 | tf_op jit(solution)/shard_map/ppermute | solution.py:74
  95.1 1.0 collective-permute-start.18
  96.2 0.3 collective-permute-done.8
  96.5 2.8 %collective-permute-done.17 = bf16[32,2048]{1,0:T(8,128)(2,1)S(1)} collective-permute-done((bf16[32,2048]{1,0:T(8,128)(2,1)S(1)}, bf16[32,2048]{1,0:T(8,128)(2,1)S(1)}, u32[]{:S(2)}, u32[]{:S(2)}) %collective-permute-start.17) | collective-permute-done | bytes 131104 | tf_op jit(solution)/shard_map/ppermute | solution.py:74
  99.3 8.3 %collective-permute-done.18 = bf16[32,2048]{1,0:T(8,128)(2,1)S(1)} collective-permute-done((bf16[32,2048]{1,0:T(8,128)(2,1)S(1)}, bf16[32,2048]{1,0:T(8,128)(2,1)S(1)}, u32[]{:S(2)}, u32[]{:S(2)}) %collective-permute-start.18) | collective-permute-done | bytes 131104 | tf_op jit(solution)/shard_map/ppermute | solution.py:74
  107.7 0.7 pad_maximum_fusion.2
  (46 shorter events, 1.2 us)
Async XLA Ops:
  0.0 55.9 %copy-start = (bf16[1,768,2048]{2,1,0:T(8,128)(2,1)S(1)}, bf16[1,768,2048]{2,1,0:T(8,128)(2,1)}, u32[]{:S(2)}) copy-start(bf16[1,768,2048]{2,1,0:T(8,128)(2,1)} %param.11) | copy-start | bytes 9437188
  6.2 9.8 %collective-permute-start = (bf16[32,2176]{1,0:T(8,128)(2,1)S(1)}, bf16[32,2176]{1,0:T(8,128)(2,1)}, u32[]{:S(2)}, u32[]{:S(2)}) collective-permute-start(bf16[32,2176]{1,0:T(8,128)(2,1)S(1)} %get-tuple-element.30), channel_id=1, source_target_pairs={{0,4},{4,8},{8,12},{12,0},{1,5},{5,9},{9,13},{13,1},{2,6},{6,10},{... | collective-permute-start | bytes 417800 | tf_op jit(solution)/shard_map/ppermute | solution.py:65
  9.3 11.9 %collective-permute-start.1 = (bf16[32,2176]{1,0:T(8,128)(2,1)S(1)}, bf16[32,2176]{1,0:T(8,128)(2,1)}, u32[]{:S(2)}, u32[]{:S(2)}) collective-permute-start(bf16[32,2176]{1,0:T(8,128)(2,1)S(1)} %get-tuple-element.30), channel_id=1, source_target_pairs={{0,8},{4,12},{8,0},{12,4},{1,9},{5,13},{9,1},{13,5},{2,10},{6,14},... | collective-permute-start | bytes 417800 | tf_op jit(solution)/shard_map/ppermute | solution.py:65
  11.9 9.3 %collective-permute-start.2 = (bf16[32,2176]{1,0:T(8,128)(2,1)S(1)}, bf16[32,2176]{1,0:T(8,128)(2,1)}, u32[]{:S(2)}, u32[]{:S(2)}) collective-permute-start(bf16[32,2176]{1,0:T(8,128)(2,1)S(1)} %get-tuple-element.30), channel_id=1, source_target_pairs={{0,12},{4,0},{8,4},{12,8},{1,13},{5,1},{9,5},{13,9},{2,14},{6,2},{... | collective-permute-start | bytes 417800 | tf_op jit(solution)/shard_map/ppermute | solution.py:65
  21.1 31.4 %copy-start.2 = (bf16[1,2048,1536]{2,1,0:T(8,128)(2,1)S(1)}, bf16[1,2048,1536]{2,1,0:T(8,128)(2,1)}, u32[]{:S(2)}) copy-start(bf16[1,2048,1536]{2,1,0:T(8,128)(2,1)} %param.10) | copy-start | bytes 18874372
  22.4 15.8 %collective-permute-start.3 = (bf16[128,2176]{1,0:T(8,128)(2,1)S(1)}, bf16[128,2176]{1,0:T(8,128)(2,1)S(1)}, u32[]{:S(2)}, u32[]{:S(2)}) collective-permute-start(bf16[128,2176]{1,0:T(8,128)(2,1)S(1)} %pad_maximum_fusion), channel_id=1, source_target_pairs={{0,2},{2,0},{1,3},{3,1},{4,6},{6,4},{5,7},{7,5},{8,10},{10,8},{9,1... | collective-permute-start | bytes 1671176 | tf_op jit(solution)/shard_map/ppermute | solution.py:65
  23.9 10.8 %collective-permute-start.10 = (bf16[32,2176]{1,0:T(8,128)(2,1)S(1)}, bf16[32,2176]{1,0:T(8,128)(2,1)S(1)}, u32[]{:S(2)}, u32[]{:S(2)}) collective-permute-start(bf16[32,2176]{1,0:T(8,128)(2,1)S(1)} %get-tuple-element.6), channel_id=1, source_target_pairs={{0,4},{4,8},{8,12},{12,0},{1,5},{5,9},{9,13},{13,1},{2,6},{6,10},{... | collective-permute-start | bytes 417800 | tf_op jit(solution)/shard_map/ppermute | solution.py:65
  27.4 10.2 %collective-permute-start.11 = (bf16[32,2176]{1,0:T(8,128)(2,1)S(1)}, bf16[32,2176]{1,0:T(8,128)(2,1)S(1)}, u32[]{:S(2)}, u32[]{:S(2)}) collective-permute-start(bf16[32,2176]{1,0:T(8,128)(2,1)S(1)} %get-tuple-element.6), channel_id=1, source_target_pairs={{0,8},{4,12},{8,0},{12,4},{1,9},{5,13},{9,1},{13,5},{2,10},{6,14},... | collective-permute-start | bytes 417800 | tf_op jit(solution)/shard_map/ppermute | solution.py:65
  29.0 8.5 %collective-permute-start.12 = (bf16[32,2176]{1,0:T(8,128)(2,1)S(1)}, bf16[32,2176]{1,0:T(8,128)(2,1)S(1)}, u32[]{:S(2)}, u32[]{:S(2)}) collective-permute-start(bf16[32,2176]{1,0:T(8,128)(2,1)S(1)} %get-tuple-element.6), channel_id=1, source_target_pairs={{0,12},{4,0},{8,4},{12,8},{1,13},{5,1},{9,5},{13,9},{2,14},{6,2},{... | collective-permute-start | bytes 417800 | tf_op jit(solution)/shard_map/ppermute | solution.py:65
  37.6 14.5 %collective-permute-start.13 = (bf16[128,2176]{1,0:T(8,128)(2,1)S(1)}, bf16[128,2176]{1,0:T(8,128)(2,1)S(1)}, u32[]{:S(2)}, u32[]{:S(2)}) collective-permute-start(bf16[128,2176]{1,0:T(8,128)(2,1)S(1)} %pad_maximum_fusion.1), channel_id=1, source_target_pairs={{0,2},{2,0},{1,3},{3,1},{4,6},{6,4},{5,7},{7,5},{8,10},{10,8},{9,1... | collective-permute-start | bytes 1671176 | tf_op jit(solution)/shard_map/ppermute | solution.py:65
  39.3 13.1 %copy-start.1 = (bf16[512,2176]{1,0:T(8,128)(2,1)S(1)}, bf16[512,2176]{1,0:T(8,128)(2,1)}, u32[]{:S(2)}) copy-start(bf16[512,2176]{1,0:T(8,128)(2,1)} %get-tuple-element.18) | copy-start | bytes 6684676
  39.3 13.1 %collective-permute-start.4 = (bf16[256,2176]{1,0:T(8,128)(2,1)}, bf16[256,2176]{1,0:T(8,128)(2,1)S(1)}, u32[]{:S(2)}, u32[]{:S(2)}) collective-permute-start(bf16[256,2176]{1,0:T(8,128)(2,1)} %get-tuple-element.17), channel_id=1, source_target_pairs={{0,1},{1,0},{2,3},{3,2},{4,5},{5,4},{6,7},{7,6},{8,9},{9,8},{10,11... | collective-permute-start | bytes 3342344 | tf_op jit(solution)/shard_map/ppermute | solution.py:65
  52.2 6.2 %collective-permute-start.14 = (bf16[256,2176]{1,0:T(8,128)(2,1)S(1)}, bf16[256,2176]{1,0:T(8,128)(2,1)S(1)}, u32[]{:S(2)}, u32[]{:S(2)}) collective-permute-start(bf16[256,2176]{1,0:T(8,128)(2,1)S(1)} %get-tuple-element.19), channel_id=1, source_target_pairs={{0,1},{1,0},{2,3},{3,2},{4,5},{5,4},{6,7},{7,6},{8,9},{9,8},{10,11... | collective-permute-start | bytes 3342344 | tf_op jit(solution)/shard_map/ppermute | solution.py:65
  57.9 6.9 %collective-permute-start.5 = (bf16[256,2048]{1,0:T(8,128)(2,1)S(1)}, bf16[256,2048]{1,0:T(8,128)(2,1)S(1)}, u32[]{:S(2)}, u32[]{:S(2)}) collective-permute-start(bf16[256,2048]{1,0:T(8,128)(2,1)S(1)} %split.82), channel_id=1, source_target_pairs={{0,1},{1,0},{2,3},{3,2},{4,5},{5,4},{6,7},{7,6},{8,9},{9,8},{10,11... | collective-permute-start | bytes 3145736 | tf_op jit(solution)/shard_map/ppermute | solution.py:115
  63.9 2.7 %collective-permute-start.15 = (bf16[256,2048]{1,0:T(8,128)(2,1)S(1)}, bf16[256,2048]{1,0:T(8,128)(2,1)S(1)}, u32[]{:S(2)}, u32[]{:S(2)}) collective-permute-start(bf16[256,2048]{1,0:T(8,128)(2,1)S(1)} %split.91), channel_id=1, source_target_pairs={{0,1},{1,0},{2,3},{3,2},{4,5},{5,4},{6,7},{7,6},{8,9},{9,8},{10,11... | collective-permute-start | bytes 3145736 | tf_op jit(solution)/shard_map/ppermute | solution.py:115
  65.3 14.9 %collective-permute-start.6 = (bf16[128,2048]{1,0:T(8,128)(2,1)S(1)}, bf16[128,2048]{1,0:T(8,128)(2,1)S(1)}, u32[]{:S(2)}, u32[]{:S(2)}) collective-permute-start(bf16[128,2048]{1,0:T(8,128)(2,1)S(1)} %split.121), channel_id=1, source_target_pairs={{0,2},{2,0},{1,3},{3,1},{4,6},{6,4},{5,7},{7,5},{8,10},{10,8},{9,1... | collective-permute-start | bytes 1572872 | tf_op jit(solution)/shard_map/ppermute | solution.py:74
  67.1 23.8 %collective-permute-start.16 = (bf16[128,2048]{1,0:T(8,128)(2,1)S(1)}, bf16[128,2048]{1,0:T(8,128)(2,1)S(1)}, u32[]{:S(2)}, u32[]{:S(2)}) collective-permute-start(bf16[128,2048]{1,0:T(8,128)(2,1)S(1)} %split.120), channel_id=1, source_target_pairs={{0,2},{2,0},{1,3},{3,1},{4,6},{6,4},{5,7},{7,5},{8,10},{10,8},{9,1... | collective-permute-start | bytes 1572872 | tf_op jit(solution)/shard_map/ppermute | solution.py:74
  80.4 15.8 %collective-permute-start.7 = (bf16[32,2048]{1,0:T(8,128)(2,1)S(1)}, bf16[32,2048]{1,0:T(8,128)(2,1)S(1)}, u32[]{:S(2)}, u32[]{:S(2)}) collective-permute-start(bf16[32,2048]{1,0:T(8,128)(2,1)S(1)} %get-tuple-element.21), channel_id=1, source_target_pairs={{0,12},{4,0},{8,4},{12,8},{1,13},{5,1},{9,5},{13,9},{2,14},{6,2},{... | collective-permute-start | bytes 393224 | tf_op jit(solution)/shard_map/ppermute | solution.py:74
  84.4 12.1 %collective-permute-start.8 = (bf16[32,2048]{1,0:T(8,128)(2,1)S(1)}, bf16[32,2048]{1,0:T(8,128)(2,1)S(1)}, u32[]{:S(2)}, u32[]{:S(2)}) collective-permute-start(bf16[32,2048]{1,0:T(8,128)(2,1)S(1)} %get-tuple-element.23), channel_id=1, source_target_pairs={{0,8},{4,12},{8,0},{12,4},{1,9},{5,13},{9,1},{13,5},{2,10},{6,14},... | collective-permute-start | bytes 393224 | tf_op jit(solution)/shard_map/ppermute | solution.py:74
  85.4 11.0 %collective-permute-start.9 = (bf16[32,2048]{1,0:T(8,128)(2,1)S(1)}, bf16[32,2048]{1,0:T(8,128)(2,1)S(1)}, u32[]{:S(2)}, u32[]{:S(2)}) collective-permute-start(bf16[32,2048]{1,0:T(8,128)(2,1)S(1)} %get-tuple-element.22), channel_id=1, source_target_pairs={{0,4},{4,8},{8,12},{12,0},{1,5},{5,9},{9,13},{13,1},{2,6},{6,10},{... | collective-permute-start | bytes 393224 | tf_op jit(solution)/shard_map/ppermute | solution.py:74
  91.1 8.2 %collective-permute-start.17 = (bf16[32,2048]{1,0:T(8,128)(2,1)S(1)}, bf16[32,2048]{1,0:T(8,128)(2,1)S(1)}, u32[]{:S(2)}, u32[]{:S(2)}) collective-permute-start(bf16[32,2048]{1,0:T(8,128)(2,1)S(1)} %get-tuple-element.24), channel_id=1, source_target_pairs={{0,12},{4,0},{8,4},{12,8},{1,13},{5,1},{9,5},{13,9},{2,14},{6,2},{... | collective-permute-start | bytes 393224 | tf_op jit(solution)/shard_map/ppermute | solution.py:74
  95.1 12.5 %collective-permute-start.18 = (bf16[32,2048]{1,0:T(8,128)(2,1)S(1)}, bf16[32,2048]{1,0:T(8,128)(2,1)S(1)}, u32[]{:S(2)}, u32[]{:S(2)}) collective-permute-start(bf16[32,2048]{1,0:T(8,128)(2,1)S(1)} %get-tuple-element.26), channel_id=1, source_target_pairs={{0,8},{4,12},{8,0},{12,4},{1,9},{5,13},{9,1},{13,5},{2,10},{6,14},... | collective-permute-start | bytes 393224 | tf_op jit(solution)/shard_map/ppermute | solution.py:74
  96.2 11.4 %collective-permute-start.19 = (bf16[32,2048]{1,0:T(8,128)(2,1)S(1)}, bf16[32,2048]{1,0:T(8,128)(2,1)S(1)}, u32[]{:S(2)}, u32[]{:S(2)}) collective-permute-start(bf16[32,2048]{1,0:T(8,128)(2,1)S(1)} %get-tuple-element.25), channel_id=1, source_target_pairs={{0,4},{4,8},{8,12},{12,0},{1,5},{5,9},{9,13},{13,1},{2,6},{6,10},{... | collective-permute-start | bytes 393224 | tf_op jit(solution)/shard_map/ppermute | solution.py:74

commit v18 on v6

--- a/solution.py
+++ b/solution.py
@@ -96,7 +96,8 @@
     pick = (jnp.arange(hosts, dtype=jnp.int32) == me).astype(jnp.float32)
     results = []
     held = None
-    for rows in jnp.split(carried, STREAMS, axis=0):
+    first = tok_rows * 5 // 8 // 8 * 8
+    for rows in (carried[:first], carried[first:]):
         if held is not None:
             held, rows = lax.optimization_barrier((held, rows))
         rows = gather_stage(rows, AXES[0], sizes[0])
@@ -112,9 +113,6 @@
             part = scatter_stage(part, axis, size)
         results.append(part)
     return jnp.concatenate(results, axis=0).astype(jnp.bfloat16)
-
-
-STREAMS = 4
 
 
 def factor_expert(mesh):

time: 117 us -> 118 us (level)
  starting transfers between devices: 46.8 us -> 24 us
  waiting for transfers between devices: 43.2 us -> 65.4 us
  local copies, waits for them, and re-layouts: 6.1 us -> 8.93 us
  matrix products: 14.4 us -> 12.9 us
    ppermute x20 -> x10, starting transfers between devices: 23.6 us -> 9.43 us  [scatter_stage(): lax.ppermute(pieces[shift].astype(jnp.bfloat16), axis, pairs)]
    ppermute x20 -> x10, waiting for transfers between devices: 20.1 us -> 31.3 us  [scatter_stage(): lax.ppermute(pieces[shift].astype(jnp.bfloat16), axis, pairs)]
    ppermute x20 -> x10, waiting for transfers between devices: 23.1 us -> 34.1 us  [gather_stage(): got.append(lax.ppermute(block, axis, pairs))]
    ppermute x20 -> x10, starting transfers between devices: 23.2 us -> 14.6 us  [gather_stage(): got.append(lax.ppermute(block, axis, pairs))]
    unnamed x27 -> x16, local copies, waits for them, and re-layouts: 3.16 us -> 5.8 us
    dot_general x4 -> x2, matrix products: 10.2 us -> 9.12 us  [expert_block(): pair = jnp.dot(rows_in, gate_up, preferred_element_type=jnp.float32)]
    dot_general x4 -> x2, matrix products: 4.23 us -> 3.75 us  [expert_block(): jnp.dot(active, down_proj, preferred_element_type=jnp.float32)]
  transfers between devices with their start and end apart: 40 -> 20, of which waited for: 16 -> 10; matrix products, arithmetic and copies ran while one was open for 14% -> 18% of each run, Pallas kernels for 0% -> 0%
where the time goes in v18:
time: 118 us
  waiting for transfers between devices  65.4 us (55%)
  starting transfers between devices  24 us (20%)
  matrix products  12.9 us (11%)
  local copies, waits for them, and re-layouts  8.93 us (8%)
  other arithmetic  6.14 us (5%)
    ppermute x10, waiting for transfers between devices, gather_stage(): got.append(lax.ppermute(block, axis, pairs))  34.1 us
    ppermute x10, waiting for transfers between devices, scatter_stage(): lax.ppermute(pieces[shift].astype(jnp.bfloat16), axis, pairs)  31.3 us
    ppermute x10, starting transfers between devices, gather_stage(): got.append(lax.ppermute(block, axis, pairs))  14.6 us
    ppermute x10, starting transfers between devices, scatter_stage(): lax.ppermute(pieces[shift].astype(jnp.bfloat16), axis, pairs)  9.43 us
    dot_general x2, matrix products, expert_block(): pair = jnp.dot(rows_in, gate_up, preferred_element_type=jnp.float32)  9.12 us
    unnamed x16, local copies, waits for them, and re-layouts  5.8 us
    dot_general x2, matrix products, expert_block(): jnp.dot(active, down_proj, preferred_element_type=jnp.float32)  3.75 us
  transfers between devices with their start and end apart: 20, of which 10 were waited for; matrix products, arithmetic and copies ran while one was open for 18% of the time, Pallas kernels for 0%

profile of v18, /device:TPU:0, one launch (start us, length us, event | category | flops | bytes accessed | tf_op | source)
XLA Modules:
  0.0 117.6 jit_solution(18351812800133182603)
XLA Ops:
  0.0 0.9 reduce_sum.36
  0.9 0.8 broadcast_divide_fusion
  1.7 0.8 select_reduce_fusion
  2.8 1.1 concatenate.32
  3.8 0.8 constant_dynamic-update-slice_fusion.4
  4.6 5.1 %collective-permute-start.2 = (bf16[40,2176]{1,0:T(8,128)(2,1)}, bf16[40,2176]{1,0:T(8,128)(2,1)}, u32[]{:S(2)}, u32[]{:S(2)}) collective-permute-start(bf16[40,2176]{1,0:T(8,128)(2,1)} %get-tuple-element.23), channel_id=1, source_target_pairs={{0,12},{4,0},{8,4},{12,8},{1,13},{5,1},{9,5},{13,9},{2,14},{6,2},{... | collective-permute-start | bytes 522248 | tf_op jit(solution)/shard_map/ppermute | solution.py:65
  9.7 1.0 collective-permute-start
  10.7 4.1 %collective-permute-done.2 = bf16[40,2176]{1,0:T(8,128)(2,1)} collective-permute-done((bf16[40,2176]{1,0:T(8,128)(2,1)}, bf16[40,2176]{1,0:T(8,128)(2,1)}, u32[]{:S(2)}, u32[]{:S(2)}) %collective-permute-start.2) | collective-permute-done | bytes 174112 | tf_op jit(solution)/shard_map/ppermute | solution.py:65
  14.9 9.9 %collective-permute-done.1 = bf16[40,2176]{1,0:T(8,128)(2,1)} collective-permute-done((bf16[40,2176]{1,0:T(8,128)(2,1)}, bf16[40,2176]{1,0:T(8,128)(2,1)}, u32[]{:S(2)}, u32[]{:S(2)}) %collective-permute-start.1) | collective-permute-done | bytes 174112 | tf_op jit(solution)/shard_map/ppermute | solution.py:65
  24.8 1.2 %pad_maximum_fusion = bf16[160,2176]{1,0:T(8,128)(2,1)S(1)} fusion(bf16[40,2176]{1,0:T(8,128)(2,1)} %collective-permute-done.2, bf16[40,2176]{1,0:T(8,128)(2,1)} %collective-permute-done.1, bf16[40,2176]{1,0:T(8,128)(2,1)} %collective-permute-done, bf16[40,2176]{1,0:T(8,128)(2,1)} %get-tuple-element.23), kind=kLoop, calls=%fused_computation.26 | loop fusion | flops 2785280 | bytes 1392640 | tf_op jit(solution)/shard_map/concatenate | solution.py:66
  26.0 0.8 collective-permute-start.12
  26.9 2.1 %collective-permute-start.11 = (bf16[24,2176]{1,0:T(8,128)(2,1)S(1)}, bf16[24,2176]{1,0:T(8,128)(2,1)S(1)}, u32[]{:S(2)}, u32[]{:S(2)}) collective-permute-start(bf16[24,2176]{1,0:T(8,128)(2,1)S(1)} %slice.72), channel_id=1, source_target_pairs={{0,8},{4,12},{8,0},{12,4},{1,9},{5,13},{9,1},{13,5},{2,10},{6,14},... | collective-permute-start | bytes 313352 | tf_op jit(solution)/shard_map/ppermute | solution.py:65
  28.9 1.9 %collective-permute-start.10 = (bf16[24,2176]{1,0:T(8,128)(2,1)S(1)}, bf16[24,2176]{1,0:T(8,128)(2,1)S(1)}, u32[]{:S(2)}, u32[]{:S(2)}) collective-permute-start(bf16[24,2176]{1,0:T(8,128)(2,1)S(1)} %slice.72), channel_id=1, source_target_pairs={{0,4},{4,8},{8,12},{12,0},{1,5},{5,9},{9,13},{13,1},{2,6},{6,10},{... | collective-permute-start | bytes 313352 | tf_op jit(solution)/shard_map/ppermute | solution.py:65
  30.9 1.5 %collective-permute-start.3 = (bf16[160,2176]{1,0:T(8,128)(2,1)S(1)}, bf16[160,2176]{1,0:T(8,128)(2,1)S(1)}, u32[]{:S(2)}, u32[]{:S(2)}) collective-permute-start(bf16[160,2176]{1,0:T(8,128)(2,1)S(1)} %pad_maximum_fusion), channel_id=1, source_target_pairs={{0,2},{2,0},{1,3},{3,1},{4,6},{6,4},{5,7},{7,5},{8,10},{10,8},{9,1... | collective-permute-start | bytes 2088968 | tf_op jit(solution)/shard_map/ppermute | solution.py:65
  32.4 1.7 %constant_dynamic-update-slice_fusion.3 = (bf16[320,2176]{1,0:T(8,128)(2,1)}, bf16[640,2176]{1,0:T(8,128)(2,1)}) fusion(bf16[320,2176]{1,0:T(8,128)(2,1)} %get-tuple-element.21, bf16[40,2176]{1,0:T(8,128)(2,1)} %collective-permute-done, bf16[640,2176]{1,0:T(8,128)(2,1)} %get-tuple-element.22), kind=kLoop, calls=%fused_computation.52 | loop fusion | bytes 522240
  34.1 3.9 %collective-permute-done.11 = bf16[24,2176]{1,0:T(8,128)(2,1)S(1)} collective-permute-done((bf16[24,2176]{1,0:T(8,128)(2,1)S(1)}, bf16[24,2176]{1,0:T(8,128)(2,1)S(1)}, u32[]{:S(2)}, u32[]{:S(2)}) %collective-permute-start.11) | collective-permute-done | bytes 104480 | tf_op jit(solution)/shard_map/ppermute | solution.py:65
  38.0 1.6 %collective-permute-start.13 = (bf16[96,2176]{1,0:T(8,128)(2,1)S(1)}, bf16[96,2176]{1,0:T(8,128)(2,1)S(1)}, u32[]{:S(2)}, u32[]{:S(2)}) collective-permute-start(bf16[96,2176]{1,0:T(8,128)(2,1)S(1)} %pad_maximum_fusion.1), channel_id=1, source_target_pairs={{0,2},{2,0},{1,3},{3,1},{4,6},{6,4},{5,7},{7,5},{8,10},{10,8},{9,1... | collective-permute-start | bytes 1253384 | tf_op jit(solution)/shard_map/ppermute | solution.py:65
  39.6 16.2 %collective-permute-done.13 = bf16[96,2176]{1,0:T(8,128)(2,1)S(1)} collective-permute-done((bf16[96,2176]{1,0:T(8,128)(2,1)S(1)}, bf16[96,2176]{1,0:T(8,128)(2,1)S(1)}, u32[]{:S(2)}, u32[]{:S(2)}) %collective-permute-start.13) | collective-permute-done | bytes 417824 | tf_op jit(solution)/shard_map/ppermute | solution.py:65
  56.0 1.6 %constant_dynamic-update-slice_fusion.2 = (bf16[320,2176]{1,0:T(8,128)(2,1)}, bf16[640,2176]{1,0:T(8,128)(2,1)S(1)}) fusion(bf16[320,2176]{1,0:T(8,128)(2,1)} %get-tuple-element.28, bf16[40,2176]{1,0:T(8,128)(2,1)} %collective-permute-done.1, bf16[640,2176]{1,0:T(8,128)(2,1)S(1)} %copy-done.1), kind=kLoop, calls=%fused_computation.51 | loop fusion | bytes 522240
  57.6 1.6 %constant_dynamic-update-slice_fusion.1 = (bf16[320,2176]{1,0:T(8,128)(2,1)}, bf16[640,2176]{1,0:T(8,128)(2,1)S(1)}) fusion(bf16[320,2176]{1,0:T(8,128)(2,1)} %get-tuple-element.26, bf16[40,2176]{1,0:T(8,128)(2,1)} %collective-permute-done.2, bf16[640,2176]{1,0:T(8,128)(2,1)S(1)} %get-tuple-element.27), kind=kLoop, calls=%fused_computation.50 | loop fusion | bytes 522240
  59.2 0.9 constant_dynamic-update-slice_fusion
  60.1 0.5 collective-permute-start.4
  60.8 0.3 fusion.29
  61.0 4.9 %fusion = f32[384,1536]{1,0:T(8,128)S(1)} fusion(bf16[1,2048,1536]{2,1,0:T(8,128)(2,1)} %param.10, bf16[384,2176]{1,0:T(8,128)(2,1)S(1)} %constant_dynamic-update-slice_fusion.16), kind=kOutput, calls=%fused_computation | convolution fusion | flops 2415919104 | bytes 10223616 | tf_op jit(solution)/shard_map/dot_general | solution.py:9
  65.9 1.5 %convert_multiply_fusion.1 = f32[384,2048]{1,0:T(8,128)S(1)} fusion(bf16[1,768,2048]{2,1,0:T(8,128)(2,1)S(1)} %copy-done, f32[384]{0:T(512)S(1)} %fusion.29, f32[384,1536]{1,0:T(8,128)S(1)} %fusion), kind=kOutput, calls=%fused_computation.9 | convolution fusion | flops 1212088320 | bytes 8652288 | tf_op jit(solution)/shard_map/dot_general | solution.py:11
  67.6 0.2 constant_dynamic-update-slice_fusion.5
  67.9 4.2 %fusion.2 = f32[640,1536]{1,0:T(8,128)S(1)} fusion(bf16[1,2048,1536]{2,1,0:T(8,128)(2,1)S(1)} %bitcast.15, bf16[640,2176]{1,0:T(8,128)(2,1)S(1)} %constant_dynamic-update-slice_fusion.5), kind=kOutput, calls=%fused_computation.2 | convolution fusion | flops 4026531840 | bytes 12845056 | tf_op jit(solution)/shard_map/dot_general | solution.py:9
  72.1 0.4 fusion.24
  72.5 2.3 %convert_multiply_fusion = f32[640,2048]{1,0:T(8,128)S(1)} fusion(bf16[1,768,2048]{2,1,0:T(8,128)(2,1)S(1)} %copy-done, f32[640]{0:T(1024)S(1)} %fusion.24, f32[640,1536]{1,0:T(8,128)S(1)} %fusion.2), kind=kOutput, calls=%fused_computation.4 | convolution fusion | flops 2020147200 | bytes 12323328 | tf_op jit(solution)/shard_map/dot_general | solution.py:11
  74.8 0.2 split.112
  75.0 0.6 collective-permute-start.5
  75.5 0.2 slice_add_fusion.1
  75.8 1.6 %collective-permute-start.16 = (bf16[96,2048]{1,0:T(8,128)(2,1)S(1)}, bf16[96,2048]{1,0:T(8,128)(2,1)S(1)}, u32[]{:S(2)}, u32[]{:S(2)}) collective-permute-start(bf16[96,2048]{1,0:T(8,128)(2,1)S(1)} %split.115), channel_id=1, source_target_pairs={{0,2},{2,0},{1,3},{3,1},{4,6},{6,4},{5,7},{7,5},{8,10},{10,8},{9,1... | collective-permute-start | bytes 1179656 | tf_op jit(solution)/shard_map/ppermute | solution.py:74
  77.3 0.8 collective-permute-done.5
  78.2 0.4 slice_add_fusion
  78.6 1.6 %collective-permute-start.6 = (bf16[160,2048]{1,0:T(8,128)(2,1)S(1)}, bf16[160,2048]{1,0:T(8,128)(2,1)S(1)}, u32[]{:S(2)}, u32[]{:S(2)}) collective-permute-start(bf16[160,2048]{1,0:T(8,128)(2,1)S(1)} %split.114), channel_id=1, source_target_pairs={{0,2},{2,0},{1,3},{3,1},{4,6},{6,4},{5,7},{7,5},{8,10},{10,8},{9,1... | collective-permute-start | bytes 1966088 | tf_op jit(solution)/shard_map/ppermute | solution.py:74
  80.2 7.6 %collective-permute-done.16 = bf16[96,2048]{1,0:T(8,128)(2,1)S(1)} collective-permute-done((bf16[96,2048]{1,0:T(8,128)(2,1)S(1)}, bf16[96,2048]{1,0:T(8,128)(2,1)S(1)}, u32[]{:S(2)}, u32[]{:S(2)}) %collective-permute-start.16) | collective-permute-done | bytes 393248 | tf_op jit(solution)/shard_map/ppermute | solution.py:74
  87.8 0.1 fusion.34
  88.0 2.2 %collective-permute-start.17 = (bf16[24,2048]{1,0:T(8,128)(2,1)S(1)}, bf16[24,2048]{1,0:T(8,128)(2,1)S(1)}, u32[]{:S(2)}, u32[]{:S(2)}) collective-permute-start(bf16[24,2048]{1,0:T(8,128)(2,1)S(1)} %get-tuple-element.18), channel_id=1, source_target_pairs={{0,12},{4,0},{8,4},{12,8},{1,13},{5,1},{9,5},{13,9},{2,14},{6,2},{... | collective-permute-start | bytes 294920 | tf_op jit(solution)/shard_map/ppermute | solution.py:74
  90.2 0.6 collective-permute-start.18
  90.8 10.1 %collective-permute-done.6 = bf16[160,2048]{1,0:T(8,128)(2,1)S(1)} collective-permute-done((bf16[160,2048]{1,0:T(8,128)(2,1)S(1)}, bf16[160,2048]{1,0:T(8,128)(2,1)S(1)}, u32[]{:S(2)}, u32[]{:S(2)}) %collective-permute-start.6) | collective-permute-done | bytes 655392 | tf_op jit(solution)/shard_map/ppermute | solution.py:74
  100.9 0.2 fusion.33
  101.2 2.2 %collective-permute-start.7 = (bf16[40,2048]{1,0:T(8,128)(2,1)S(1)}, bf16[40,2048]{1,0:T(8,128)(2,1)S(1)}, u32[]{:S(2)}, u32[]{:S(2)}) collective-permute-start(bf16[40,2048]{1,0:T(8,128)(2,1)S(1)} %get-tuple-element.13), channel_id=1, source_target_pairs={{0,12},{4,0},{8,4},{12,8},{1,13},{5,1},{9,5},{13,9},{2,14},{6,2},{... | collective-permute-start | bytes 491528 | tf_op jit(solution)/shard_map/ppermute | solution.py:74
  103.4 0.6 collective-permute-start.8
  104.1 5.2 %collective-permute-done.7 = bf16[40,2048]{1,0:T(8,128)(2,1)S(1)} collective-permute-done((bf16[40,2048]{1,0:T(8,128)(2,1)S(1)}, bf16[40,2048]{1,0:T(8,128)(2,1)S(1)}, u32[]{:S(2)}, u32[]{:S(2)}) %collective-permute-start.7) | collective-permute-done | bytes 163872 | tf_op jit(solution)/shard_map/ppermute | solution.py:74
  109.3 3.0 %collective-permute-done.9 = bf16[40,2048]{1,0:T(8,128)(2,1)S(1)} collective-permute-done((bf16[40,2048]{1,0:T(8,128)(2,1)S(1)}, bf16[40,2048]{1,0:T(8,128)(2,1)S(1)}, u32[]{:S(2)}, u32[]{:S(2)}) %collective-permute-start.9) | collective-permute-done | bytes 163872 | tf_op jit(solution)/shard_map/ppermute | solution.py:74
  112.3 4.5 %collective-permute-done.8 = bf16[40,2048]{1,0:T(8,128)(2,1)S(1)} collective-permute-done((bf16[40,2048]{1,0:T(8,128)(2,1)S(1)}, bf16[40,2048]{1,0:T(8,128)(2,1)S(1)}, u32[]{:S(2)}, u32[]{:S(2)}) %collective-permute-start.8) | collective-permute-done | bytes 163872 | tf_op jit(solution)/shard_map/ppermute | solution.py:74
  116.9 0.7 pad_maximum_fusion.2
  (47 shorter events, 1.3 us)
Async XLA Ops:
  0.0 65.9 %copy-start = (bf16[1,768,2048]{2,1,0:T(8,128)(2,1)S(1)}, bf16[1,768,2048]{2,1,0:T(8,128)(2,1)}, u32[]{:S(2)}) copy-start(bf16[1,768,2048]{2,1,0:T(8,128)(2,1)} %param.11) | copy-start | bytes 9437188
  4.6 10.2 %collective-permute-start.2 = (bf16[40,2176]{1,0:T(8,128)(2,1)}, bf16[40,2176]{1,0:T(8,128)(2,1)}, u32[]{:S(2)}, u32[]{:S(2)}) collective-permute-start(bf16[40,2176]{1,0:T(8,128)(2,1)} %get-tuple-element.23), channel_id=1, source_target_pairs={{0,12},{4,0},{8,4},{12,8},{1,13},{5,1},{9,5},{13,9},{2,14},{6,2},{... | collective-permute-start | bytes 522248 | tf_op jit(solution)/shard_map/ppermute | solution.py:65
  9.7 15.1 %collective-permute-start.1 = (bf16[40,2176]{1,0:T(8,128)(2,1)}, bf16[40,2176]{1,0:T(8,128)(2,1)}, u32[]{:S(2)}, u32[]{:S(2)}) collective-permute-start(bf16[40,2176]{1,0:T(8,128)(2,1)} %get-tuple-element.23), channel_id=1, source_target_pairs={{0,8},{4,12},{8,0},{12,4},{1,9},{5,13},{9,1},{13,5},{2,10},{6,14},... | collective-permute-start | bytes 522248 | tf_op jit(solution)/shard_map/ppermute | solution.py:65
  9.7 15.1 %collective-permute-start = (bf16[40,2176]{1,0:T(8,128)(2,1)}, bf16[40,2176]{1,0:T(8,128)(2,1)}, u32[]{:S(2)}, u32[]{:S(2)}) collective-permute-start(bf16[40,2176]{1,0:T(8,128)(2,1)} %get-tuple-element.23), channel_id=1, source_target_pairs={{0,4},{4,8},{8,12},{12,0},{1,5},{5,9},{9,13},{13,1},{2,6},{6,10},{... | collective-permute-start | bytes 522248 | tf_op jit(solution)/shard_map/ppermute | solution.py:65
  26.0 8.1 %collective-permute-start.12 = (bf16[24,2176]{1,0:T(8,128)(2,1)S(1)}, bf16[24,2176]{1,0:T(8,128)(2,1)S(1)}, u32[]{:S(2)}, u32[]{:S(2)}) collective-permute-start(bf16[24,2176]{1,0:T(8,128)(2,1)S(1)} %slice.72), channel_id=1, source_target_pairs={{0,12},{4,0},{8,4},{12,8},{1,13},{5,1},{9,5},{13,9},{2,14},{6,2},{... | collective-permute-start | bytes 313352 | tf_op jit(solution)/shard_map/ppermute | solution.py:65
  26.9 11.1 %collective-permute-start.11 = (bf16[24,2176]{1,0:T(8,128)(2,1)S(1)}, bf16[24,2176]{1,0:T(8,128)(2,1)S(1)}, u32[]{:S(2)}, u32[]{:S(2)}) collective-permute-start(bf16[24,2176]{1,0:T(8,128)(2,1)S(1)} %slice.72), channel_id=1, source_target_pairs={{0,8},{4,12},{8,0},{12,4},{1,9},{5,13},{9,1},{13,5},{2,10},{6,14},... | collective-permute-start | bytes 313352 | tf_op jit(solution)/shard_map/ppermute | solution.py:65
  28.9 9.0 %collective-permute-start.10 = (bf16[24,2176]{1,0:T(8,128)(2,1)S(1)}, bf16[24,2176]{1,0:T(8,128)(2,1)S(1)}, u32[]{:S(2)}, u32[]{:S(2)}) collective-permute-start(bf16[24,2176]{1,0:T(8,128)(2,1)S(1)} %slice.72), channel_id=1, source_target_pairs={{0,4},{4,8},{8,12},{12,0},{1,5},{5,9},{9,13},{13,1},{2,6},{6,10},{... | collective-permute-start | bytes 313352 | tf_op jit(solution)/shard_map/ppermute | solution.py:65
  30.9 28.3 %collective-permute-start.3 = (bf16[160,2176]{1,0:T(8,128)(2,1)S(1)}, bf16[160,2176]{1,0:T(8,128)(2,1)S(1)}, u32[]{:S(2)}, u32[]{:S(2)}) collective-permute-start(bf16[160,2176]{1,0:T(8,128)(2,1)S(1)} %pad_maximum_fusion), channel_id=1, source_target_pairs={{0,2},{2,0},{1,3},{3,1},{4,6},{6,4},{5,7},{7,5},{8,10},{10,8},{9,1... | collective-permute-start | bytes 2088968 | tf_op jit(solution)/shard_map/ppermute | solution.py:65
  34.1 21.9 %copy-start.1 = (bf16[640,2176]{1,0:T(8,128)(2,1)S(1)}, bf16[640,2176]{1,0:T(8,128)(2,1)}, u32[]{:S(2)}) copy-start(bf16[640,2176]{1,0:T(8,128)(2,1)} %get-tuple-element.29) | copy-start | bytes 8355844
  38.0 17.8 %collective-permute-start.13 = (bf16[96,2176]{1,0:T(8,128)(2,1)S(1)}, bf16[96,2176]{1,0:T(8,128)(2,1)S(1)}, u32[]{:S(2)}, u32[]{:S(2)}) collective-permute-start(bf16[96,2176]{1,0:T(8,128)(2,1)S(1)} %pad_maximum_fusion.1), channel_id=1, source_target_pairs={{0,2},{2,0},{1,3},{3,1},{4,6},{6,4},{5,7},{7,5},{8,10},{10,8},{9,1... | collective-permute-start | bytes 1253384 | tf_op jit(solution)/shard_map/ppermute | solution.py:65
  55.9 4.7 %collective-permute-start.14 = (bf16[192,2176]{1,0:T(8,128)(2,1)S(1)}, bf16[192,2176]{1,0:T(8,128)(2,1)S(1)}, u32[]{:S(2)}, u32[]{:S(2)}) collective-permute-start(bf16[192,2176]{1,0:T(8,128)(2,1)S(1)} %get-tuple-element.16), channel_id=1, source_target_pairs={{0,1},{1,0},{2,3},{3,2},{4,5},{5,4},{6,7},{7,6},{8,9},{9,8},{10,11... | collective-permute-start | bytes 2506760 | tf_op jit(solution)/shard_map/ppermute | solution.py:65
  60.1 7.5 %collective-permute-start.4 = (bf16[320,2176]{1,0:T(8,128)(2,1)}, bf16[320,2176]{1,0:T(8,128)(2,1)S(1)}, u32[]{:S(2)}, u32[]{:S(2)}) collective-permute-start(bf16[320,2176]{1,0:T(8,128)(2,1)} %get-tuple-element.11), channel_id=1, source_target_pairs={{0,1},{1,0},{2,3},{3,2},{4,5},{5,4},{6,7},{7,6},{8,9},{9,8},{10,11... | collective-permute-start | bytes 4177928 | tf_op jit(solution)/shard_map/ppermute | solution.py:65
  60.7 7.1 %slice-start = ((s8[6291456]{0:T(1024)(128)(4,1)}), s8[4194304]{0:T(1024)(128)(4,1)S(1)}, s32[]{:S(2)}) async-start(s8[6291456]{0:T(1024)(128)(4,1)} %bitcast.14), calls=%async_computation | async-start | bytes 8388608
  61.0 6.9 %slice-start.1 = ((s8[6291456]{0:T(1024)(128)(4,1)}), s8[2097152]{0:T(1024)(128)(4,1)S(1)}, s32[]{:S(2)}) async-start(s8[6291456]{0:T(1024)(128)(4,1)} %bitcast.14), calls=%async_computation.1 | async-start | bytes 4194304
  67.5 8.0 %collective-permute-start.15 = (bf16[192,2048]{1,0:T(8,128)(2,1)S(1)}, bf16[192,2048]{1,0:T(8,128)(2,1)S(1)}, u32[]{:S(2)}, u32[]{:S(2)}) collective-permute-start(bf16[192,2048]{1,0:T(8,128)(2,1)S(1)} %split.113), channel_id=1, source_target_pairs={{0,1},{1,0},{2,3},{3,2},{4,5},{5,4},{6,7},{7,6},{8,9},{9,8},{10,11... | collective-permute-start | bytes 2359304 | tf_op jit(solution)/shard_map/ppermute | solution.py:74
  75.0 3.2 %collective-permute-start.5 = (bf16[320,2048]{1,0:T(8,128)(2,1)S(1)}, bf16[320,2048]{1,0:T(8,128)(2,1)S(1)}, u32[]{:S(2)}, u32[]{:S(2)}) collective-permute-start(bf16[320,2048]{1,0:T(8,128)(2,1)S(1)} %split.112), channel_id=1, source_target_pairs={{0,1},{1,0},{2,3},{3,2},{4,5},{5,4},{6,7},{7,6},{8,9},{9,8},{10,11... | collective-permute-start | bytes 3932168 | tf_op jit(solution)/shard_map/ppermute | solution.py:74
  75.8 12.1 %collective-permute-start.16 = (bf16[96,2048]{1,0:T(8,128)(2,1)S(1)}, bf16[96,2048]{1,0:T(8,128)(2,1)S(1)}, u32[]{:S(2)}, u32[]{:S(2)}) collective-permute-start(bf16[96,2048]{1,0:T(8,128)(2,1)S(1)} %split.115), channel_id=1, source_target_pairs={{0,2},{2,0},{1,3},{3,1},{4,6},{6,4},{5,7},{7,5},{8,10},{10,8},{9,1... | collective-permute-start | bytes 1179656 | tf_op jit(solution)/shard_map/ppermute | solution.py:74
  78.6 22.3 %collective-permute-start.6 = (bf16[160,2048]{1,0:T(8,128)(2,1)S(1)}, bf16[160,2048]{1,0:T(8,128)(2,1)S(1)}, u32[]{:S(2)}, u32[]{:S(2)}) collective-permute-start(bf16[160,2048]{1,0:T(8,128)(2,1)S(1)} %split.114), channel_id=1, source_target_pairs={{0,2},{2,0},{1,3},{3,1},{4,6},{6,4},{5,7},{7,5},{8,10},{10,8},{9,1... | collective-permute-start | bytes 1966088 | tf_op jit(solution)/shard_map/ppermute | solution.py:74
  88.0 15.4 %collective-permute-start.17 = (bf16[24,2048]{1,0:T(8,128)(2,1)S(1)}, bf16[24,2048]{1,0:T(8,128)(2,1)S(1)}, u32[]{:S(2)}, u32[]{:S(2)}) collective-permute-start(bf16[24,2048]{1,0:T(8,128)(2,1)S(1)} %get-tuple-element.18), channel_id=1, source_target_pairs={{0,12},{4,0},{8,4},{12,8},{1,13},{5,1},{9,5},{13,9},{2,14},{6,2},{... | collective-permute-start | bytes 294920 | tf_op jit(solution)/shard_map/ppermute | solution.py:74
  90.2 13.8 %collective-permute-start.19 = (bf16[24,2048]{1,0:T(8,128)(2,1)S(1)}, bf16[24,2048]{1,0:T(8,128)(2,1)S(1)}, u32[]{:S(2)}, u32[]{:S(2)}) collective-permute-start(bf16[24,2048]{1,0:T(8,128)(2,1)S(1)} %get-tuple-element.19), channel_id=1, source_target_pairs={{0,4},{4,8},{8,12},{12,0},{1,5},{5,9},{9,13},{13,1},{2,6},{6,10},{... | collective-permute-start | bytes 294920 | tf_op jit(solution)/shard_map/ppermute | solution.py:74
  90.2 13.8 %collective-permute-start.18 = (bf16[24,2048]{1,0:T(8,128)(2,1)S(1)}, bf16[24,2048]{1,0:T(8,128)(2,1)S(1)}, u32[]{:S(2)}, u32[]{:S(2)}) collective-permute-start(bf16[24,2048]{1,0:T(8,128)(2,1)S(1)} %get-tuple-element.20), channel_id=1, source_target_pairs={{0,8},{4,12},{8,0},{12,4},{1,9},{5,13},{9,1},{13,5},{2,10},{6,14},... | collective-permute-start | bytes 294920 | tf_op jit(solution)/shard_map/ppermute | solution.py:74
  101.2 8.1 %collective-permute-start.7 = (bf16[40,2048]{1,0:T(8,128)(2,1)S(1)}, bf16[40,2048]{1,0:T(8,128)(2,1)S(1)}, u32[]{:S(2)}, u32[]{:S(2)}) collective-permute-start(bf16[40,2048]{1,0:T(8,128)(2,1)S(1)} %get-tuple-element.13), channel_id=1, source_target_pairs={{0,12},{4,0},{8,4},{12,8},{1,13},{5,1},{9,5},{13,9},{2,14},{6,2},{... | collective-permute-start | bytes 491528 | tf_op jit(solution)/shard_map/ppermute | solution.py:74
  103.4 8.9 %collective-permute-start.9 = (bf16[40,2048]{1,0:T(8,128)(2,1)S(1)}, bf16[40,2048]{1,0:T(8,128)(2,1)S(1)}, u32[]{:S(2)}, u32[]{:S(2)}) collective-permute-start(bf16[40,2048]{1,0:T(8,128)(2,1)S(1)} %get-tuple-element.14), channel_id=1, source_target_pairs={{0,4},{4,8},{8,12},{12,0},{1,5},{5,9},{9,13},{13,1},{2,6},{6,10},{... | collective-permute-start | bytes 491528 | tf_op jit(solution)/shard_map/ppermute | solution.py:74
  103.4 13.4 %collective-permute-start.8 = (bf16[40,2048]{1,0:T(8,128)(2,1)S(1)}, bf16[40,2048]{1,0:T(8,128)(2,1)S(1)}, u32[]{:S(2)}, u32[]{:S(2)}) collective-permute-start(bf16[40,2048]{1,0:T(8,128)(2,1)S(1)} %get-tuple-element.15), channel_id=1, source_target_pairs={{0,8},{4,12},{8,0},{12,4},{1,9},{5,13},{9,1},{13,5},{2,10},{6,14},... | collective-permute-start | bytes 491528 | tf_op jit(solution)/shard_map/ppermute | solution.py:74

commit v19 on v18

--- a/solution.py
+++ b/solution.py
@@ -96,7 +96,7 @@
     pick = (jnp.arange(hosts, dtype=jnp.int32) == me).astype(jnp.float32)
     results = []
     held = None
-    first = tok_rows * 5 // 8 // 8 * 8
+    first = tok_rows * 3 // 8 // 8 * 8
     for rows in (carried[:first], carried[first:]):
         if held is not None:
             held, rows = lax.optimization_barrier((held, rows))

time: 118 us -> 113 us (0.958)
  waiting for transfers between devices: 65.4 us -> 59.3 us
  starting transfers between devices: 24 us -> 27.8 us
  matrix products: 12.9 us -> 10.5 us
    ppermute x10, waiting for transfers between devices: 34.1 us -> 27.2 us  [gather_stage(): got.append(lax.ppermute(block, axis, pairs))]
    ppermute x10, starting transfers between devices: 9.43 us -> 13.5 us  [scatter_stage(): lax.ppermute(pieces[shift].astype(jnp.bfloat16), axis, pairs)]
    dot_general x2, matrix products: 9.12 us -> 6.84 us  [expert_block(): pair = jnp.dot(rows_in, gate_up, preferred_element_type=jnp.float32)]
  transfers between devices with their start and end apart: 20 -> 20, of which waited for: 10 -> 10; matrix products, arithmetic and copies ran while one was open for 18% -> 17% of each run, Pallas kernels for 0% -> 0%
where the time goes in v19:
time: 113 us
  waiting for transfers between devices  59.3 us (52%)
  starting transfers between devices  27.8 us (25%)
  matrix products  10.5 us (9%)
  local copies, waits for them, and re-layouts  9.02 us (8%)
  other arithmetic  6.11 us (5%)
    ppermute x10, waiting for transfers between devices, scatter_stage(): lax.ppermute(pieces[shift].astype(jnp.bfloat16), axis, pairs)  32.1 us
    ppermute x10, waiting for transfers between devices, gather_stage(): got.append(lax.ppermute(block, axis, pairs))  27.2 us
    ppermute x10, starting transfers between devices, gather_stage(): got.append(lax.ppermute(block, axis, pairs))  14.3 us
    ppermute x10, starting transfers between devices, scatter_stage(): lax.ppermute(pieces[shift].astype(jnp.bfloat16), axis, pairs)  13.5 us
    dot_general x2, matrix products, expert_block(): pair = jnp.dot(rows_in, gate_up, preferred_element_type=jnp.float32)  6.84 us
    unnamed x16, local copies, waits for them, and re-layouts  4.84 us
    dot_general x2, matrix products, expert_block(): jnp.dot(active, down_proj, preferred_element_type=jnp.float32)  3.68 us
  transfers between devices with their start and end apart: 20, of which 10 were waited for; matrix products, arithmetic and copies ran while one was open for 17% of the time, Pallas kernels for 0%

profile of v19, /device:TPU:0, one launch (start us, length us, event | category | flops | bytes accessed | tf_op | source)
XLA Modules:
  0.0 113.1 jit_solution(14911726589707580648)
XLA Ops:
  0.0 0.9 reduce_sum.36
  0.9 0.8 broadcast_divide_fusion
  1.7 0.8 select_reduce_fusion
  2.8 1.1 concatenate.32
  3.8 0.8 constant_dynamic-update-slice_fusion.4
  4.6 3.1 %collective-permute-start = (bf16[24,2176]{1,0:T(8,128)(2,1)}, bf16[24,2176]{1,0:T(8,128)(2,1)}, u32[]{:S(2)}, u32[]{:S(2)}) collective-permute-start(bf16[24,2176]{1,0:T(8,128)(2,1)} %get-tuple-element.23), channel_id=1, source_target_pairs={{0,4},{4,8},{8,12},{12,0},{1,5},{5,9},{9,13},{13,1},{2,6},{6,10},{... | collective-permute-start | bytes 313352 | tf_op jit(solution)/shard_map/ppermute | solution.py:65
  7.7 2.6 %collective-permute-start.1 = (bf16[24,2176]{1,0:T(8,128)(2,1)}, bf16[24,2176]{1,0:T(8,128)(2,1)}, u32[]{:S(2)}, u32[]{:S(2)}) collective-permute-start(bf16[24,2176]{1,0:T(8,128)(2,1)} %get-tuple-element.23), channel_id=1, source_target_pairs={{0,8},{4,12},{8,0},{12,4},{1,9},{5,13},{9,1},{13,5},{2,10},{6,14},... | collective-permute-start | bytes 313352 | tf_op jit(solution)/shard_map/ppermute | solution.py:65
  10.3 1.3 %collective-permute-start.2 = (bf16[24,2176]{1,0:T(8,128)(2,1)}, bf16[24,2176]{1,0:T(8,128)(2,1)S(1)}, u32[]{:S(2)}, u32[]{:S(2)}) collective-permute-start(bf16[24,2176]{1,0:T(8,128)(2,1)} %get-tuple-element.23), channel_id=1, source_target_pairs={{0,12},{4,0},{8,4},{12,8},{1,13},{5,1},{9,5},{13,9},{2,14},{6,2},{... | collective-permute-start | bytes 313352 | tf_op jit(solution)/shard_map/ppermute | solution.py:65
  11.6 0.9 slice.72
  12.6 1.3 %collective-permute-done = bf16[24,2176]{1,0:T(8,128)(2,1)} collective-permute-done((bf16[24,2176]{1,0:T(8,128)(2,1)}, bf16[24,2176]{1,0:T(8,128)(2,1)}, u32[]{:S(2)}, u32[]{:S(2)}) %collective-permute-start) | collective-permute-done | bytes 104480 | tf_op jit(solution)/shard_map/ppermute | solution.py:65
  13.9 3.7 %collective-permute-done.1 = bf16[24,2176]{1,0:T(8,128)(2,1)} collective-permute-done((bf16[24,2176]{1,0:T(8,128)(2,1)}, bf16[24,2176]{1,0:T(8,128)(2,1)}, u32[]{:S(2)}, u32[]{:S(2)}) %collective-permute-start.1) | collective-permute-done | bytes 104480 | tf_op jit(solution)/shard_map/ppermute | solution.py:65
  17.6 1.2 %pad_maximum_fusion.1 = bf16[96,2176]{1,0:T(8,128)(2,1)S(1)} fusion(bf16[24,2176]{1,0:T(8,128)(2,1)S(1)} %collective-permute-done.2, bf16[24,2176]{1,0:T(8,128)(2,1)} %collective-permute-done.1, bf16[24,2176]{1,0:T(8,128)(2,1)} %collective-permute-done, bf16[24,2176]{1,0:T(8,128)(2,1)} %get-tuple-element.23), kind=kLoop, calls=%fused_computation.28 | loop fusion | flops 1671168 | bytes 835584 | tf_op jit(solution)/shard_map/concatenate | solution.py:66
  18.7 1.6 %collective-permute-start.3 = (bf16[96,2176]{1,0:T(8,128)(2,1)S(1)}, bf16[96,2176]{1,0:T(8,128)(2,1)S(1)}, u32[]{:S(2)}, u32[]{:S(2)}) collective-permute-start(bf16[96,2176]{1,0:T(8,128)(2,1)S(1)} %pad_maximum_fusion.1), channel_id=1, source_target_pairs={{0,2},{2,0},{1,3},{3,1},{4,6},{6,4},{5,7},{7,5},{8,10},{10,8},{9,1... | collective-permute-start | bytes 1253384 | tf_op jit(solution)/shard_map/ppermute | solution.py:65
  20.3 2.7 %collective-permute-start.10 = (bf16[40,2176]{1,0:T(8,128)(2,1)S(1)}, bf16[40,2176]{1,0:T(8,128)(2,1)S(1)}, u32[]{:S(2)}, u32[]{:S(2)}) collective-permute-start(bf16[40,2176]{1,0:T(8,128)(2,1)S(1)} %slice.72), channel_id=1, source_target_pairs={{0,4},{4,8},{8,12},{12,0},{1,5},{5,9},{9,13},{13,1},{2,6},{6,10},{... | collective-permute-start | bytes 522248 | tf_op jit(solution)/shard_map/ppermute | solution.py:65
  23.0 1.7 %collective-permute-start.11 = (bf16[40,2176]{1,0:T(8,128)(2,1)S(1)}, bf16[40,2176]{1,0:T(8,128)(2,1)S(1)}, u32[]{:S(2)}, u32[]{:S(2)}) collective-permute-start(bf16[40,2176]{1,0:T(8,128)(2,1)S(1)} %slice.72), channel_id=1, source_target_pairs={{0,8},{4,12},{8,0},{12,4},{1,9},{5,13},{9,1},{13,5},{2,10},{6,14},... | collective-permute-start | bytes 522248 | tf_op jit(solution)/shard_map/ppermute | solution.py:65
  24.7 0.7 collective-permute-start.12
  25.4 1.6 %constant_dynamic-update-slice_fusion.3 = (bf16[192,2176]{1,0:T(8,128)(2,1)}, bf16[384,2176]{1,0:T(8,128)(2,1)}) fusion(bf16[192,2176]{1,0:T(8,128)(2,1)} %get-tuple-element.21, bf16[24,2176]{1,0:T(8,128)(2,1)} %collective-permute-done, bf16[384,2176]{1,0:T(8,128)(2,1)} %get-tuple-element.22), kind=kLoop, calls=%fused_computation.52 | loop fusion | bytes 313344
  27.0 1.6 %constant_dynamic-update-slice_fusion.2 = (bf16[192,2176]{1,0:T(8,128)(2,1)}, bf16[384,2176]{1,0:T(8,128)(2,1)}) fusion(bf16[192,2176]{1,0:T(8,128)(2,1)} %get-tuple-element.36, bf16[24,2176]{1,0:T(8,128)(2,1)} %collective-permute-done.1, bf16[384,2176]{1,0:T(8,128)(2,1)} %get-tuple-element.37), kind=kLoop, calls=%fused_computation.51 | loop fusion | bytes 313344
  28.6 0.7 constant_dynamic-update-slice_fusion.1
  29.3 0.3 collective-permute-done.10
  29.6 6.1 %collective-permute-done.11 = bf16[40,2176]{1,0:T(8,128)(2,1)S(1)} collective-permute-done((bf16[40,2176]{1,0:T(8,128)(2,1)S(1)}, bf16[40,2176]{1,0:T(8,128)(2,1)S(1)}, u32[]{:S(2)}, u32[]{:S(2)}) %collective-permute-start.11) | collective-permute-done | bytes 174112 | tf_op jit(solution)/shard_map/ppermute | solution.py:65
  35.8 0.6 collective-permute-start.13
  36.4 1.0 constant_dynamic-update-slice_fusion
  37.5 15.8 %collective-permute-done.13 = bf16[160,2176]{1,0:T(8,128)(2,1)S(1)} collective-permute-done((bf16[160,2176]{1,0:T(8,128)(2,1)S(1)}, bf16[160,2176]{1,0:T(8,128)(2,1)S(1)}, u32[]{:S(2)}, u32[]{:S(2)}) %collective-permute-start.13) | collective-permute-done | bytes 696352 | tf_op jit(solution)/shard_map/ppermute | solution.py:65
  53.7 0.3 fusion.29
  54.0 2.6 %fusion.2 = f32[384,1536]{1,0:T(8,128)S(1)} fusion(bf16[1,2048,1536]{2,1,0:T(8,128)(2,1)S(1)} %copy-done.3, bf16[384,2176]{1,0:T(8,128)(2,1)S(1)} %constant_dynamic-update-slice_fusion.5), kind=kOutput, calls=%fused_computation.2 | convolution fusion | flops 2415919104 | bytes 10223616 | tf_op jit(solution)/shard_map/dot_general | solution.py:9
  56.6 1.4 %convert_multiply_fusion.1 = f32[384,2048]{1,0:T(8,128)S(1)} fusion(bf16[1,768,2048]{2,1,0:T(8,128)(2,1)S(1)} %copy-done, f32[384]{0:T(512)S(1)} %fusion.29, f32[384,1536]{1,0:T(8,128)S(1)} %fusion.2), kind=kOutput, calls=%fused_computation.9 | convolution fusion | flops 1212088320 | bytes 8652288 | tf_op jit(solution)/shard_map/dot_general | solution.py:11
  58.2 0.5 collective-permute-start.5
  58.7 0.2 constant_dynamic-update-slice_fusion.16
  58.9 4.2 %fusion = f32[640,1536]{1,0:T(8,128)S(1)} fusion(bf16[1,2048,1536]{2,1,0:T(8,128)(2,1)S(1)} %copy-done.3, bf16[640,2176]{1,0:T(8,128)(2,1)S(1)} %constant_dynamic-update-slice_fusion.16), kind=kOutput, calls=%fused_computation | convolution fusion | flops 4026531840 | bytes 12845056 | tf_op jit(solution)/shard_map/dot_general | solution.py:9
  63.2 0.4 fusion.24
  63.5 2.2 %convert_multiply_fusion = f32[640,2048]{1,0:T(8,128)S(1)} fusion(bf16[1,768,2048]{2,1,0:T(8,128)(2,1)S(1)} %copy-done, f32[640]{0:T(1024)S(1)} %fusion.24, f32[640,1536]{1,0:T(8,128)S(1)} %fusion), kind=kOutput, calls=%fused_computation.4 | convolution fusion | flops 2020147200 | bytes 12323328 | tf_op jit(solution)/shard_map/dot_general | solution.py:11
  65.8 0.2 split.112
  66.1 0.2 slice_add_fusion.1
  66.4 0.6 collective-permute-start.6
  66.9 2.1 %collective-permute-done.15 = bf16[320,2048]{1,0:T(8,128)(2,1)S(1)} collective-permute-done((bf16[320,2048]{1,0:T(8,128)(2,1)S(1)}, bf16[320,2048]{1,0:T(8,128)(2,1)S(1)}, u32[]{:S(2)}, u32[]{:S(2)}) %collective-permute-start.15) | collective-permute-done | bytes 1310752 | tf_op jit(solution)/shard_map/ppermute | solution.py:74
  69.1 0.4 slice_add_fusion
  69.5 0.6 collective-permute-start.16
  70.1 8.3 %collective-permute-done.6 = bf16[96,2048]{1,0:T(8,128)(2,1)S(1)} collective-permute-done((bf16[96,2048]{1,0:T(8,128)(2,1)S(1)}, bf16[96,2048]{1,0:T(8,128)(2,1)S(1)}, u32[]{:S(2)}, u32[]{:S(2)}) %collective-permute-start.6) | collective-permute-done | bytes 393248 | tf_op jit(solution)/shard_map/ppermute | solution.py:74
  78.6 4.4 %collective-permute-start.7 = (bf16[24,2048]{1,0:T(8,128)(2,1)S(1)}, bf16[24,2048]{1,0:T(8,128)(2,1)S(1)}, u32[]{:S(2)}, u32[]{:S(2)}) collective-permute-start(bf16[24,2048]{1,0:T(8,128)(2,1)S(1)} %get-tuple-element.18), channel_id=1, source_target_pairs={{0,12},{4,0},{8,4},{12,8},{1,13},{5,1},{9,5},{13,9},{2,14},{6,2},{... | collective-permute-start | bytes 294920 | tf_op jit(solution)/shard_map/ppermute | solution.py:74
  83.0 1.4 %collective-permute-start.8 = (bf16[24,2048]{1,0:T(8,128)(2,1)S(1)}, bf16[24,2048]{1,0:T(8,128)(2,1)S(1)}, u32[]{:S(2)}, u32[]{:S(2)}) collective-permute-start(bf16[24,2048]{1,0:T(8,128)(2,1)S(1)} %get-tuple-element.20), channel_id=1, source_target_pairs={{0,8},{4,12},{8,0},{12,4},{1,9},{5,13},{9,1},{13,5},{2,10},{6,14},... | collective-permute-start | bytes 294920 | tf_op jit(solution)/shard_map/ppermute | solution.py:74
  84.4 7.6 %collective-permute-done.16 = bf16[160,2048]{1,0:T(8,128)(2,1)S(1)} collective-permute-done((bf16[160,2048]{1,0:T(8,128)(2,1)S(1)}, bf16[160,2048]{1,0:T(8,128)(2,1)S(1)}, u32[]{:S(2)}, u32[]{:S(2)}) %collective-permute-start.16) | collective-permute-done | bytes 655392 | tf_op jit(solution)/shard_map/ppermute | solution.py:74
  91.9 0.2 fusion.34
  92.2 4.4 %collective-permute-start.17 = (bf16[40,2048]{1,0:T(8,128)(2,1)S(1)}, bf16[40,2048]{1,0:T(8,128)(2,1)S(1)}, u32[]{:S(2)}, u32[]{:S(2)}) collective-permute-start(bf16[40,2048]{1,0:T(8,128)(2,1)S(1)} %get-tuple-element.13), channel_id=1, source_target_pairs={{0,12},{4,0},{8,4},{12,8},{1,13},{5,1},{9,5},{13,9},{2,14},{6,2},{... | collective-permute-start | bytes 491528 | tf_op jit(solution)/shard_map/ppermute | solution.py:74
  96.6 1.4 %collective-permute-start.18 = (bf16[40,2048]{1,0:T(8,128)(2,1)S(1)}, bf16[40,2048]{1,0:T(8,128)(2,1)S(1)}, u32[]{:S(2)}, u32[]{:S(2)}) collective-permute-start(bf16[40,2048]{1,0:T(8,128)(2,1)S(1)} %get-tuple-element.15), channel_id=1, source_target_pairs={{0,8},{4,12},{8,0},{12,4},{1,9},{5,13},{9,1},{13,5},{2,10},{6,14},... | collective-permute-start | bytes 491528 | tf_op jit(solution)/shard_map/ppermute | solution.py:74
  98.1 3.2 %collective-permute-done.17 = bf16[40,2048]{1,0:T(8,128)(2,1)S(1)} collective-permute-done((bf16[40,2048]{1,0:T(8,128)(2,1)S(1)}, bf16[40,2048]{1,0:T(8,128)(2,1)S(1)}, u32[]{:S(2)}, u32[]{:S(2)}) %collective-permute-start.17) | collective-permute-done | bytes 163872 | tf_op jit(solution)/shard_map/ppermute | solution.py:74
  101.3 11.0 %collective-permute-done.18 = bf16[40,2048]{1,0:T(8,128)(2,1)S(1)} collective-permute-done((bf16[40,2048]{1,0:T(8,128)(2,1)S(1)}, bf16[40,2048]{1,0:T(8,128)(2,1)S(1)}, u32[]{:S(2)}, u32[]{:S(2)}) %collective-permute-start.18) | collective-permute-done | bytes 163872 | tf_op jit(solution)/shard_map/ppermute | solution.py:74
  112.3 0.7 pad_maximum_fusion.2
  (46 shorter events, 1.6 us)
Async XLA Ops:
  0.0 56.6 %copy-start = (bf16[1,768,2048]{2,1,0:T(8,128)(2,1)S(1)}, bf16[1,768,2048]{2,1,0:T(8,128)(2,1)}, u32[]{:S(2)}) copy-start(bf16[1,768,2048]{2,1,0:T(8,128)(2,1)} %param.11) | copy-start | bytes 9437188
  3.8 7.8 %copy-start.1 = (bf16[64,2176]{1,0:T(8,128)(2,1)}, bf16[64,2176]{1,0:T(8,128)(2,1)S(1)}, u32[]{:S(2)}) copy-start(bf16[64,2176]{1,0:T(8,128)(2,1)S(1)} %concatenate.32) | copy-start | bytes 835588
  4.6 9.3 %collective-permute-start = (bf16[24,2176]{1,0:T(8,128)(2,1)}, bf16[24,2176]{1,0:T(8,128)(2,1)}, u32[]{:S(2)}, u32[]{:S(2)}) collective-permute-start(bf16[24,2176]{1,0:T(8,128)(2,1)} %get-tuple-element.23), channel_id=1, source_target_pairs={{0,4},{4,8},{8,12},{12,0},{1,5},{5,9},{9,13},{13,1},{2,6},{6,10},{... | collective-permute-start | bytes 313352 | tf_op jit(solution)/shard_map/ppermute | solution.py:65
  7.7 9.9 %collective-permute-start.1 = (bf16[24,2176]{1,0:T(8,128)(2,1)}, bf16[24,2176]{1,0:T(8,128)(2,1)}, u32[]{:S(2)}, u32[]{:S(2)}) collective-permute-start(bf16[24,2176]{1,0:T(8,128)(2,1)} %get-tuple-element.23), channel_id=1, source_target_pairs={{0,8},{4,12},{8,0},{12,4},{1,9},{5,13},{9,1},{13,5},{2,10},{6,14},... | collective-permute-start | bytes 313352 | tf_op jit(solution)/shard_map/ppermute | solution.py:65
  10.3 7.3 %collective-permute-start.2 = (bf16[24,2176]{1,0:T(8,128)(2,1)}, bf16[24,2176]{1,0:T(8,128)(2,1)S(1)}, u32[]{:S(2)}, u32[]{:S(2)}) collective-permute-start(bf16[24,2176]{1,0:T(8,128)(2,1)} %get-tuple-element.23), channel_id=1, source_target_pairs={{0,12},{4,0},{8,4},{12,8},{1,13},{5,1},{9,5},{13,9},{2,14},{6,2},{... | collective-permute-start | bytes 313352 | tf_op jit(solution)/shard_map/ppermute | solution.py:65
  17.6 36.4 %copy-start.3 = (bf16[1,2048,1536]{2,1,0:T(8,128)(2,1)S(1)}, bf16[1,2048,1536]{2,1,0:T(8,128)(2,1)}, u32[]{:S(2)}) copy-start(bf16[1,2048,1536]{2,1,0:T(8,128)(2,1)} %param.10) | copy-start | bytes 18874372
  18.7 17.7 %collective-permute-start.3 = (bf16[96,2176]{1,0:T(8,128)(2,1)S(1)}, bf16[96,2176]{1,0:T(8,128)(2,1)S(1)}, u32[]{:S(2)}, u32[]{:S(2)}) collective-permute-start(bf16[96,2176]{1,0:T(8,128)(2,1)S(1)} %pad_maximum_fusion.1), channel_id=1, source_target_pairs={{0,2},{2,0},{1,3},{3,1},{4,6},{6,4},{5,7},{7,5},{8,10},{10,8},{9,1... | collective-permute-start | bytes 1253384 | tf_op jit(solution)/shard_map/ppermute | solution.py:65
  20.3 9.3 %collective-permute-start.10 = (bf16[40,2176]{1,0:T(8,128)(2,1)S(1)}, bf16[40,2176]{1,0:T(8,128)(2,1)S(1)}, u32[]{:S(2)}, u32[]{:S(2)}) collective-permute-start(bf16[40,2176]{1,0:T(8,128)(2,1)S(1)} %slice.72), channel_id=1, source_target_pairs={{0,4},{4,8},{8,12},{12,0},{1,5},{5,9},{9,13},{13,1},{2,6},{6,10},{... | collective-permute-start | bytes 522248 | tf_op jit(solution)/shard_map/ppermute | solution.py:65
  23.0 12.8 %collective-permute-start.11 = (bf16[40,2176]{1,0:T(8,128)(2,1)S(1)}, bf16[40,2176]{1,0:T(8,128)(2,1)S(1)}, u32[]{:S(2)}, u32[]{:S(2)}) collective-permute-start(bf16[40,2176]{1,0:T(8,128)(2,1)S(1)} %slice.72), channel_id=1, source_target_pairs={{0,8},{4,12},{8,0},{12,4},{1,9},{5,13},{9,1},{13,5},{2,10},{6,14},... | collective-permute-start | bytes 522248 | tf_op jit(solution)/shard_map/ppermute | solution.py:65
  24.7 11.1 %collective-permute-start.12 = (bf16[40,2176]{1,0:T(8,128)(2,1)S(1)}, bf16[40,2176]{1,0:T(8,128)(2,1)S(1)}, u32[]{:S(2)}, u32[]{:S(2)}) collective-permute-start(bf16[40,2176]{1,0:T(8,128)(2,1)S(1)} %slice.72), channel_id=1, source_target_pairs={{0,12},{4,0},{8,4},{12,8},{1,13},{5,1},{9,5},{13,9},{2,14},{6,2},{... | collective-permute-start | bytes 522248 | tf_op jit(solution)/shard_map/ppermute | solution.py:65
  35.8 17.5 %collective-permute-start.13 = (bf16[160,2176]{1,0:T(8,128)(2,1)S(1)}, bf16[160,2176]{1,0:T(8,128)(2,1)S(1)}, u32[]{:S(2)}, u32[]{:S(2)}) collective-permute-start(bf16[160,2176]{1,0:T(8,128)(2,1)S(1)} %pad_maximum_fusion), channel_id=1, source_target_pairs={{0,2},{2,0},{1,3},{3,1},{4,6},{6,4},{5,7},{7,5},{8,10},{10,8},{9,1... | collective-permute-start | bytes 2088968 | tf_op jit(solution)/shard_map/ppermute | solution.py:65
  37.4 16.2 %copy-start.2 = (bf16[384,2176]{1,0:T(8,128)(2,1)S(1)}, bf16[384,2176]{1,0:T(8,128)(2,1)}, u32[]{:S(2)}) copy-start(bf16[384,2176]{1,0:T(8,128)(2,1)} %get-tuple-element.17) | copy-start | bytes 5013508
  37.4 16.1 %collective-permute-start.4 = (bf16[192,2176]{1,0:T(8,128)(2,1)}, bf16[192,2176]{1,0:T(8,128)(2,1)S(1)}, u32[]{:S(2)}, u32[]{:S(2)}) collective-permute-start(bf16[192,2176]{1,0:T(8,128)(2,1)} %get-tuple-element.16), channel_id=1, source_target_pairs={{0,1},{1,0},{2,3},{3,2},{4,5},{5,4},{6,7},{7,6},{8,9},{9,8},{10,11... | collective-permute-start | bytes 2506760 | tf_op jit(solution)/shard_map/ppermute | solution.py:65
  53.5 5.2 %collective-permute-start.14 = (bf16[320,2176]{1,0:T(8,128)(2,1)S(1)}, bf16[320,2176]{1,0:T(8,128)(2,1)S(1)}, u32[]{:S(2)}, u32[]{:S(2)}) collective-permute-start(bf16[320,2176]{1,0:T(8,128)(2,1)S(1)} %get-tuple-element.11), channel_id=1, source_target_pairs={{0,1},{1,0},{2,3},{3,2},{4,5},{5,4},{6,7},{7,6},{8,9},{9,8},{10,11... | collective-permute-start | bytes 4177928 | tf_op jit(solution)/shard_map/ppermute | solution.py:65
  58.2 7.9 %collective-permute-start.5 = (bf16[192,2048]{1,0:T(8,128)(2,1)S(1)}, bf16[192,2048]{1,0:T(8,128)(2,1)S(1)}, u32[]{:S(2)}, u32[]{:S(2)}) collective-permute-start(bf16[192,2048]{1,0:T(8,128)(2,1)S(1)} %split.113), channel_id=1, source_target_pairs={{0,1},{1,0},{2,3},{3,2},{4,5},{5,4},{6,7},{7,6},{8,9},{9,8},{10,11... | collective-permute-start | bytes 2359304 | tf_op jit(solution)/shard_map/ppermute | solution.py:74
  66.0 3.1 %collective-permute-start.15 = (bf16[320,2048]{1,0:T(8,128)(2,1)S(1)}, bf16[320,2048]{1,0:T(8,128)(2,1)S(1)}, u32[]{:S(2)}, u32[]{:S(2)}) collective-permute-start(bf16[320,2048]{1,0:T(8,128)(2,1)S(1)} %split.112), channel_id=1, source_target_pairs={{0,1},{1,0},{2,3},{3,2},{4,5},{5,4},{6,7},{7,6},{8,9},{9,8},{10,11... | collective-permute-start | bytes 3932168 | tf_op jit(solution)/shard_map/ppermute | solution.py:74
  66.4 12.1 %collective-permute-start.6 = (bf16[96,2048]{1,0:T(8,128)(2,1)S(1)}, bf16[96,2048]{1,0:T(8,128)(2,1)S(1)}, u32[]{:S(2)}, u32[]{:S(2)}) collective-permute-start(bf16[96,2048]{1,0:T(8,128)(2,1)S(1)} %split.115), channel_id=1, source_target_pairs={{0,2},{2,0},{1,3},{3,1},{4,6},{6,4},{5,7},{7,5},{8,10},{10,8},{9,1... | collective-permute-start | bytes 1179656 | tf_op jit(solution)/shard_map/ppermute | solution.py:74
  69.5 22.4 %collective-permute-start.16 = (bf16[160,2048]{1,0:T(8,128)(2,1)S(1)}, bf16[160,2048]{1,0:T(8,128)(2,1)S(1)}, u32[]{:S(2)}, u32[]{:S(2)}) collective-permute-start(bf16[160,2048]{1,0:T(8,128)(2,1)S(1)} %split.114), channel_id=1, source_target_pairs={{0,2},{2,0},{1,3},{3,1},{4,6},{6,4},{5,7},{7,5},{8,10},{10,8},{9,1... | collective-permute-start | bytes 1966088 | tf_op jit(solution)/shard_map/ppermute | solution.py:74
  78.6 19.5 %collective-permute-start.7 = (bf16[24,2048]{1,0:T(8,128)(2,1)S(1)}, bf16[24,2048]{1,0:T(8,128)(2,1)S(1)}, u32[]{:S(2)}, u32[]{:S(2)}) collective-permute-start(bf16[24,2048]{1,0:T(8,128)(2,1)S(1)} %get-tuple-element.18), channel_id=1, source_target_pairs={{0,12},{4,0},{8,4},{12,8},{1,13},{5,1},{9,5},{13,9},{2,14},{6,2},{... | collective-permute-start | bytes 294920 | tf_op jit(solution)/shard_map/ppermute | solution.py:74
  83.0 15.1 %collective-permute-start.8 = (bf16[24,2048]{1,0:T(8,128)(2,1)S(1)}, bf16[24,2048]{1,0:T(8,128)(2,1)S(1)}, u32[]{:S(2)}, u32[]{:S(2)}) collective-permute-start(bf16[24,2048]{1,0:T(8,128)(2,1)S(1)} %get-tuple-element.20), channel_id=1, source_target_pairs={{0,8},{4,12},{8,0},{12,4},{1,9},{5,13},{9,1},{13,5},{2,10},{6,14},... | collective-permute-start | bytes 294920 | tf_op jit(solution)/shard_map/ppermute | solution.py:74
  84.4 13.7 %collective-permute-start.9 = (bf16[24,2048]{1,0:T(8,128)(2,1)S(1)}, bf16[24,2048]{1,0:T(8,128)(2,1)S(1)}, u32[]{:S(2)}, u32[]{:S(2)}) collective-permute-start(bf16[24,2048]{1,0:T(8,128)(2,1)S(1)} %get-tuple-element.19), channel_id=1, source_target_pairs={{0,4},{4,8},{8,12},{12,0},{1,5},{5,9},{9,13},{13,1},{2,6},{6,10},{... | collective-permute-start | bytes 294920 | tf_op jit(solution)/shard_map/ppermute | solution.py:74
  92.2 9.1 %collective-permute-start.17 = (bf16[40,2048]{1,0:T(8,128)(2,1)S(1)}, bf16[40,2048]{1,0:T(8,128)(2,1)S(1)}, u32[]{:S(2)}, u32[]{:S(2)}) collective-permute-start(bf16[40,2048]{1,0:T(8,128)(2,1)S(1)} %get-tuple-element.13), channel_id=1, source_target_pairs={{0,12},{4,0},{8,4},{12,8},{1,13},{5,1},{9,5},{13,9},{2,14},{6,2},{... | collective-permute-start | bytes 491528 | tf_op jit(solution)/shard_map/ppermute | solution.py:74
  96.6 15.6 %collective-permute-start.18 = (bf16[40,2048]{1,0:T(8,128)(2,1)S(1)}, bf16[40,2048]{1,0:T(8,128)(2,1)S(1)}, u32[]{:S(2)}, u32[]{:S(2)}) collective-permute-start(bf16[40,2048]{1,0:T(8,128)(2,1)S(1)} %get-tuple-element.15), channel_id=1, source_target_pairs={{0,8},{4,12},{8,0},{12,4},{1,9},{5,13},{9,1},{13,5},{2,10},{6,14},... | collective-permute-start | bytes 491528 | tf_op jit(solution)/shard_map/ppermute | solution.py:74
  98.0 14.2 %collective-permute-start.19 = (bf16[40,2048]{1,0:T(8,128)(2,1)S(1)}, bf16[40,2048]{1,0:T(8,128)(2,1)S(1)}, u32[]{:S(2)}, u32[]{:S(2)}) collective-permute-start(bf16[40,2048]{1,0:T(8,128)(2,1)S(1)} %get-tuple-element.14), channel_id=1, source_target_pairs={{0,4},{4,8},{8,12},{12,0},{1,5},{5,9},{9,13},{13,1},{2,6},{6,10},{... | collective-permute-start | bytes 491528 | tf_op jit(solution)/shard_map/ppermute | solution.py:74

commit v20 on v5

--- a/solution.py
+++ b/solution.py
@@ -109,6 +109,8 @@
         out = expert_block(rows[:, :width_model], w_in[0], w_down[0], hidden_width)
         part = out.astype(jnp.float32) * mine[:, None]
         for axis, size in list(zip(AXES, sizes))[::-1]:
+            if axis == AXES[0] and results:
+                _, part = lax.optimization_barrier((results[-1], part))
             part = scatter_stage(part, axis, size)
         results.append(part)
     return jnp.concatenate(results, axis=0).astype(jnp.bfloat16)

time: 106 us -> 110 us (1.038)
  waiting for transfers between devices: 48.5 us -> 56.8 us
  starting transfers between devices: 29.1 us -> 25.1 us
    ppermute x10, waiting for transfers between devices: 25 us -> 33.3 us  [scatter_stage(): lax.ppermute(pieces[shift].astype(jnp.bfloat16), axis, pairs)]
    ppermute x10, starting transfers between devices: 13.9 us -> 10.1 us  [scatter_stage(): lax.ppermute(pieces[shift].astype(jnp.bfloat16), axis, pairs)]
    unnamed x13 -> x14, local copies, waits for them, and re-layouts: 5 us -> 6.76 us
    split x1 -> x0, local copies, waits for them, and re-layouts: 1.74 us -> none  [dense_shards(): jnp.split(carried, STREAMS, axis=0)]
  transfers between devices with their start and end apart: 20 -> 20, of which waited for: 10 -> 11; matrix products, arithmetic and copies ran while one was open for 12% -> 12% of each run, Pallas kernels for 0% -> 0%
where the time goes in v20:
time: 110 us
  waiting for transfers between devices  56.8 us (52%)
  starting transfers between devices  25.1 us (23%)
  local copies, waits for them, and re-layouts  10.8 us (10%)
  matrix products  10.6 us (10%)
  other arithmetic  6.15 us (6%)
    ppermute x10, waiting for transfers between devices, scatter_stage(): lax.ppermute(pieces[shift].astype(jnp.bfloat16), axis, pairs)  33.3 us
    ppermute x10, waiting for transfers between devices, gather_stage(): got.append(lax.ppermute(block, axis, pairs))  23.5 us
    ppermute x10, starting transfers between devices, gather_stage(): got.append(lax.ppermute(block, axis, pairs))  15 us
    ppermute x10, starting transfers between devices, scatter_stage(): lax.ppermute(pieces[shift].astype(jnp.bfloat16), axis, pairs)  10.1 us
    dot_general x2, matrix products, expert_block(): pair = jnp.dot(rows_in, gate_up, preferred_element_type=jnp.float32)  6.9 us
    unnamed x14, local copies, waits for them, and re-layouts  6.76 us
    dot_general x2, matrix products, expert_block(): jnp.dot(active, down_proj, preferred_element_type=jnp.float32)  3.69 us
  transfers between devices with their start and end apart: 20, of which 11 were waited for; matrix products, arithmetic and copies ran while one was open for 12% of the time, Pallas kernels for 0%

profile of v20, /device:TPU:0, one launch (start us, length us, event | category | flops | bytes accessed | tf_op | source)
XLA Modules:
  0.0 109.7 jit_solution(11126602165495423446)
XLA Ops:
  0.0 0.9 reduce_sum.36
  0.9 0.8 broadcast_divide_fusion
  1.7 0.8 select_reduce_fusion
  2.8 1.7 %concatenate.32 = bf16[64,2176]{1,0:T(8,128)(2,1)} concatenate(bf16[64,2048]{1,0:T(8,128)(2,1)} %param.6, bf16[64,16]{1,0:T(8,128)(2,1)S(1)} %copy.9, bf16[64,16]{1,0:T(8,128)(2,1)S(1)} %copy.10, bf16[64,16]{1,0:T(8,128)(2,1)S(1)} %copy.11, bf16[64,80]{1,0:T(8,128)(2,1)S(1)} %broadcast_in_dim.16), dimensions={1} | concatenate | bytes 557056 | tf_op jit(solution)/shard_map/concatenate | solution.py:95
  4.5 1.7 %constant_dynamic-update-slice_fusion.4 = (bf16[256,2176]{1,0:T(8,128)(2,1)}, bf16[512,2176]{1,0:T(8,128)(2,1)}, bf16[32,2176]{1,0:T(8,128)(2,1)S(1)}, bf16[32,2176]{1,0:T(8,128)(2,1)S(1)}) fusion(bf16[64,2176]{1,0:T(8,128)(2,1)} %concatenate.32), kind=kLoop, calls=%fused_computation.50 | loop fusion | bytes 835584
  6.2 3.1 %collective-permute-start = (bf16[32,2176]{1,0:T(8,128)(2,1)S(1)}, bf16[32,2176]{1,0:T(8,128)(2,1)}, u32[]{:S(2)}, u32[]{:S(2)}) collective-permute-start(bf16[32,2176]{1,0:T(8,128)(2,1)S(1)} %get-tuple-element.26), channel_id=1, source_target_pairs={{0,4},{4,8},{8,12},{12,0},{1,5},{5,9},{9,13},{13,1},{2,6},{6,10},{... | collective-permute-start | bytes 417800 | tf_op jit(solution)/shard_map/ppermute | solution.py:65
  9.3 2.6 %collective-permute-start.1 = (bf16[32,2176]{1,0:T(8,128)(2,1)S(1)}, bf16[32,2176]{1,0:T(8,128)(2,1)}, u32[]{:S(2)}, u32[]{:S(2)}) collective-permute-start(bf16[32,2176]{1,0:T(8,128)(2,1)S(1)} %get-tuple-element.26), channel_id=1, source_target_pairs={{0,8},{4,12},{8,0},{12,4},{1,9},{5,13},{9,1},{13,5},{2,10},{6,14},... | collective-permute-start | bytes 417800 | tf_op jit(solution)/shard_map/ppermute | solution.py:65
  11.9 1.3 %collective-permute-start.2 = (bf16[32,2176]{1,0:T(8,128)(2,1)S(1)}, bf16[32,2176]{1,0:T(8,128)(2,1)}, u32[]{:S(2)}, u32[]{:S(2)}) collective-permute-start(bf16[32,2176]{1,0:T(8,128)(2,1)S(1)} %get-tuple-element.26), channel_id=1, source_target_pairs={{0,12},{4,0},{8,4},{12,8},{1,13},{5,1},{9,5},{13,9},{2,14},{6,2},{... | collective-permute-start | bytes 417800 | tf_op jit(solution)/shard_map/ppermute | solution.py:65
  13.2 2.8 %collective-permute-done = bf16[32,2176]{1,0:T(8,128)(2,1)} collective-permute-done((bf16[32,2176]{1,0:T(8,128)(2,1)S(1)}, bf16[32,2176]{1,0:T(8,128)(2,1)}, u32[]{:S(2)}, u32[]{:S(2)}) %collective-permute-start) | collective-permute-done | bytes 139296 | tf_op jit(solution)/shard_map/ppermute | solution.py:65
  16.0 5.1 %collective-permute-done.1 = bf16[32,2176]{1,0:T(8,128)(2,1)} collective-permute-done((bf16[32,2176]{1,0:T(8,128)(2,1)S(1)}, bf16[32,2176]{1,0:T(8,128)(2,1)}, u32[]{:S(2)}, u32[]{:S(2)}) %collective-permute-start.1) | collective-permute-done | bytes 139296 | tf_op jit(solution)/shard_map/ppermute | solution.py:65
  21.1 1.2 %pad_maximum_fusion = bf16[128,2176]{1,0:T(8,128)(2,1)S(1)} fusion(bf16[32,2176]{1,0:T(8,128)(2,1)} %collective-permute-done.2, bf16[32,2176]{1,0:T(8,128)(2,1)} %collective-permute-done.1, bf16[32,2176]{1,0:T(8,128)(2,1)} %collective-permute-done, bf16[32,2176]{1,0:T(8,128)(2,1)S(1)} %get-tuple-element.26), kind=kLoop, calls=%fused_computation.28 | loop fusion | flops 2228224 | bytes 1114112 | tf_op jit(solution)/shard_map/concatenate | solution.py:66
  22.4 1.6 %collective-permute-start.3 = (bf16[128,2176]{1,0:T(8,128)(2,1)S(1)}, bf16[128,2176]{1,0:T(8,128)(2,1)S(1)}, u32[]{:S(2)}, u32[]{:S(2)}) collective-permute-start(bf16[128,2176]{1,0:T(8,128)(2,1)S(1)} %pad_maximum_fusion), channel_id=1, source_target_pairs={{0,2},{2,0},{1,3},{3,1},{4,6},{6,4},{5,7},{7,5},{8,10},{10,8},{9,1... | collective-permute-start | bytes 1671176 | tf_op jit(solution)/shard_map/ppermute | solution.py:65
  23.9 3.5 %collective-permute-start.10 = (bf16[32,2176]{1,0:T(8,128)(2,1)S(1)}, bf16[32,2176]{1,0:T(8,128)(2,1)S(1)}, u32[]{:S(2)}, u32[]{:S(2)}) collective-permute-start(bf16[32,2176]{1,0:T(8,128)(2,1)S(1)} %get-tuple-element.7), channel_id=1, source_target_pairs={{0,4},{4,8},{8,12},{12,0},{1,5},{5,9},{9,13},{13,1},{2,6},{6,10},{... | collective-permute-start | bytes 417800 | tf_op jit(solution)/shard_map/ppermute | solution.py:65
  27.4 1.6 %collective-permute-start.11 = (bf16[32,2176]{1,0:T(8,128)(2,1)S(1)}, bf16[32,2176]{1,0:T(8,128)(2,1)S(1)}, u32[]{:S(2)}, u32[]{:S(2)}) collective-permute-start(bf16[32,2176]{1,0:T(8,128)(2,1)S(1)} %get-tuple-element.7), channel_id=1, source_target_pairs={{0,8},{4,12},{8,0},{12,4},{1,9},{5,13},{9,1},{13,5},{2,10},{6,14},... | collective-permute-start | bytes 417800 | tf_op jit(solution)/shard_map/ppermute | solution.py:65
  29.0 0.7 collective-permute-start.12
  29.8 1.7 %constant_dynamic-update-slice_fusion.3 = (bf16[256,2176]{1,0:T(8,128)(2,1)}, bf16[512,2176]{1,0:T(8,128)(2,1)}) fusion(bf16[256,2176]{1,0:T(8,128)(2,1)} %get-tuple-element.23, bf16[32,2176]{1,0:T(8,128)(2,1)} %collective-permute-done, bf16[512,2176]{1,0:T(8,128)(2,1)} %get-tuple-element.24), kind=kLoop, calls=%fused_computation.49 | loop fusion | bytes 417792
  31.4 1.6 %constant_dynamic-update-slice_fusion.2 = (bf16[256,2176]{1,0:T(8,128)(2,1)}, bf16[512,2176]{1,0:T(8,128)(2,1)}) fusion(bf16[256,2176]{1,0:T(8,128)(2,1)} %get-tuple-element.31, bf16[32,2176]{1,0:T(8,128)(2,1)} %collective-permute-done.1, bf16[512,2176]{1,0:T(8,128)(2,1)} %get-tuple-element.32), kind=kLoop, calls=%fused_computation.48 | loop fusion | bytes 417792
  33.1 1.6 %constant_dynamic-update-slice_fusion.1 = (bf16[256,2176]{1,0:T(8,128)(2,1)}, bf16[512,2176]{1,0:T(8,128)(2,1)}) fusion(bf16[256,2176]{1,0:T(8,128)(2,1)} %get-tuple-element.29, bf16[32,2176]{1,0:T(8,128)(2,1)} %collective-permute-done.2, bf16[512,2176]{1,0:T(8,128)(2,1)} %get-tuple-element.30), kind=kLoop, calls=%fused_computation.47 | loop fusion | bytes 417792
  34.7 2.8 %collective-permute-done.11 = bf16[32,2176]{1,0:T(8,128)(2,1)S(1)} collective-permute-done((bf16[32,2176]{1,0:T(8,128)(2,1)S(1)}, bf16[32,2176]{1,0:T(8,128)(2,1)S(1)}, u32[]{:S(2)}, u32[]{:S(2)}) %collective-permute-start.11) | collective-permute-done | bytes 139296 | tf_op jit(solution)/shard_map/ppermute | solution.py:65
  37.6 0.6 collective-permute-start.13
  38.2 1.1 constant_dynamic-update-slice_fusion
  39.4 12.7 %collective-permute-done.13 = bf16[128,2176]{1,0:T(8,128)(2,1)S(1)} collective-permute-done((bf16[128,2176]{1,0:T(8,128)(2,1)S(1)}, bf16[128,2176]{1,0:T(8,128)(2,1)S(1)}, u32[]{:S(2)}, u32[]{:S(2)}) %collective-permute-start.13) | collective-permute-done | bytes 557088 | tf_op jit(solution)/shard_map/ppermute | solution.py:65
  52.3 0.1 constant_dynamic-update-slice_fusion.5
  52.5 3.4 %fusion.2 = f32[512,1536]{1,0:T(8,128)S(1)} fusion(bf16[1,2048,1536]{2,1,0:T(8,128)(2,1)S(1)} %copy-done.2, bf16[512,2176]{1,0:T(8,128)(2,1)S(1)} %constant_dynamic-update-slice_fusion.5), kind=kOutput, calls=%fused_computation.2 | convolution fusion | flops 3221225472 | bytes 11534336 | tf_op jit(solution)/shard_map/dot_general | solution.py:9
  56.0 0.1 constant_dynamic-update-slice_fusion.16
  56.2 3.4 %fusion = f32[512,1536]{1,0:T(8,128)S(1)} fusion(bf16[1,2048,1536]{2,1,0:T(8,128)(2,1)S(1)} %copy-done.2, bf16[512,2176]{1,0:T(8,128)(2,1)S(1)} %constant_dynamic-update-slice_fusion.16), kind=kOutput, calls=%fused_computation | convolution fusion | flops 3221225472 | bytes 11534336 | tf_op jit(solution)/shard_map/dot_general | solution.py:9
  59.6 0.5 fusion.27
  60.2 1.8 %convert_multiply_fusion.1 = f32[512,2048]{1,0:T(8,128)S(1)} fusion(bf16[1,768,2048]{2,1,0:T(8,128)(2,1)S(1)} %copy-done, f32[512]{0:T(512)S(1)} %get-tuple-element.10, f32[512,1536]{1,0:T(8,128)S(1)} %fusion.2), kind=kOutput, calls=%fused_computation.5 | convolution fusion | flops 1616117760 | bytes 10487808 | tf_op jit(solution)/shard_map/dot_general | solution.py:11
  62.2 0.5 collective-permute-start.5
  62.7 1.8 %convert_multiply_fusion = f32[512,2048]{1,0:T(8,128)S(1)} fusion(bf16[1,768,2048]{2,1,0:T(8,128)(2,1)S(1)} %copy-done, f32[512]{0:T(512)S(1)} %get-tuple-element.9, f32[512,1536]{1,0:T(8,128)S(1)} %fusion), kind=kOutput, calls=%fused_computation.4 | convolution fusion | flops 1616117760 | bytes 10487808 | tf_op jit(solution)/shard_map/dot_general | solution.py:11
  64.8 0.2 collective-permute-done.5
  65.0 0.3 slice_add_fusion.1
  65.4 0.6 collective-permute-start.6
  66.0 1.4 %collective-permute-done.15 = bf16[256,2048]{1,0:T(8,128)(2,1)S(1)} collective-permute-done((bf16[256,2048]{1,0:T(8,128)(2,1)S(1)}, bf16[256,2048]{1,0:T(8,128)(2,1)S(1)}, u32[]{:S(2)}, u32[]{:S(2)}) %collective-permute-start.15) | collective-permute-done | bytes 1048608 | tf_op jit(solution)/shard_map/ppermute | solution.py:74
  67.4 0.3 slice_add_fusion
  67.9 0.6 collective-permute-start.16
  68.5 11.8 %collective-permute-done.6 = bf16[128,2048]{1,0:T(8,128)(2,1)S(1)} collective-permute-done((bf16[128,2048]{1,0:T(8,128)(2,1)S(1)}, bf16[128,2048]{1,0:T(8,128)(2,1)S(1)}, u32[]{:S(2)}, u32[]{:S(2)}) %collective-permute-start.6) | collective-permute-done | bytes 524320 | tf_op jit(solution)/shard_map/ppermute | solution.py:74
  80.3 0.1 fusion.35
  80.5 4.0 %collective-permute-start.7 = (bf16[32,2048]{1,0:T(8,128)(2,1)S(1)}, bf16[32,2048]{1,0:T(8,128)(2,1)S(1)}, u32[]{:S(2)}, u32[]{:S(2)}) collective-permute-start(bf16[32,2048]{1,0:T(8,128)(2,1)S(1)} %get-tuple-element.20), channel_id=1, source_target_pairs={{0,12},{4,0},{8,4},{12,8},{1,13},{5,1},{9,5},{13,9},{2,14},{6,2},{... | collective-permute-start | bytes 393224 | tf_op jit(solution)/shard_map/ppermute | solution.py:74
  84.5 1.1 collective-permute-start.8
  85.6 5.4 %collective-permute-done.16 = bf16[128,2048]{1,0:T(8,128)(2,1)S(1)} collective-permute-done((bf16[128,2048]{1,0:T(8,128)(2,1)S(1)}, bf16[128,2048]{1,0:T(8,128)(2,1)S(1)}, u32[]{:S(2)}, u32[]{:S(2)}) %collective-permute-start.16) | collective-permute-done | bytes 524320 | tf_op jit(solution)/shard_map/ppermute | solution.py:74
  91.1 5.2 %collective-permute-done.8 = bf16[32,2048]{1,0:T(8,128)(2,1)S(1)} collective-permute-done((bf16[32,2048]{1,0:T(8,128)(2,1)S(1)}, bf16[32,2048]{1,0:T(8,128)(2,1)S(1)}, u32[]{:S(2)}, u32[]{:S(2)}) %collective-permute-start.8) | collective-permute-done | bytes 131104 | tf_op jit(solution)/shard_map/ppermute | solution.py:74
  96.5 0.2 collective-permute-start.17
  96.6 1.1 collective-permute-start.18
  97.7 1.9 %collective-permute-start.19 = (bf16[32,2048]{1,0:T(8,128)(2,1)S(1)}, bf16[32,2048]{1,0:T(8,128)(2,1)S(1)}, u32[]{:S(2)}, u32[]{:S(2)}) collective-permute-start(bf16[32,2048]{1,0:T(8,128)(2,1)S(1)} %get-tuple-element.18), channel_id=1, source_target_pairs={{0,4},{4,8},{8,12},{12,0},{1,5},{5,9},{9,13},{13,1},{2,6},{6,10},{... | collective-permute-start | bytes 393224 | tf_op jit(solution)/shard_map/ppermute | solution.py:74
  99.6 2.2 %collective-permute-done.17 = bf16[32,2048]{1,0:T(8,128)(2,1)S(1)} collective-permute-done((bf16[32,2048]{1,0:T(8,128)(2,1)S(1)}, bf16[32,2048]{1,0:T(8,128)(2,1)S(1)}, u32[]{:S(2)}, u32[]{:S(2)}) %collective-permute-start.17) | collective-permute-done | bytes 131104 | tf_op jit(solution)/shard_map/ppermute | solution.py:74
  101.9 7.0 %collective-permute-done.18 = bf16[32,2048]{1,0:T(8,128)(2,1)S(1)} collective-permute-done((bf16[32,2048]{1,0:T(8,128)(2,1)S(1)}, bf16[32,2048]{1,0:T(8,128)(2,1)S(1)}, u32[]{:S(2)}, u32[]{:S(2)}) %collective-permute-start.18) | collective-permute-done | bytes 131104 | tf_op jit(solution)/shard_map/ppermute | solution.py:74
  108.9 0.7 pad_maximum_fusion.2
  (43 shorter events, 1.6 us)
Async XLA Ops:
  0.0 60.2 %copy-start = (bf16[1,768,2048]{2,1,0:T(8,128)(2,1)S(1)}, bf16[1,768,2048]{2,1,0:T(8,128)(2,1)}, u32[]{:S(2)}) copy-start(bf16[1,768,2048]{2,1,0:T(8,128)(2,1)} %param.11) | copy-start | bytes 9437188
  6.2 9.8 %collective-permute-start = (bf16[32,2176]{1,0:T(8,128)(2,1)S(1)}, bf16[32,2176]{1,0:T(8,128)(2,1)}, u32[]{:S(2)}, u32[]{:S(2)}) collective-permute-start(bf16[32,2176]{1,0:T(8,128)(2,1)S(1)} %get-tuple-element.26), channel_id=1, source_target_pairs={{0,4},{4,8},{8,12},{12,0},{1,5},{5,9},{9,13},{13,1},{2,6},{6,10},{... | collective-permute-start | bytes 417800 | tf_op jit(solution)/shard_map/ppermute | solution.py:65
  9.3 11.9 %collective-permute-start.1 = (bf16[32,2176]{1,0:T(8,128)(2,1)S(1)}, bf16[32,2176]{1,0:T(8,128)(2,1)}, u32[]{:S(2)}, u32[]{:S(2)}) collective-permute-start(bf16[32,2176]{1,0:T(8,128)(2,1)S(1)} %get-tuple-element.26), channel_id=1, source_target_pairs={{0,8},{4,12},{8,0},{12,4},{1,9},{5,13},{9,1},{13,5},{2,10},{6,14},... | collective-permute-start | bytes 417800 | tf_op jit(solution)/shard_map/ppermute | solution.py:65
  11.9 9.3 %collective-permute-start.2 = (bf16[32,2176]{1,0:T(8,128)(2,1)S(1)}, bf16[32,2176]{1,0:T(8,128)(2,1)}, u32[]{:S(2)}, u32[]{:S(2)}) collective-permute-start(bf16[32,2176]{1,0:T(8,128)(2,1)S(1)} %get-tuple-element.26), channel_id=1, source_target_pairs={{0,12},{4,0},{8,4},{12,8},{1,13},{5,1},{9,5},{13,9},{2,14},{6,2},{... | collective-permute-start | bytes 417800 | tf_op jit(solution)/shard_map/ppermute | solution.py:65
  21.1 31.4 %copy-start.2 = (bf16[1,2048,1536]{2,1,0:T(8,128)(2,1)S(1)}, bf16[1,2048,1536]{2,1,0:T(8,128)(2,1)}, u32[]{:S(2)}) copy-start(bf16[1,2048,1536]{2,1,0:T(8,128)(2,1)} %param.10) | copy-start | bytes 18874372
  22.4 15.8 %collective-permute-start.3 = (bf16[128,2176]{1,0:T(8,128)(2,1)S(1)}, bf16[128,2176]{1,0:T(8,128)(2,1)S(1)}, u32[]{:S(2)}, u32[]{:S(2)}) collective-permute-start(bf16[128,2176]{1,0:T(8,128)(2,1)S(1)} %pad_maximum_fusion), channel_id=1, source_target_pairs={{0,2},{2,0},{1,3},{3,1},{4,6},{6,4},{5,7},{7,5},{8,10},{10,8},{9,1... | collective-permute-start | bytes 1671176 | tf_op jit(solution)/shard_map/ppermute | solution.py:65
  23.9 10.8 %collective-permute-start.10 = (bf16[32,2176]{1,0:T(8,128)(2,1)S(1)}, bf16[32,2176]{1,0:T(8,128)(2,1)S(1)}, u32[]{:S(2)}, u32[]{:S(2)}) collective-permute-start(bf16[32,2176]{1,0:T(8,128)(2,1)S(1)} %get-tuple-element.7), channel_id=1, source_target_pairs={{0,4},{4,8},{8,12},{12,0},{1,5},{5,9},{9,13},{13,1},{2,6},{6,10},{... | collective-permute-start | bytes 417800 | tf_op jit(solution)/shard_map/ppermute | solution.py:65
  27.4 10.2 %collective-permute-start.11 = (bf16[32,2176]{1,0:T(8,128)(2,1)S(1)}, bf16[32,2176]{1,0:T(8,128)(2,1)S(1)}, u32[]{:S(2)}, u32[]{:S(2)}) collective-permute-start(bf16[32,2176]{1,0:T(8,128)(2,1)S(1)} %get-tuple-element.7), channel_id=1, source_target_pairs={{0,8},{4,12},{8,0},{12,4},{1,9},{5,13},{9,1},{13,5},{2,10},{6,14},... | collective-permute-start | bytes 417800 | tf_op jit(solution)/shard_map/ppermute | solution.py:65
  29.0 8.5 %collective-permute-start.12 = (bf16[32,2176]{1,0:T(8,128)(2,1)S(1)}, bf16[32,2176]{1,0:T(8,128)(2,1)S(1)}, u32[]{:S(2)}, u32[]{:S(2)}) collective-permute-start(bf16[32,2176]{1,0:T(8,128)(2,1)S(1)} %get-tuple-element.7), channel_id=1, source_target_pairs={{0,12},{4,0},{8,4},{12,8},{1,13},{5,1},{9,5},{13,9},{2,14},{6,2},{... | collective-permute-start | bytes 417800 | tf_op jit(solution)/shard_map/ppermute | solution.py:65
  37.6 14.5 %collective-permute-start.13 = (bf16[128,2176]{1,0:T(8,128)(2,1)S(1)}, bf16[128,2176]{1,0:T(8,128)(2,1)S(1)}, u32[]{:S(2)}, u32[]{:S(2)}) collective-permute-start(bf16[128,2176]{1,0:T(8,128)(2,1)S(1)} %pad_maximum_fusion.1), channel_id=1, source_target_pairs={{0,2},{2,0},{1,3},{3,1},{4,6},{6,4},{5,7},{7,5},{8,10},{10,8},{9,1... | collective-permute-start | bytes 1671176 | tf_op jit(solution)/shard_map/ppermute | solution.py:65
  39.3 13.1 %copy-start.1 = (bf16[512,2176]{1,0:T(8,128)(2,1)S(1)}, bf16[512,2176]{1,0:T(8,128)(2,1)}, u32[]{:S(2)}) copy-start(bf16[512,2176]{1,0:T(8,128)(2,1)} %get-tuple-element.14) | copy-start | bytes 6684676
  39.3 13.1 %collective-permute-start.4 = (bf16[256,2176]{1,0:T(8,128)(2,1)}, bf16[256,2176]{1,0:T(8,128)(2,1)S(1)}, u32[]{:S(2)}, u32[]{:S(2)}) collective-permute-start(bf16[256,2176]{1,0:T(8,128)(2,1)} %get-tuple-element.13), channel_id=1, source_target_pairs={{0,1},{1,0},{2,3},{3,2},{4,5},{5,4},{6,7},{7,6},{8,9},{9,8},{10,11... | collective-permute-start | bytes 3342344 | tf_op jit(solution)/shard_map/ppermute | solution.py:65
  52.2 3.7 %collective-permute-start.14 = (bf16[256,2176]{1,0:T(8,128)(2,1)S(1)}, bf16[256,2176]{1,0:T(8,128)(2,1)S(1)}, u32[]{:S(2)}, u32[]{:S(2)}) collective-permute-start(bf16[256,2176]{1,0:T(8,128)(2,1)S(1)} %get-tuple-element.15), channel_id=1, source_target_pairs={{0,1},{1,0},{2,3},{3,2},{4,5},{5,4},{6,7},{7,6},{8,9},{9,8},{10,11... | collective-permute-start | bytes 3342344 | tf_op jit(solution)/shard_map/ppermute | solution.py:65
  62.2 2.8 %collective-permute-start.5 = (bf16[256,2048]{1,0:T(8,128)(2,1)S(1)}, bf16[256,2048]{1,0:T(8,128)(2,1)S(1)}, u32[]{:S(2)}, u32[]{:S(2)}) collective-permute-start(bf16[256,2048]{1,0:T(8,128)(2,1)S(1)} %split.116), channel_id=1, source_target_pairs={{0,1},{1,0},{2,3},{3,2},{4,5},{5,4},{6,7},{7,6},{8,9},{9,8},{10,11... | collective-permute-start | bytes 3145736 | tf_op jit(solution)/shard_map/ppermute | solution.py:74
  64.7 2.7 %collective-permute-start.15 = (bf16[256,2048]{1,0:T(8,128)(2,1)S(1)}, bf16[256,2048]{1,0:T(8,128)(2,1)S(1)}, u32[]{:S(2)}, u32[]{:S(2)}) collective-permute-start(bf16[256,2048]{1,0:T(8,128)(2,1)S(1)} %split.115), channel_id=1, source_target_pairs={{0,1},{1,0},{2,3},{3,2},{4,5},{5,4},{6,7},{7,6},{8,9},{9,8},{10,11... | collective-permute-start | bytes 3145736 | tf_op jit(solution)/shard_map/ppermute | solution.py:74
  65.4 14.9 %collective-permute-start.6 = (bf16[128,2048]{1,0:T(8,128)(2,1)S(1)}, bf16[128,2048]{1,0:T(8,128)(2,1)S(1)}, u32[]{:S(2)}, u32[]{:S(2)}) collective-permute-start(bf16[128,2048]{1,0:T(8,128)(2,1)S(1)} %split.118), channel_id=1, source_target_pairs={{0,2},{2,0},{1,3},{3,1},{4,6},{6,4},{5,7},{7,5},{8,10},{10,8},{9,1... | collective-permute-start | bytes 1572872 | tf_op jit(solution)/shard_map/ppermute | solution.py:74
  67.9 23.1 %collective-permute-start.16 = (bf16[128,2048]{1,0:T(8,128)(2,1)S(1)}, bf16[128,2048]{1,0:T(8,128)(2,1)S(1)}, u32[]{:S(2)}, u32[]{:S(2)}) collective-permute-start(bf16[128,2048]{1,0:T(8,128)(2,1)S(1)} %split.117), channel_id=1, source_target_pairs={{0,2},{2,0},{1,3},{3,1},{4,6},{6,4},{5,7},{7,5},{8,10},{10,8},{9,1... | collective-permute-start | bytes 1572872 | tf_op jit(solution)/shard_map/ppermute | solution.py:74
  80.5 10.6 %collective-permute-start.7 = (bf16[32,2048]{1,0:T(8,128)(2,1)S(1)}, bf16[32,2048]{1,0:T(8,128)(2,1)S(1)}, u32[]{:S(2)}, u32[]{:S(2)}) collective-permute-start(bf16[32,2048]{1,0:T(8,128)(2,1)S(1)} %get-tuple-element.20), channel_id=1, source_target_pairs={{0,12},{4,0},{8,4},{12,8},{1,13},{5,1},{9,5},{13,9},{2,14},{6,2},{... | collective-permute-start | bytes 393224 | tf_op jit(solution)/shard_map/ppermute | solution.py:74
  84.5 11.8 %collective-permute-start.8 = (bf16[32,2048]{1,0:T(8,128)(2,1)S(1)}, bf16[32,2048]{1,0:T(8,128)(2,1)S(1)}, u32[]{:S(2)}, u32[]{:S(2)}) collective-permute-start(bf16[32,2048]{1,0:T(8,128)(2,1)S(1)} %get-tuple-element.22), channel_id=1, source_target_pairs={{0,8},{4,12},{8,0},{12,4},{1,9},{5,13},{9,1},{13,5},{2,10},{6,14},... | collective-permute-start | bytes 393224 | tf_op jit(solution)/shard_map/ppermute | solution.py:74
  85.5 10.7 %collective-permute-start.9 = (bf16[32,2048]{1,0:T(8,128)(2,1)S(1)}, bf16[32,2048]{1,0:T(8,128)(2,1)S(1)}, u32[]{:S(2)}, u32[]{:S(2)}) collective-permute-start(bf16[32,2048]{1,0:T(8,128)(2,1)S(1)} %get-tuple-element.21), channel_id=1, source_target_pairs={{0,4},{4,8},{8,12},{12,0},{1,5},{5,9},{9,13},{13,1},{2,6},{6,10},{... | collective-permute-start | bytes 393224 | tf_op jit(solution)/shard_map/ppermute | solution.py:74
  96.5 5.4 %collective-permute-start.17 = (bf16[32,2048]{1,0:T(8,128)(2,1)S(1)}, bf16[32,2048]{1,0:T(8,128)(2,1)S(1)}, u32[]{:S(2)}, u32[]{:S(2)}) collective-permute-start(bf16[32,2048]{1,0:T(8,128)(2,1)S(1)} %get-tuple-element.17), channel_id=1, source_target_pairs={{0,12},{4,0},{8,4},{12,8},{1,13},{5,1},{9,5},{13,9},{2,14},{6,2},{... | collective-permute-start | bytes 393224 | tf_op jit(solution)/shard_map/ppermute | solution.py:74
  96.6 12.3 %collective-permute-start.18 = (bf16[32,2048]{1,0:T(8,128)(2,1)S(1)}, bf16[32,2048]{1,0:T(8,128)(2,1)S(1)}, u32[]{:S(2)}, u32[]{:S(2)}) collective-permute-start(bf16[32,2048]{1,0:T(8,128)(2,1)S(1)} %get-tuple-element.19), channel_id=1, source_target_pairs={{0,8},{4,12},{8,0},{12,4},{1,9},{5,13},{9,1},{13,5},{2,10},{6,14},... | collective-permute-start | bytes 393224 | tf_op jit(solution)/shard_map/ppermute | solution.py:74
  97.7 11.2 %collective-permute-start.19 = (bf16[32,2048]{1,0:T(8,128)(2,1)S(1)}, bf16[32,2048]{1,0:T(8,128)(2,1)S(1)}, u32[]{:S(2)}, u32[]{:S(2)}) collective-permute-start(bf16[32,2048]{1,0:T(8,128)(2,1)S(1)} %get-tuple-element.18), channel_id=1, source_target_pairs={{0,4},{4,8},{8,12},{12,0},{1,5},{5,9},{9,13},{13,1},{2,6},{6,10},{... | collective-permute-start | bytes 393224 | tf_op jit(solution)/shard_map/ppermute | solution.py:74

commit v21 on v5

--- a/solution.py
+++ b/solution.py
@@ -61,7 +61,7 @@
 def gather_stage(block, axis, size):
     got = [block]
     for shift in range(1, size):
-        pairs = [(i, (i + shift) % size) for i in range(size)]
+        pairs = [(i, i ^ shift if size & (size - 1) == 0 else (i + shift) % size) for i in range(size)]
         got.append(lax.ppermute(block, axis, pairs))
     return jnp.concatenate(got, axis=0)
 
@@ -70,7 +70,7 @@
     pieces = jnp.split(part, size, axis=0)
     total = pieces[0].astype(jnp.float32)
     for shift in range(1, size):
-        pairs = [(i, (i - shift) % size) for i in range(size)]
+        pairs = [(i, i ^ shift if size & (size - 1) == 0 else (i - shift) % size) for i in range(size)]
         total = total + lax.ppermute(pieces[shift].astype(jnp.bfloat16), axis, pairs).astype(jnp.float32)
     return total
 

time: 106 us -> 107 us (level)
  waiting for transfers between devices: 48.5 us -> 50.5 us
    ppermute x10, starting transfers between devices: 15.2 us -> 12.6 us  [gather_stage(): got.append(lax.ppermute(block, axis, pairs))]
    ppermute x10, starting transfers between devices: 13.9 us -> 16.2 us  [scatter_stage(): lax.ppermute(pieces[shift].astype(jnp.bfloat16), axis, pairs)]
where the time goes in v21:
time: 107 us
  waiting for transfers between devices  50.5 us (47%)
  starting transfers between devices  28.8 us (27%)
  local copies, waits for them, and re-layouts  10.8 us (10%)
  matrix products  10.6 us (10%)
  other arithmetic  6.12 us (6%)
    ppermute x10, waiting for transfers between devices, scatter_stage(): lax.ppermute(pieces[shift].astype(jnp.bfloat16), axis, pairs)  25.9 us
    ppermute x10, waiting for transfers between devices, gather_stage(): got.append(lax.ppermute(block, axis, pairs))  24.6 us
    ppermute x10, starting transfers between devices, scatter_stage(): lax.ppermute(pieces[shift].astype(jnp.bfloat16), axis, pairs)  16.2 us
    ppermute x10, starting transfers between devices, gather_stage(): got.append(lax.ppermute(block, axis, pairs))  12.6 us
    dot_general x2, matrix products, expert_block(): pair = jnp.dot(rows_in, gate_up, preferred_element_type=jnp.float32)  6.9 us
    unnamed x13, local copies, waits for them, and re-layouts  5 us
    dot_general x2, matrix products, expert_block(): jnp.dot(active, down_proj, preferred_element_type=jnp.float32)  3.69 us
  transfers between devices with their start and end apart: 20, of which 10 were waited for; matrix products, arithmetic and copies ran while one was open for 12% of the time, Pallas kernels for 0%

profile of v21, /device:TPU:0, one launch (start us, length us, event | category | flops | bytes accessed | tf_op | source)
XLA Modules:
  0.0 107.0 jit_solution(5693304090635001777)
XLA Ops:
  0.0 0.9 reduce_sum.36
  0.9 0.8 broadcast_divide_fusion
  1.7 0.8 select_reduce_fusion
  2.8 1.7 %concatenate.32 = bf16[64,2176]{1,0:T(8,128)(2,1)} concatenate(bf16[64,2048]{1,0:T(8,128)(2,1)} %param.6, bf16[64,16]{1,0:T(8,128)(2,1)S(1)} %copy.9, bf16[64,16]{1,0:T(8,128)(2,1)S(1)} %copy.10, bf16[64,16]{1,0:T(8,128)(2,1)S(1)} %copy.11, bf16[64,80]{1,0:T(8,128)(2,1)S(1)} %broadcast_in_dim.16), dimensions={1} | concatenate | bytes 557056 | tf_op jit(solution)/shard_map/concatenate | solution.py:95
  4.5 1.7 %fusion.43 = (bf16[32,2176]{1,0:T(8,128)(2,1)S(1)}, bf16[256,2176]{1,0:T(8,128)(2,1)}, bf16[512,2176]{1,0:T(8,128)(2,1)}, bf16[32,2176]{1,0:T(8,128)(2,1)S(1)}) fusion(bf16[64,2176]{1,0:T(8,128)(2,1)} %concatenate.32), kind=kLoop, calls=%fused_computation.85 | loop fusion | bytes 835584 | tf_op jit(solution)/shard_map/split | solution.py:99
  6.2 3.1 %collective-permute-start = (bf16[32,2176]{1,0:T(8,128)(2,1)S(1)}, bf16[32,2176]{1,0:T(8,128)(2,1)}, u32[]{:S(2)}, u32[]{:S(2)}) collective-permute-start(bf16[32,2176]{1,0:T(8,128)(2,1)S(1)} %get-tuple-element.26), channel_id=1, source_target_pairs={{0,4},{4,0},{8,12},{12,8},{1,5},{5,1},{9,13},{13,9},{2,6},{6,2},{1... | collective-permute-start | bytes 417800 | tf_op jit(solution)/shard_map/ppermute | solution.py:65
  9.3 2.6 %collective-permute-start.1 = (bf16[32,2176]{1,0:T(8,128)(2,1)S(1)}, bf16[32,2176]{1,0:T(8,128)(2,1)}, u32[]{:S(2)}, u32[]{:S(2)}) collective-permute-start(bf16[32,2176]{1,0:T(8,128)(2,1)S(1)} %get-tuple-element.26), channel_id=1, source_target_pairs={{0,8},{4,12},{8,0},{12,4},{1,9},{5,13},{9,1},{13,5},{2,10},{6,14},... | collective-permute-start | bytes 417800 | tf_op jit(solution)/shard_map/ppermute | solution.py:65
  11.9 3.0 %collective-permute-done = bf16[32,2176]{1,0:T(8,128)(2,1)} collective-permute-done((bf16[32,2176]{1,0:T(8,128)(2,1)S(1)}, bf16[32,2176]{1,0:T(8,128)(2,1)}, u32[]{:S(2)}, u32[]{:S(2)}) %collective-permute-start) | collective-permute-done | bytes 139296 | tf_op jit(solution)/shard_map/ppermute | solution.py:65
  14.9 7.9 %collective-permute-done.1 = bf16[32,2176]{1,0:T(8,128)(2,1)} collective-permute-done((bf16[32,2176]{1,0:T(8,128)(2,1)S(1)}, bf16[32,2176]{1,0:T(8,128)(2,1)}, u32[]{:S(2)}, u32[]{:S(2)}) %collective-permute-start.1) | collective-permute-done | bytes 139296 | tf_op jit(solution)/shard_map/ppermute | solution.py:65
  22.8 1.2 %pad_maximum_fusion = bf16[128,2176]{1,0:T(8,128)(2,1)S(1)} fusion(bf16[32,2176]{1,0:T(8,128)(2,1)} %collective-permute-done.2, bf16[32,2176]{1,0:T(8,128)(2,1)} %collective-permute-done.1, bf16[32,2176]{1,0:T(8,128)(2,1)} %collective-permute-done, bf16[32,2176]{1,0:T(8,128)(2,1)S(1)} %get-tuple-element.26), kind=kLoop, calls=%fused_computation.28 | loop fusion | flops 2228224 | bytes 1114112 | tf_op jit(solution)/shard_map/concatenate | solution.py:66
  24.0 1.6 %collective-permute-start.3 = (bf16[128,2176]{1,0:T(8,128)(2,1)S(1)}, bf16[128,2176]{1,0:T(8,128)(2,1)S(1)}, u32[]{:S(2)}, u32[]{:S(2)}) collective-permute-start(bf16[128,2176]{1,0:T(8,128)(2,1)S(1)} %pad_maximum_fusion), channel_id=1, source_target_pairs={{0,2},{2,0},{1,3},{3,1},{4,6},{6,4},{5,7},{7,5},{8,10},{10,8},{9,1... | collective-permute-start | bytes 1671176 | tf_op jit(solution)/shard_map/ppermute | solution.py:65
  25.6 2.2 %collective-permute-start.10 = (bf16[32,2176]{1,0:T(8,128)(2,1)S(1)}, bf16[32,2176]{1,0:T(8,128)(2,1)S(1)}, u32[]{:S(2)}, u32[]{:S(2)}) collective-permute-start(bf16[32,2176]{1,0:T(8,128)(2,1)S(1)} %get-tuple-element.6), channel_id=1, source_target_pairs={{0,4},{4,0},{8,12},{12,8},{1,5},{5,1},{9,13},{13,9},{2,6},{6,2},{1... | collective-permute-start | bytes 417800 | tf_op jit(solution)/shard_map/ppermute | solution.py:65
  27.9 1.1 %collective-permute-start.11 = (bf16[32,2176]{1,0:T(8,128)(2,1)S(1)}, bf16[32,2176]{1,0:T(8,128)(2,1)S(1)}, u32[]{:S(2)}, u32[]{:S(2)}) collective-permute-start(bf16[32,2176]{1,0:T(8,128)(2,1)S(1)} %get-tuple-element.6), channel_id=1, source_target_pairs={{0,8},{4,12},{8,0},{12,4},{1,9},{5,13},{9,1},{13,5},{2,10},{6,14},... | collective-permute-start | bytes 417800 | tf_op jit(solution)/shard_map/ppermute | solution.py:65
  29.0 1.4 %collective-permute-start.12 = (bf16[32,2176]{1,0:T(8,128)(2,1)S(1)}, bf16[32,2176]{1,0:T(8,128)(2,1)S(1)}, u32[]{:S(2)}, u32[]{:S(2)}) collective-permute-start(bf16[32,2176]{1,0:T(8,128)(2,1)S(1)} %get-tuple-element.6), channel_id=1, source_target_pairs={{0,12},{4,8},{8,4},{12,0},{1,13},{5,9},{9,5},{13,1},{2,14},{6,10},... | collective-permute-start | bytes 417800 | tf_op jit(solution)/shard_map/ppermute | solution.py:65
  30.3 1.6 %constant_dynamic-update-slice_fusion.3 = (bf16[256,2176]{1,0:T(8,128)(2,1)}, bf16[512,2176]{1,0:T(8,128)(2,1)}) fusion(bf16[256,2176]{1,0:T(8,128)(2,1)} %get-tuple-element.24, bf16[32,2176]{1,0:T(8,128)(2,1)} %collective-permute-done, bf16[512,2176]{1,0:T(8,128)(2,1)} %get-tuple-element.25), kind=kLoop, calls=%fused_computation.53 | loop fusion | bytes 417792
  32.0 1.6 %constant_dynamic-update-slice_fusion.2 = (bf16[256,2176]{1,0:T(8,128)(2,1)}, bf16[512,2176]{1,0:T(8,128)(2,1)}) fusion(bf16[256,2176]{1,0:T(8,128)(2,1)} %get-tuple-element.39, bf16[32,2176]{1,0:T(8,128)(2,1)} %collective-permute-done.1, bf16[512,2176]{1,0:T(8,128)(2,1)} %get-tuple-element.40), kind=kLoop, calls=%fused_computation.52 | loop fusion | bytes 417792
  33.6 1.6 %constant_dynamic-update-slice_fusion.1 = (bf16[256,2176]{1,0:T(8,128)(2,1)}, bf16[512,2176]{1,0:T(8,128)(2,1)}) fusion(bf16[256,2176]{1,0:T(8,128)(2,1)} %get-tuple-element.37, bf16[32,2176]{1,0:T(8,128)(2,1)} %collective-permute-done.2, bf16[512,2176]{1,0:T(8,128)(2,1)} %get-tuple-element.38), kind=kLoop, calls=%fused_computation.51 | loop fusion | bytes 417792
  35.2 4.8 %collective-permute-done.11 = bf16[32,2176]{1,0:T(8,128)(2,1)S(1)} collective-permute-done((bf16[32,2176]{1,0:T(8,128)(2,1)S(1)}, bf16[32,2176]{1,0:T(8,128)(2,1)S(1)}, u32[]{:S(2)}, u32[]{:S(2)}) %collective-permute-start.11) | collective-permute-done | bytes 139296 | tf_op jit(solution)/shard_map/ppermute | solution.py:65
  40.1 0.6 collective-permute-start.13
  40.7 1.1 %constant_dynamic-update-slice_fusion = (bf16[256,2176]{1,0:T(8,128)(2,1)}, bf16[512,2176]{1,0:T(8,128)(2,1)}) fusion(bf16[256,2176]{1,0:T(8,128)(2,1)} %get-tuple-element.35, bf16[128,2176]{1,0:T(8,128)(2,1)S(1)} %collective-permute-done.3, bf16[512,2176]{1,0:T(8,128)(2,1)} %get-tuple-element.36), kind=kLoop, calls=%fused_computation.50 | loop fusion | bytes 1671168 | tf_op jit(solution)/shard_map/concatenate | solution.py:66
  41.9 8.8 %collective-permute-done.13 = bf16[128,2176]{1,0:T(8,128)(2,1)S(1)} collective-permute-done((bf16[128,2176]{1,0:T(8,128)(2,1)S(1)}, bf16[128,2176]{1,0:T(8,128)(2,1)S(1)}, u32[]{:S(2)}, u32[]{:S(2)}) %collective-permute-start.13) | collective-permute-done | bytes 557088 | tf_op jit(solution)/shard_map/ppermute | solution.py:65
  50.9 0.1 constant_dynamic-update-slice_fusion.5
  51.1 3.4 %fusion.2 = f32[512,1536]{1,0:T(8,128)S(1)} fusion(bf16[1,2048,1536]{2,1,0:T(8,128)(2,1)S(1)} %copy-done.2, bf16[512,2176]{1,0:T(8,128)(2,1)S(1)} %constant_dynamic-update-slice_fusion.5), kind=kOutput, calls=%fused_computation.2 | convolution fusion | flops 3221225472 | bytes 11534336 | tf_op jit(solution)/shard_map/dot_general | solution.py:9
  54.6 0.1 constant_dynamic-update-slice_fusion.16
  54.8 3.4 %fusion = f32[512,1536]{1,0:T(8,128)S(1)} fusion(bf16[1,2048,1536]{2,1,0:T(8,128)(2,1)S(1)} %copy-done.2, bf16[512,2176]{1,0:T(8,128)(2,1)S(1)} %constant_dynamic-update-slice_fusion.16), kind=kOutput, calls=%fused_computation | convolution fusion | flops 3221225472 | bytes 11534336 | tf_op jit(solution)/shard_map/dot_general | solution.py:9
  58.2 0.5 fusion.35
  58.8 1.8 %convert_multiply_fusion = f32[512,2048]{1,0:T(8,128)S(1)} fusion(bf16[1,768,2048]{2,1,0:T(8,128)(2,1)S(1)} %copy-done, f32[512]{0:T(512)S(1)} %get-tuple-element.8, f32[512,1536]{1,0:T(8,128)S(1)} %fusion), kind=kOutput, calls=%fused_computation.4 | convolution fusion | flops 1616117760 | bytes 10487808 | tf_op jit(solution)/shard_map/dot_general | solution.py:11
  60.8 0.5 collective-permute-start.15
  61.3 1.8 %convert_multiply_fusion.1 = f32[512,2048]{1,0:T(8,128)S(1)} fusion(bf16[1,768,2048]{2,1,0:T(8,128)(2,1)S(1)} %copy-done, f32[512]{0:T(512)S(1)} %get-tuple-element.7, f32[512,1536]{1,0:T(8,128)S(1)} %fusion.2), kind=kOutput, calls=%fused_computation.5 | convolution fusion | flops 1616117760 | bytes 10487808 | tf_op jit(solution)/shard_map/dot_general | solution.py:11
  63.4 0.2 collective-permute-done.15
  63.6 0.3 slice_add_fusion
  64.0 0.6 collective-permute-start.16
  64.6 1.4 %collective-permute-done.5 = bf16[256,2048]{1,0:T(8,128)(2,1)S(1)} collective-permute-done((bf16[256,2048]{1,0:T(8,128)(2,1)S(1)}, bf16[256,2048]{1,0:T(8,128)(2,1)S(1)}, u32[]{:S(2)}, u32[]{:S(2)}) %collective-permute-start.5) | collective-permute-done | bytes 1048608 | tf_op jit(solution)/shard_map/ppermute | solution.py:74
  66.0 0.3 slice_add_fusion.1
  66.5 0.6 collective-permute-start.6
  67.1 11.8 %collective-permute-done.16 = bf16[128,2048]{1,0:T(8,128)(2,1)S(1)} collective-permute-done((bf16[128,2048]{1,0:T(8,128)(2,1)S(1)}, bf16[128,2048]{1,0:T(8,128)(2,1)S(1)}, u32[]{:S(2)}, u32[]{:S(2)}) %collective-permute-start.16) | collective-permute-done | bytes 524320 | tf_op jit(solution)/shard_map/ppermute | solution.py:74
  78.9 0.1 fusion.40
  79.1 4.5 %collective-permute-start.19 = (bf16[32,2048]{1,0:T(8,128)(2,1)S(1)}, bf16[32,2048]{1,0:T(8,128)(2,1)S(1)}, u32[]{:S(2)}, u32[]{:S(2)}) collective-permute-start(bf16[32,2048]{1,0:T(8,128)(2,1)S(1)} %get-tuple-element.21), channel_id=1, source_target_pairs={{0,12},{4,8},{8,4},{12,0},{1,13},{5,9},{9,5},{13,1},{2,14},{6,10},... | collective-permute-start | bytes 393224 | tf_op jit(solution)/shard_map/ppermute | solution.py:74
  83.6 2.2 %collective-permute-start.18 = (bf16[32,2048]{1,0:T(8,128)(2,1)S(1)}, bf16[32,2048]{1,0:T(8,128)(2,1)S(1)}, u32[]{:S(2)}, u32[]{:S(2)}) collective-permute-start(bf16[32,2048]{1,0:T(8,128)(2,1)S(1)} %get-tuple-element.22), channel_id=1, source_target_pairs={{0,8},{4,12},{8,0},{12,4},{1,9},{5,13},{9,1},{13,5},{2,10},{6,14},... | collective-permute-start | bytes 393224 | tf_op jit(solution)/shard_map/ppermute | solution.py:74
  85.7 0.5 collective-permute-start.17
  86.2 3.3 %collective-permute-done.6 = bf16[128,2048]{1,0:T(8,128)(2,1)S(1)} collective-permute-done((bf16[128,2048]{1,0:T(8,128)(2,1)S(1)}, bf16[128,2048]{1,0:T(8,128)(2,1)S(1)}, u32[]{:S(2)}, u32[]{:S(2)}) %collective-permute-start.6) | collective-permute-done | bytes 524320 | tf_op jit(solution)/shard_map/ppermute | solution.py:74
  89.5 0.2 fusion.39
  89.7 4.5 %collective-permute-start.9 = (bf16[32,2048]{1,0:T(8,128)(2,1)S(1)}, bf16[32,2048]{1,0:T(8,128)(2,1)S(1)}, u32[]{:S(2)}, u32[]{:S(2)}) collective-permute-start(bf16[32,2048]{1,0:T(8,128)(2,1)S(1)} %get-tuple-element.18), channel_id=1, source_target_pairs={{0,12},{4,8},{8,4},{12,0},{1,13},{5,9},{9,5},{13,1},{2,14},{6,10},... | collective-permute-start | bytes 393224 | tf_op jit(solution)/shard_map/ppermute | solution.py:74
  94.2 2.2 %collective-permute-start.8 = (bf16[32,2048]{1,0:T(8,128)(2,1)S(1)}, bf16[32,2048]{1,0:T(8,128)(2,1)S(1)}, u32[]{:S(2)}, u32[]{:S(2)}) collective-permute-start(bf16[32,2048]{1,0:T(8,128)(2,1)S(1)} %get-tuple-element.19), channel_id=1, source_target_pairs={{0,8},{4,12},{8,0},{12,4},{1,9},{5,13},{9,1},{13,5},{2,10},{6,14},... | collective-permute-start | bytes 393224 | tf_op jit(solution)/shard_map/ppermute | solution.py:74
  96.4 0.5 collective-permute-start.7
  96.9 1.1 %collective-permute-done.18 = bf16[32,2048]{1,0:T(8,128)(2,1)S(1)} collective-permute-done((bf16[32,2048]{1,0:T(8,128)(2,1)S(1)}, bf16[32,2048]{1,0:T(8,128)(2,1)S(1)}, u32[]{:S(2)}, u32[]{:S(2)}) %collective-permute-start.18) | collective-permute-done | bytes 131104 | tf_op jit(solution)/shard_map/ppermute | solution.py:74
  98.1 8.1 %collective-permute-done.8 = bf16[32,2048]{1,0:T(8,128)(2,1)S(1)} collective-permute-done((bf16[32,2048]{1,0:T(8,128)(2,1)S(1)}, bf16[32,2048]{1,0:T(8,128)(2,1)S(1)}, u32[]{:S(2)}, u32[]{:S(2)}) %collective-permute-start.8) | collective-permute-done | bytes 131104 | tf_op jit(solution)/shard_map/ppermute | solution.py:74
  106.3 0.7 pad_maximum_fusion.2
  (42 shorter events, 1.4 us)
Async XLA Ops:
  0.0 58.7 %copy-start = (bf16[1,768,2048]{2,1,0:T(8,128)(2,1)S(1)}, bf16[1,768,2048]{2,1,0:T(8,128)(2,1)}, u32[]{:S(2)}) copy-start(bf16[1,768,2048]{2,1,0:T(8,128)(2,1)} %param.11) | copy-start | bytes 9437188
  6.2 8.6 %collective-permute-start = (bf16[32,2176]{1,0:T(8,128)(2,1)S(1)}, bf16[32,2176]{1,0:T(8,128)(2,1)}, u32[]{:S(2)}, u32[]{:S(2)}) collective-permute-start(bf16[32,2176]{1,0:T(8,128)(2,1)S(1)} %get-tuple-element.26), channel_id=1, source_target_pairs={{0,4},{4,0},{8,12},{12,8},{1,5},{5,1},{9,13},{13,9},{2,6},{6,2},{1... | collective-permute-start | bytes 417800 | tf_op jit(solution)/shard_map/ppermute | solution.py:65
  9.3 13.5 %collective-permute-start.1 = (bf16[32,2176]{1,0:T(8,128)(2,1)S(1)}, bf16[32,2176]{1,0:T(8,128)(2,1)}, u32[]{:S(2)}, u32[]{:S(2)}) collective-permute-start(bf16[32,2176]{1,0:T(8,128)(2,1)S(1)} %get-tuple-element.26), channel_id=1, source_target_pairs={{0,8},{4,12},{8,0},{12,4},{1,9},{5,13},{9,1},{13,5},{2,10},{6,14},... | collective-permute-start | bytes 417800 | tf_op jit(solution)/shard_map/ppermute | solution.py:65
  11.9 10.9 %collective-permute-start.2 = (bf16[32,2176]{1,0:T(8,128)(2,1)S(1)}, bf16[32,2176]{1,0:T(8,128)(2,1)}, u32[]{:S(2)}, u32[]{:S(2)}) collective-permute-start(bf16[32,2176]{1,0:T(8,128)(2,1)S(1)} %get-tuple-element.26), channel_id=1, source_target_pairs={{0,12},{4,8},{8,4},{12,0},{1,13},{5,9},{9,5},{13,1},{2,14},{6,10},... | collective-permute-start | bytes 417800 | tf_op jit(solution)/shard_map/ppermute | solution.py:65
  22.8 28.3 %copy-start.2 = (bf16[1,2048,1536]{2,1,0:T(8,128)(2,1)S(1)}, bf16[1,2048,1536]{2,1,0:T(8,128)(2,1)}, u32[]{:S(2)}) copy-start(bf16[1,2048,1536]{2,1,0:T(8,128)(2,1)} %param.10) | copy-start | bytes 18874372
  24.0 16.6 %collective-permute-start.3 = (bf16[128,2176]{1,0:T(8,128)(2,1)S(1)}, bf16[128,2176]{1,0:T(8,128)(2,1)S(1)}, u32[]{:S(2)}, u32[]{:S(2)}) collective-permute-start(bf16[128,2176]{1,0:T(8,128)(2,1)S(1)} %pad_maximum_fusion), channel_id=1, source_target_pairs={{0,2},{2,0},{1,3},{3,1},{4,6},{6,4},{5,7},{7,5},{8,10},{10,8},{9,1... | collective-permute-start | bytes 1671176 | tf_op jit(solution)/shard_map/ppermute | solution.py:65
  25.6 9.6 %collective-permute-start.10 = (bf16[32,2176]{1,0:T(8,128)(2,1)S(1)}, bf16[32,2176]{1,0:T(8,128)(2,1)S(1)}, u32[]{:S(2)}, u32[]{:S(2)}) collective-permute-start(bf16[32,2176]{1,0:T(8,128)(2,1)S(1)} %get-tuple-element.6), channel_id=1, source_target_pairs={{0,4},{4,0},{8,12},{12,8},{1,5},{5,1},{9,13},{13,9},{2,6},{6,2},{1... | collective-permute-start | bytes 417800 | tf_op jit(solution)/shard_map/ppermute | solution.py:65
  27.9 12.2 %collective-permute-start.11 = (bf16[32,2176]{1,0:T(8,128)(2,1)S(1)}, bf16[32,2176]{1,0:T(8,128)(2,1)S(1)}, u32[]{:S(2)}, u32[]{:S(2)}) collective-permute-start(bf16[32,2176]{1,0:T(8,128)(2,1)S(1)} %get-tuple-element.6), channel_id=1, source_target_pairs={{0,8},{4,12},{8,0},{12,4},{1,9},{5,13},{9,1},{13,5},{2,10},{6,14},... | collective-permute-start | bytes 417800 | tf_op jit(solution)/shard_map/ppermute | solution.py:65
  29.0 11.1 %collective-permute-start.12 = (bf16[32,2176]{1,0:T(8,128)(2,1)S(1)}, bf16[32,2176]{1,0:T(8,128)(2,1)S(1)}, u32[]{:S(2)}, u32[]{:S(2)}) collective-permute-start(bf16[32,2176]{1,0:T(8,128)(2,1)S(1)} %get-tuple-element.6), channel_id=1, source_target_pairs={{0,12},{4,8},{8,4},{12,0},{1,13},{5,9},{9,5},{13,1},{2,14},{6,10},... | collective-permute-start | bytes 417800 | tf_op jit(solution)/shard_map/ppermute | solution.py:65
  40.1 10.6 %collective-permute-start.13 = (bf16[128,2176]{1,0:T(8,128)(2,1)S(1)}, bf16[128,2176]{1,0:T(8,128)(2,1)S(1)}, u32[]{:S(2)}, u32[]{:S(2)}) collective-permute-start(bf16[128,2176]{1,0:T(8,128)(2,1)S(1)} %pad_maximum_fusion.1), channel_id=1, source_target_pairs={{0,2},{2,0},{1,3},{3,1},{4,6},{6,4},{5,7},{7,5},{8,10},{10,8},{9,1... | collective-permute-start | bytes 1671176 | tf_op jit(solution)/shard_map/ppermute | solution.py:65
  41.8 9.1 %copy-start.1 = (bf16[512,2176]{1,0:T(8,128)(2,1)S(1)}, bf16[512,2176]{1,0:T(8,128)(2,1)}, u32[]{:S(2)}) copy-start(bf16[512,2176]{1,0:T(8,128)(2,1)} %get-tuple-element.16) | copy-start | bytes 6684676
  41.8 9.1 %collective-permute-start.4 = (bf16[256,2176]{1,0:T(8,128)(2,1)}, bf16[256,2176]{1,0:T(8,128)(2,1)S(1)}, u32[]{:S(2)}, u32[]{:S(2)}) collective-permute-start(bf16[256,2176]{1,0:T(8,128)(2,1)} %get-tuple-element.15), channel_id=1, source_target_pairs={{0,1},{1,0},{2,3},{3,2},{4,5},{5,4},{6,7},{7,6},{8,9},{9,8},{10,11... | collective-permute-start | bytes 3342344 | tf_op jit(solution)/shard_map/ppermute | solution.py:65
  50.8 3.7 %collective-permute-start.14 = (bf16[256,2176]{1,0:T(8,128)(2,1)S(1)}, bf16[256,2176]{1,0:T(8,128)(2,1)S(1)}, u32[]{:S(2)}, u32[]{:S(2)}) collective-permute-start(bf16[256,2176]{1,0:T(8,128)(2,1)S(1)} %get-tuple-element.13), channel_id=1, source_target_pairs={{0,1},{1,0},{2,3},{3,2},{4,5},{5,4},{6,7},{7,6},{8,9},{9,8},{10,11... | collective-permute-start | bytes 3342344 | tf_op jit(solution)/shard_map/ppermute | solution.py:65
  60.8 2.8 %collective-permute-start.15 = (bf16[256,2048]{1,0:T(8,128)(2,1)S(1)}, bf16[256,2048]{1,0:T(8,128)(2,1)S(1)}, u32[]{:S(2)}, u32[]{:S(2)}) collective-permute-start(bf16[256,2048]{1,0:T(8,128)(2,1)S(1)} %split.124), channel_id=1, source_target_pairs={{0,1},{1,0},{2,3},{3,2},{4,5},{5,4},{6,7},{7,6},{8,9},{9,8},{10,11... | collective-permute-start | bytes 3145736 | tf_op jit(solution)/shard_map/ppermute | solution.py:74
  63.3 2.7 %collective-permute-start.5 = (bf16[256,2048]{1,0:T(8,128)(2,1)S(1)}, bf16[256,2048]{1,0:T(8,128)(2,1)S(1)}, u32[]{:S(2)}, u32[]{:S(2)}) collective-permute-start(bf16[256,2048]{1,0:T(8,128)(2,1)S(1)} %split.125), channel_id=1, source_target_pairs={{0,1},{1,0},{2,3},{3,2},{4,5},{5,4},{6,7},{7,6},{8,9},{9,8},{10,11... | collective-permute-start | bytes 3145736 | tf_op jit(solution)/shard_map/ppermute | solution.py:74
  64.0 14.9 %collective-permute-start.16 = (bf16[128,2048]{1,0:T(8,128)(2,1)S(1)}, bf16[128,2048]{1,0:T(8,128)(2,1)S(1)}, u32[]{:S(2)}, u32[]{:S(2)}) collective-permute-start(bf16[128,2048]{1,0:T(8,128)(2,1)S(1)} %split.126), channel_id=1, source_target_pairs={{0,2},{2,0},{1,3},{3,1},{4,6},{6,4},{5,7},{7,5},{8,10},{10,8},{9,1... | collective-permute-start | bytes 1572872 | tf_op jit(solution)/shard_map/ppermute | solution.py:74
  66.5 23.1 %collective-permute-start.6 = (bf16[128,2048]{1,0:T(8,128)(2,1)S(1)}, bf16[128,2048]{1,0:T(8,128)(2,1)S(1)}, u32[]{:S(2)}, u32[]{:S(2)}) collective-permute-start(bf16[128,2048]{1,0:T(8,128)(2,1)S(1)} %split.127), channel_id=1, source_target_pairs={{0,2},{2,0},{1,3},{3,1},{4,6},{6,4},{5,7},{7,5},{8,10},{10,8},{9,1... | collective-permute-start | bytes 1572872 | tf_op jit(solution)/shard_map/ppermute | solution.py:74
  79.1 17.3 %collective-permute-start.19 = (bf16[32,2048]{1,0:T(8,128)(2,1)S(1)}, bf16[32,2048]{1,0:T(8,128)(2,1)S(1)}, u32[]{:S(2)}, u32[]{:S(2)}) collective-permute-start(bf16[32,2048]{1,0:T(8,128)(2,1)S(1)} %get-tuple-element.21), channel_id=1, source_target_pairs={{0,12},{4,8},{8,4},{12,0},{1,13},{5,9},{9,5},{13,1},{2,14},{6,10},... | collective-permute-start | bytes 393224 | tf_op jit(solution)/shard_map/ppermute | solution.py:74
  83.6 14.4 %collective-permute-start.18 = (bf16[32,2048]{1,0:T(8,128)(2,1)S(1)}, bf16[32,2048]{1,0:T(8,128)(2,1)S(1)}, u32[]{:S(2)}, u32[]{:S(2)}) collective-permute-start(bf16[32,2048]{1,0:T(8,128)(2,1)S(1)} %get-tuple-element.22), channel_id=1, source_target_pairs={{0,8},{4,12},{8,0},{12,4},{1,9},{5,13},{9,1},{13,5},{2,10},{6,14},... | collective-permute-start | bytes 393224 | tf_op jit(solution)/shard_map/ppermute | solution.py:74
  85.7 12.3 %collective-permute-start.17 = (bf16[32,2048]{1,0:T(8,128)(2,1)S(1)}, bf16[32,2048]{1,0:T(8,128)(2,1)S(1)}, u32[]{:S(2)}, u32[]{:S(2)}) collective-permute-start(bf16[32,2048]{1,0:T(8,128)(2,1)S(1)} %get-tuple-element.20), channel_id=1, source_target_pairs={{0,4},{4,0},{8,12},{12,8},{1,5},{5,1},{9,13},{13,9},{2,6},{6,2},{1... | collective-permute-start | bytes 393224 | tf_op jit(solution)/shard_map/ppermute | solution.py:74
  89.7 8.4 %collective-permute-start.9 = (bf16[32,2048]{1,0:T(8,128)(2,1)S(1)}, bf16[32,2048]{1,0:T(8,128)(2,1)S(1)}, u32[]{:S(2)}, u32[]{:S(2)}) collective-permute-start(bf16[32,2048]{1,0:T(8,128)(2,1)S(1)} %get-tuple-element.18), channel_id=1, source_target_pairs={{0,12},{4,8},{8,4},{12,0},{1,13},{5,9},{9,5},{13,1},{2,14},{6,10},... | collective-permute-start | bytes 393224 | tf_op jit(solution)/shard_map/ppermute | solution.py:74
  94.2 12.0 %collective-permute-start.8 = (bf16[32,2048]{1,0:T(8,128)(2,1)S(1)}, bf16[32,2048]{1,0:T(8,128)(2,1)S(1)}, u32[]{:S(2)}, u32[]{:S(2)}) collective-permute-start(bf16[32,2048]{1,0:T(8,128)(2,1)S(1)} %get-tuple-element.19), channel_id=1, source_target_pairs={{0,8},{4,12},{8,0},{12,4},{1,9},{5,13},{9,1},{13,5},{2,10},{6,14},... | collective-permute-start | bytes 393224 | tf_op jit(solution)/shard_map/ppermute | solution.py:74
  96.4 9.8 %collective-permute-start.7 = (bf16[32,2048]{1,0:T(8,128)(2,1)S(1)}, bf16[32,2048]{1,0:T(8,128)(2,1)S(1)}, u32[]{:S(2)}, u32[]{:S(2)}) collective-permute-start(bf16[32,2048]{1,0:T(8,128)(2,1)S(1)} %get-tuple-element.17), channel_id=1, source_target_pairs={{0,4},{4,0},{8,12},{12,8},{1,5},{5,1},{9,13},{13,9},{2,6},{6,2},{1... | collective-permute-start | bytes 393224 | tf_op jit(solution)/shard_map/ppermute | solution.py:74

commit v22 on v5

--- a/solution.py
+++ b/solution.py
@@ -96,13 +96,17 @@
     pick = (jnp.arange(hosts, dtype=jnp.int32) == me).astype(jnp.float32)
     results = []
     held = None
+    crossed = None
     for rows in jnp.split(carried, STREAMS, axis=0):
         if held is not None:
             held, rows = lax.optimization_barrier((held, rows))
         rows = gather_stage(rows, AXES[0], sizes[0])
+        if crossed is not None:
+            crossed, rows = lax.optimization_barrier((crossed, rows))
         held = rows
-        for axis, size in zip(AXES[1:], sizes[1:]):
-            rows = gather_stage(rows, axis, size)
+        rows = gather_stage(rows, AXES[1], sizes[1])
+        crossed = rows
+        rows = gather_stage(rows, AXES[2], sizes[2])
         tail = rows[:, width_model:width_model + 3 * hosts].astype(jnp.float32)
         gate = tail[:, :hosts] + tail[:, hosts:2 * hosts] + tail[:, 2 * hosts:]
         mine = jnp.sum(gate * pick[None, :], axis=1)

time: 106 us -> 112 us (1.057)
  waiting for transfers between devices: 48.5 us -> 60.3 us
  starting transfers between devices: 29.1 us -> 24.4 us
  local copies, waits for them, and re-layouts: 10.8 us -> 7.14 us
  matrix products: 10.6 us -> 12.8 us
    ppermute x10, waiting for transfers between devices: 23.5 us -> 30.1 us  [gather_stage(): got.append(lax.ppermute(block, axis, pairs))]
    ppermute x10, starting transfers between devices: 13.9 us -> 8.39 us  [scatter_stage(): lax.ppermute(pieces[shift].astype(jnp.bfloat16), axis, pairs)]
    ppermute x10, waiting for transfers between devices: 25 us -> 30.2 us  [scatter_stage(): lax.ppermute(pieces[shift].astype(jnp.bfloat16), axis, pairs)]
    dot_general x2, matrix products: 6.9 us -> 9.13 us  [expert_block(): pair = jnp.dot(rows_in, gate_up, preferred_element_type=jnp.float32)]
    split x1, local copies, waits for them, and re-layouts: 1.74 us -> 0.05 us  [dense_shards(): jnp.split(carried, STREAMS, axis=0)]
    unnamed x13 -> x17, local copies, waits for them, and re-layouts: 5 us -> 4.84 us
  transfers between devices with their start and end apart: 20 -> 20, of which waited for: 10 -> 12; matrix products, arithmetic and copies ran while one was open for 12% -> 12% of each run, Pallas kernels for 0% -> 0%
where the time goes in v22:
time: 112 us
  waiting for transfers between devices  60.3 us (54%)
  starting transfers between devices  24.4 us (22%)
  matrix products  12.8 us (11%)
  local copies, waits for them, and re-layouts  7.14 us (6%)
  other arithmetic  7.04 us (6%)
    ppermute x10, waiting for transfers between devices, scatter_stage(): lax.ppermute(pieces[shift].astype(jnp.bfloat16), axis, pairs)  30.2 us
    ppermute x10, waiting for transfers between devices, gather_stage(): got.append(lax.ppermute(block, axis, pairs))  30.1 us
    ppermute x10, starting transfers between devices, gather_stage(): got.append(lax.ppermute(block, axis, pairs))  16 us
    dot_general x2, matrix products, expert_block(): pair = jnp.dot(rows_in, gate_up, preferred_element_type=jnp.float32)  9.13 us
    ppermute x10, starting transfers between devices, scatter_stage(): lax.ppermute(pieces[shift].astype(jnp.bfloat16), axis, pairs)  8.39 us
    unnamed x17, local copies, waits for them, and re-layouts  4.84 us
    dot_general x2, matrix products, expert_block(): jnp.dot(active, down_proj, preferred_element_type=jnp.float32)  3.69 us
  transfers between devices with their start and end apart: 20, of which 12 were waited for; matrix products, arithmetic and copies ran while one was open for 12% of the time, Pallas kernels for 0%

profile of v22, /device:TPU:0, one launch (start us, length us, event | category | flops | bytes accessed | tf_op | source)
XLA Modules:
  0.0 112.0 jit_solution(11079408484152460783)
XLA Ops:
  0.0 0.9 reduce_sum.36
  0.9 0.8 broadcast_divide_fusion
  1.7 0.8 select_reduce_fusion
  2.8 1.1 concatenate.31
  3.9 3.1 %collective-permute-start = (bf16[32,2176]{1,0:T(8,128)(2,1)S(1)}, bf16[32,2176]{1,0:T(8,128)(2,1)S(1)}, u32[]{:S(2)}, u32[]{:S(2)}) collective-permute-start(bf16[32,2176]{1,0:T(8,128)(2,1)S(1)} %get-tuple-element.26), channel_id=1, source_target_pairs={{0,4},{4,8},{8,12},{12,0},{1,5},{5,9},{9,13},{13,1},{2,6},{6,10},{... | collective-permute-start | bytes 417800 | tf_op jit(solution)/shard_map/ppermute | solution.py:65
  7.0 2.6 %collective-permute-start.1 = (bf16[32,2176]{1,0:T(8,128)(2,1)S(1)}, bf16[32,2176]{1,0:T(8,128)(2,1)S(1)}, u32[]{:S(2)}, u32[]{:S(2)}) collective-permute-start(bf16[32,2176]{1,0:T(8,128)(2,1)S(1)} %get-tuple-element.26), channel_id=1, source_target_pairs={{0,8},{4,12},{8,0},{12,4},{1,9},{5,13},{9,1},{13,5},{2,10},{6,14},... | collective-permute-start | bytes 417800 | tf_op jit(solution)/shard_map/ppermute | solution.py:65
  9.6 1.3 %collective-permute-start.2 = (bf16[32,2176]{1,0:T(8,128)(2,1)S(1)}, bf16[32,2176]{1,0:T(8,128)(2,1)S(1)}, u32[]{:S(2)}, u32[]{:S(2)}) collective-permute-start(bf16[32,2176]{1,0:T(8,128)(2,1)S(1)} %get-tuple-element.26), channel_id=1, source_target_pairs={{0,12},{4,0},{8,4},{12,8},{1,13},{5,1},{9,5},{13,9},{2,14},{6,2},{... | collective-permute-start | bytes 417800 | tf_op jit(solution)/shard_map/ppermute | solution.py:65
  10.9 2.7 %collective-permute-done = bf16[32,2176]{1,0:T(8,128)(2,1)S(1)} collective-permute-done((bf16[32,2176]{1,0:T(8,128)(2,1)S(1)}, bf16[32,2176]{1,0:T(8,128)(2,1)S(1)}, u32[]{:S(2)}, u32[]{:S(2)}) %collective-permute-start) | collective-permute-done | bytes 139296 | tf_op jit(solution)/shard_map/ppermute | solution.py:65
  13.6 5.1 %collective-permute-done.1 = bf16[32,2176]{1,0:T(8,128)(2,1)S(1)} collective-permute-done((bf16[32,2176]{1,0:T(8,128)(2,1)S(1)}, bf16[32,2176]{1,0:T(8,128)(2,1)S(1)}, u32[]{:S(2)}, u32[]{:S(2)}) %collective-permute-start.1) | collective-permute-done | bytes 139296 | tf_op jit(solution)/shard_map/ppermute | solution.py:65
  18.8 3.5 %collective-permute-start.10 = (bf16[32,2176]{1,0:T(8,128)(2,1)S(1)}, bf16[32,2176]{1,0:T(8,128)(2,1)S(1)}, u32[]{:S(2)}, u32[]{:S(2)}) collective-permute-start(bf16[32,2176]{1,0:T(8,128)(2,1)S(1)} %get-tuple-element.7), channel_id=1, source_target_pairs={{0,4},{4,8},{8,12},{12,0},{1,5},{5,9},{9,13},{13,1},{2,6},{6,10},{... | collective-permute-start | bytes 417800 | tf_op jit(solution)/shard_map/ppermute | solution.py:65
  22.3 1.6 %collective-permute-start.11 = (bf16[32,2176]{1,0:T(8,128)(2,1)S(1)}, bf16[32,2176]{1,0:T(8,128)(2,1)S(1)}, u32[]{:S(2)}, u32[]{:S(2)}) collective-permute-start(bf16[32,2176]{1,0:T(8,128)(2,1)S(1)} %get-tuple-element.7), channel_id=1, source_target_pairs={{0,8},{4,12},{8,0},{12,4},{1,9},{5,13},{9,1},{13,5},{2,10},{6,14},... | collective-permute-start | bytes 417800 | tf_op jit(solution)/shard_map/ppermute | solution.py:65
  23.9 0.8 collective-permute-start.12
  24.7 1.5 %collective-permute-start.3 = (bf16[128,2176]{1,0:T(8,128)(2,1)S(1)}, bf16[128,2176]{1,0:T(8,128)(2,1)S(1)}, u32[]{:S(2)}, u32[]{:S(2)}) collective-permute-start(bf16[128,2176]{1,0:T(8,128)(2,1)S(1)} %pad_maximum_fusion.1), channel_id=1, source_target_pairs={{0,2},{2,0},{1,3},{3,1},{4,6},{6,4},{5,7},{7,5},{8,10},{10,8},{9,1... | collective-permute-start | bytes 1671176 | tf_op jit(solution)/shard_map/ppermute | solution.py:65
  26.3 1.3 %collective-permute-done.10 = bf16[32,2176]{1,0:T(8,128)(2,1)S(1)} collective-permute-done((bf16[32,2176]{1,0:T(8,128)(2,1)S(1)}, bf16[32,2176]{1,0:T(8,128)(2,1)S(1)}, u32[]{:S(2)}, u32[]{:S(2)}) %collective-permute-start.10) | collective-permute-done | bytes 139296 | tf_op jit(solution)/shard_map/ppermute | solution.py:65
  27.6 4.9 %collective-permute-done.11 = bf16[32,2176]{1,0:T(8,128)(2,1)S(1)} collective-permute-done((bf16[32,2176]{1,0:T(8,128)(2,1)S(1)}, bf16[32,2176]{1,0:T(8,128)(2,1)S(1)}, u32[]{:S(2)}, u32[]{:S(2)}) %collective-permute-start.11) | collective-permute-done | bytes 139296 | tf_op jit(solution)/shard_map/ppermute | solution.py:65
  32.4 0.8 pad_maximum_fusion.2
  33.3 5.4 %collective-permute-done.3 = bf16[128,2176]{1,0:T(8,128)(2,1)S(1)} collective-permute-done((bf16[128,2176]{1,0:T(8,128)(2,1)S(1)}, bf16[128,2176]{1,0:T(8,128)(2,1)S(1)}, u32[]{:S(2)}, u32[]{:S(2)}) %collective-permute-start.3) | collective-permute-done | bytes 557088 | tf_op jit(solution)/shard_map/ppermute | solution.py:65
  38.9 1.4 %copy-done.1 = bf16[512,2176]{1,0:T(8,128)(2,1)} copy-done((bf16[512,2176]{1,0:T(8,128)(2,1)}, bf16[512,2176]{1,0:T(8,128)(2,1)S(1)}, u32[]{:S(2)}) %copy-start.1) | copy-done | bytes 2228248
  40.2 1.0 copy-done.3
  41.2 1.5 %collective-permute-start.13 = (bf16[128,2176]{1,0:T(8,128)(2,1)}, bf16[128,2176]{1,0:T(8,128)(2,1)}, u32[]{:S(2)}, u32[]{:S(2)}) collective-permute-start(bf16[128,2176]{1,0:T(8,128)(2,1)} %pad_maximum_fusion.2), channel_id=1, source_target_pairs={{0,2},{2,0},{1,3},{3,1},{4,6},{6,4},{5,7},{7,5},{8,10},{10,8},{9,1... | collective-permute-start | bytes 1671176 | tf_op jit(solution)/shard_map/ppermute | solution.py:65
  42.7 1.2 %constant_dynamic-update-slice_fusion.13 = bf16[512,2176]{1,0:T(8,128)(2,1)S(1)} fusion(bf16[128,2176]{1,0:T(8,128)(2,1)} %pad_maximum_fusion.2), kind=kLoop, calls=%fused_computation.64 | loop fusion | bytes 1114112
  44.0 10.7 %collective-permute-done.13 = bf16[128,2176]{1,0:T(8,128)(2,1)} collective-permute-done((bf16[128,2176]{1,0:T(8,128)(2,1)}, bf16[128,2176]{1,0:T(8,128)(2,1)}, u32[]{:S(2)}, u32[]{:S(2)}) %collective-permute-start.13) | collective-permute-done | bytes 557088 | tf_op jit(solution)/shard_map/ppermute | solution.py:65
  54.7 1.3 %pad_maximum_fusion = bf16[256,2176]{1,0:T(8,128)(2,1)S(1)} fusion(bf16[128,2176]{1,0:T(8,128)(2,1)} %collective-permute-done.13, bf16[128,2176]{1,0:T(8,128)(2,1)} %pad_maximum_fusion.2), kind=kLoop, calls=%fused_computation.22 | loop fusion | flops 2228224 | bytes 2228224 | tf_op jit(solution)/shard_map/concatenate | solution.py:66
  56.1 1.1 constant_dynamic-update-slice_fusion.12
  57.4 5.7 %fusion.2 = f32[512,1536]{1,0:T(8,128)S(1)} fusion(bf16[1,2048,1536]{2,1,0:T(8,128)(2,1)} %param.10, bf16[512,2176]{1,0:T(8,128)(2,1)S(1)} %constant_dynamic-update-slice_fusion.5), kind=kOutput, calls=%fused_computation.2 | convolution fusion | flops 3221225472 | bytes 11534336 | tf_op jit(solution)/shard_map/dot_general | solution.py:9
  63.2 0.1 constant_dynamic-update-slice_fusion.11
  63.4 3.4 %fusion = f32[512,1536]{1,0:T(8,128)S(1)} fusion(bf16[1,2048,1536]{2,1,0:T(8,128)(2,1)S(1)} %bitcast.19, bf16[512,2176]{1,0:T(8,128)(2,1)S(1)} %constant_dynamic-update-slice_fusion.11), kind=kOutput, calls=%fused_computation | convolution fusion | flops 3221225472 | bytes 11534336 | tf_op jit(solution)/shard_map/dot_general | solution.py:9
  66.8 0.5 fusion.35
  67.3 1.8 %convert_multiply_fusion.1 = f32[512,2048]{1,0:T(8,128)S(1)} fusion(bf16[1,768,2048]{2,1,0:T(8,128)(2,1)S(1)} %copy-done, f32[512]{0:T(512)S(1)} %get-tuple-element.9, f32[512,1536]{1,0:T(8,128)S(1)} %fusion.2), kind=kOutput, calls=%fused_computation.5 | convolution fusion | flops 1616117760 | bytes 10487808 | tf_op jit(solution)/shard_map/dot_general | solution.py:11
  69.3 0.6 collective-permute-start.5
  69.9 1.8 %convert_multiply_fusion = f32[512,2048]{1,0:T(8,128)S(1)} fusion(bf16[1,768,2048]{2,1,0:T(8,128)(2,1)S(1)} %copy-done, f32[512]{0:T(512)S(1)} %get-tuple-element.10, f32[512,1536]{1,0:T(8,128)S(1)} %fusion), kind=kOutput, calls=%fused_computation.4 | convolution fusion | flops 1616117760 | bytes 10487808 | tf_op jit(solution)/shard_map/dot_general | solution.py:11
  72.0 0.2 collective-permute-done.5
  72.2 0.3 slice_add_fusion.1
  72.6 1.6 %collective-permute-start.6 = (bf16[128,2048]{1,0:T(8,128)(2,1)S(1)}, bf16[128,2048]{1,0:T(8,128)(2,1)S(1)}, u32[]{:S(2)}, u32[]{:S(2)}) collective-permute-start(bf16[128,2048]{1,0:T(8,128)(2,1)S(1)} %split.127), channel_id=1, source_target_pairs={{0,2},{2,0},{1,3},{3,1},{4,6},{6,4},{5,7},{7,5},{8,10},{10,8},{9,1... | collective-permute-start | bytes 1572872 | tf_op jit(solution)/shard_map/ppermute | solution.py:74
  74.1 0.5 collective-permute-done.15
  74.6 0.3 slice_add_fusion
  75.0 1.6 %collective-permute-start.16 = (bf16[128,2048]{1,0:T(8,128)(2,1)S(1)}, bf16[128,2048]{1,0:T(8,128)(2,1)S(1)}, u32[]{:S(2)}, u32[]{:S(2)}) collective-permute-start(bf16[128,2048]{1,0:T(8,128)(2,1)S(1)} %split.126), channel_id=1, source_target_pairs={{0,2},{2,0},{1,3},{3,1},{4,6},{6,4},{5,7},{7,5},{8,10},{10,8},{9,1... | collective-permute-start | bytes 1572872 | tf_op jit(solution)/shard_map/ppermute | solution.py:74
  76.6 10.9 %collective-permute-done.6 = bf16[128,2048]{1,0:T(8,128)(2,1)S(1)} collective-permute-done((bf16[128,2048]{1,0:T(8,128)(2,1)S(1)}, bf16[128,2048]{1,0:T(8,128)(2,1)S(1)}, u32[]{:S(2)}, u32[]{:S(2)}) %collective-permute-start.6) | collective-permute-done | bytes 524320 | tf_op jit(solution)/shard_map/ppermute | solution.py:74
  87.5 0.1 fusion.39
  87.6 1.4 %collective-permute-start.7 = (bf16[32,2048]{1,0:T(8,128)(2,1)S(1)}, bf16[32,2048]{1,0:T(8,128)(2,1)S(1)}, u32[]{:S(2)}, u32[]{:S(2)}) collective-permute-start(bf16[32,2048]{1,0:T(8,128)(2,1)S(1)} %get-tuple-element.17), channel_id=1, source_target_pairs={{0,12},{4,0},{8,4},{12,8},{1,13},{5,1},{9,5},{13,9},{2,14},{6,2},{... | collective-permute-start | bytes 393224 | tf_op jit(solution)/shard_map/ppermute | solution.py:74
  89.1 0.9 collective-permute-start.9
  90.0 8.1 %collective-permute-done.16 = bf16[128,2048]{1,0:T(8,128)(2,1)S(1)} collective-permute-done((bf16[128,2048]{1,0:T(8,128)(2,1)S(1)}, bf16[128,2048]{1,0:T(8,128)(2,1)S(1)}, u32[]{:S(2)}, u32[]{:S(2)}) %collective-permute-start.16) | collective-permute-done | bytes 524320 | tf_op jit(solution)/shard_map/ppermute | solution.py:74
  98.1 0.2 fusion.40
  98.3 1.4 %collective-permute-start.17 = (bf16[32,2048]{1,0:T(8,128)(2,1)S(1)}, bf16[32,2048]{1,0:T(8,128)(2,1)S(1)}, u32[]{:S(2)}, u32[]{:S(2)}) collective-permute-start(bf16[32,2048]{1,0:T(8,128)(2,1)S(1)} %get-tuple-element.20), channel_id=1, source_target_pairs={{0,12},{4,0},{8,4},{12,8},{1,13},{5,1},{9,5},{13,9},{2,14},{6,2},{... | collective-permute-start | bytes 393224 | tf_op jit(solution)/shard_map/ppermute | solution.py:74
  99.7 0.9 collective-permute-start.19
  100.7 3.0 %collective-permute-done.17 = bf16[32,2048]{1,0:T(8,128)(2,1)S(1)} collective-permute-done((bf16[32,2048]{1,0:T(8,128)(2,1)S(1)}, bf16[32,2048]{1,0:T(8,128)(2,1)S(1)}, u32[]{:S(2)}, u32[]{:S(2)}) %collective-permute-start.17) | collective-permute-done | bytes 131104 | tf_op jit(solution)/shard_map/ppermute | solution.py:74
  103.7 7.6 %collective-permute-done.18 = bf16[32,2048]{1,0:T(8,128)(2,1)S(1)} collective-permute-done((bf16[32,2048]{1,0:T(8,128)(2,1)S(1)}, bf16[32,2048]{1,0:T(8,128)(2,1)S(1)}, u32[]{:S(2)}, u32[]{:S(2)}) %collective-permute-start.18) | collective-permute-done | bytes 131104 | tf_op jit(solution)/shard_map/ppermute | solution.py:74
  111.3 0.7 pad_maximum_fusion.3
  (47 shorter events, 1.6 us)
Async XLA Ops:
  0.0 67.3 %copy-start = (bf16[1,768,2048]{2,1,0:T(8,128)(2,1)S(1)}, bf16[1,768,2048]{2,1,0:T(8,128)(2,1)}, u32[]{:S(2)}) copy-start(bf16[1,768,2048]{2,1,0:T(8,128)(2,1)} %param.11) | copy-start | bytes 9437188
  3.9 9.8 %collective-permute-start = (bf16[32,2176]{1,0:T(8,128)(2,1)S(1)}, bf16[32,2176]{1,0:T(8,128)(2,1)S(1)}, u32[]{:S(2)}, u32[]{:S(2)}) collective-permute-start(bf16[32,2176]{1,0:T(8,128)(2,1)S(1)} %get-tuple-element.26), channel_id=1, source_target_pairs={{0,4},{4,8},{8,12},{12,0},{1,5},{5,9},{9,13},{13,1},{2,6},{6,10},{... | collective-permute-start | bytes 417800 | tf_op jit(solution)/shard_map/ppermute | solution.py:65
  7.0 11.8 %collective-permute-start.1 = (bf16[32,2176]{1,0:T(8,128)(2,1)S(1)}, bf16[32,2176]{1,0:T(8,128)(2,1)S(1)}, u32[]{:S(2)}, u32[]{:S(2)}) collective-permute-start(bf16[32,2176]{1,0:T(8,128)(2,1)S(1)} %get-tuple-element.26), channel_id=1, source_target_pairs={{0,8},{4,12},{8,0},{12,4},{1,9},{5,13},{9,1},{13,5},{2,10},{6,14},... | collective-permute-start | bytes 417800 | tf_op jit(solution)/shard_map/ppermute | solution.py:65
  9.6 9.2 %collective-permute-start.2 = (bf16[32,2176]{1,0:T(8,128)(2,1)S(1)}, bf16[32,2176]{1,0:T(8,128)(2,1)S(1)}, u32[]{:S(2)}, u32[]{:S(2)}) collective-permute-start(bf16[32,2176]{1,0:T(8,128)(2,1)S(1)} %get-tuple-element.26), channel_id=1, source_target_pairs={{0,12},{4,0},{8,4},{12,8},{1,13},{5,1},{9,5},{13,9},{2,14},{6,2},{... | collective-permute-start | bytes 417800 | tf_op jit(solution)/shard_map/ppermute | solution.py:65
  18.8 8.8 %collective-permute-start.10 = (bf16[32,2176]{1,0:T(8,128)(2,1)S(1)}, bf16[32,2176]{1,0:T(8,128)(2,1)S(1)}, u32[]{:S(2)}, u32[]{:S(2)}) collective-permute-start(bf16[32,2176]{1,0:T(8,128)(2,1)S(1)} %get-tuple-element.7), channel_id=1, source_target_pairs={{0,4},{4,8},{8,12},{12,0},{1,5},{5,9},{9,13},{13,1},{2,6},{6,10},{... | collective-permute-start | bytes 417800 | tf_op jit(solution)/shard_map/ppermute | solution.py:65
  22.3 10.2 %collective-permute-start.11 = (bf16[32,2176]{1,0:T(8,128)(2,1)S(1)}, bf16[32,2176]{1,0:T(8,128)(2,1)S(1)}, u32[]{:S(2)}, u32[]{:S(2)}) collective-permute-start(bf16[32,2176]{1,0:T(8,128)(2,1)S(1)} %get-tuple-element.7), channel_id=1, source_target_pairs={{0,8},{4,12},{8,0},{12,4},{1,9},{5,13},{9,1},{13,5},{2,10},{6,14},... | collective-permute-start | bytes 417800 | tf_op jit(solution)/shard_map/ppermute | solution.py:65
  23.9 8.5 %collective-permute-start.12 = (bf16[32,2176]{1,0:T(8,128)(2,1)S(1)}, bf16[32,2176]{1,0:T(8,128)(2,1)S(1)}, u32[]{:S(2)}, u32[]{:S(2)}) collective-permute-start(bf16[32,2176]{1,0:T(8,128)(2,1)S(1)} %get-tuple-element.7), channel_id=1, source_target_pairs={{0,12},{4,0},{8,4},{12,8},{1,13},{5,1},{9,5},{13,9},{2,14},{6,2},{... | collective-permute-start | bytes 417800 | tf_op jit(solution)/shard_map/ppermute | solution.py:65
  24.7 14.0 %collective-permute-start.3 = (bf16[128,2176]{1,0:T(8,128)(2,1)S(1)}, bf16[128,2176]{1,0:T(8,128)(2,1)S(1)}, u32[]{:S(2)}, u32[]{:S(2)}) collective-permute-start(bf16[128,2176]{1,0:T(8,128)(2,1)S(1)} %pad_maximum_fusion.1), channel_id=1, source_target_pairs={{0,2},{2,0},{1,3},{3,1},{4,6},{6,4},{5,7},{7,5},{8,10},{10,8},{9,1... | collective-permute-start | bytes 1671176 | tf_op jit(solution)/shard_map/ppermute | solution.py:65
  38.8 1.4 %copy-start.1 = (bf16[512,2176]{1,0:T(8,128)(2,1)}, bf16[512,2176]{1,0:T(8,128)(2,1)S(1)}, u32[]{:S(2)}) copy-start(bf16[512,2176]{1,0:T(8,128)(2,1)S(1)} %get-tuple-element.16) | copy-start | bytes 6684676
  40.2 1.0 copy-start.3
  41.2 13.4 %collective-permute-start.13 = (bf16[128,2176]{1,0:T(8,128)(2,1)}, bf16[128,2176]{1,0:T(8,128)(2,1)}, u32[]{:S(2)}, u32[]{:S(2)}) collective-permute-start(bf16[128,2176]{1,0:T(8,128)(2,1)} %pad_maximum_fusion.2), channel_id=1, source_target_pairs={{0,2},{2,0},{1,3},{3,1},{4,6},{6,4},{5,7},{7,5},{8,10},{10,8},{9,1... | collective-permute-start | bytes 1671176 | tf_op jit(solution)/shard_map/ppermute | solution.py:65
  42.7 14.5 %collective-permute-start.4 = (bf16[256,2176]{1,0:T(8,128)(2,1)}, bf16[256,2176]{1,0:T(8,128)(2,1)S(1)}, u32[]{:S(2)}, u32[]{:S(2)}) collective-permute-start(bf16[256,2176]{1,0:T(8,128)(2,1)} %copy-done.3), channel_id=1, source_target_pairs={{0,1},{1,0},{2,3},{3,2},{4,5},{5,4},{6,7},{7,6},{8,9},{9,8},{10,11... | collective-permute-start | bytes 3342344 | tf_op jit(solution)/shard_map/ppermute | solution.py:65
  42.7 14.5 %copy-start.2 = (bf16[512,2176]{1,0:T(8,128)(2,1)S(1)}, bf16[512,2176]{1,0:T(8,128)(2,1)}, u32[]{:S(2)}) copy-start(bf16[512,2176]{1,0:T(8,128)(2,1)} %copy-done.1) | copy-start | bytes 6684676
  56.0 7.2 %collective-permute-start.14 = (bf16[256,2176]{1,0:T(8,128)(2,1)S(1)}, bf16[256,2176]{1,0:T(8,128)(2,1)S(1)}, u32[]{:S(2)}, u32[]{:S(2)}) collective-permute-start(bf16[256,2176]{1,0:T(8,128)(2,1)S(1)} %pad_maximum_fusion), channel_id=1, source_target_pairs={{0,1},{1,0},{2,3},{3,2},{4,5},{5,4},{6,7},{7,6},{8,9},{9,8},{10,11... | collective-permute-start | bytes 3342344 | tf_op jit(solution)/shard_map/ppermute | solution.py:65
  57.2 6.1 %slice-start = ((s8[6291456]{0:T(1024)(128)(4,1)}), s8[4194304]{0:T(1024)(128)(4,1)S(1)}, s32[]{:S(2)}) async-start(s8[6291456]{0:T(1024)(128)(4,1)} %bitcast.18), calls=%async_computation | async-start | bytes 8388608
  57.4 5.9 %slice-start.1 = ((s8[6291456]{0:T(1024)(128)(4,1)}), s8[2097152]{0:T(1024)(128)(4,1)S(1)}, s32[]{:S(2)}) async-start(s8[6291456]{0:T(1024)(128)(4,1)} %bitcast.18), calls=%async_computation.1 | async-start | bytes 4194304
  69.3 2.8 %collective-permute-start.5 = (bf16[256,2048]{1,0:T(8,128)(2,1)S(1)}, bf16[256,2048]{1,0:T(8,128)(2,1)S(1)}, u32[]{:S(2)}, u32[]{:S(2)}) collective-permute-start(bf16[256,2048]{1,0:T(8,128)(2,1)S(1)} %split.125), channel_id=1, source_target_pairs={{0,1},{1,0},{2,3},{3,2},{4,5},{5,4},{6,7},{7,6},{8,9},{9,8},{10,11... | collective-permute-start | bytes 3145736 | tf_op jit(solution)/shard_map/ppermute | solution.py:74
  71.9 2.7 %collective-permute-start.15 = (bf16[256,2048]{1,0:T(8,128)(2,1)S(1)}, bf16[256,2048]{1,0:T(8,128)(2,1)S(1)}, u32[]{:S(2)}, u32[]{:S(2)}) collective-permute-start(bf16[256,2048]{1,0:T(8,128)(2,1)S(1)} %split.124), channel_id=1, source_target_pairs={{0,1},{1,0},{2,3},{3,2},{4,5},{5,4},{6,7},{7,6},{8,9},{9,8},{10,11... | collective-permute-start | bytes 3145736 | tf_op jit(solution)/shard_map/ppermute | solution.py:74
  72.6 14.9 %collective-permute-start.6 = (bf16[128,2048]{1,0:T(8,128)(2,1)S(1)}, bf16[128,2048]{1,0:T(8,128)(2,1)S(1)}, u32[]{:S(2)}, u32[]{:S(2)}) collective-permute-start(bf16[128,2048]{1,0:T(8,128)(2,1)S(1)} %split.127), channel_id=1, source_target_pairs={{0,2},{2,0},{1,3},{3,1},{4,6},{6,4},{5,7},{7,5},{8,10},{10,8},{9,1... | collective-permute-start | bytes 1572872 | tf_op jit(solution)/shard_map/ppermute | solution.py:74
  75.0 23.1 %collective-permute-start.16 = (bf16[128,2048]{1,0:T(8,128)(2,1)S(1)}, bf16[128,2048]{1,0:T(8,128)(2,1)S(1)}, u32[]{:S(2)}, u32[]{:S(2)}) collective-permute-start(bf16[128,2048]{1,0:T(8,128)(2,1)S(1)} %split.126), channel_id=1, source_target_pairs={{0,2},{2,0},{1,3},{3,1},{4,6},{6,4},{5,7},{7,5},{8,10},{10,8},{9,1... | collective-permute-start | bytes 1572872 | tf_op jit(solution)/shard_map/ppermute | solution.py:74
  87.6 12.1 %collective-permute-start.7 = (bf16[32,2048]{1,0:T(8,128)(2,1)S(1)}, bf16[32,2048]{1,0:T(8,128)(2,1)S(1)}, u32[]{:S(2)}, u32[]{:S(2)}) collective-permute-start(bf16[32,2048]{1,0:T(8,128)(2,1)S(1)} %get-tuple-element.17), channel_id=1, source_target_pairs={{0,12},{4,0},{8,4},{12,8},{1,13},{5,1},{9,5},{13,9},{2,14},{6,2},{... | collective-permute-start | bytes 393224 | tf_op jit(solution)/shard_map/ppermute | solution.py:74
  89.1 11.5 %collective-permute-start.8 = (bf16[32,2048]{1,0:T(8,128)(2,1)S(1)}, bf16[32,2048]{1,0:T(8,128)(2,1)S(1)}, u32[]{:S(2)}, u32[]{:S(2)}) collective-permute-start(bf16[32,2048]{1,0:T(8,128)(2,1)S(1)} %get-tuple-element.19), channel_id=1, source_target_pairs={{0,8},{4,12},{8,0},{12,4},{1,9},{5,13},{9,1},{13,5},{2,10},{6,14},... | collective-permute-start | bytes 393224 | tf_op jit(solution)/shard_map/ppermute | solution.py:74
  89.1 11.5 %collective-permute-start.9 = (bf16[32,2048]{1,0:T(8,128)(2,1)S(1)}, bf16[32,2048]{1,0:T(8,128)(2,1)S(1)}, u32[]{:S(2)}, u32[]{:S(2)}) collective-permute-start(bf16[32,2048]{1,0:T(8,128)(2,1)S(1)} %get-tuple-element.18), channel_id=1, source_target_pairs={{0,4},{4,8},{8,12},{12,0},{1,5},{5,9},{9,13},{13,1},{2,6},{6,10},{... | collective-permute-start | bytes 393224 | tf_op jit(solution)/shard_map/ppermute | solution.py:74
  98.3 5.4 %collective-permute-start.17 = (bf16[32,2048]{1,0:T(8,128)(2,1)S(1)}, bf16[32,2048]{1,0:T(8,128)(2,1)S(1)}, u32[]{:S(2)}, u32[]{:S(2)}) collective-permute-start(bf16[32,2048]{1,0:T(8,128)(2,1)S(1)} %get-tuple-element.20), channel_id=1, source_target_pairs={{0,12},{4,0},{8,4},{12,8},{1,13},{5,1},{9,5},{13,9},{2,14},{6,2},{... | collective-permute-start | bytes 393224 | tf_op jit(solution)/shard_map/ppermute | solution.py:74
  99.7 11.5 %collective-permute-start.18 = (bf16[32,2048]{1,0:T(8,128)(2,1)S(1)}, bf16[32,2048]{1,0:T(8,128)(2,1)S(1)}, u32[]{:S(2)}, u32[]{:S(2)}) collective-permute-start(bf16[32,2048]{1,0:T(8,128)(2,1)S(1)} %get-tuple-element.22), channel_id=1, source_target_pairs={{0,8},{4,12},{8,0},{12,4},{1,9},{5,13},{9,1},{13,5},{2,10},{6,14},... | collective-permute-start | bytes 393224 | tf_op jit(solution)/shard_map/ppermute | solution.py:74
  99.7 11.5 %collective-permute-start.19 = (bf16[32,2048]{1,0:T(8,128)(2,1)S(1)}, bf16[32,2048]{1,0:T(8,128)(2,1)S(1)}, u32[]{:S(2)}, u32[]{:S(2)}) collective-permute-start(bf16[32,2048]{1,0:T(8,128)(2,1)S(1)} %get-tuple-element.21), channel_id=1, source_target_pairs={{0,4},{4,8},{8,12},{12,0},{1,5},{5,9},{9,13},{13,1},{2,6},{6,10},{... | collective-permute-start | bytes 393224 | tf_op jit(solution)/shard_map/ppermute | solution.py:74
